TPU v7x, 32 devices: a whole 2x2x4 slice. The times are simulated.
32 devices in a mesh: slab: 4 (over z), tx: 4 (over y, x), ty: 2 (over core).
Axes of the slice: x: 2, y: 2, z: 4, core: 2. Of those that a mesh axis runs over, the one named last changes fastest.
Arguments:
- forcing: float32 [2, 2, 2, 256, 16, 256], P(None, None, None, 'slab', 'tx', 'ty'), may hold values from -4 to 4
- wavenumber_sq: float32 [256, 16, 256], P('slab', 'tx', 'ty'), may hold values from 1.2 to 3.6
- line_inverse: float32 [4, 4, 2, 64, 64], P('slab'), may hold values from -0.15 to 0.45
- column_class: int32 [4, 16, 256], P('slab', 'tx', 'ty'), may hold values from 0 to 3
- batch_order: int32 [2, 4, 2], P(None, 'slab'), may hold values from 0 to 1, each once within a row
- pending_trace: float32 [2, 2, 4, 16, 256], P(None, None, 'slab', 'tx', 'ty'), may hold values from -6 to 6
Outputs:
- solutions: float32 [2, 2, 2, 256, 16, 256], P(None, None, None, 'slab', 'tx', 'ty')
- final_trace: float32 [2, 2, 4, 16, 256], P(None, None, 'slab', 'tx', 'ty')
Inputs may be any that keep to these rules, and one draw needn't show every extreme that they name: `batch_order`: each row names every slot once.
All inputs are finite; a program needn't handle non-finite values.
Results may differ from a plain program's by a relative error of at most 0.00028.
Values sent between devices are 32-bit elements; how exact they have to be, the bound alone decides.
No kernel may reach another device: no remote copies, remote signals or barrier semaphores. Data moves between devices by JAX's collectives and lax.ppermute only.
A program may use at most 128 MiB of HBM per device.

v0:
```python
import functools

import jax
import jax.numpy as jnp
from jax import lax
from jax.experimental import pallas as pl
from jax.experimental.pallas import tpu as pltpu
from jax.sharding import PartitionSpec as P

CORR = 3
TICKS = 2


DAMPING = 0.25
PRECISE = lax.Precision.HIGHEST


def fetch(block, axes, offsets):
    sizes = [lax.axis_size(a) for a in axes]
    pairs = []
    total = 1
    for s in sizes:
        total *= s
    for linear in range(total):
        coords = []
        rest = linear
        for s in reversed(sizes):
            coords.append(rest % s)
            rest //= s
        coords = coords[::-1]
        source = [c + d for c, d in zip(coords, offsets)]
        if all(0 <= c < s for c, s in zip(source, sizes)):
            src_linear = 0
            for c, s in zip(source, sizes):
                src_linear = src_linear * s + c
            pairs.append((src_linear, linear))
    if len(axes) == 1:
        return lax.ppermute(block, axes[0], pairs)
    return lax.ppermute(block, tuple(axes), pairs)


def with_halo(block, width, lead_axes=(), lead_offsets=()):
    nx, ny = block.shape[-2], block.shape[-1]
    rows = {-1: slice(nx - width, nx), 0: slice(0, nx), 1: slice(0, width)}
    cols = {-1: slice(ny - width, ny), 0: slice(0, ny), 1: slice(0, width)}
    bands = []
    for dx in (-1, 0, 1):
        parts = []
        for dy in (-1, 0, 1):
            piece = block[..., rows[dx], cols[dy]]
            if dx == 0 and dy == 0 and not lead_axes:
                parts.append(piece)
            else:
                parts.append(
                    fetch(piece, tuple(lead_axes) + ("tx", "ty"), tuple(lead_offsets) + (dx, dy))
                )
        bands.append(jnp.concatenate(parts, axis=-1))
    return jnp.concatenate(bands, axis=-2)


def tick_kernel(rhs_ref, dr_ref, di_ref, hot_ref, ins_ref, blk_ref, out_ref, *, row, depth):
    nsrc, rows, cols = rhs_ref.shape
    classes = hot_ref.shape[0]
    dr = dr_ref[...]
    di = di_ref[...]
    ins = ins_ref[...]
    hots = [hot_ref[k : k + 1, :] for k in range(classes)]
    blks = [blk_ref[k] for k in range(classes)]
    zrow = lax.broadcasted_iota(jnp.int32, (rows, cols), 0) % depth
    top = zrow == 0
    bottom = zrow == depth - 1

    def precond(x):
        acc = None
        for k in range(classes):
            t = jnp.dot(blks[k], x * hots[k], precision=PRECISE, preferred_element_type=jnp.float32)
            acc = t if acc is None else acc + t
        return acc

    def apply_a(u):
        real = u[:depth]
        imaginary = u[depth:]
        diagonal = jnp.concatenate(
            [dr * real - di * imaginary, dr * imaginary + di * real], axis=0
        )
        down = jnp.where(top, 0.0, pltpu.roll(u, 1, 0))
        up = jnp.where(bottom, 0.0, pltpu.roll(u, rows - 1, 0))
        beside = up + down
        beside = beside + pltpu.roll(u, cols - row, 1) + pltpu.roll(u, row, 1)
        beside = beside + pltpu.roll(u, cols - 1, 1) + pltpu.roll(u, 1, 1)
        return diagonal - beside

    for s in range(nsrc):
        rhs = rhs_ref[s]
        u = precond(rhs)
        for _ in range(CORR):
            u = u + precond(ins * (rhs - apply_a(u)))
        out_ref[s] = u


def run_tick(rhs, dr, di, hot, ins, blocks, row, depth):
    nsrc, rows, cols = rhs.shape
    classes = hot.shape[0]
    flops = nsrc * (CORR + 1) * classes * 2 * rows * rows * cols
    return pl.pallas_call(
        functools.partial(tick_kernel, row=row, depth=depth),
        out_shape=jax.ShapeDtypeStruct(rhs.shape, jnp.float32),
        in_specs=[pl.BlockSpec(memory_space=pltpu.VMEM)] * 6,
        out_specs=pl.BlockSpec(memory_space=pltpu.VMEM),
        cost_estimate=pl.CostEstimate(
            flops=flops, transcendentals=0, bytes_accessed=4 * (2 * rhs.size + 4 * dr.size)
        ),
    )(rhs, dr, di, hot, ins, blocks)


def block_matrix(inverse):
    real = inverse[:, 0]
    imaginary = inverse[:, 1]
    upper = jnp.concatenate([real, -imaginary], axis=2)
    lower = jnp.concatenate([imaginary, real], axis=2)
    return jnp.concatenate([upper, lower], axis=1)


def per_device(forcing, wavenumber_sq, line_inverse, column_class, batch_order, pending_trace):
    width = CORR
    ticks, nsrc, two, depth, nx, ny = forcing.shape
    classes = line_inverse.shape[1]
    ntx = lax.axis_size("tx")
    nty = lax.axis_size("ty")
    ex, ey = nx + 2 * width, ny + 2 * width
    cols = ex * ey

    packed = jnp.concatenate(
        [
            forcing.reshape(-1, nx, ny),
            wavenumber_sq,
            pending_trace.reshape(-1, nx, ny),
            column_class[0][None].astype(jnp.float32),
        ],
        axis=0,
    )
    extended = with_halo(packed, width)
    nf = ticks * nsrc * two * depth
    npend = nsrc * two
    forcing_e = extended[:nf].reshape(ticks, nsrc, two, depth, cols)
    wavenumber_e = extended[nf : nf + depth].reshape(depth, cols)
    pending_e = extended[nf + depth : nf + depth + npend].reshape(nsrc, two, cols)
    class_e = extended[nf + depth + npend].reshape(cols).astype(jnp.int32)

    padded = -(-cols // 128) * 128

    def flat(x):
        return jnp.pad(x, [(0, 0)] * (x.ndim - 1) + [(0, padded - cols)])

    gx = lax.axis_index("tx") * nx - width + jnp.arange(ex)
    gy = lax.axis_index("ty") * ny - width + jnp.arange(ey)
    inside = ((gx >= 0) & (gx < nx * ntx))[:, None] & ((gy >= 0) & (gy < ny * nty))[None, :]
    inside = flat(inside.reshape(1, cols).astype(jnp.float32))

    blocks = block_matrix(line_inverse[0])
    onehot = flat(
        (class_e[None, :] == jnp.arange(classes, dtype=jnp.int32)[:, None]).astype(jnp.float32)
    )
    diag_real = flat(6.0 - wavenumber_e)
    diag_imaginary = flat(-DAMPING * wavenumber_e)
    orders = batch_order[:, 0]

    incoming = pending_e
    solutions = []
    trace = None
    for tick in range(ticks):
        rhs = jnp.take(forcing_e[tick], orders[tick], axis=0)
        rhs = rhs.at[:, :, 0].add(incoming)
        rhs = flat(rhs).reshape(nsrc, two * depth, padded)
        field = run_tick(rhs, diag_real, diag_imaginary, onehot, inside, blocks, ey, depth)
        field = field.reshape(nsrc, two, depth, padded)[..., :cols]
        tile = field.reshape(nsrc, two, depth, ex, ey)[:, :, :, width : width + nx, width : width + ny]
        solutions.append(tile)
        trace = tile[:, :, depth - 1]
        if tick + 1 < ticks:
            incoming = with_halo(trace, width, ("slab",), (-1,)).reshape(nsrc, two, cols)
    return (jnp.stack(solutions, axis=0), trace[:, :, None])


def solution(mesh):
    in_specs = (
        P(None, None, None, "slab", "tx", "ty"),
        P("slab", "tx", "ty"),
        P("slab", None, None, None, None),
        P("slab", "tx", "ty"),
        P(None, "slab", None),
        P(None, None, "slab", "tx", "ty"),
    )
    out_specs = (P(None, None, None, "slab", "tx", "ty"), P(None, None, "slab", "tx", "ty"))
    return jax.shard_map(
        per_device, mesh=mesh, in_specs=in_specs, out_specs=out_specs, check_vma=False
    )
```

profile of v0, /device:TPU:12, one launch (start us, length us, event | category | flops | bytes accessed | tf_op | source)
XLA Modules:
  0.0 356.1 jit_solution(3090460385776717756)
XLA Ops:
  2.9 1.4 copy.87
  4.4 1.3 fusion.4
  5.8 3.4 collective-permute-start.1
  9.2 3.3 collective-permute-start.6
  12.5 2.1 fusion.3
  14.6 2.1 copy.100
  18.0 2.1 copy.99
  20.1 3.1 collective-permute-start.5
  24.2 1.8 collective-permute-start
  28.4 1.4 fusion.5
  29.8 1.7 copy.95
  32.9 1.3 collective-permute-start.4
  34.2 14.2 %collective-permute-done.5 = f32[581,3,3]{0,2,1:T(4,128)S(1)} collective-permute-done((f32[581,3,3]{0,2,1:T(4,128)}, f32[581,3,3]{0,2,1:T(4,128)S(1)}, u32[]{:S(2)}, u32[]{:S(2)}) %collective-permute-start.5) | collective-permute-done | bytes 20948 | tf_op jit(solution)/shard_map/ppermute | solution.py:39
  48.4 2.7 collective-permute-start.3
  51.2 1.5 collective-permute-start.2
  57.4 1.3 copy.94
  60.3 8.8 %maximum_maximum_fusion = f32[581,10,134]{2,0,1:T(8,128)S(1)} fusion(f32[581,3,3]{2,0,1:T(8,128)} %copy.102, f32[581,3,128]{2,0,1:T(8,128)} %collective-permute-done.6, f32[581,3,3]{2,0,1:T(8,128)} %copy.101, f32[581,4,3]{2,0,1:T(8,128)S(1)} %copy.98, f32[1,4,128]{2,0,1:T(1,128)S(1)} %bitcast.45, f32[4,4,128]{2,0,1:T(4,128)S(1)} %copy.89, ...), kind=kLoop, calls=%fused_computation.2 | loop fusion | flops 8563940 | bytes 6228320 | tf_op jit(solution)/shard_map/concatenate | solution.py:58
  70.1 2.1 fusion.2
  73.0 3.0 copy.103
  76.0 2.5 copy.120
  78.4 2.3 reshape.202
  80.7 1.4 copy.119
  82.1 1.6 reshape.201
  83.7 1.8 pad.32.di_ref
  86.2 4.1 %squeeze.25 = f32[2,2,64,1340]{2,1,0,3:T(2,128)} reshape(f32[256,10,134]{0,2,1:T(8,128)} %copy.103) | data formatting | bytes 2744320 | tf_op jit(solution)/shard_map/squeeze | solution.py:172
  90.3 1.8 copy.113
  92.2 4.2 %squeeze.30 = f32[2,2,64,1340]{2,1,0,3:T(2,128)} reshape(f32[256,10,134]{0,2,1:T(8,128)} %copy.113) | data formatting | bytes 2744320 | tf_op jit(solution)/shard_map/squeeze | solution.py:172
  96.3 3.5 copy.105
  99.9 5.7 %gather_fusion = f32[2,2,64,1340]{2,1,3,0:T(2,128)} fusion(f32[2,2,64,1340]{2,1,0,3:T(2,128)S(1)} %copy-done.2, s32[1024]{0:T(1024)S(1)} %pad_clamp_fusion.1), kind=kCustom, calls=%fused_computation.clone | custom fusion | bytes 2744328 | tf_op jit(solution)/shard_map/jit(_take)/gather | solution.py:172
  105.6 7.5 %gather_fusion.1 = f32[2,2,64,1340]{2,1,3,0:T(2,128)} fusion(f32[2,2,64,1340]{2,1,0,3:T(2,128)} %squeeze.30, s32[1024]{0:T(1024)} %pad_clamp_fusion), kind=kCustom, calls=%fused_computation.1.clone | custom fusion | bytes 2744328 | tf_op jit(solution)/shard_map/jit(_take)/gather | solution.py:172
  113.1 4.8 %broadcast_select_fusion = (f32[2,2,64,1340]{2,1,3,0:T(2,128)S(1)}, f32[2,2,64,1340]{2,1,3,0:T(2,128)S(1)}) fusion(f32[2,2,64,1340]{2,1,3,0:T(2,128)} %gather_fusion.1, pred[2]{0:T(512)(128)(4,1)S(1)} %copy-done.8, f32[2,2,64,1340]{2,1,3,0:T(2,128)} %gather_fusion, pred[2]{0:T(512)(128)(4,1)S(1)} %copy-done.7), kind=kLoop, calls=%fused_computation.5 | loop fusion | flops 686080 | bytes 5488644 | tf_op jit(solution)/shard_map/jit(_take)/select_n | solution.py:172
  118.0 1.6 copy-done
  119.5 2.8 slice_add_fusion.1
  122.3 43.9 %scatter-add.6 = f32[2,2,64,1340]{2,1,3,0:T(2,128)} dynamic-update-slice(f32[2,2,64,1340]{2,1,3,0:T(2,128)} %copy-done, f32[2,2,1,1340]{2,1,3,0:T(2,128)} %slice_add_fusion.1, s32[]{:T(128)} %constant.76.clone.1, s32[]{:T(128)} %constant.76.clone.1, s32[]{:T(128)} %constant.76.clone.1, s32[]{:T(128)} %constant.76.clone.1) | dynamic-update-slice | bytes 42884 | tf_op jit(solution)/shard_map/scatter-add | solution.py:173
  166.2 5.6 %copy.125 = f32[2,2,64,1340]{3,2,1,0:T(8,128)} copy(f32[2,2,64,1340]{2,1,3,0:T(2,128)} %scatter-add.6) | data formatting | bytes 2744320
  171.9 2.6 pad.30.clone
  174.4 33.2 %shard_map.77 = f32[2,128,1408]{2,1,0:T(8,128)} custom-call(f32[2,128,1408]{2,1,0:T(8,128)} %bitcast.42, f32[64,1408]{1,0:T(8,128)} %pad.31.dr_ref, f32[64,1408]{1,0:T(8,128)} %pad.32.di_ref, f32[4,1408]{1,0:T(4,128)} %pad_convert_fusion.1.hot_ref, f32[1,1408]{1,0:T(1,128)} %pad_convert_fusion.ins_ref, f32[4,128,128]{2,1,0:T(8,128)} %maximum_maximum_fusion.1.blk_ref), custom_call_target="tpu_custom_call" | custom-call | flops 1476395008 | bytes 4325376 | tf_op jit(solution)/shard_map/pallas_call | solution.py:105
  207.7 3.1 copy.123
  210.8 3.0 reshape.174
  213.7 1.9 slice_reduce_fusion
  215.7 3.5 collective-permute-start.12
  219.3 1.9 collective-permute-start.9
  221.2 7.0 %collective-permute-start.15 = (f32[2,2,3,128]{3,2,1,0:T(4,128)S(1)}, f32[2,2,3,128]{3,2,1,0:T(4,128)S(1)}, u32[]{:S(2)}, u32[]{:S(2)}) collective-permute-start(f32[2,2,3,128]{3,2,1,0:T(4,128)S(1)} %get-tuple-element.60), channel_id=1, source_target_pairs={{2,8},{3,9},{4,10},{5,11},{6,12},{7,13},{10,16},{11,17},{12,18},{1... | collective-permute-start | bytes 18440 | tf_op jit(solution)/shard_map/ppermute | solution.py:39
  228.2 1.3 collective-permute-start.8
  229.5 1.3 collective-permute-start.16
  230.8 4.8 %collective-permute-start.14 = (f32[2,2,3,3]{3,2,1,0:T(4,128)S(1)}, f32[2,2,3,3]{3,2,1,0:T(4,128)S(1)}, u32[]{:S(2)}, u32[]{:S(2)}) collective-permute-start(f32[2,2,3,3]{3,2,1,0:T(4,128)S(1)} %get-tuple-element.57), channel_id=1, source_target_pairs={{2,9},{4,11},{6,13},{10,17},{12,19},{14,21},{18,25},{20,27},{22,29}} | collective-permute-start | bytes 440 | tf_op jit(solution)/shard_map/ppermute | solution.py:39
  235.6 1.3 collective-permute-start.10
  236.9 3.6 %collective-permute-start.11 = (f32[2,2,4,3]{3,2,1,0:T(4,128)S(1)}, f32[2,2,4,3]{3,2,1,0:T(4,128)S(1)}, u32[]{:S(2)}, u32[]{:S(2)}) collective-permute-start(f32[2,2,4,3]{3,2,1,0:T(4,128)S(1)} %get-tuple-element.61), channel_id=1, source_target_pairs={{0,9},{2,11},{4,13},{6,15},{8,17},{10,19},{12,21},{14,23},{16,25},... | collective-permute-start | bytes 584 | tf_op jit(solution)/shard_map/ppermute | solution.py:39
  240.5 1.8 collective-permute-done.10
  242.4 1.3 collective-permute-start.13
  243.6 2.4 slice_bitcast_fusion.1
  246.0 1.3 collective-permute-done.13
  247.6 3.4 copy.114
  250.9 4.9 %slice_add_fusion = f32[2,2,1,1340]{2,1,3,0:T(2,128)} fusion(f32[2,2,1,1340]{2,1,3,0:T(2,128)} %copy.114, f32[2,2,64,1340]{2,1,3,0:T(2,128)S(1)} %get-tuple-element.65), kind=kLoop, calls=%fused_computation.3 | loop fusion | flops 5360 | bytes 64320 | tf_op jit(solution)/shard_map/add | solution.py:173
  255.8 48.3 %scatter-add.9 = f32[2,2,64,1340]{2,1,3,0:T(2,128)S(1)} dynamic-update-slice(f32[2,2,64,1340]{2,1,3,0:T(2,128)S(1)} %get-tuple-element.65, f32[2,2,1,1340]{2,1,3,0:T(2,128)} %slice_add_fusion, s32[]{:T(128)} %constant.76.clone.1, s32[]{:T(128)} %constant.76.clone.1, s32[]{:T(128)} %constant.76.clone.1, s32[]{:T(128)} %constant.76.clone.1) | dynamic-update-slice | bytes 42884 | tf_op jit(solution)/shard_map/scatter-add | solution.py:173
  304.1 4.4 %copy.126 = f32[2,2,64,1340]{3,2,1,0:T(8,128)} copy(f32[2,2,64,1340]{2,1,3,0:T(2,128)S(1)} %scatter-add.9) | data formatting | bytes 2744320
  308.5 2.6 pad.37.clone
  311.1 33.2 %shard_map.78 = f32[2,128,1408]{2,1,0:T(8,128)} custom-call(f32[2,128,1408]{2,1,0:T(8,128)} %bitcast.40, f32[64,1408]{1,0:T(8,128)} %pad.31.dr_ref, f32[64,1408]{1,0:T(8,128)} %pad.32.di_ref, f32[4,1408]{1,0:T(4,128)} %pad_convert_fusion.1.hot_ref, f32[1,1408]{1,0:T(1,128)} %pad_convert_fusion.ins_ref, f32[4,128,128]{2,1,0:T(8,128)} %maximum_maximum_fusion.1.blk_ref), custom_call_target="tpu_custom_call" | custom-call | flops 1476395008 | bytes 4325376 | tf_op jit(solution)/shard_map/pallas_call | solution.py:105
  344.3 2.0 copy.124
  346.3 1.6 reshape.178
  347.9 1.7 slice.223
  349.6 2.3 slice_bitcast_fusion
  352.9 1.4 pad_maximum_fusion
  354.3 1.6 copy.117
  (77 shorter events, 18.6 us)
Async XLA Ops:
  2.9 2.8 copy-start.5
  5.8 54.5 %collective-permute-start.1 = (f32[581,3,128]{2,0,1:T(8,128)}, f32[581,3,128]{2,0,1:T(8,128)}, u32[]{:S(2)}, u32[]{:S(2)}) collective-permute-start(f32[581,3,128]{2,0,1:T(8,128)} %get-tuple-element.49), channel_id=1, source_target_pairs={{0,2},{1,3},{2,4},{3,5},{4,6},{5,7},{8,10},{9,11},{10,12},{11,13},... | collective-permute-start | bytes 2677256 | tf_op jit(solution)/shard_map/ppermute | solution.py:39
  9.2 51.1 %collective-permute-start.6 = (f32[581,3,128]{2,0,1:T(8,128)}, f32[581,3,128]{2,0,1:T(8,128)}, u32[]{:S(2)}, u32[]{:S(2)}) collective-permute-start(f32[581,3,128]{2,0,1:T(8,128)} %get-tuple-element.50), channel_id=1, source_target_pairs={{2,0},{3,1},{4,2},{5,3},{6,4},{7,5},{10,8},{11,9},{12,10},{13,11},... | collective-permute-start | bytes 2677256 | tf_op jit(solution)/shard_map/ppermute | solution.py:39
  14.6 11.4 %copy-start.6 = (f32[1,4,2,64,64]{4,3,2,1,0:T(8,128)S(1)}, f32[1,4,2,64,64]{4,3,2,1,0:T(8,128)}, u32[]{:S(2)}) copy-start(f32[1,4,2,64,64]{4,3,2,1,0:T(8,128)} %param.14) | copy-start | bytes 393220
  14.6 11.6 %copy-start.11 = (s32[2,1,2]{2,1,0:T(1,128)S(1)}, s32[2,1,2]{2,1,0:T(1,128)}, u32[]{:S(2)}) copy-start(s32[2,1,2]{2,1,0:T(1,128)} %param.16) | copy-start | bytes 52
  16.7 16.1 %collective-permute-start.7 = (f32[581,3,3]{0,2,1:T(4,128)}, f32[581,3,3]{0,2,1:T(4,128)S(1)}, u32[]{:S(2)}, u32[]{:S(2)}) collective-permute-start(f32[581,3,3]{0,2,1:T(4,128)} %copy.100), channel_id=1, source_target_pairs={{3,0},{5,2},{7,4},{11,8},{13,10},{15,12},{19,16},{21,18},{23,20},{... | collective-permute-start | bytes 62756 | tf_op jit(solution)/shard_map/ppermute | solution.py:39
  20.1 28.3 %collective-permute-start.5 = (f32[581,3,3]{0,2,1:T(4,128)}, f32[581,3,3]{0,2,1:T(4,128)S(1)}, u32[]{:S(2)}, u32[]{:S(2)}) collective-permute-start(f32[581,3,3]{0,2,1:T(4,128)} %copy.99), channel_id=1, source_target_pairs={{2,1},{4,3},{6,5},{10,9},{12,11},{14,13},{18,17},{20,19},{22,21},{... | collective-permute-start | bytes 62756 | tf_op jit(solution)/shard_map/ppermute | solution.py:39
  24.2 27.0 %collective-permute-start = (f32[581,3,3]{0,2,1:T(4,128)}, f32[581,3,3]{0,2,1:T(4,128)S(1)}, u32[]{:S(2)}, u32[]{:S(2)}) collective-permute-start(f32[581,3,3]{0,2,1:T(4,128)} %copy.91), channel_id=1, source_target_pairs={{0,3},{2,5},{4,7},{8,11},{10,13},{12,15},{16,19},{18,21},{20,23},{... | collective-permute-start | bytes 62756 | tf_op jit(solution)/shard_map/ppermute | solution.py:39
  26.9 2.9 copy-start.10
  29.8 2.8 copy-start.4
  29.8 22.9 %copy-start.9 = (s32[2]{0:T(128)S(1)}, s32[2]{0:T(128)}, u32[]{:S(2)}) copy-start(s32[2]{0:T(128)} %get-tuple-element.64) | copy-start | bytes 28
  32.9 26.2 %collective-permute-start.4 = (f32[581,4,3]{0,1,2:T(4,128)}, f32[581,4,3]{0,1,2:T(4,128)}, u32[]{:S(2)}, u32[]{:S(2)}) collective-permute-start(f32[581,4,3]{0,1,2:T(4,128)} %copy.96), channel_id=1, source_target_pairs={{1,0},{3,2},{5,4},{7,6},{9,8},{11,10},{13,12},{15,14},{17,16},{19,... | collective-permute-start | bytes 83672 | tf_op jit(solution)/shard_map/ppermute | solution.py:39
  48.4 10.3 %collective-permute-start.3 = (f32[581,4,3]{0,1,2:T(4,128)S(1)}, f32[581,4,3]{0,1,2:T(4,128)S(1)}, u32[]{:S(2)}, u32[]{:S(2)}) collective-permute-start(f32[581,4,3]{0,1,2:T(4,128)S(1)} %copy.95), channel_id=1, source_target_pairs={{0,1},{2,3},{4,5},{6,7},{8,9},{10,11},{12,13},{14,15},{16,17},{18,... | collective-permute-start | bytes 83672 | tf_op jit(solution)/shard_map/ppermute | solution.py:39
  51.2 6.2 %collective-permute-start.2 = (f32[581,3,3]{0,2,1:T(4,128)S(1)}, f32[581,3,3]{0,2,1:T(4,128)S(1)}, u32[]{:S(2)}, u32[]{:S(2)}) collective-permute-start(f32[581,3,3]{0,2,1:T(4,128)S(1)} %copy.92), channel_id=1, source_target_pairs={{1,2},{3,4},{5,6},{9,10},{11,12},{13,14},{17,18},{19,20},{21,22},{... | collective-permute-start | bytes 62756 | tf_op jit(solution)/shard_map/ppermute | solution.py:39
  92.2 7.7 %copy-start.2 = (f32[2,2,64,1340]{2,1,0,3:T(2,128)S(1)}, f32[2,2,64,1340]{2,1,0,3:T(2,128)}, u32[]{:S(2)}) copy-start(f32[2,2,64,1340]{2,1,0,3:T(2,128)} %squeeze.25) | copy-start | bytes 4116484
  99.9 13.3 %copy-start.7 = (pred[2]{0:T(512)(128)(4,1)S(1)}, pred[2]{0:T(512)(128)(4,1)}, u32[]{:S(2)}) copy-start(pred[2]{0:T(512)(128)(4,1)} %get-tuple-element.37) | copy-start | bytes 10
  99.9 13.2 %copy-start.8 = (pred[2]{0:T(512)(128)(4,1)S(1)}, pred[2]{0:T(512)(128)(4,1)}, u32[]{:S(2)}) copy-start(pred[2]{0:T(512)(128)(4,1)} %get-tuple-element.63) | copy-start | bytes 10
  113.1 6.4 %copy-start.1 = (f32[2,2,1,1340]{2,1,3,0:T(2,128)S(1)}, f32[2,2,1,1340]{2,1,3,0:T(2,128)}, u32[]{:S(2)}) copy-start(f32[2,2,1,1340]{2,1,3,0:T(2,128)} %copy.105) | copy-start | bytes 64324
  117.9 1.6 copy-start
  215.7 31.6 %collective-permute-start.12 = (f32[2,2,4,128]{3,2,1,0:T(4,128)S(1)}, f32[2,2,4,128]{3,2,1,0:T(4,128)S(1)}, u32[]{:S(2)}, u32[]{:S(2)}) collective-permute-start(f32[2,2,4,128]{3,2,1,0:T(4,128)S(1)} %slice_reduce_fusion), channel_id=1, source_target_pairs={{0,8},{1,9},{2,10},{3,11},{4,12},{5,13},{6,14},{7,15},{8,16},{9,17... | collective-permute-start | bytes 24584 | tf_op jit(solution)/shard_map/ppermute | solution.py:39
  219.3 28.0 %collective-permute-start.9 = (f32[2,2,3,128]{3,2,1,0:T(4,128)S(1)}, f32[2,2,3,128]{3,2,1,0:T(4,128)S(1)}, u32[]{:S(2)}, u32[]{:S(2)}) collective-permute-start(f32[2,2,3,128]{3,2,1,0:T(4,128)S(1)} %get-tuple-element.59), channel_id=1, source_target_pairs={{0,10},{1,11},{2,12},{3,13},{4,14},{5,15},{8,18},{9,19},{10,20},{1... | collective-permute-start | bytes 18440 | tf_op jit(solution)/shard_map/ppermute | solution.py:39
  221.2 26.1 %collective-permute-start.15 = (f32[2,2,3,128]{3,2,1,0:T(4,128)S(1)}, f32[2,2,3,128]{3,2,1,0:T(4,128)S(1)}, u32[]{:S(2)}, u32[]{:S(2)}) collective-permute-start(f32[2,2,3,128]{3,2,1,0:T(4,128)S(1)} %get-tuple-element.60), channel_id=1, source_target_pairs={{2,8},{3,9},{4,10},{5,11},{6,12},{7,13},{10,16},{11,17},{12,18},{1... | collective-permute-start | bytes 18440 | tf_op jit(solution)/shard_map/ppermute | solution.py:39
  228.2 2.6 collective-permute-start.8
  229.5 6.1 %collective-permute-start.16 = (f32[2,2,3,3]{3,2,1,0:T(4,128)S(1)}, f32[2,2,3,3]{3,2,1,0:T(4,128)S(1)}, u32[]{:S(2)}, u32[]{:S(2)}) collective-permute-start(f32[2,2,3,3]{3,2,1,0:T(4,128)S(1)} %get-tuple-element.56), channel_id=1, source_target_pairs={{3,8},{5,10},{7,12},{11,16},{13,18},{15,20},{19,24},{21,26},{23,28}} | collective-permute-start | bytes 440 | tf_op jit(solution)/shard_map/ppermute | solution.py:39
  230.8 6.1 %collective-permute-start.14 = (f32[2,2,3,3]{3,2,1,0:T(4,128)S(1)}, f32[2,2,3,3]{3,2,1,0:T(4,128)S(1)}, u32[]{:S(2)}, u32[]{:S(2)}) collective-permute-start(f32[2,2,3,3]{3,2,1,0:T(4,128)S(1)} %get-tuple-element.57), channel_id=1, source_target_pairs={{2,9},{4,11},{6,13},{10,17},{12,19},{14,21},{18,25},{20,27},{22,29}} | collective-permute-start | bytes 440 | tf_op jit(solution)/shard_map/ppermute | solution.py:39
  235.6 6.8 %collective-permute-start.10 = (f32[2,2,3,3]{3,2,1,0:T(4,128)S(1)}, f32[2,2,3,3]{3,2,1,0:T(4,128)S(1)}, u32[]{:S(2)}, u32[]{:S(2)}) collective-permute-start(f32[2,2,3,3]{3,2,1,0:T(4,128)S(1)} %get-tuple-element.58), channel_id=1, source_target_pairs={{1,10},{3,12},{5,14},{9,18},{11,20},{13,22},{17,26},{19,28},{21,30}} | collective-permute-start | bytes 440 | tf_op jit(solution)/shard_map/ppermute | solution.py:39
  236.9 9.1 %collective-permute-start.11 = (f32[2,2,4,3]{3,2,1,0:T(4,128)S(1)}, f32[2,2,4,3]{3,2,1,0:T(4,128)S(1)}, u32[]{:S(2)}, u32[]{:S(2)}) collective-permute-start(f32[2,2,4,3]{3,2,1,0:T(4,128)S(1)} %get-tuple-element.61), channel_id=1, source_target_pairs={{0,9},{2,11},{4,13},{6,15},{8,17},{10,19},{12,21},{14,23},{16,25},... | collective-permute-start | bytes 584 | tf_op jit(solution)/shard_map/ppermute | solution.py:39
  242.4 5.0 %collective-permute-start.13 = (f32[2,2,4,3]{3,2,1,0:T(4,128)S(1)}, f32[2,2,4,3]{3,2,1,0:T(4,128)S(1)}, u32[]{:S(2)}, u32[]{:S(2)}) collective-permute-start(f32[2,2,4,3]{3,2,1,0:T(4,128)S(1)} %get-tuple-element.62), channel_id=1, source_target_pairs={{1,8},{3,10},{5,12},{7,14},{9,16},{11,18},{13,20},{15,22},{17,24},... | collective-permute-start | bytes 584 | tf_op jit(solution)/shard_map/ppermute | solution.py:39
  347.9 4.9 %copy-start.3 = (f32[1,2,2,64,4,128]{3,5,4,2,1,0:T(8,128)S(1)}, f32[1,2,2,64,4,128]{3,5,4,2,1,0:T(8,128)}, u32[]{:S(2)}) copy-start(f32[1,2,2,64,4,128]{3,5,4,2,1,0:T(8,128)} %slice_bitcast_fusion.1) | copy-start | bytes 1572868
where the time goes:
time: 362 us; the launch traced here: 356 us
  local copies, waits for them, and re-layouts  198 us (55%)
  Pallas kernels  66.4 us (18%)
  starting transfers between devices  44.4 us (12%)
  other arithmetic  27.9 us (8%)
  waiting for transfers between devices  17.8 us (5%)
    scatter-add x2, local copies, waits for them, and re-layouts, per_device(): rhs = rhs.at[:, :, 0].add(incoming)  92.2 us
    pallas_call x2, Pallas kernels, run_tick(): pl.pallas_call(functools.partial(tick_kernel, row=row, depth=depth), out_...  66.4 us
    ppermute x17, starting transfers between devices, fetch(): return lax.ppermute(block, tuple(axes), pairs)  44.4 us
    unnamed x33, local copies, waits for them, and re-layouts  21.6 us
    ppermute x17, waiting for transfers between devices, fetch(): return lax.ppermute(block, tuple(axes), pairs)  17.8 us
    slice x12, local copies, waits for them, and re-layouts, with_halo(): piece = block[..., rows[dx], cols[dy]]  13.2 us
    gather x2, local copies, waits for them, and re-layouts, per_device(): rhs = jnp.take(forcing_e[tick], orders[tick], axis=0)  13.2 us
    concatenate x2, other arithmetic, with_halo(): return jnp.concatenate(bands, axis=-2)  8.88 us
  transfers between devices with their start and end apart: 17, of which 4 were waited for; matrix products, arithmetic and copies ran while one was open for 7% of the time, Pallas kernels for 0%

commit v1 on v0

--- a/solution.py
+++ b/solution.py
@@ -13,6 +13,7 @@
 
 DAMPING = 0.25
 PRECISE = lax.Precision.HIGHEST
+SPLIT = 65537.0
 
 
 def fetch(block, axes, offsets):
@@ -58,26 +59,31 @@
     return jnp.concatenate(bands, axis=-2)
 
 
-def tick_kernel(rhs_ref, dr_ref, di_ref, hot_ref, ins_ref, blk_ref, out_ref, *, row, depth):
-    nsrc, rows, cols = rhs_ref.shape
+def tick_kernel(
+    order_ref, frc_ref, inc_ref, dr_ref, di_ref, hot_ref, ins_ref, bhi_ref, blo_ref, out_ref, *, row, depth
+):
+    nsrc, rows, cols = frc_ref.shape
     classes = hot_ref.shape[0]
-    dr = dr_ref[...]
-    di = di_ref[...]
-    ins = ins_ref[...]
-    hots = [hot_ref[k : k + 1, :] for k in range(classes)]
-    blks = [blk_ref[k] for k in range(classes)]
     zrow = lax.broadcasted_iota(jnp.int32, (rows, cols), 0) % depth
     top = zrow == 0
     bottom = zrow == depth - 1
 
     def precond(x):
-        acc = None
-        for k in range(classes):
-            t = jnp.dot(blks[k], x * hots[k], precision=PRECISE, preferred_element_type=jnp.float32)
-            acc = t if acc is None else acc + t
-        return acc
+        scaled = x * SPLIT
+        high = scaled - (scaled - x)
+        low = x - high
+        hots = [hot_ref[k : k + 1, :] for k in range(classes)]
+        high = jnp.concatenate([high * h for h in hots], axis=0).astype(jnp.bfloat16)
+        low = jnp.concatenate([low * h for h in hots], axis=0).astype(jnp.bfloat16)
+        bhi = bhi_ref[...]
+        blo = blo_ref[...]
+        out = jnp.dot(bhi, low, preferred_element_type=jnp.float32)
+        out = out + jnp.dot(blo, high, preferred_element_type=jnp.float32)
+        return out + jnp.dot(bhi, high, preferred_element_type=jnp.float32)
 
     def apply_a(u):
+        dr = dr_ref[...]
+        di = di_ref[...]
         real = u[:depth]
         imaginary = u[depth:]
         diagonal = jnp.concatenate(
@@ -90,27 +96,41 @@
         beside = beside + pltpu.roll(u, cols - 1, 1) + pltpu.roll(u, 1, 1)
         return diagonal - beside
 
-    for s in range(nsrc):
-        rhs = rhs_ref[s]
-        u = precond(rhs)
-        for _ in range(CORR):
-            u = u + precond(ins * (rhs - apply_a(u)))
-        out_ref[s] = u
-
-
-def run_tick(rhs, dr, di, hot, ins, blocks, row, depth):
-    nsrc, rows, cols = rhs.shape
-    classes = hot.shape[0]
-    flops = nsrc * (CORR + 1) * classes * 2 * rows * rows * cols
+    def one_source(s, carry):
+        forcing = frc_ref[order_ref[s]]
+        incoming = inc_ref[s]
+        layer = jnp.concatenate(
+            [
+                jnp.broadcast_to(incoming[0:1], (depth, cols)),
+                jnp.broadcast_to(incoming[1:2], (depth, cols)),
+            ],
+            axis=0,
+        )
+        rhs = jnp.where(top, forcing + layer, forcing)
+
+        def correct(i, u):
+            return u + precond(ins_ref[...] * (rhs - apply_a(u)))
+
+        out_ref[s] = lax.fori_loop(0, CORR, correct, precond(rhs))
+        return carry
+
+    lax.fori_loop(0, nsrc, one_source, 0)
+
+
+def run_tick(order, forcing, incoming, dr, di, hot, ins, bhi, blo, row, depth):
+    nsrc, rows, cols = forcing.shape
+    width = bhi.shape[1]
+    flops = nsrc * (CORR + 1) * 3 * 2 * rows * width * cols
+    vmem = pl.BlockSpec(memory_space=pltpu.VMEM)
     return pl.pallas_call(
         functools.partial(tick_kernel, row=row, depth=depth),
-        out_shape=jax.ShapeDtypeStruct(rhs.shape, jnp.float32),
-        in_specs=[pl.BlockSpec(memory_space=pltpu.VMEM)] * 6,
-        out_specs=pl.BlockSpec(memory_space=pltpu.VMEM),
+        out_shape=jax.ShapeDtypeStruct(forcing.shape, jnp.float32),
+        in_specs=[pl.BlockSpec(memory_space=pltpu.SMEM)] + [vmem] * 8,
+        out_specs=vmem,
         cost_estimate=pl.CostEstimate(
-            flops=flops, transcendentals=0, bytes_accessed=4 * (2 * rhs.size + 4 * dr.size)
+            flops=flops, transcendentals=0, bytes_accessed=4 * (2 * forcing.size + 4 * dr.size)
         ),
-    )(rhs, dr, di, hot, ins, blocks)
+    )(order, forcing, incoming, dr, di, hot, ins, bhi, blo)
 
 
 def block_matrix(inverse):
@@ -158,27 +178,32 @@
     inside = flat(inside.reshape(1, cols).astype(jnp.float32))
 
     blocks = block_matrix(line_inverse[0])
+    side_by_side = jnp.concatenate([blocks[k] for k in range(classes)], axis=1)
+    rounded = lax.reduce_precision(side_by_side, exponent_bits=8, mantissa_bits=7)
+    bhi = rounded.astype(jnp.bfloat16)
+    blo = (side_by_side - rounded).astype(jnp.bfloat16)
     onehot = flat(
         (class_e[None, :] == jnp.arange(classes, dtype=jnp.int32)[:, None]).astype(jnp.float32)
     )
     diag_real = flat(6.0 - wavenumber_e)
     diag_imaginary = flat(-DAMPING * wavenumber_e)
     orders = batch_order[:, 0]
-
-    incoming = pending_e
+    forcing_f = flat(forcing_e).reshape(ticks, nsrc, two * depth, padded)
+
+    incoming = flat(pending_e)
     solutions = []
     trace = None
     for tick in range(ticks):
-        rhs = jnp.take(forcing_e[tick], orders[tick], axis=0)
-        rhs = rhs.at[:, :, 0].add(incoming)
-        rhs = flat(rhs).reshape(nsrc, two * depth, padded)
-        field = run_tick(rhs, diag_real, diag_imaginary, onehot, inside, blocks, ey, depth)
+        field = run_tick(
+            orders[tick], forcing_f[tick], incoming, diag_real, diag_imaginary, onehot, inside,
+            bhi, blo, ey, depth,
+        )
         field = field.reshape(nsrc, two, depth, padded)[..., :cols]
         tile = field.reshape(nsrc, two, depth, ex, ey)[:, :, :, width : width + nx, width : width + ny]
         solutions.append(tile)
         trace = tile[:, :, depth - 1]
         if tick + 1 < ticks:
-            incoming = with_halo(trace, width, ("slab",), (-1,)).reshape(nsrc, two, cols)
+            incoming = flat(with_halo(trace, width, ("slab",), (-1,)).reshape(nsrc, two, cols))
     return (jnp.stack(solutions, axis=0), trace[:, :, None])
 
 

time: 362 us -> 176 us (0.49)
  the two profiles are of different devices: /device:TPU:12 before, /device:TPU:5 now
where the time goes in v1:
time: 176 us; the launch traced here: 174 us
  local copies, waits for them, and re-layouts  78.9 us (45%)
  starting transfers between devices  49.8 us (28%)
  Pallas kernels  29.5 us (17%)
  other arithmetic  14.8 us (8%)
    ppermute x17, starting transfers between devices, fetch(): return lax.ppermute(block, tuple(axes), pairs)  49.8 us
    pallas_call x2, Pallas kernels, run_tick(): pl.pallas_call(functools.partial(tick_kernel, row=row, depth=depth), out_...  29.5 us
    slice x3, local copies, waits for them, and re-layouts, per_device(): forcing_f[tick]  15.5 us
    slice x12, local copies, waits for them, and re-layouts, with_halo(): piece = block[..., rows[dx], cols[dy]]  14.4 us
    unnamed x23, local copies, waits for them, and re-layouts  11.7 us
    reshape x1, local copies, waits for them, and re-layouts, per_device(): forcing_e = extended[:nf].reshape(ticks, nsrc, two, depth, cols)  5.48 us
    ppermute x4, local copies, waits for them, and re-layouts, fetch(): return lax.ppermute(block, tuple(axes), pairs)  5.3 us
    another operation x2, local copies, waits for them, and re-layouts, per_device(): return (jnp.stack(solutions, axis=0), trace[:, :, None])  4.7 us
  transfers between devices with their start and end apart: 17, of which 2 were waited for; matrix products, arithmetic and copies ran while one was open for 17% of the time, Pallas kernels for 0%

profile of v1, /device:TPU:5, one launch (start us, length us, event | category | flops | bytes accessed | tf_op | source)
XLA Modules:
  0.0 174.3 jit_solution(1640192571280636089)
XLA Ops:
  0.6 0.7 convert_element_type.44
  1.3 0.7 copy.57
  2.0 0.9 copy.56
  2.9 1.4 copy.55
  4.4 1.3 fusion.4
  5.8 3.1 %collective-permute-start.1 = (f32[581,3,128]{2,0,1:T(8,128)}, f32[581,3,128]{2,0,1:T(8,128)}, u32[]{:S(2)}, u32[]{:S(2)}) collective-permute-start(f32[581,3,128]{2,0,1:T(8,128)} %get-tuple-element.18), channel_id=1, source_target_pairs={{0,2},{1,3},{2,4},{3,5},{4,6},{5,7},{8,10},{9,11},{10,12},{11,13},... | collective-permute-start | bytes 2677256 | tf_op jit(solution)/shard_map/ppermute | solution.py:40
  8.9 3.1 %collective-permute-start.6 = (f32[581,3,128]{2,0,1:T(8,128)}, f32[581,3,128]{2,0,1:T(8,128)}, u32[]{:S(2)}, u32[]{:S(2)}) collective-permute-start(f32[581,3,128]{2,0,1:T(8,128)} %get-tuple-element.19), channel_id=1, source_target_pairs={{2,0},{3,1},{4,2},{5,3},{6,4},{7,5},{10,8},{11,9},{12,10},{13,11},... | collective-permute-start | bytes 2677256 | tf_op jit(solution)/shard_map/ppermute | solution.py:40
  12.0 1.4 fusion.5
  13.4 2.3 %copy.63 = f32[581,4,3]{0,1,2:T(4,128)} copy(f32[581,4,3]{2,0,1:T(8,128)} %get-tuple-element.21) | data formatting | bytes 55776 | tf_op jit(solution)/shard_map/slice | solution.py:51
  15.7 3.7 %collective-permute-start.4 = (f32[581,4,3]{0,1,2:T(4,128)}, f32[581,4,3]{0,1,2:T(4,128)}, u32[]{:S(2)}, u32[]{:S(2)}) collective-permute-start(f32[581,4,3]{0,1,2:T(4,128)} %copy.63), channel_id=1, source_target_pairs={{1,0},{3,2},{5,4},{7,6},{9,8},{11,10},{13,12},{15,14},{17,16},{19,... | collective-permute-start | bytes 83672 | tf_op jit(solution)/shard_map/ppermute | solution.py:40
  19.4 1.0 copy.62
  20.4 1.4 collective-permute-start.3
  21.8 2.1 %fusion.3 = (f32[581,3,3]{2,0,1:T(8,128)}, f32[581,3,3]{2,0,1:T(8,128)}, f32[581,3,3]{2,0,1:T(8,128)S(1)}, f32[581,3,3]{2,0,1:T(8,128)}) fusion(f32[581,4,128]{2,0,1:T(8,128)S(1)} %pad_maximum_fusion.2), kind=kLoop, calls=%fused_computation.37 | loop fusion | bytes 167328 | tf_op jit(solution)/shard_map/slice | solution.py:51
  23.9 2.2 %copy.60 = f32[581,3,3]{0,2,1:T(4,128)} copy(f32[581,3,3]{2,0,1:T(8,128)} %get-tuple-element.17) | data formatting | bytes 41832 | tf_op jit(solution)/shard_map/slice | solution.py:51
  26.1 5.3 %collective-permute-start.2 = (f32[581,3,3]{0,2,1:T(4,128)}, f32[581,3,3]{0,2,1:T(4,128)}, u32[]{:S(2)}, u32[]{:S(2)}) collective-permute-start(f32[581,3,3]{0,2,1:T(4,128)} %copy.60), channel_id=1, source_target_pairs={{1,2},{3,4},{5,6},{9,10},{11,12},{13,14},{17,18},{19,20},{21,22},{... | collective-permute-start | bytes 62756 | tf_op jit(solution)/shard_map/ppermute | solution.py:40
  33.0 0.7 fusion.1
  33.8 2.1 %copy.59 = f32[581,3,3]{0,2,1:T(4,128)} copy(f32[581,3,3]{2,0,1:T(8,128)} %get-tuple-element.14) | data formatting | bytes 41832 | tf_op jit(solution)/shard_map/slice | solution.py:51
  35.9 0.9 copy.66
  36.8 0.9 copy.67
  37.8 1.3 collective-permute-start.7
  39.1 1.1 copy.64
  40.2 1.3 collective-permute-start.5
  41.5 1.1 copy.65
  42.7 1.5 collective-permute-start
  44.2 3.3 %pad_maximum_fusion = f32[581,4,134]{2,0,1:T(8,128)} fusion(f32[581,4,3]{2,0,1:T(8,128)S(1)} %copy.65, f32[1,4,128]{2,0,1:T(1,128)S(1)} %bitcast.53, f32[4,4,128]{2,0,1:T(4,128)S(1)} %copy.57, f32[64,4,128]{2,0,1:T(8,128)} %copy-done.4, f32[512,4,128]{2,0,1:T(8,128)S(1)} %bitcast.45, f32[581,4,3]{2,0,1:T(8,128)S(1)} %copy.64), kind=kLoop, calls=%fused_computation.3 | loop fusion | flops 1557080 | bytes 2491328 | tf_op jit(solution)/shard_map/concatenate | solution.py:58
  47.5 2.0 %copy.69 = f32[581,4,134]{0,2,1:T(8,128)S(1)} copy(f32[581,4,134]{2,0,1:T(8,128)} %pad_maximum_fusion) | data formatting | bytes 2491328 | tf_op jit(solution)/shard_map/concatenate | solution.py:58
  49.5 1.5 copy.61
  51.0 1.5 copy.68
  52.6 1.4 fusion
  54.7 1.8 %maximum_maximum_fusion.2 = f32[4,10,134]{0,2,1:T(8,128)} fusion(f32[581,3,3]{0,2,1:T(4,128)S(1)} %collective-permute-done.7, f32[581,4,134]{0,2,1:T(8,128)S(1)} %copy.69, f32[581,3,128]{0,2,1:T(8,128)S(1)} %copy.68, f32[581,3,3]{0,2,1:T(4,128)S(1)} %collective-permute-done.5, f32[581,3,3]{0,2,1:T(4,128)} %collective-permute-done.2, ...), kind=kLoop, calls=%fused_computation.12 | loop fusion | flops 32160 | bytes 3135600 | tf_op jit(solution)/shard_map/slice | solution.py:167
  56.5 1.7 copy.71
  58.2 0.7 reshape.96
  58.9 1.0 maximum_maximum_fusion
  59.9 1.7 copy-done
  61.7 1.9 %broadcast_multiply_fusion = (f32[64,10,134]{0,2,1:T(8,128)}, f32[64,10,134]{0,2,1:T(8,128)}) fusion(f32[581,3,3]{0,2,1:T(4,128)S(1)} %collective-permute-done.7, f32[581,3,128]{0,2,1:T(8,128)S(1)} %copy.68, f32[581,3,3]{0,2,1:T(4,128)S(1)} %collective-permute-done.5, f32[581,4,134]{0,2,1:T(8,128)S(1)} %copy.69, f32[581,3,3]{0,2,1:T(4,128)} %collective-permute-done.2, ...), kind=kLoop, calls=%fused_computation.15 | loop fusion | flops 600320 | bytes 3800240 | tf_op jit(solution)/shard_map/mul | solution.py:189
  63.5 1.2 mul.17
  65.6 0.8 pad.33.di_ref
  66.5 0.9 broadcast_subtract_fusion
  67.4 1.3 sub.20
  68.7 1.0 copy.72
  69.7 1.8 %pad.32.dr_ref = f32[64,1408]{1,0:T(8,128)} pad(f32[64,1340]{1,0:T(8,128)} %copy.72, f32[]{:T(128)} %constant.12.clone.1), padding=0_0x0_68 | pad | bytes 703492 | tf_op jit(solution)/shard_map/jit(_pad)/pad | solution.py:173
  71.4 5.5 %reshape.95 = f32[2,2,2,64,1340]{3,2,1,0,4:T(2,128)} reshape(f32[512,10,134]{0,2,1:T(8,128)S(1)} %slice-done) | data formatting | bytes 5488640 | tf_op jit(solution)/shard_map/reshape | solution.py:165
  76.9 6.4 %pad_slice_fusion.1 = (f32[1,2,2,64,1408]{3,2,1,0,4:T(2,128)}, f32[1,2,2,64,1408]{3,2,1,0,4:T(2,128)S(1)}) fusion(f32[2,2,2,64,1340]{3,2,1,0,4:T(2,128)} %reshape.95), kind=kLoop, calls=%fused_computation.1 | loop fusion | bytes 5627904 | tf_op jit(solution)/shard_map/slice | solution.py:198
  83.3 5.2 %copy.70 = f32[1,2,2,64,1408]{4,3,2,1,0:T(8,128)} copy(f32[1,2,2,64,1408]{3,2,1,0,4:T(2,128)} %get-tuple-element.12) | data formatting | bytes 2883584 | tf_op jit(solution)/shard_map/slice | solution.py:198
  88.5 14.8 %shard_map.77 = f32[2,128,1408]{2,1,0:T(8,128)} custom-call(s32[2]{0:T(128)} %get-tuple-element.38.order_ref, f32[2,128,1408]{2,1,0:T(8,128)} %bitcast.50, f32[2,2,1408]{2,1,0:T(2,128)} %pad.31.inc_ref, f32[64,1408]{1,0:T(8,128)} %pad.32.dr_ref, f32[64,1408]{1,0:T(8,128)} %pad.33.di_ref, f32[4,1408]{1,0:T(4,128)} %pad_convert_fusion.1.hot_ref, ...), custom_call_target="tpu_custom_call" | custom-call | flops 4429185024 | bytes 4325376 | tf_op jit(solution)/shard_map/pallas_call | solution.py:125
  103.3 3.1 %copy.80 = f32[2,2,64,1340]{2,3,1,0:T(8,128)} copy(f32[2,2,64,1340]{3,2,1,0:T(8,128)} %bitcast.51) | data formatting | bytes 2744320
  106.4 3.0 %reshape.98 = f32[2,2,64,10,134]{2,4,3,1,0:T(8,128)} reshape(f32[2,2,64,1340]{2,3,1,0:T(8,128)} %copy.80) | data formatting | bytes 2744320 | tf_op jit(solution)/shard_map/reshape | solution.py:202
  109.4 1.9 %slice_reduce_fusion = f32[2,2,4,128]{3,2,1,0:T(4,128)S(1)} fusion(f32[2,2,64,10,134]{2,4,3,1,0:T(8,128)} %reshape.98), kind=kLoop, calls=%fused_computation.7 | loop fusion | bytes 16384 | tf_op jit(solution)/shard_map/slice | solution.py:204
  111.3 2.4 %slice_bitcast_fusion.1 = f32[1,2,2,64,4,128]{3,5,4,2,1,0:T(8,128)} fusion(f32[2,2,64,10,134]{2,4,3,1,0:T(8,128)} %reshape.98), kind=kLoop, calls=%fused_computation.8 | loop fusion | bytes 1048576 | tf_op jit(solution)/shard_map/stack | solution.py:207
  113.6 3.2 %collective-permute-start.12 = (f32[2,2,4,128]{3,2,1,0:T(4,128)S(1)}, f32[2,2,4,128]{3,2,1,0:T(4,128)S(1)}, u32[]{:S(2)}, u32[]{:S(2)}) collective-permute-start(f32[2,2,4,128]{3,2,1,0:T(4,128)S(1)} %slice_reduce_fusion), channel_id=1, source_target_pairs={{0,8},{1,9},{2,10},{3,11},{4,12},{5,13},{6,14},{7,15},{8,16},{9,17... | collective-permute-start | bytes 24584 | tf_op jit(solution)/shard_map/ppermute | solution.py:40
  116.9 1.9 %collective-permute-start.9 = (f32[2,2,3,128]{3,2,1,0:T(4,128)S(1)}, f32[2,2,3,128]{3,2,1,0:T(4,128)S(1)}, u32[]{:S(2)}, u32[]{:S(2)}) collective-permute-start(f32[2,2,3,128]{3,2,1,0:T(4,128)S(1)} %get-tuple-element.34), channel_id=1, source_target_pairs={{0,10},{1,11},{2,12},{3,13},{4,14},{5,15},{8,18},{9,19},{10,20},{1... | collective-permute-start | bytes 18440 | tf_op jit(solution)/shard_map/ppermute | solution.py:40
  118.8 6.3 %collective-permute-start.15 = (f32[2,2,3,128]{3,2,1,0:T(4,128)S(1)}, f32[2,2,3,128]{3,2,1,0:T(4,128)S(1)}, u32[]{:S(2)}, u32[]{:S(2)}) collective-permute-start(f32[2,2,3,128]{3,2,1,0:T(4,128)S(1)} %get-tuple-element.35), channel_id=1, source_target_pairs={{2,8},{3,9},{4,10},{5,11},{6,12},{7,13},{10,16},{11,17},{12,18},{1... | collective-permute-start | bytes 18440 | tf_op jit(solution)/shard_map/ppermute | solution.py:40
  125.9 5.1 %collective-permute-start.16 = (f32[2,2,3,3]{3,2,1,0:T(4,128)S(1)}, f32[2,2,3,3]{3,2,1,0:T(4,128)S(1)}, u32[]{:S(2)}, u32[]{:S(2)}) collective-permute-start(f32[2,2,3,3]{3,2,1,0:T(4,128)S(1)} %get-tuple-element.31), channel_id=1, source_target_pairs={{3,8},{5,10},{7,12},{11,16},{13,18},{15,20},{19,24},{21,26},{23,28}} | collective-permute-start | bytes 440 | tf_op jit(solution)/shard_map/ppermute | solution.py:40
  131.8 5.1 %collective-permute-start.10 = (f32[2,2,3,3]{3,2,1,0:T(4,128)S(1)}, f32[2,2,3,3]{3,2,1,0:T(4,128)S(1)}, u32[]{:S(2)}, u32[]{:S(2)}) collective-permute-start(f32[2,2,3,3]{3,2,1,0:T(4,128)S(1)} %get-tuple-element.33), channel_id=1, source_target_pairs={{1,10},{3,12},{5,14},{9,18},{11,20},{13,22},{17,26},{19,28},{21,30}} | collective-permute-start | bytes 440 | tf_op jit(solution)/shard_map/ppermute | solution.py:40
  137.6 5.6 %collective-permute-start.13 = (f32[2,2,4,3]{3,2,1,0:T(4,128)S(1)}, f32[2,2,4,3]{3,2,1,0:T(4,128)S(1)}, u32[]{:S(2)}, u32[]{:S(2)}) collective-permute-start(f32[2,2,4,3]{3,2,1,0:T(4,128)S(1)} %get-tuple-element.37), channel_id=1, source_target_pairs={{1,8},{3,10},{5,12},{7,14},{9,16},{11,18},{13,20},{15,22},{17,24},... | collective-permute-start | bytes 584 | tf_op jit(solution)/shard_map/ppermute | solution.py:40
  143.2 3.9 %copy.76 = f32[1,2,2,64,1408]{4,3,2,1,0:T(8,128)} copy(f32[1,2,2,64,1408]{3,2,1,0,4:T(2,128)S(1)} %get-tuple-element.13) | data formatting | bytes 2883584 | tf_op jit(solution)/shard_map/slice | solution.py:198
  148.0 14.7 %shard_map.78 = f32[2,128,1408]{2,1,0:T(8,128)} custom-call(s32[2]{0:T(128)} %get-tuple-element.39.order_ref, f32[2,128,1408]{2,1,0:T(8,128)} %bitcast.48, f32[2,2,1408]{2,1,0:T(2,128)} %pad.38.inc_ref, f32[64,1408]{1,0:T(8,128)} %pad.32.dr_ref, f32[64,1408]{1,0:T(8,128)} %pad.33.di_ref, f32[4,1408]{1,0:T(4,128)} %pad_convert_fusion.1.hot_ref, ...), custom_call_target="tpu_custom_call" | custom-call | flops 4429185024 | bytes 4325376 | tf_op jit(solution)/shard_map/pallas_call | solution.py:125
  162.7 2.0 %copy.81 = f32[2,2,64,1340]{2,3,1,0:T(8,128)S(1)} copy(f32[2,2,64,1340]{3,2,1,0:T(8,128)} %bitcast.49) | data formatting | bytes 2744320
  164.7 1.6 reshape.101
  166.3 1.7 slice.178
  168.0 2.3 %slice_bitcast_fusion = f32[1,2,2,64,4,128]{3,5,4,2,1,0:T(8,128)} fusion(f32[2,2,64,10,134]{2,4,3,1,0:T(8,128)} %reshape.101), kind=kLoop, calls=%fused_computation.6 | loop fusion | bytes 1048576 | tf_op jit(solution)/shard_map/stack | solution.py:207
  170.3 0.9 copy.79
  171.3 1.4 pad_maximum_fusion.1
  172.7 1.6 copy.78
  (60 shorter events, 6.5 us)
Async XLA Ops:
  2.9 2.9 %copy-start.4 = (f32[64,4,128]{2,0,1:T(8,128)}, f32[64,4,128]{2,0,1:T(8,128)S(1)}, u32[]{:S(2)}) copy-start(f32[64,4,128]{2,0,1:T(8,128)S(1)} %copy.56) | copy-start | bytes 393220
  5.8 36.9 %collective-permute-start.1 = (f32[581,3,128]{2,0,1:T(8,128)}, f32[581,3,128]{2,0,1:T(8,128)}, u32[]{:S(2)}, u32[]{:S(2)}) collective-permute-start(f32[581,3,128]{2,0,1:T(8,128)} %get-tuple-element.18), channel_id=1, source_target_pairs={{0,2},{1,3},{2,4},{3,5},{4,6},{5,7},{8,10},{9,11},{10,12},{11,13},... | collective-permute-start | bytes 2677256 | tf_op jit(solution)/shard_map/ppermute | solution.py:40
  8.9 42.1 %collective-permute-start.6 = (f32[581,3,128]{2,0,1:T(8,128)}, f32[581,3,128]{2,0,1:T(8,128)}, u32[]{:S(2)}, u32[]{:S(2)}) collective-permute-start(f32[581,3,128]{2,0,1:T(8,128)} %get-tuple-element.19), channel_id=1, source_target_pairs={{2,0},{3,1},{4,2},{5,3},{6,4},{7,5},{10,8},{11,9},{12,10},{13,11},... | collective-permute-start | bytes 2677256 | tf_op jit(solution)/shard_map/ppermute | solution.py:40
  15.7 24.6 %collective-permute-start.4 = (f32[581,4,3]{0,1,2:T(4,128)}, f32[581,4,3]{0,1,2:T(4,128)}, u32[]{:S(2)}, u32[]{:S(2)}) collective-permute-start(f32[581,4,3]{0,1,2:T(4,128)} %copy.63), channel_id=1, source_target_pairs={{1,0},{3,2},{5,4},{7,6},{9,8},{11,10},{13,12},{15,14},{17,16},{19,... | collective-permute-start | bytes 83672 | tf_op jit(solution)/shard_map/ppermute | solution.py:40
  20.4 11.0 %copy-start.5 = (f32[1,4,2,64,64]{4,3,2,1,0:T(8,128)S(1)}, f32[1,4,2,64,64]{4,3,2,1,0:T(8,128)}, u32[]{:S(2)}) copy-start(f32[1,4,2,64,64]{4,3,2,1,0:T(8,128)} %param.8) | copy-start | bytes 393220
  20.4 11.2 %copy-start.7 = (s32[2,1,2]{2,1,0:T(1,128)S(1)}, s32[2,1,2]{2,1,0:T(1,128)}, u32[]{:S(2)}) copy-start(s32[2,1,2]{2,1,0:T(1,128)} %param.10) | copy-start | bytes 52
  20.4 17.4 %collective-permute-start.3 = (f32[581,4,3]{0,1,2:T(4,128)}, f32[581,4,3]{0,1,2:T(4,128)}, u32[]{:S(2)}, u32[]{:S(2)}) collective-permute-start(f32[581,4,3]{0,1,2:T(4,128)} %copy.62), channel_id=1, source_target_pairs={{0,1},{2,3},{4,5},{6,7},{8,9},{10,11},{12,13},{14,15},{16,17},{18,... | collective-permute-start | bytes 83672 | tf_op jit(solution)/shard_map/ppermute | solution.py:40
  23.9 12.0 %copy-start.2 = (f32[581,3,3]{2,0,1:T(8,128)S(1)}, f32[581,3,3]{2,0,1:T(8,128)}, u32[]{:S(2)}) copy-start(f32[581,3,3]{2,0,1:T(8,128)} %get-tuple-element.15) | copy-start | bytes 62752
  26.1 26.5 %collective-permute-start.2 = (f32[581,3,3]{0,2,1:T(4,128)}, f32[581,3,3]{0,2,1:T(4,128)}, u32[]{:S(2)}, u32[]{:S(2)}) collective-permute-start(f32[581,3,3]{0,2,1:T(4,128)} %copy.60), channel_id=1, source_target_pairs={{1,2},{3,4},{5,6},{9,10},{11,12},{13,14},{17,18},{19,20},{21,22},{... | collective-permute-start | bytes 62756 | tf_op jit(solution)/shard_map/ppermute | solution.py:40
  37.8 14.8 %collective-permute-start.7 = (f32[581,3,3]{0,2,1:T(4,128)}, f32[581,3,3]{0,2,1:T(4,128)S(1)}, u32[]{:S(2)}, u32[]{:S(2)}) collective-permute-start(f32[581,3,3]{0,2,1:T(4,128)} %copy.67), channel_id=1, source_target_pairs={{3,0},{5,2},{7,4},{11,8},{13,10},{15,12},{19,16},{21,18},{23,20},{... | collective-permute-start | bytes 62756 | tf_op jit(solution)/shard_map/ppermute | solution.py:40
  40.2 12.3 %collective-permute-start.5 = (f32[581,3,3]{0,2,1:T(4,128)}, f32[581,3,3]{0,2,1:T(4,128)S(1)}, u32[]{:S(2)}, u32[]{:S(2)}) collective-permute-start(f32[581,3,3]{0,2,1:T(4,128)} %copy.66), channel_id=1, source_target_pairs={{2,1},{4,3},{6,5},{10,9},{12,11},{14,13},{18,17},{20,19},{22,21},{... | collective-permute-start | bytes 62756 | tf_op jit(solution)/shard_map/ppermute | solution.py:40
  42.7 9.9 %collective-permute-start = (f32[581,3,3]{0,2,1:T(4,128)}, f32[581,3,3]{0,2,1:T(4,128)S(1)}, u32[]{:S(2)}, u32[]{:S(2)}) collective-permute-start(f32[581,3,3]{0,2,1:T(4,128)} %copy.59), channel_id=1, source_target_pairs={{0,3},{2,5},{4,7},{8,11},{10,13},{12,15},{16,19},{18,21},{20,23},{... | collective-permute-start | bytes 62756 | tf_op jit(solution)/shard_map/ppermute | solution.py:40
  59.9 1.7 copy-start
  63.5 1.5 copy-start.6
  63.5 2.9 %copy-start.3 = (f32[64,10,134]{0,2,1:T(8,128)S(1)}, f32[64,10,134]{0,2,1:T(8,128)}, u32[]{:S(2)}) copy-start(f32[64,10,134]{0,2,1:T(8,128)} %get-tuple-element.11) | copy-start | bytes 1029124
  66.5 5.0 %slice-start = ((f32[581,10,134]{0,2,1:T(8,128)}), f32[512,10,134]{0,2,1:T(8,128)S(1)}, s32[]{:S(2)}) async-start(f32[581,10,134]{0,2,1:T(8,128)} %copy-done), calls=%async_computation | async-start | bytes 5570560 | tf_op jit(solution)/shard_map/slice | solution.py:165
  113.6 33.5 %collective-permute-start.12 = (f32[2,2,4,128]{3,2,1,0:T(4,128)S(1)}, f32[2,2,4,128]{3,2,1,0:T(4,128)S(1)}, u32[]{:S(2)}, u32[]{:S(2)}) collective-permute-start(f32[2,2,4,128]{3,2,1,0:T(4,128)S(1)} %slice_reduce_fusion), channel_id=1, source_target_pairs={{0,8},{1,9},{2,10},{3,11},{4,12},{5,13},{6,14},{7,15},{8,16},{9,17... | collective-permute-start | bytes 24584 | tf_op jit(solution)/shard_map/ppermute | solution.py:40
  116.9 30.2 %collective-permute-start.9 = (f32[2,2,3,128]{3,2,1,0:T(4,128)S(1)}, f32[2,2,3,128]{3,2,1,0:T(4,128)S(1)}, u32[]{:S(2)}, u32[]{:S(2)}) collective-permute-start(f32[2,2,3,128]{3,2,1,0:T(4,128)S(1)} %get-tuple-element.34), channel_id=1, source_target_pairs={{0,10},{1,11},{2,12},{3,13},{4,14},{5,15},{8,18},{9,19},{10,20},{1... | collective-permute-start | bytes 18440 | tf_op jit(solution)/shard_map/ppermute | solution.py:40
  118.8 28.3 %collective-permute-start.15 = (f32[2,2,3,128]{3,2,1,0:T(4,128)S(1)}, f32[2,2,3,128]{3,2,1,0:T(4,128)S(1)}, u32[]{:S(2)}, u32[]{:S(2)}) collective-permute-start(f32[2,2,3,128]{3,2,1,0:T(4,128)S(1)} %get-tuple-element.35), channel_id=1, source_target_pairs={{2,8},{3,9},{4,10},{5,11},{6,12},{7,13},{10,16},{11,17},{12,18},{1... | collective-permute-start | bytes 18440 | tf_op jit(solution)/shard_map/ppermute | solution.py:40
  125.2 5.8 %collective-permute-start.8 = (f32[2,2,3,3]{3,2,1,0:T(4,128)S(1)}, f32[2,2,3,3]{3,2,1,0:T(4,128)S(1)}, u32[]{:S(2)}, u32[]{:S(2)}) collective-permute-start(f32[2,2,3,3]{3,2,1,0:T(4,128)S(1)} %get-tuple-element.30), channel_id=1, source_target_pairs={{0,11},{2,13},{4,15},{8,19},{10,21},{12,23},{16,27},{18,29},{20,31}} | collective-permute-start | bytes 440 | tf_op jit(solution)/shard_map/ppermute | solution.py:40
  125.9 5.9 %collective-permute-start.16 = (f32[2,2,3,3]{3,2,1,0:T(4,128)S(1)}, f32[2,2,3,3]{3,2,1,0:T(4,128)S(1)}, u32[]{:S(2)}, u32[]{:S(2)}) collective-permute-start(f32[2,2,3,3]{3,2,1,0:T(4,128)S(1)} %get-tuple-element.31), channel_id=1, source_target_pairs={{3,8},{5,10},{7,12},{11,16},{13,18},{15,20},{19,24},{21,26},{23,28}} | collective-permute-start | bytes 440 | tf_op jit(solution)/shard_map/ppermute | solution.py:40
  131.0 5.9 %collective-permute-start.14 = (f32[2,2,3,3]{3,2,1,0:T(4,128)S(1)}, f32[2,2,3,3]{3,2,1,0:T(4,128)S(1)}, u32[]{:S(2)}, u32[]{:S(2)}) collective-permute-start(f32[2,2,3,3]{3,2,1,0:T(4,128)S(1)} %get-tuple-element.32), channel_id=1, source_target_pairs={{2,9},{4,11},{6,13},{10,17},{12,19},{14,21},{18,25},{20,27},{22,29}} | collective-permute-start | bytes 440 | tf_op jit(solution)/shard_map/ppermute | solution.py:40
  131.8 5.9 %collective-permute-start.10 = (f32[2,2,3,3]{3,2,1,0:T(4,128)S(1)}, f32[2,2,3,3]{3,2,1,0:T(4,128)S(1)}, u32[]{:S(2)}, u32[]{:S(2)}) collective-permute-start(f32[2,2,3,3]{3,2,1,0:T(4,128)S(1)} %get-tuple-element.33), channel_id=1, source_target_pairs={{1,10},{3,12},{5,14},{9,18},{11,20},{13,22},{17,26},{19,28},{21,30}} | collective-permute-start | bytes 440 | tf_op jit(solution)/shard_map/ppermute | solution.py:40
  136.9 10.2 %collective-permute-start.11 = (f32[2,2,4,3]{3,2,1,0:T(4,128)S(1)}, f32[2,2,4,3]{3,2,1,0:T(4,128)S(1)}, u32[]{:S(2)}, u32[]{:S(2)}) collective-permute-start(f32[2,2,4,3]{3,2,1,0:T(4,128)S(1)} %get-tuple-element.36), channel_id=1, source_target_pairs={{0,9},{2,11},{4,13},{6,15},{8,17},{10,19},{12,21},{14,23},{16,25},... | collective-permute-start | bytes 584 | tf_op jit(solution)/shard_map/ppermute | solution.py:40
  137.6 9.4 %collective-permute-start.13 = (f32[2,2,4,3]{3,2,1,0:T(4,128)S(1)}, f32[2,2,4,3]{3,2,1,0:T(4,128)S(1)}, u32[]{:S(2)}, u32[]{:S(2)}) collective-permute-start(f32[2,2,4,3]{3,2,1,0:T(4,128)S(1)} %get-tuple-element.37), channel_id=1, source_target_pairs={{1,8},{3,10},{5,12},{7,14},{9,16},{11,18},{13,20},{15,22},{17,24},... | collective-permute-start | bytes 584 | tf_op jit(solution)/shard_map/ppermute | solution.py:40
  166.3 4.9 %copy-start.1 = (f32[1,2,2,64,4,128]{3,5,4,2,1,0:T(8,128)S(1)}, f32[1,2,2,64,4,128]{3,5,4,2,1,0:T(8,128)}, u32[]{:S(2)}) copy-start(f32[1,2,2,64,4,128]{3,5,4,2,1,0:T(8,128)} %slice_bitcast_fusion.1) | copy-start | bytes 1572868

commit v2 on v1

v2 whole, which is shorter than its diff:
```python
import functools

import jax
import jax.numpy as jnp
from jax import lax
from jax.experimental import pallas as pl
from jax.experimental.pallas import tpu as pltpu
from jax.sharding import PartitionSpec as P

CORR = 3
TICKS = 2


DAMPING = 0.25
PRECISE = lax.Precision.HIGHEST
SPLIT = 65537.0


def fetch(block, axes, offsets):
    sizes = [lax.axis_size(a) for a in axes]
    pairs = []
    total = 1
    for s in sizes:
        total *= s
    for linear in range(total):
        coords = []
        rest = linear
        for s in reversed(sizes):
            coords.append(rest % s)
            rest //= s
        coords = coords[::-1]
        source = [c + d for c, d in zip(coords, offsets)]
        if all(0 <= c < s for c, s in zip(source, sizes)):
            src_linear = 0
            for c, s in zip(source, sizes):
                src_linear = src_linear * s + c
            pairs.append((src_linear, linear))
    if len(axes) == 1:
        return lax.ppermute(block, axes[0], pairs)
    return lax.ppermute(block, tuple(axes), pairs)


def halo_pieces(block, width, lead_axes=(), lead_offsets=()):
    nx, ny = block.shape[-2], block.shape[-1]
    rows = {-1: slice(nx - width, nx), 0: slice(0, nx), 1: slice(0, width)}
    cols = {-1: slice(ny - width, ny), 0: slice(0, ny), 1: slice(0, width)}
    pieces = {}
    for dx in (-1, 0, 1):
        for dy in (-1, 0, 1):
            piece = block[..., rows[dx], cols[dy]]
            if dx == 0 and dy == 0 and not lead_axes:
                pieces[dx, dy] = piece
            else:
                pieces[dx, dy] = fetch(
                    piece, tuple(lead_axes) + ("tx", "ty"), tuple(lead_offsets) + (dx, dy)
                )
    return pieces


def flat_extended(pieces, nx, width, padded):
    segments = []
    for ix in range(nx + 2 * width):
        dx = -1 if ix < width else (0 if ix < width + nx else 1)
        r = ix - (0 if dx == -1 else (width if dx == 0 else width + nx))
        for dy in (-1, 0, 1):
            segments.append(pieces[dx, dy][..., r, :])
    used = sum(s.shape[-1] for s in segments)
    lead = segments[0].shape[:-1]
    segments.append(jnp.zeros(lead + (padded - used,), segments[0].dtype))
    return jnp.concatenate(segments, axis=-1)


def tick_kernel(order_ref, pk_ref, inc_ref, ins_ref, bhi_ref, blo_ref, out_ref, *, tick, row, depth, width):
    nsrc, rows, owned = out_ref.shape
    cols = pk_ref.shape[1]
    classes = bhi_ref.shape[1] // rows
    lanes = 128
    waves = tick * nsrc * rows
    wave0 = pk_ref.shape[0] - depth - 2 * nsrc - 1
    zrow = lax.broadcasted_iota(jnp.int32, (rows, cols), 0) % depth
    top = zrow == 0
    bottom = zrow == depth - 1

    def precond(x):
        scaled = x * SPLIT
        high = scaled - (scaled - x)
        low = x - high
        label = pk_ref[pl.ds(wave0 + depth + 2 * nsrc, 1), :]
        hots = [(label == float(k)).astype(jnp.float32) for k in range(classes)]
        high = jnp.concatenate([high * h for h in hots], axis=0).astype(jnp.bfloat16)
        low = jnp.concatenate([low * h for h in hots], axis=0).astype(jnp.bfloat16)
        bhi = bhi_ref[...]
        blo = blo_ref[...]
        out = jnp.dot(bhi, low, preferred_element_type=jnp.float32)
        out = out + jnp.dot(blo, high, preferred_element_type=jnp.float32)
        return out + jnp.dot(bhi, high, preferred_element_type=jnp.float32)

    def apply_a(u):
        wave = pk_ref[pl.ds(wave0, depth), :]
        dr = 6.0 - wave
        di = -DAMPING * wave
        real = u[:depth]
        imaginary = u[depth:]
        diagonal = jnp.concatenate(
            [dr * real - di * imaginary, dr * imaginary + di * real], axis=0
        )
        down = jnp.where(top, 0.0, pltpu.roll(u, 1, 0))
        up = jnp.where(bottom, 0.0, pltpu.roll(u, rows - 1, 0))
        beside = up + down
        beside = beside + pltpu.roll(u, cols - row, 1) + pltpu.roll(u, row, 1)
        beside = beside + pltpu.roll(u, cols - 1, 1) + pltpu.roll(u, 1, 1)
        return diagonal - beside

    def one_source(s, carry):
        first = pl.multiple_of(waves + order_ref[s] * rows, rows)
        forcing = pk_ref[pl.ds(first, rows), :]
        incoming = inc_ref[s]
        layer = jnp.concatenate(
            [
                jnp.broadcast_to(incoming[0:1], (depth, cols)),
                jnp.broadcast_to(incoming[1:2], (depth, cols)),
            ],
            axis=0,
        )
        rhs = jnp.where(top, forcing + layer, forcing)

        def correct(i, u):
            return u + precond(ins_ref[...] * (rhs - apply_a(u)))

        u = lax.fori_loop(0, CORR, correct, precond(rhs))
        for x in range(owned // lanes):
            begin = (x + width) * row + width
            out_ref[s, :, x * lanes : (x + 1) * lanes] = pltpu.roll(u, cols - begin, 1)[:, :lanes]
        return carry

    lax.fori_loop(0, nsrc, one_source, 0)


def run_tick(order, packed, incoming, ins, bhi, blo, tick, row, depth, width, owned):
    nsrc = incoming.shape[0]
    rows, stacked = bhi.shape
    cols = packed.shape[1]
    flops = nsrc * (CORR + 1) * 3 * 2 * rows * stacked * cols
    vmem = pl.BlockSpec(memory_space=pltpu.VMEM)
    return pl.pallas_call(
        functools.partial(tick_kernel, tick=tick, row=row, depth=depth, width=width),
        out_shape=jax.ShapeDtypeStruct((nsrc, rows, owned), jnp.float32),
        in_specs=[pl.BlockSpec(memory_space=pltpu.SMEM)] + [vmem] * 5,
        out_specs=vmem,
        cost_estimate=pl.CostEstimate(
            flops=flops, transcendentals=0, bytes_accessed=4 * (packed.size // 2 + nsrc * rows * owned)
        ),
    )(order, packed, incoming, ins, bhi, blo)


def block_matrix(inverse):
    real = inverse[:, 0]
    imaginary = inverse[:, 1]
    upper = jnp.concatenate([real, -imaginary], axis=2)
    lower = jnp.concatenate([imaginary, real], axis=2)
    return jnp.concatenate([upper, lower], axis=1)


def per_device(forcing, wavenumber_sq, line_inverse, column_class, batch_order, pending_trace):
    width = CORR
    ticks, nsrc, two, depth, nx, ny = forcing.shape
    classes = line_inverse.shape[1]
    ntx = lax.axis_size("tx")
    nty = lax.axis_size("ty")
    ex, ey = nx + 2 * width, ny + 2 * width
    cols = ex * ey
    padded = -(-cols // 128) * 128
    assert width <= nx and width <= ny

    packed = jnp.concatenate(
        [
            forcing.reshape(-1, nx, ny),
            wavenumber_sq,
            pending_trace.reshape(-1, nx, ny),
            column_class[0][None].astype(jnp.float32),
        ],
        axis=0,
    )
    packed = flat_extended(halo_pieces(packed, width), nx, width, padded)
    first_pending = ticks * nsrc * two * depth + depth

    gx = lax.axis_index("tx") * nx - width + jnp.arange(ex)
    gy = lax.axis_index("ty") * ny - width + jnp.arange(ey)
    inside = ((gx >= 0) & (gx < nx * ntx))[:, None] & ((gy >= 0) & (gy < ny * nty))[None, :]
    inside = jnp.pad(inside.reshape(1, cols).astype(jnp.float32), ((0, 0), (0, padded - cols)))

    blocks = block_matrix(line_inverse[0])
    side_by_side = jnp.concatenate([blocks[k] for k in range(classes)], axis=1)
    rounded = lax.reduce_precision(side_by_side, exponent_bits=8, mantissa_bits=7)
    bhi = rounded.astype(jnp.bfloat16)
    blo = (side_by_side - rounded).astype(jnp.bfloat16)
    orders = batch_order[:, 0]

    incoming = packed[first_pending : first_pending + nsrc * two].reshape(nsrc, two, padded)
    solutions = []
    trace = None
    for tick in range(ticks):
        field = run_tick(
            orders[tick], packed, incoming, inside, bhi, blo, tick, ey, depth, width, nx * ny
        )
        tile = field.reshape(nsrc, two, depth, nx, ny)
        solutions.append(tile)
        trace = tile[:, :, depth - 1]
        if tick + 1 < ticks:
            incoming = flat_extended(halo_pieces(trace, width, ("slab",), (-1,)), nx, width, padded)
    return (jnp.stack(solutions, axis=0), trace[:, :, None])


def solution(mesh):
    in_specs = (
        P(None, None, None, "slab", "tx", "ty"),
        P("slab", "tx", "ty"),
        P("slab", None, None, None, None),
        P("slab", "tx", "ty"),
        P(None, "slab", None),
        P(None, None, "slab", "tx", "ty"),
    )
    out_specs = (P(None, None, None, "slab", "tx", "ty"), P(None, None, "slab", "tx", "ty"))
    return jax.shard_map(
        per_device, mesh=mesh, in_specs=in_specs, out_specs=out_specs, check_vma=False
    )
```

time: 176 us -> 146 us (0.83)
  the two profiles are of different devices: /device:TPU:5 before, /device:TPU:12 now
where the time goes in v2:
time: 146 us; the launch traced here: 145 us
  local copies, waits for them, and re-layouts  49.1 us (34%)
  starting transfers between devices  39.6 us (27%)
  Pallas kernels  30.3 us (21%)
  waiting for transfers between devices  21.4 us (15%)
  other arithmetic  2.87 us (2%)
    ppermute x17, starting transfers between devices, fetch(): return lax.ppermute(block, tuple(axes), pairs)  39.6 us
    pallas_call x2, Pallas kernels, run_tick(): pl.pallas_call(functools.partial(tick_kernel, tick=tick, row=row, depth=d...  30.3 us
    ppermute x17, waiting for transfers between devices, fetch(): return lax.ppermute(block, tuple(axes), pairs)  21.4 us
    unnamed x43, local copies, waits for them, and re-layouts  20.3 us
    slice x12, local copies, waits for them, and re-layouts, halo_pieces(): piece = block[..., rows[dx], cols[dy]]  11.3 us
    concatenate x2, local copies, waits for them, and re-layouts, flat_extended(): return jnp.concatenate(segments, axis=-1)  7.64 us
    squeeze x12, local copies, waits for them, and re-layouts, flat_extended(): segments.append(pieces[dx, dy][..., r, :])  4.2 us
  transfers between devices with their start and end apart: 17, of which 4 were waited for; matrix products, arithmetic and copies ran while one was open for 21% of the time, Pallas kernels for 0%

profile of v2, /device:TPU:12, one launch (start us, length us, event | category | flops | bytes accessed | tf_op | source)
XLA Modules:
  0.0 144.5 jit_solution(3071626125280816111)
XLA Ops:
  0.7 1.4 copy.19
  2.2 1.8 %fusion.2 = (f32[581,3,3]{2,0,1:T(8,128)S(1)}, f32[581,3,3]{2,0,1:T(8,128)S(1)}, f32[581,3,3]{2,0,1:T(8,128)}, f32[581,3,3]{2,0,1:T(8,128)}) fusion(f32[581,4,128]{2,0,1:T(8,128)S(1)} %pad_maximum_fusion), kind=kLoop, calls=%fused_computation.62 | loop fusion | bytes 167328 | tf_op jit(solution)/shard_map/slice | solution.py:50
  4.0 2.1 %copy.23 = f32[581,3,3]{0,2,1:T(4,128)} copy(f32[581,3,3]{2,0,1:T(8,128)} %get-tuple-element.5) | data formatting | bytes 41832 | tf_op jit(solution)/shard_map/slice | solution.py:50
  6.1 2.8 %collective-permute-start = (f32[581,3,3]{0,2,1:T(4,128)}, f32[581,3,3]{0,2,1:T(4,128)S(1)}, u32[]{:S(2)}, u32[]{:S(2)}) collective-permute-start(f32[581,3,3]{0,2,1:T(4,128)} %copy.23), channel_id=1, source_target_pairs={{0,3},{2,5},{4,7},{8,11},{10,13},{12,15},{16,19},{18,21},{20,23},{... | collective-permute-start | bytes 62756 | tf_op jit(solution)/shard_map/ppermute | solution.py:40
  8.9 2.1 %copy.25 = f32[581,3,3]{0,2,1:T(4,128)} copy(f32[581,3,3]{2,0,1:T(8,128)} %get-tuple-element.4) | data formatting | bytes 41832 | tf_op jit(solution)/shard_map/slice | solution.py:50
  11.0 1.3 collective-permute-start.2
  12.6 5.2 %collective-permute-start.5 = (f32[581,3,3]{0,2,1:T(4,128)S(1)}, f32[581,3,3]{0,2,1:T(4,128)S(1)}, u32[]{:S(2)}, u32[]{:S(2)}) collective-permute-start(f32[581,3,3]{0,2,1:T(4,128)S(1)} %copy.41), channel_id=1, source_target_pairs={{2,1},{4,3},{6,5},{10,9},{12,11},{14,13},{18,17},{20,19},{22,21},{... | collective-permute-start | bytes 62756 | tf_op jit(solution)/shard_map/ppermute | solution.py:40
  18.1 1.3 collective-permute-start.7
  19.5 1.5 %fusion.4 = (f32[581,4,3]{2,0,1:T(8,128)S(1)}, f32[581,4,3]{2,0,1:T(8,128)}) fusion(f32[581,4,128]{2,0,1:T(8,128)S(1)} %pad_maximum_fusion), kind=kLoop, calls=%fused_computation.64 | loop fusion | bytes 111552 | tf_op jit(solution)/shard_map/slice | solution.py:50
  20.9 1.7 %copy.31 = f32[581,4,3]{0,1,2:T(4,128)S(1)} copy(f32[581,4,3]{2,0,1:T(8,128)} %get-tuple-element.13) | data formatting | bytes 55776 | tf_op jit(solution)/shard_map/slice | solution.py:50
  22.6 3.2 %collective-permute-start.3 = (f32[581,4,3]{0,1,2:T(4,128)S(1)}, f32[581,4,3]{0,1,2:T(4,128)S(1)}, u32[]{:S(2)}, u32[]{:S(2)}) collective-permute-start(f32[581,4,3]{0,1,2:T(4,128)S(1)} %copy.31), channel_id=1, source_target_pairs={{0,1},{2,3},{4,5},{6,7},{8,9},{10,11},{12,13},{14,15},{16,17},{18,... | collective-permute-start | bytes 83672 | tf_op jit(solution)/shard_map/ppermute | solution.py:40
  25.8 1.0 fusion.3
  26.8 1.1 slice_bitcast_fusion.3
  28.3 0.6 pad_convert_fusion.ins_ref
  29.5 0.7 fusion
  30.6 1.3 collective-permute-start.4
  31.9 1.9 %collective-permute-start.6 = (f32[581,3,128]{2,0,1:T(8,128)S(1)}, f32[581,3,128]{2,0,1:T(8,128)S(1)}, u32[]{:S(2)}, u32[]{:S(2)}) collective-permute-start(f32[581,3,128]{2,0,1:T(8,128)S(1)} %copy-done.3), channel_id=1, source_target_pairs={{2,0},{3,1},{4,2},{5,3},{6,4},{7,5},{10,8},{11,9},{12,10},{13,11},... | collective-permute-start | bytes 2677256 | tf_op jit(solution)/shard_map/ppermute | solution.py:40
  33.9 4.0 %collective-permute-start.1 = (f32[581,3,128]{2,0,1:T(8,128)S(1)}, f32[581,3,128]{2,0,1:T(8,128)}, u32[]{:S(2)}, u32[]{:S(2)}) collective-permute-start(f32[581,3,128]{2,0,1:T(8,128)S(1)} %get-tuple-element.7), channel_id=1, source_target_pairs={{0,2},{1,3},{2,4},{3,5},{4,6},{5,7},{8,10},{9,11},{10,12},{11,13},... | collective-permute-start | bytes 2677256 | tf_op jit(solution)/shard_map/ppermute | solution.py:40
  37.9 0.9 copy.55
  38.8 0.9 copy.56
  39.7 0.9 copy.65
  40.6 0.9 copy.66
  41.5 0.9 copy.67
  42.4 0.9 copy.68
  43.3 0.9 copy.69
  44.2 0.9 copy.70
  45.1 0.9 copy.51
  46.0 0.9 copy.52
  46.9 0.9 copy.53
  47.7 0.9 copy.54
  48.7 0.9 copy.57
  49.6 0.9 copy.58
  50.5 0.9 copy.59
  51.4 0.9 copy.60
  52.3 0.9 copy.61
  53.1 0.9 copy.62
  54.0 0.9 copy.63
  54.9 0.9 copy.64
  55.8 0.7 collective-permute-done.6
  56.5 1.0 slice_bitcast_fusion
  57.5 15.5 %collective-permute-done.1 = f32[581,3,128]{2,0,1:T(8,128)} collective-permute-done((f32[581,3,128]{2,0,1:T(8,128)S(1)}, f32[581,3,128]{2,0,1:T(8,128)}, u32[]{:S(2)}, u32[]{:S(2)}) %collective-permute-start.1) | collective-permute-done | bytes 892448 | tf_op jit(solution)/shard_map/ppermute | solution.py:40
  73.0 2.1 %slice_bitcast_fusion.7 = (f32[581,128]{1,0:T(8,128)}, f32[581,128]{1,0:T(8,128)}, f32[581,128]{1,0:T(8,128)}) fusion(f32[581,3,128]{2,0,1:T(8,128)} %collective-permute-done.1), kind=kLoop, calls=%fused_computation.11 | loop fusion | bytes 1784832 | tf_op jit(solution)/shard_map/squeeze | solution.py:66
  75.1 0.7 broadcast_in_dim.8
  75.9 6.9 %concatenate.22.pk_ref = f32[581,1408]{1,0:T(8,128)S(1)} concatenate(f32[581,3]{1,0:T(8,128)} %bitcast.138, f32[581,128]{1,0:T(8,128)} %get-tuple-element.19, f32[581,3]{1,0:T(8,128)} %bitcast.139, f32[581,3]{1,0:T(8,128)} %bitcast.140, f32[581,128]{1,0:T(8,128)} %get-tuple-element.18, f32[581,3]{1,0:T(8,128)} %bitcast.141, f32[581,3]{1,0:T(8,128)} %bitcast.130, ...), dimensions={1} | concatenate | bytes 6544384 | tf_op jit(solution)/shard_map/concatenate | solution.py:70
  82.8 0.7 reshape.67.inc_ref
  83.5 1.0 copy-done
  84.4 15.1 %shard_map.77 = f32[2,128,512]{2,1,0:T(8,128)} custom-call(s32[2]{0:T(128)} %get-tuple-element.86.order_ref, f32[581,1408]{1,0:T(8,128)} %copy-done, f32[2,2,1408]{2,1,0:T(2,128)} %reshape.67.inc_ref, f32[1,1408]{1,0:T(1,128)} %pad_convert_fusion.ins_ref, bf16[128,512]{1,0:T(8,128)(2,1)} %get-tuple-element.21.bhi_ref, bf16[128,512]{1,0:T(8,128)(2,1)} %get-tuple-element.20.blo_ref), custom_call_target="tpu_custom_call" | custom-call | flops 4429185024 | bytes 2160384 | tf_op jit(solution)/shard_map/pallas_call | solution.py:145
  99.6 1.3 reshape.68
  101.0 3.5 %collective-permute-start.12 = (f32[2,2,4,128]{3,1,0,2:T(2,128)S(1)}, f32[2,2,4,128]{3,1,0,2:T(2,128)S(1)}, u32[]{:S(2)}, u32[]{:S(2)}) collective-permute-start(f32[2,2,4,128]{3,1,0,2:T(2,128)S(1)} %bitcast.153), channel_id=1, source_target_pairs={{0,8},{1,9},{2,10},{3,11},{4,12},{5,13},{6,14},{7,15},{8,16},{9,17... | collective-permute-start | bytes 24584 | tf_op jit(solution)/shard_map/ppermute | solution.py:40
  104.7 1.3 collective-permute-start.16
  106.0 1.4 collective-permute-start.14
  107.4 1.3 collective-permute-start.10
  108.7 3.7 %collective-permute-start.8 = (f32[2,2,3,3]{3,1,0,2:T(2,128)S(1)}, f32[2,2,3,3]{3,1,0,2:T(2,128)S(1)}, u32[]{:S(2)}, u32[]{:S(2)}) collective-permute-start(f32[2,2,3,3]{3,1,0,2:T(2,128)S(1)} %get-tuple-element.51), channel_id=1, source_target_pairs={{0,11},{2,13},{4,15},{8,19},{10,21},{12,23},{16,27},{18,29},{20,31}} | collective-permute-start | bytes 440 | tf_op jit(solution)/shard_map/ppermute | solution.py:40
  112.4 1.3 collective-permute-start.13
  113.7 2.3 %collective-permute-start.11 = (f32[2,2,4,3]{3,1,0,2:T(2,128)S(1)}, f32[2,2,4,3]{3,1,0,2:T(2,128)S(1)}, u32[]{:S(2)}, u32[]{:S(2)}) collective-permute-start(f32[2,2,4,3]{3,1,0,2:T(2,128)S(1)} %get-tuple-element.67), channel_id=1, source_target_pairs={{0,9},{2,11},{4,13},{6,15},{8,17},{10,19},{12,21},{14,23},{16,25},... | collective-permute-start | bytes 584 | tf_op jit(solution)/shard_map/ppermute | solution.py:40
  116.0 1.9 %collective-permute-start.15 = (f32[2,2,3,128]{3,1,0,2:T(2,128)S(1)}, f32[2,2,3,128]{3,1,0,2:T(2,128)S(1)}, u32[]{:S(2)}, u32[]{:S(2)}) collective-permute-start(f32[2,2,3,128]{3,1,0,2:T(2,128)S(1)} %get-tuple-element.52), channel_id=1, source_target_pairs={{2,8},{3,9},{4,10},{5,11},{6,12},{7,13},{10,16},{11,17},{12,18},{1... | collective-permute-start | bytes 18440 | tf_op jit(solution)/shard_map/ppermute | solution.py:40
  118.0 2.1 %collective-permute-start.9 = (f32[2,2,3,128]{3,1,0,2:T(2,128)S(1)}, f32[2,2,3,128]{3,1,0,2:T(2,128)S(1)}, u32[]{:S(2)}, u32[]{:S(2)}) collective-permute-start(f32[2,2,3,128]{3,1,0,2:T(2,128)S(1)} %get-tuple-element.53), channel_id=1, source_target_pairs={{0,10},{1,11},{2,12},{3,13},{4,14},{5,15},{8,18},{9,19},{10,20},{1... | collective-permute-start | bytes 18440 | tf_op jit(solution)/shard_map/ppermute | solution.py:40
  120.1 2.3 %collective-permute-done.15 = f32[2,2,3,128]{3,1,0,2:T(2,128)S(1)} collective-permute-done((f32[2,2,3,128]{3,1,0,2:T(2,128)S(1)}, f32[2,2,3,128]{3,1,0,2:T(2,128)S(1)}, u32[]{:S(2)}, u32[]{:S(2)}) %collective-permute-start.15) | collective-permute-done | bytes 6176 | tf_op jit(solution)/shard_map/ppermute | solution.py:40
  122.4 2.8 %collective-permute-done.9 = f32[2,2,3,128]{3,1,0,2:T(2,128)S(1)} collective-permute-done((f32[2,2,3,128]{3,1,0,2:T(2,128)S(1)}, f32[2,2,3,128]{3,1,0,2:T(2,128)S(1)}, u32[]{:S(2)}, u32[]{:S(2)}) %collective-permute-start.9) | collective-permute-done | bytes 6176 | tf_op jit(solution)/shard_map/ppermute | solution.py:40
  125.3 0.8 concatenate.27.inc_ref
  126.1 15.1 %shard_map.78 = f32[2,128,512]{2,1,0:T(8,128)} custom-call(s32[2]{0:T(128)} %get-tuple-element.87.order_ref, f32[581,1408]{1,0:T(8,128)} %copy-done, f32[2,2,1408]{2,1,0:T(2,128)} %concatenate.27.inc_ref, f32[1,1408]{1,0:T(1,128)} %pad_convert_fusion.ins_ref, bf16[128,512]{1,0:T(8,128)(2,1)} %get-tuple-element.21.bhi_ref, ...), custom_call_target="tpu_custom_call" | custom-call | flops 4429185024 | bytes 2160384 | tf_op jit(solution)/shard_map/pallas_call | solution.py:145
  141.2 1.3 stack_reshape.7
  142.7 0.6 slice.434
  143.3 1.2 pad_maximum_fusion.1
  (71 shorter events, 2.8 us)
Async XLA Ops:
  0.6 1.4 %copy-start.5 = (f32[64,4,128]{2,1,0:T(4,128)S(1)}, f32[64,4,128]{2,1,0:T(4,128)}, u32[]{:S(2)}) copy-start(f32[64,4,128]{2,1,0:T(4,128)} %param.7) | copy-start | bytes 393220
  0.6 1.5 %copy-start.6 = (f32[2,2,1,4,128]{4,3,2,1,0:T(4,128)S(1)}, f32[2,2,1,4,128]{4,3,2,1,0:T(4,128)}, u32[]{:S(2)}) copy-start(f32[2,2,1,4,128]{4,3,2,1,0:T(4,128)} %param.11) | copy-start | bytes 24580
  0.7 1.5 %copy-start.7 = (s32[1,4,128]{2,1,0:T(4,128)S(1)}, s32[1,4,128]{2,1,0:T(4,128)}, u32[]{:S(2)}) copy-start(s32[1,4,128]{2,1,0:T(4,128)} %param.9) | copy-start | bytes 6148
  6.1 24.5 %collective-permute-start = (f32[581,3,3]{0,2,1:T(4,128)}, f32[581,3,3]{0,2,1:T(4,128)S(1)}, u32[]{:S(2)}, u32[]{:S(2)}) collective-permute-start(f32[581,3,3]{0,2,1:T(4,128)} %copy.23), channel_id=1, source_target_pairs={{0,3},{2,5},{4,7},{8,11},{10,13},{12,15},{16,19},{18,21},{20,23},{... | collective-permute-start | bytes 62756 | tf_op jit(solution)/shard_map/ppermute | solution.py:40
  11.0 20.9 %collective-permute-start.2 = (f32[581,3,3]{0,2,1:T(4,128)}, f32[581,3,3]{0,2,1:T(4,128)S(1)}, u32[]{:S(2)}, u32[]{:S(2)}) collective-permute-start(f32[581,3,3]{0,2,1:T(4,128)} %copy.25), channel_id=1, source_target_pairs={{1,2},{3,4},{5,6},{9,10},{11,12},{13,14},{17,18},{19,20},{21,22},{... | collective-permute-start | bytes 62756 | tf_op jit(solution)/shard_map/ppermute | solution.py:40
  12.6 21.2 %collective-permute-start.5 = (f32[581,3,3]{0,2,1:T(4,128)S(1)}, f32[581,3,3]{0,2,1:T(4,128)S(1)}, u32[]{:S(2)}, u32[]{:S(2)}) collective-permute-start(f32[581,3,3]{0,2,1:T(4,128)S(1)} %copy.41), channel_id=1, source_target_pairs={{2,1},{4,3},{6,5},{10,9},{12,11},{14,13},{18,17},{20,19},{22,21},{... | collective-permute-start | bytes 62756 | tf_op jit(solution)/shard_map/ppermute | solution.py:40
  18.1 19.8 %collective-permute-start.7 = (f32[581,3,3]{0,2,1:T(4,128)S(1)}, f32[581,3,3]{0,2,1:T(4,128)S(1)}, u32[]{:S(2)}, u32[]{:S(2)}) collective-permute-start(f32[581,3,3]{0,2,1:T(4,128)S(1)} %copy.43), channel_id=1, source_target_pairs={{3,0},{5,2},{7,4},{11,8},{13,10},{15,12},{19,16},{21,18},{23,20},{... | collective-permute-start | bytes 62756 | tf_op jit(solution)/shard_map/ppermute | solution.py:40
  22.6 26.1 %collective-permute-start.3 = (f32[581,4,3]{0,1,2:T(4,128)S(1)}, f32[581,4,3]{0,1,2:T(4,128)S(1)}, u32[]{:S(2)}, u32[]{:S(2)}) collective-permute-start(f32[581,4,3]{0,1,2:T(4,128)S(1)} %copy.31), channel_id=1, source_target_pairs={{0,1},{2,3},{4,5},{6,7},{8,9},{10,11},{12,13},{14,15},{16,17},{18,... | collective-permute-start | bytes 83672 | tf_op jit(solution)/shard_map/ppermute | solution.py:40
  26.8 1.1 copy-start.4
  27.9 1.1 copy-start.8
  28.1 3.9 %copy-start.3 = (f32[581,3,128]{2,0,1:T(8,128)S(1)}, f32[581,3,128]{2,0,1:T(8,128)}, u32[]{:S(2)}) copy-start(f32[581,3,128]{2,0,1:T(8,128)} %get-tuple-element.6) | copy-start | bytes 2677252
  30.6 19.0 %collective-permute-start.4 = (f32[581,4,3]{0,1,2:T(4,128)S(1)}, f32[581,4,3]{0,1,2:T(4,128)S(1)}, u32[]{:S(2)}, u32[]{:S(2)}) collective-permute-start(f32[581,4,3]{0,1,2:T(4,128)S(1)} %copy.33), channel_id=1, source_target_pairs={{1,0},{3,2},{5,4},{7,6},{9,8},{11,10},{13,12},{15,14},{17,16},{19,... | collective-permute-start | bytes 83672 | tf_op jit(solution)/shard_map/ppermute | solution.py:40
  31.9 24.5 %collective-permute-start.6 = (f32[581,3,128]{2,0,1:T(8,128)S(1)}, f32[581,3,128]{2,0,1:T(8,128)S(1)}, u32[]{:S(2)}, u32[]{:S(2)}) collective-permute-start(f32[581,3,128]{2,0,1:T(8,128)S(1)} %copy-done.3), channel_id=1, source_target_pairs={{2,0},{3,1},{4,2},{5,3},{6,4},{7,5},{10,8},{11,9},{12,10},{13,11},... | collective-permute-start | bytes 2677256 | tf_op jit(solution)/shard_map/ppermute | solution.py:40
  33.9 39.1 %collective-permute-start.1 = (f32[581,3,128]{2,0,1:T(8,128)S(1)}, f32[581,3,128]{2,0,1:T(8,128)}, u32[]{:S(2)}, u32[]{:S(2)}) collective-permute-start(f32[581,3,128]{2,0,1:T(8,128)S(1)} %get-tuple-element.7), channel_id=1, source_target_pairs={{0,2},{1,3},{2,4},{3,5},{4,6},{5,7},{8,10},{9,11},{10,12},{11,13},... | collective-permute-start | bytes 2677256 | tf_op jit(solution)/shard_map/ppermute | solution.py:40
  82.7 1.7 %copy-start = (f32[581,1408]{1,0:T(8,128)}, f32[581,1408]{1,0:T(8,128)S(1)}, u32[]{:S(2)}) copy-start(f32[581,1408]{1,0:T(8,128)S(1)} %concatenate.22.pk_ref) | copy-start | bytes 9816580
  99.6 5.0 %copy-start.1 = (f32[2,128,512]{2,1,0:T(8,128)S(1)}, f32[2,128,512]{2,1,0:T(8,128)}, u32[]{:S(2)}) copy-start(f32[2,128,512]{2,1,0:T(8,128)} %shard_map.77) | copy-start | bytes 1572868
  101.0 24.3 %collective-permute-start.12 = (f32[2,2,4,128]{3,1,0,2:T(2,128)S(1)}, f32[2,2,4,128]{3,1,0,2:T(2,128)S(1)}, u32[]{:S(2)}, u32[]{:S(2)}) collective-permute-start(f32[2,2,4,128]{3,1,0,2:T(2,128)S(1)} %bitcast.153), channel_id=1, source_target_pairs={{0,8},{1,9},{2,10},{3,11},{4,12},{5,13},{6,14},{7,15},{8,16},{9,17... | collective-permute-start | bytes 24584 | tf_op jit(solution)/shard_map/ppermute | solution.py:40
  104.7 7.7 %collective-permute-start.16 = (f32[2,2,3,3]{3,1,0,2:T(2,128)S(1)}, f32[2,2,3,3]{3,1,0,2:T(2,128)S(1)}, u32[]{:S(2)}, u32[]{:S(2)}) collective-permute-start(f32[2,2,3,3]{3,1,0,2:T(2,128)S(1)} %get-tuple-element.48), channel_id=1, source_target_pairs={{3,8},{5,10},{7,12},{11,16},{13,18},{15,20},{19,24},{21,26},{23,28}} | collective-permute-start | bytes 440 | tf_op jit(solution)/shard_map/ppermute | solution.py:40
  106.0 7.7 %collective-permute-start.14 = (f32[2,2,3,3]{3,1,0,2:T(2,128)S(1)}, f32[2,2,3,3]{3,1,0,2:T(2,128)S(1)}, u32[]{:S(2)}, u32[]{:S(2)}) collective-permute-start(f32[2,2,3,3]{3,1,0,2:T(2,128)S(1)} %get-tuple-element.49), channel_id=1, source_target_pairs={{2,9},{4,11},{6,13},{10,17},{12,19},{14,21},{18,25},{20,27},{22,29}} | collective-permute-start | bytes 440 | tf_op jit(solution)/shard_map/ppermute | solution.py:40
  107.4 8.6 %collective-permute-start.10 = (f32[2,2,3,3]{3,1,0,2:T(2,128)S(1)}, f32[2,2,3,3]{3,1,0,2:T(2,128)S(1)}, u32[]{:S(2)}, u32[]{:S(2)}) collective-permute-start(f32[2,2,3,3]{3,1,0,2:T(2,128)S(1)} %get-tuple-element.50), channel_id=1, source_target_pairs={{1,10},{3,12},{5,14},{9,18},{11,20},{13,22},{17,26},{19,28},{21,30}} | collective-permute-start | bytes 440 | tf_op jit(solution)/shard_map/ppermute | solution.py:40
  108.7 9.3 %collective-permute-start.8 = (f32[2,2,3,3]{3,1,0,2:T(2,128)S(1)}, f32[2,2,3,3]{3,1,0,2:T(2,128)S(1)}, u32[]{:S(2)}, u32[]{:S(2)}) collective-permute-start(f32[2,2,3,3]{3,1,0,2:T(2,128)S(1)} %get-tuple-element.51), channel_id=1, source_target_pairs={{0,11},{2,13},{4,15},{8,19},{10,21},{12,23},{16,27},{18,29},{20,31}} | collective-permute-start | bytes 440 | tf_op jit(solution)/shard_map/ppermute | solution.py:40
  112.4 7.7 %collective-permute-start.13 = (f32[2,2,4,3]{3,1,0,2:T(2,128)S(1)}, f32[2,2,4,3]{3,1,0,2:T(2,128)S(1)}, u32[]{:S(2)}, u32[]{:S(2)}) collective-permute-start(f32[2,2,4,3]{3,1,0,2:T(2,128)S(1)} %get-tuple-element.66), channel_id=1, source_target_pairs={{1,8},{3,10},{5,12},{7,14},{9,16},{11,18},{13,20},{15,22},{17,24},... | collective-permute-start | bytes 584 | tf_op jit(solution)/shard_map/ppermute | solution.py:40
  113.7 6.4 %collective-permute-start.11 = (f32[2,2,4,3]{3,1,0,2:T(2,128)S(1)}, f32[2,2,4,3]{3,1,0,2:T(2,128)S(1)}, u32[]{:S(2)}, u32[]{:S(2)}) collective-permute-start(f32[2,2,4,3]{3,1,0,2:T(2,128)S(1)} %get-tuple-element.67), channel_id=1, source_target_pairs={{0,9},{2,11},{4,13},{6,15},{8,17},{10,19},{12,21},{14,23},{16,25},... | collective-permute-start | bytes 584 | tf_op jit(solution)/shard_map/ppermute | solution.py:40
  116.0 6.4 %collective-permute-start.15 = (f32[2,2,3,128]{3,1,0,2:T(2,128)S(1)}, f32[2,2,3,128]{3,1,0,2:T(2,128)S(1)}, u32[]{:S(2)}, u32[]{:S(2)}) collective-permute-start(f32[2,2,3,128]{3,1,0,2:T(2,128)S(1)} %get-tuple-element.52), channel_id=1, source_target_pairs={{2,8},{3,9},{4,10},{5,11},{6,12},{7,13},{10,16},{11,17},{12,18},{1... | collective-permute-start | bytes 18440 | tf_op jit(solution)/shard_map/ppermute | solution.py:40
  118.0 7.3 %collective-permute-start.9 = (f32[2,2,3,128]{3,1,0,2:T(2,128)S(1)}, f32[2,2,3,128]{3,1,0,2:T(2,128)S(1)}, u32[]{:S(2)}, u32[]{:S(2)}) collective-permute-start(f32[2,2,3,128]{3,1,0,2:T(2,128)S(1)} %get-tuple-element.53), channel_id=1, source_target_pairs={{0,10},{1,11},{2,12},{3,13},{4,14},{5,15},{8,18},{9,19},{10,20},{1... | collective-permute-start | bytes 18440 | tf_op jit(solution)/shard_map/ppermute | solution.py:40
  141.2 1.3 copy-start.2

commit v3 on v2

--- a/solution.py
+++ b/solution.py
@@ -70,12 +70,11 @@
     return jnp.concatenate(segments, axis=-1)
 
 
-def tick_kernel(order_ref, pk_ref, inc_ref, ins_ref, bhi_ref, blo_ref, out_ref, *, tick, row, depth, width):
+def tick_kernel(order_ref, frc_ref, pk_ref, inc_ref, ins_ref, bhi_ref, blo_ref, out_ref, *, row, depth, width):
     nsrc, rows, owned = out_ref.shape
     cols = pk_ref.shape[1]
     classes = bhi_ref.shape[1] // rows
     lanes = 128
-    waves = tick * nsrc * rows
     wave0 = pk_ref.shape[0] - depth - 2 * nsrc - 1
     zrow = lax.broadcasted_iota(jnp.int32, (rows, cols), 0) % depth
     top = zrow == 0
@@ -112,8 +111,8 @@
         return diagonal - beside
 
     def one_source(s, carry):
-        first = pl.multiple_of(waves + order_ref[s] * rows, rows)
-        forcing = pk_ref[pl.ds(first, rows), :]
+        first = pl.multiple_of(order_ref[s] * rows, rows)
+        forcing = frc_ref[pl.ds(first, rows), :]
         incoming = inc_ref[s]
         layer = jnp.concatenate(
             [
@@ -136,21 +135,23 @@
     lax.fori_loop(0, nsrc, one_source, 0)
 
 
-def run_tick(order, packed, incoming, ins, bhi, blo, tick, row, depth, width, owned):
+def run_tick(order, forcing, packed, incoming, ins, bhi, blo, row, depth, width, owned):
     nsrc = incoming.shape[0]
     rows, stacked = bhi.shape
     cols = packed.shape[1]
     flops = nsrc * (CORR + 1) * 3 * 2 * rows * stacked * cols
     vmem = pl.BlockSpec(memory_space=pltpu.VMEM)
     return pl.pallas_call(
-        functools.partial(tick_kernel, tick=tick, row=row, depth=depth, width=width),
+        functools.partial(tick_kernel, row=row, depth=depth, width=width),
         out_shape=jax.ShapeDtypeStruct((nsrc, rows, owned), jnp.float32),
-        in_specs=[pl.BlockSpec(memory_space=pltpu.SMEM)] + [vmem] * 5,
+        in_specs=[pl.BlockSpec(memory_space=pltpu.SMEM)] + [vmem] * 6,
         out_specs=vmem,
         cost_estimate=pl.CostEstimate(
-            flops=flops, transcendentals=0, bytes_accessed=4 * (packed.size // 2 + nsrc * rows * owned)
+            flops=flops,
+            transcendentals=0,
+            bytes_accessed=4 * (forcing.size + packed.size // 4 + nsrc * rows * owned),
         ),
-    )(order, packed, incoming, ins, bhi, blo)
+    )(order, forcing, packed, incoming, ins, bhi, blo)
 
 
 def block_matrix(inverse):
@@ -172,9 +173,10 @@
     padded = -(-cols // 128) * 128
     assert width <= nx and width <= ny
 
+    per_tick = forcing.reshape(ticks, -1, nx, ny)
     packed = jnp.concatenate(
         [
-            forcing.reshape(-1, nx, ny),
+            per_tick[0],
             wavenumber_sq,
             pending_trace.reshape(-1, nx, ny),
             column_class[0][None].astype(jnp.float32),
@@ -182,7 +184,8 @@
         axis=0,
     )
     packed = flat_extended(halo_pieces(packed, width), nx, width, padded)
-    first_pending = ticks * nsrc * two * depth + depth
+    later = [halo_pieces(per_tick[t], width) for t in range(1, ticks)]
+    first_pending = nsrc * two * depth + depth
 
     gx = lax.axis_index("tx") * nx - width + jnp.arange(ex)
     gy = lax.axis_index("ty") * ny - width + jnp.arange(ey)
@@ -199,10 +202,14 @@
     incoming = packed[first_pending : first_pending + nsrc * two].reshape(nsrc, two, padded)
     solutions = []
     trace = None
+    forcing_f = packed
     for tick in range(ticks):
         field = run_tick(
-            orders[tick], packed, incoming, inside, bhi, blo, tick, ey, depth, width, nx * ny
+            orders[tick], forcing_f, packed, incoming, inside, bhi, blo, ey, depth, width, nx * ny
         )
+        if tick + 1 < ticks:
+            field, pieces = lax.optimization_barrier((field, later[tick]))
+            forcing_f = flat_extended(pieces, nx, width, padded)
         tile = field.reshape(nsrc, two, depth, nx, ny)
         solutions.append(tile)
         trace = tile[:, :, depth - 1]

time: 146 us -> 177 us (1.21)
  the two profiles are of different devices: /device:TPU:12 before, /device:TPU:16 now
where the time goes in v3:
time: 177 us; the launch traced here: 175 us
  local copies, waits for them, and re-layouts  52.9 us (30%)
  starting transfers between devices  50.6 us (29%)
  waiting for transfers between devices  36.7 us (21%)
  Pallas kernels  30.3 us (17%)
  other arithmetic  3.51 us (2%)
    ppermute x25, starting transfers between devices, fetch(): return lax.ppermute(block, tuple(axes), pairs)  50.6 us
    ppermute x25, waiting for transfers between devices, fetch(): return lax.ppermute(block, tuple(axes), pairs)  36.7 us
    pallas_call x2, Pallas kernels, run_tick(): pl.pallas_call(functools.partial(tick_kernel, row=row, depth=depth, width...  30.3 us
    squeeze x21, local copies, waits for them, and re-layouts, flat_extended(): segments.append(pieces[dx, dy][..., r, :])  19.8 us
    concatenate x3, local copies, waits for them, and re-layouts, flat_extended(): return jnp.concatenate(segments, axis=-1)  10.4 us
    slice x11, local copies, waits for them, and re-layouts, halo_pieces(): piece = block[..., rows[dx], cols[dy]]  8.86 us
    unnamed x32, local copies, waits for them, and re-layouts  4.22 us
  transfers between devices with their start and end apart: 25, of which 4 were waited for; matrix products, arithmetic and copies ran while one was open for 24% of the time, Pallas kernels for 9%

profile of v3, /device:TPU:16, one launch (start us, length us, event | category | flops | bytes accessed | tf_op | source)
XLA Modules:
  0.0 175.1 jit_solution(1276466235013213204)
XLA Ops:
  1.3 0.7 copy.22
  2.0 0.9 copy.23
  2.9 1.3 fusion.2
  4.3 1.6 fusion.3
  5.9 3.6 %collective-permute-start = (f32[325,3,3]{2,0,1:T(8,128)}, f32[325,3,3]{2,0,1:T(8,128)}, u32[]{:S(2)}, u32[]{:S(2)}) collective-permute-start(f32[325,3,3]{2,0,1:T(8,128)} %get-tuple-element.27), channel_id=1, source_target_pairs={{0,3},{2,5},{4,7},{8,11},{10,13},{12,15},{16,19},{18,21},{20,23},{... | collective-permute-start | bytes 35108 | tf_op jit(solution)/shard_map/ppermute | solution.py:40
  9.6 1.1 fusion.4
  10.6 4.2 %collective-permute-start.1 = (f32[325,3,128]{2,0,1:T(8,128)}, f32[325,3,128]{2,0,1:T(8,128)}, u32[]{:S(2)}, u32[]{:S(2)}) collective-permute-start(f32[325,3,128]{2,0,1:T(8,128)} %get-tuple-element.29), channel_id=1, source_target_pairs={{0,2},{1,3},{2,4},{3,5},{4,6},{5,7},{8,10},{9,11},{10,12},{11,13},... | collective-permute-start | bytes 1497608 | tf_op jit(solution)/shard_map/ppermute | solution.py:40
  14.8 1.4 collective-permute-start.2
  16.7 4.0 %collective-permute-start.3 = (f32[325,4,3]{0,1,2:T(4,128)S(1)}, f32[325,4,3]{0,1,2:T(4,128)S(1)}, u32[]{:S(2)}, u32[]{:S(2)}) collective-permute-start(f32[325,4,3]{0,1,2:T(4,128)S(1)} %copy.25), channel_id=1, source_target_pairs={{0,1},{2,3},{4,5},{6,7},{8,9},{10,11},{12,13},{14,15},{16,17},{18,... | collective-permute-start | bytes 46808 | tf_op jit(solution)/shard_map/ppermute | solution.py:40
  21.0 1.3 collective-permute-start.4
  22.3 0.9 slice_bitcast_fusion.9
  23.3 1.4 fusion.6
  24.7 0.9 fusion.7
  25.7 1.1 fusion.8
  28.4 0.7 fusion
  29.8 1.9 %slice_bitcast_fusion.15 = (f32[325,3]{1,0:T(8,128)}, f32[325,3]{1,0:T(8,128)}, f32[325,3]{1,0:T(8,128)}) fusion(f32[325,3,3]{2,0,1:T(8,128)} %collective-permute-done), kind=kLoop, calls=%fused_computation.23 | loop fusion | bytes 23400 | tf_op jit(solution)/shard_map/squeeze | solution.py:66
  31.8 1.3 collective-permute-start.6
  33.0 1.9 %slice_bitcast_fusion.13 = (f32[325,3]{1,0:T(8,128)}, f32[325,3]{1,0:T(8,128)}, f32[325,3]{1,0:T(8,128)}) fusion(f32[325,3,3]{2,0,1:T(8,128)} %collective-permute-done.2), kind=kLoop, calls=%fused_computation.21 | loop fusion | bytes 23400 | tf_op jit(solution)/shard_map/squeeze | solution.py:66
  35.0 1.3 collective-permute-start.7
  36.3 0.8 slice_bitcast_fusion.2
  37.1 19.8 %collective-permute-done.7 = f32[325,3,3]{2,0,1:T(8,128)S(1)} collective-permute-done((f32[325,3,3]{2,0,1:T(8,128)S(1)}, f32[325,3,3]{2,0,1:T(8,128)S(1)}, u32[]{:S(2)}, u32[]{:S(2)}) %collective-permute-start.7) | collective-permute-done | bytes 11732 | tf_op jit(solution)/shard_map/ppermute | solution.py:40
  56.9 2.0 %collective-permute-start.8 = (f32[256,3,3]{2,0,1:T(8,128)}, f32[256,3,3]{2,0,1:T(8,128)}, u32[]{:S(2)}, u32[]{:S(2)}) collective-permute-start(f32[256,3,3]{2,0,1:T(8,128)} %get-tuple-element.51), channel_id=1, source_target_pairs={{0,3},{2,5},{4,7},{8,11},{10,13},{12,15},{16,19},{18,21},{20,23},{... | collective-permute-start | bytes 27656 | tf_op jit(solution)/shard_map/ppermute | solution.py:40
  58.9 0.8 slice_bitcast_fusion
  59.7 3.6 %collective-permute-start.9 = (f32[256,3,128]{2,0,1:T(8,128)}, f32[256,3,128]{2,0,1:T(8,128)}, u32[]{:S(2)}, u32[]{:S(2)}) collective-permute-start(f32[256,3,128]{2,0,1:T(8,128)} %get-tuple-element.53), channel_id=1, source_target_pairs={{0,2},{1,3},{2,4},{3,5},{4,6},{5,7},{8,10},{9,11},{10,12},{11,13},... | collective-permute-start | bytes 1179656 | tf_op jit(solution)/shard_map/ppermute | solution.py:40
  63.5 1.4 collective-permute-start.10
  65.8 0.8 copy.45
  66.6 3.3 %collective-permute-start.11 = (f32[256,4,3]{2,0,1:T(8,128)}, f32[256,4,3]{2,0,1:T(8,128)}, u32[]{:S(2)}, u32[]{:S(2)}) collective-permute-start(f32[256,4,3]{2,0,1:T(8,128)} %get-tuple-element.55), channel_id=1, source_target_pairs={{0,1},{2,3},{4,5},{6,7},{8,9},{10,11},{12,13},{14,15},{16,17},{18,... | collective-permute-start | bytes 36872 | tf_op jit(solution)/shard_map/ppermute | solution.py:40
  70.0 1.9 %slice_bitcast_fusion.14 = (f32[325,128]{1,0:T(8,128)}, f32[325,128]{1,0:T(8,128)}, f32[325,128]{1,0:T(8,128)}) fusion(f32[325,3,128]{2,0,1:T(8,128)} %collective-permute-done.1), kind=kLoop, calls=%fused_computation.22 | loop fusion | bytes 998400 | tf_op jit(solution)/shard_map/squeeze | solution.py:66
  71.9 1.4 collective-permute-start.13
  73.3 0.8 slice_bitcast_fusion.1
  74.1 0.7 broadcast_in_dim.11
  74.8 4.3 %concatenate.25.frc_ref.pk_ref = f32[325,1408]{1,0:T(8,128)S(1)} concatenate(f32[325,3]{1,0:T(8,128)} %get-tuple-element.73, f32[325,128]{1,0:T(8,128)} %get-tuple-element.70, f32[325,3]{1,0:T(8,128)} %get-tuple-element.67, f32[325,3]{1,0:T(8,128)} %get-tuple-element.72, f32[325,128]{1,0:T(8,128)} %get-tuple-element.69, f32[325,3]{1,0:T(8,128)} %get-tuple-element.66, ...), dimensions={1} | concatenate | bytes 3660800 | tf_op jit(solution)/shard_map/concatenate | solution.py:70
  79.1 0.7 reshape.68.inc_ref
  79.8 1.3 collective-permute-start.12
  81.1 1.3 collective-permute-start.14
  82.4 1.3 collective-permute-start.15
  83.8 15.3 %shard_map.77 = f32[2,128,512]{2,1,0:T(8,128)} custom-call(s32[2]{0:T(128)} %get-tuple-element.146.order_ref, f32[325,1408]{1,0:T(8,128)} %copy-done, f32[325,1408]{1,0:T(8,128)} %copy-done, f32[2,2,1408]{2,1,0:T(2,128)} %reshape.68.inc_ref, f32[1,1408]{1,0:T(1,128)} %pad_convert_fusion.ins_ref, bf16[128,512]{1,0:T(8,128)(2,1)} %get-tuple-element.93.bhi_ref, ...), custom_call_target="tpu_custom_call" | custom-call | flops 4429185024 | bytes 2812288 | tf_op jit(solution)/shard_map/pallas_call | solution.py:144
  99.5 0.7 copy-done.6
  100.2 1.2 reshape.69
  103.4 3.5 %collective-permute-start.20 = (f32[2,2,4,128]{3,1,0,2:T(2,128)S(1)}, f32[2,2,4,128]{3,1,0,2:T(2,128)S(1)}, u32[]{:S(2)}, u32[]{:S(2)}) collective-permute-start(f32[2,2,4,128]{3,1,0,2:T(2,128)S(1)} %bitcast.218), channel_id=1, source_target_pairs={{0,8},{1,9},{2,10},{3,11},{4,12},{5,13},{6,14},{7,15},{8,16},{9,17... | collective-permute-start | bytes 24584 | tf_op jit(solution)/shard_map/ppermute | solution.py:40
  106.9 1.2 stack_reshape.6
  108.1 1.8 %slice_bitcast_fusion.46 = (f32[256,128]{1,0:T(8,128)}, f32[256,128]{1,0:T(8,128)}, f32[256,128]{1,0:T(8,128)}) fusion(f32[256,3,128]{2,0,1:T(8,128)} %collective-permute-done.9), kind=kLoop, calls=%fused_computation.54 | loop fusion | bytes 786432 | tf_op jit(solution)/shard_map/squeeze | solution.py:66
  109.9 4.0 %collective-permute-start.16 = (f32[2,2,3,3]{3,1,0,2:T(2,128)}, f32[2,2,3,3]{3,1,0,2:T(2,128)}, u32[]{:S(2)}, u32[]{:S(2)}) collective-permute-start(f32[2,2,3,3]{3,1,0,2:T(2,128)} %get-tuple-element.111), channel_id=1, source_target_pairs={{0,11},{2,13},{4,15},{8,19},{10,21},{12,23},{16,27},{18,29},{20,31}} | collective-permute-start | bytes 440 | tf_op jit(solution)/shard_map/ppermute | solution.py:40
  113.9 1.9 %collective-permute-start.17 = (f32[2,2,3,128]{3,1,0,2:T(2,128)}, f32[2,2,3,128]{3,1,0,2:T(2,128)}, u32[]{:S(2)}, u32[]{:S(2)}) collective-permute-start(f32[2,2,3,128]{3,1,0,2:T(2,128)} %get-tuple-element.113), channel_id=1, source_target_pairs={{0,10},{1,11},{2,12},{3,13},{4,14},{5,15},{8,18},{9,19},{10,20},{1... | collective-permute-start | bytes 18440 | tf_op jit(solution)/shard_map/ppermute | solution.py:40
  115.8 1.2 collective-permute-start.18
  117.0 1.9 %collective-permute-start.19 = (f32[2,2,4,3]{3,1,0,2:T(2,128)}, f32[2,2,4,3]{3,1,0,2:T(2,128)}, u32[]{:S(2)}, u32[]{:S(2)}) collective-permute-start(f32[2,2,4,3]{3,1,0,2:T(2,128)} %get-tuple-element.127), channel_id=1, source_target_pairs={{0,9},{2,11},{4,13},{6,15},{8,17},{10,19},{12,21},{14,23},{16,25},... | collective-permute-start | bytes 584 | tf_op jit(solution)/shard_map/ppermute | solution.py:40
  118.9 1.3 slice_bitcast_fusion.45
  120.2 1.9 %slice_bitcast_fusion.33 = (f32[256,3]{1,0:T(8,128)S(1)}, f32[256,3]{1,0:T(8,128)S(1)}, f32[256,3]{1,0:T(8,128)S(1)}, f32[256,3]{1,0:T(8,128)S(1)}, f32[256,3]{1...) fusion(f32[256,4,3]{2,0,1:T(8,128)S(1)} %collective-permute-done.12, ...), kind=kLoop, calls=%fused_computation.41 | loop fusion | bytes 49152 | tf_op jit(solution)/shard_map/squeeze | solution.py:66
  122.1 1.1 slice_bitcast_fusion.25
  123.2 1.9 %slice_bitcast_fusion.24 = (f32[256,3]{1,0:T(8,128)S(1)}, f32[256,3]{1,0:T(8,128)S(1)}, f32[256,3]{1,0:T(8,128)}, f32[256,3]{1,0:T(8,128)}, f32[256,3]{1,0:T(8,128)}, /*index=5*/f32[256,3]{1,0:T(8,128)}) fusion(f32[256,3,3]{2,0,1:T(8,128)S(1)} %copy-done.7, f32[256,3,3]{2,0,1:T(8,128)} %collective-permute-done.13), kind=kLoop, calls=%fused_computation.32 | loop fusion | bytes 36864 | tf_op jit(solution)/shard_map/squeeze | solution.py:66
  125.8 5.3 %concatenate.30.frc_ref = f32[256,1408]{1,0:T(8,128)} concatenate(f32[256,3]{1,0:T(8,128)S(1)} %get-tuple-element.159, f32[256,128]{1,0:T(8,128)} %get-tuple-element.88, f32[256,3]{1,0:T(8,128)S(1)} %get-tuple-element.85, f32[256,3]{1,0:T(8,128)S(1)} %get-tuple-element.160, f32[256,128]{1,0:T(8,128)} %get-tuple-element.87, f32[256,3]{1,0:T(8,128)S(1)} %get-tuple-element.84, ...), dimensions={1} | concatenate | bytes 2883584 | tf_op jit(solution)/shard_map/concatenate | solution.py:70
  131.1 1.3 collective-permute-start.21
  132.4 0.7 slice_bitcast_fusion.81
  134.5 1.3 collective-permute-start.24
  135.8 12.7 %collective-permute-done.24 = f32[2,2,3,3]{3,1,0,2:T(2,128)S(1)} collective-permute-done((f32[2,2,3,3]{3,1,0,2:T(2,128)}, f32[2,2,3,3]{3,1,0,2:T(2,128)S(1)}, u32[]{:S(2)}, u32[]{:S(2)}) %collective-permute-start.24) | collective-permute-done | bytes 176 | tf_op jit(solution)/shard_map/ppermute | solution.py:40
  148.4 1.5 collective-permute-start.23
  149.9 0.7 slice_bitcast_fusion.69
  150.6 0.7 slice_bitcast_fusion.80
  151.3 3.7 %collective-permute-done.23 = f32[2,2,3,128]{3,1,0,2:T(2,128)S(1)} collective-permute-done((f32[2,2,3,128]{3,1,0,2:T(2,128)}, f32[2,2,3,128]{3,1,0,2:T(2,128)S(1)}, u32[]{:S(2)}, u32[]{:S(2)}) %collective-permute-start.23) | collective-permute-done | bytes 6176 | tf_op jit(solution)/shard_map/ppermute | solution.py:40
  155.1 0.8 concatenate.31.inc_ref
  155.8 15.1 %shard_map.78 = f32[2,128,512]{2,1,0:T(8,128)} custom-call(s32[2]{0:T(128)} %get-tuple-element.147.order_ref, f32[256,1408]{1,0:T(8,128)} %concatenate.30.frc_ref, f32[325,1408]{1,0:T(8,128)} %copy-done, f32[2,2,1408]{2,1,0:T(2,128)} %concatenate.31.inc_ref, f32[1,1408]{1,0:T(1,128)} %pad_convert_fusion.ins_ref, bf16[128,512]{1,0:T(8,128)(2,1)} %get-tuple-element.93.bhi_ref, ...), custom_call_target="tpu_custom_call" | custom-call | flops 4429185024 | bytes 2423680 | tf_op jit(solution)/shard_map/pallas_call | solution.py:144
  170.9 1.2 stack_reshape.7
  172.1 1.2 reshape.70
  173.9 1.2 pad_maximum_fusion
  (85 shorter events, 10.0 us)
Async XLA Ops:
  5.9 23.2 %collective-permute-start = (f32[325,3,3]{2,0,1:T(8,128)}, f32[325,3,3]{2,0,1:T(8,128)}, u32[]{:S(2)}, u32[]{:S(2)}) collective-permute-start(f32[325,3,3]{2,0,1:T(8,128)} %get-tuple-element.27), channel_id=1, source_target_pairs={{0,3},{2,5},{4,7},{8,11},{10,13},{12,15},{16,19},{18,21},{20,23},{... | collective-permute-start | bytes 35108 | tf_op jit(solution)/shard_map/ppermute | solution.py:40
  10.6 56.0 %collective-permute-start.1 = (f32[325,3,128]{2,0,1:T(8,128)}, f32[325,3,128]{2,0,1:T(8,128)}, u32[]{:S(2)}, u32[]{:S(2)}) collective-permute-start(f32[325,3,128]{2,0,1:T(8,128)} %get-tuple-element.29), channel_id=1, source_target_pairs={{0,2},{1,3},{2,4},{3,5},{4,6},{5,7},{8,10},{9,11},{10,12},{11,13},... | collective-permute-start | bytes 1497608 | tf_op jit(solution)/shard_map/ppermute | solution.py:40
  14.8 17.0 %collective-permute-start.2 = (f32[325,3,3]{2,0,1:T(8,128)}, f32[325,3,3]{2,0,1:T(8,128)}, u32[]{:S(2)}, u32[]{:S(2)}) collective-permute-start(f32[325,3,3]{2,0,1:T(8,128)} %get-tuple-element.26), channel_id=1, source_target_pairs={{1,2},{3,4},{5,6},{9,10},{11,12},{13,14},{17,18},{19,20},{21,22},{... | collective-permute-start | bytes 35108 | tf_op jit(solution)/shard_map/ppermute | solution.py:40
  16.5 6.7 %copy-start.8 = (f32[1,4,2,64,64]{4,3,2,1,0:T(8,128)S(1)}, f32[1,4,2,64,64]{4,3,2,1,0:T(8,128)}, u32[]{:S(2)}) copy-start(f32[1,4,2,64,64]{4,3,2,1,0:T(8,128)} %param.8) | copy-start | bytes 393220
  16.7 43.0 %collective-permute-start.3 = (f32[325,4,3]{0,1,2:T(4,128)S(1)}, f32[325,4,3]{0,1,2:T(4,128)S(1)}, u32[]{:S(2)}, u32[]{:S(2)}) collective-permute-start(f32[325,4,3]{0,1,2:T(4,128)S(1)} %copy.25), channel_id=1, source_target_pairs={{0,1},{2,3},{4,5},{6,7},{8,9},{10,11},{12,13},{14,15},{16,17},{18,... | collective-permute-start | bytes 46808 | tf_op jit(solution)/shard_map/ppermute | solution.py:40
  21.0 42.5 %collective-permute-start.4 = (f32[325,4,3]{0,1,2:T(4,128)S(1)}, f32[325,4,3]{0,1,2:T(4,128)S(1)}, u32[]{:S(2)}, u32[]{:S(2)}) collective-permute-start(f32[325,4,3]{0,1,2:T(4,128)S(1)} %copy.27), channel_id=1, source_target_pairs={{1,0},{3,2},{5,4},{7,6},{9,8},{11,10},{13,12},{15,14},{17,16},{19,... | collective-permute-start | bytes 46808 | tf_op jit(solution)/shard_map/ppermute | solution.py:40
  24.7 2.1 %copy-start.9 = (s32[2,1,2]{2,1,0:T(1,128)S(1)}, s32[2,1,2]{2,1,0:T(1,128)}, u32[]{:S(2)}) copy-start(s32[2,1,2]{2,1,0:T(1,128)} %param.10) | copy-start | bytes 52
  25.7 3.4 %copy-start.4 = (f32[325,3,3]{2,0,1:T(8,128)S(1)}, f32[325,3,3]{2,0,1:T(8,128)}, u32[]{:S(2)}) copy-start(f32[325,3,3]{2,0,1:T(8,128)} %get-tuple-element.25) | copy-start | bytes 35104
  26.8 4.9 %copy-start.5 = (f32[325,3,128]{2,0,1:T(8,128)S(1)}, f32[325,3,128]{2,0,1:T(8,128)}, u32[]{:S(2)}) copy-start(f32[325,3,128]{2,0,1:T(8,128)} %get-tuple-element.28) | copy-start | bytes 1497604
  28.2 6.8 %copy-start.3 = (f32[325,3,3]{2,0,1:T(8,128)S(1)}, f32[325,3,3]{2,0,1:T(8,128)}, u32[]{:S(2)}) copy-start(f32[325,3,3]{2,0,1:T(8,128)} %get-tuple-element.24) | copy-start | bytes 35104
  29.1 5.9 %collective-permute-start.5 = (f32[325,3,3]{2,0,1:T(8,128)S(1)}, f32[325,3,3]{2,0,1:T(8,128)S(1)}, u32[]{:S(2)}, u32[]{:S(2)}) collective-permute-start(f32[325,3,3]{2,0,1:T(8,128)S(1)} %copy-done.4), channel_id=1, source_target_pairs={{2,1},{4,3},{6,5},{10,9},{12,11},{14,13},{18,17},{20,19},{22,21},{... | collective-permute-start | bytes 35108 | tf_op jit(solution)/shard_map/ppermute | solution.py:40
  31.8 40.1 %collective-permute-start.6 = (f32[325,3,128]{2,0,1:T(8,128)S(1)}, f32[325,3,128]{2,0,1:T(8,128)S(1)}, u32[]{:S(2)}, u32[]{:S(2)}) collective-permute-start(f32[325,3,128]{2,0,1:T(8,128)S(1)} %copy-done.5), channel_id=1, source_target_pairs={{2,0},{3,1},{4,2},{5,3},{6,4},{7,5},{10,8},{11,9},{12,10},{13,11},... | collective-permute-start | bytes 1497608 | tf_op jit(solution)/shard_map/ppermute | solution.py:40
  35.0 21.9 %collective-permute-start.7 = (f32[325,3,3]{2,0,1:T(8,128)S(1)}, f32[325,3,3]{2,0,1:T(8,128)S(1)}, u32[]{:S(2)}, u32[]{:S(2)}) collective-permute-start(f32[325,3,3]{2,0,1:T(8,128)S(1)} %copy-done.3), channel_id=1, source_target_pairs={{3,0},{5,2},{7,4},{11,8},{13,10},{15,12},{19,16},{21,18},{23,20},{... | collective-permute-start | bytes 35108 | tf_op jit(solution)/shard_map/ppermute | solution.py:40
  56.9 23.0 %collective-permute-start.8 = (f32[256,3,3]{2,0,1:T(8,128)}, f32[256,3,3]{2,0,1:T(8,128)}, u32[]{:S(2)}, u32[]{:S(2)}) collective-permute-start(f32[256,3,3]{2,0,1:T(8,128)} %get-tuple-element.51), channel_id=1, source_target_pairs={{0,3},{2,5},{4,7},{8,11},{10,13},{12,15},{16,19},{18,21},{20,23},{... | collective-permute-start | bytes 27656 | tf_op jit(solution)/shard_map/ppermute | solution.py:40
  59.7 39.7 %collective-permute-start.9 = (f32[256,3,128]{2,0,1:T(8,128)}, f32[256,3,128]{2,0,1:T(8,128)}, u32[]{:S(2)}, u32[]{:S(2)}) collective-permute-start(f32[256,3,128]{2,0,1:T(8,128)} %get-tuple-element.53), channel_id=1, source_target_pairs={{0,2},{1,3},{2,4},{3,5},{4,6},{5,7},{8,10},{9,11},{10,12},{11,13},... | collective-permute-start | bytes 1179656 | tf_op jit(solution)/shard_map/ppermute | solution.py:40
  63.5 17.7 %collective-permute-start.10 = (f32[256,3,3]{2,0,1:T(8,128)}, f32[256,3,3]{2,0,1:T(8,128)}, u32[]{:S(2)}, u32[]{:S(2)}) collective-permute-start(f32[256,3,3]{2,0,1:T(8,128)} %get-tuple-element.50), channel_id=1, source_target_pairs={{1,2},{3,4},{5,6},{9,10},{11,12},{13,14},{17,18},{19,20},{21,22},{... | collective-permute-start | bytes 27656 | tf_op jit(solution)/shard_map/ppermute | solution.py:40
  66.6 32.8 %collective-permute-start.11 = (f32[256,4,3]{2,0,1:T(8,128)}, f32[256,4,3]{2,0,1:T(8,128)}, u32[]{:S(2)}, u32[]{:S(2)}) collective-permute-start(f32[256,4,3]{2,0,1:T(8,128)} %get-tuple-element.55), channel_id=1, source_target_pairs={{0,1},{2,3},{4,5},{6,7},{8,9},{10,11},{12,13},{14,15},{16,17},{18,... | collective-permute-start | bytes 36872 | tf_op jit(solution)/shard_map/ppermute | solution.py:40
  71.9 10.6 %collective-permute-start.13 = (f32[256,3,3]{2,0,1:T(8,128)}, f32[256,3,3]{2,0,1:T(8,128)}, u32[]{:S(2)}, u32[]{:S(2)}) collective-permute-start(f32[256,3,3]{2,0,1:T(8,128)} %get-tuple-element.49), channel_id=1, source_target_pairs={{2,1},{4,3},{6,5},{10,9},{12,11},{14,13},{18,17},{20,19},{22,21},{... | collective-permute-start | bytes 27656 | tf_op jit(solution)/shard_map/ppermute | solution.py:40
  79.1 4.6 %copy-start = (f32[325,1408]{1,0:T(8,128)}, f32[325,1408]{1,0:T(8,128)S(1)}, u32[]{:S(2)}) copy-start(f32[325,1408]{1,0:T(8,128)S(1)} %concatenate.25.frc_ref.pk_ref) | copy-start | bytes 5491204
  79.8 19.6 %collective-permute-start.12 = (f32[256,4,3]{2,0,1:T(8,128)}, f32[256,4,3]{2,0,1:T(8,128)S(1)}, u32[]{:S(2)}, u32[]{:S(2)}) collective-permute-start(f32[256,4,3]{2,0,1:T(8,128)} %get-tuple-element.54), channel_id=1, source_target_pairs={{1,0},{3,2},{5,4},{7,6},{9,8},{11,10},{13,12},{15,14},{17,16},{19,... | collective-permute-start | bytes 36872 | tf_op jit(solution)/shard_map/ppermute | solution.py:40
  81.1 19.1 %collective-permute-start.14 = (f32[256,3,128]{2,0,1:T(8,128)}, f32[256,3,128]{2,0,1:T(8,128)}, u32[]{:S(2)}, u32[]{:S(2)}) collective-permute-start(f32[256,3,128]{2,0,1:T(8,128)} %get-tuple-element.52), channel_id=1, source_target_pairs={{2,0},{3,1},{4,2},{5,3},{6,4},{7,5},{10,8},{11,9},{12,10},{13,11},... | collective-permute-start | bytes 1179656 | tf_op jit(solution)/shard_map/ppermute | solution.py:40
  82.4 17.0 %collective-permute-start.15 = (f32[256,3,3]{2,0,1:T(8,128)}, f32[256,3,3]{2,0,1:T(8,128)S(1)}, u32[]{:S(2)}, u32[]{:S(2)}) collective-permute-start(f32[256,3,3]{2,0,1:T(8,128)} %get-tuple-element.48), channel_id=1, source_target_pairs={{3,0},{5,2},{7,4},{11,8},{13,10},{15,12},{19,16},{21,18},{23,20},{... | collective-permute-start | bytes 27656 | tf_op jit(solution)/shard_map/ppermute | solution.py:40
  99.4 0.8 copy-start.6
  103.4 51.6 %collective-permute-start.20 = (f32[2,2,4,128]{3,1,0,2:T(2,128)S(1)}, f32[2,2,4,128]{3,1,0,2:T(2,128)S(1)}, u32[]{:S(2)}, u32[]{:S(2)}) collective-permute-start(f32[2,2,4,128]{3,1,0,2:T(2,128)S(1)} %bitcast.218), channel_id=1, source_target_pairs={{0,8},{1,9},{2,10},{3,11},{4,12},{5,13},{6,14},{7,15},{8,16},{9,17... | collective-permute-start | bytes 24584 | tf_op jit(solution)/shard_map/ppermute | solution.py:40
  109.9 21.2 %collective-permute-start.16 = (f32[2,2,3,3]{3,1,0,2:T(2,128)}, f32[2,2,3,3]{3,1,0,2:T(2,128)}, u32[]{:S(2)}, u32[]{:S(2)}) collective-permute-start(f32[2,2,3,3]{3,1,0,2:T(2,128)} %get-tuple-element.111), channel_id=1, source_target_pairs={{0,11},{2,13},{4,15},{8,19},{10,21},{12,23},{16,27},{18,29},{20,31}} | collective-permute-start | bytes 440 | tf_op jit(solution)/shard_map/ppermute | solution.py:40
  113.9 36.7 %collective-permute-start.17 = (f32[2,2,3,128]{3,1,0,2:T(2,128)}, f32[2,2,3,128]{3,1,0,2:T(2,128)}, u32[]{:S(2)}, u32[]{:S(2)}) collective-permute-start(f32[2,2,3,128]{3,1,0,2:T(2,128)} %get-tuple-element.113), channel_id=1, source_target_pairs={{0,10},{1,11},{2,12},{3,13},{4,14},{5,15},{8,18},{9,19},{10,20},{1... | collective-permute-start | bytes 18440 | tf_op jit(solution)/shard_map/ppermute | solution.py:40
  115.8 17.3 %collective-permute-start.18 = (f32[2,2,3,3]{3,1,0,2:T(2,128)}, f32[2,2,3,3]{3,1,0,2:T(2,128)}, u32[]{:S(2)}, u32[]{:S(2)}) collective-permute-start(f32[2,2,3,3]{3,1,0,2:T(2,128)} %get-tuple-element.110), channel_id=1, source_target_pairs={{1,10},{3,12},{5,14},{9,18},{11,20},{13,22},{17,26},{19,28},{21,30}} | collective-permute-start | bytes 440 | tf_op jit(solution)/shard_map/ppermute | solution.py:40
  117.0 32.9 %collective-permute-start.19 = (f32[2,2,4,3]{3,1,0,2:T(2,128)}, f32[2,2,4,3]{3,1,0,2:T(2,128)}, u32[]{:S(2)}, u32[]{:S(2)}) collective-permute-start(f32[2,2,4,3]{3,1,0,2:T(2,128)} %get-tuple-element.127), channel_id=1, source_target_pairs={{0,9},{2,11},{4,13},{6,15},{8,17},{10,19},{12,21},{14,23},{16,25},... | collective-permute-start | bytes 584 | tf_op jit(solution)/shard_map/ppermute | solution.py:40
  120.2 3.0 %copy-start.7 = (f32[256,3,3]{2,0,1:T(8,128)S(1)}, f32[256,3,3]{2,0,1:T(8,128)}, u32[]{:S(2)}) copy-start(f32[256,3,3]{2,0,1:T(8,128)} %copy-done.6) | copy-start | bytes 27652
  123.2 2.6 %copy-start.1 = (f32[256,3]{1,0:T(8,128)S(1)}, f32[256,3]{1,0:T(8,128)}, u32[]{:S(2)}) copy-start(f32[256,3]{1,0:T(8,128)} %get-tuple-element.157) | copy-start | bytes 9220
  123.2 2.6 %copy-start.2 = (f32[256,3]{1,0:T(8,128)S(1)}, f32[256,3]{1,0:T(8,128)}, u32[]{:S(2)}) copy-start(f32[256,3]{1,0:T(8,128)} %get-tuple-element.158) | copy-start | bytes 9220
  131.1 19.5 %collective-permute-start.21 = (f32[2,2,4,3]{3,1,0,2:T(2,128)}, f32[2,2,4,3]{3,1,0,2:T(2,128)S(1)}, u32[]{:S(2)}, u32[]{:S(2)}) collective-permute-start(f32[2,2,4,3]{3,1,0,2:T(2,128)} %get-tuple-element.126), channel_id=1, source_target_pairs={{1,8},{3,10},{5,12},{7,14},{9,16},{11,18},{13,20},{15,22},{17,24},... | collective-permute-start | bytes 584 | tf_op jit(solution)/shard_map/ppermute | solution.py:40
  133.1 1.3 collective-permute-start.22
  134.5 14.0 %collective-permute-start.24 = (f32[2,2,3,3]{3,1,0,2:T(2,128)}, f32[2,2,3,3]{3,1,0,2:T(2,128)S(1)}, u32[]{:S(2)}, u32[]{:S(2)}) collective-permute-start(f32[2,2,3,3]{3,1,0,2:T(2,128)} %get-tuple-element.108), channel_id=1, source_target_pairs={{3,8},{5,10},{7,12},{11,16},{13,18},{15,20},{19,24},{21,26},{23,28}} | collective-permute-start | bytes 440 | tf_op jit(solution)/shard_map/ppermute | solution.py:40
  148.4 6.6 %collective-permute-start.23 = (f32[2,2,3,128]{3,1,0,2:T(2,128)}, f32[2,2,3,128]{3,1,0,2:T(2,128)S(1)}, u32[]{:S(2)}, u32[]{:S(2)}) collective-permute-start(f32[2,2,3,128]{3,1,0,2:T(2,128)} %get-tuple-element.112), channel_id=1, source_target_pairs={{2,8},{3,9},{4,10},{5,11},{6,12},{7,13},{10,16},{11,17},{12,18},{1... | collective-permute-start | bytes 18440 | tf_op jit(solution)/shard_map/ppermute | solution.py:40

commit v4 on v2

--- a/solution.py
+++ b/solution.py
@@ -40,30 +40,28 @@
     return lax.ppermute(block, tuple(axes), pairs)
 
 
-def halo_pieces(block, width, lead_axes=(), lead_offsets=()):
-    nx, ny = block.shape[-2], block.shape[-1]
-    rows = {-1: slice(nx - width, nx), 0: slice(0, nx), 1: slice(0, width)}
-    cols = {-1: slice(ny - width, ny), 0: slice(0, ny), 1: slice(0, width)}
-    pieces = {}
-    for dx in (-1, 0, 1):
-        for dy in (-1, 0, 1):
-            piece = block[..., rows[dx], cols[dy]]
-            if dx == 0 and dy == 0 and not lead_axes:
-                pieces[dx, dy] = piece
-            else:
-                pieces[dx, dy] = fetch(
-                    piece, tuple(lead_axes) + ("tx", "ty"), tuple(lead_offsets) + (dx, dy)
-                )
-    return pieces
-
-
-def flat_extended(pieces, nx, width, padded):
+def extend_y(block, width):
+    ny = block.shape[-1]
+    low = fetch(block[..., ny - width :], ("ty",), (-1,))
+    high = fetch(block[..., :width], ("ty",), (1,))
+    return jnp.concatenate([low, block, high], axis=-1)
+
+
+def flat_extended(block, width, padded, lead_axes=(), lead_offsets=()):
+    nx = block.shape[-2]
+    pieces = {
+        -1: fetch(block[..., nx - width :, :], tuple(lead_axes) + ("tx",), tuple(lead_offsets) + (-1,)),
+        1: fetch(block[..., :width, :], tuple(lead_axes) + ("tx",), tuple(lead_offsets) + (1,)),
+    }
+    if lead_axes:
+        pieces[0] = fetch(block, tuple(lead_axes) + ("tx",), tuple(lead_offsets) + (0,))
+    else:
+        pieces[0] = block
     segments = []
     for ix in range(nx + 2 * width):
         dx = -1 if ix < width else (0 if ix < width + nx else 1)
         r = ix - (0 if dx == -1 else (width if dx == 0 else width + nx))
-        for dy in (-1, 0, 1):
-            segments.append(pieces[dx, dy][..., r, :])
+        segments.append(pieces[dx][..., r, :])
     used = sum(s.shape[-1] for s in segments)
     lead = segments[0].shape[:-1]
     segments.append(jnp.zeros(lead + (padded - used,), segments[0].dtype))
@@ -181,7 +179,7 @@
         ],
         axis=0,
     )
-    packed = flat_extended(halo_pieces(packed, width), nx, width, padded)
+    packed = flat_extended(extend_y(packed, width), width, padded)
     first_pending = ticks * nsrc * two * depth + depth
 
     gx = lax.axis_index("tx") * nx - width + jnp.arange(ex)
@@ -207,7 +205,7 @@
         solutions.append(tile)
         trace = tile[:, :, depth - 1]
         if tick + 1 < ticks:
-            incoming = flat_extended(halo_pieces(trace, width, ("slab",), (-1,)), nx, width, padded)
+            incoming = flat_extended(extend_y(trace, width), width, padded, ("slab",), (-1,))
     return (jnp.stack(solutions, axis=0), trace[:, :, None])
 
 

time: 146 us -> 139 us (0.952)
  starting transfers between devices: 39.6 us -> 23.2 us
  waiting for transfers between devices: 21.4 us -> 36.6 us
  local copies, waits for them, and re-layouts: 49.1 us -> 39.9 us
  other arithmetic: 2.87 us -> 7.04 us
    ppermute x0 -> x6, waiting for transfers between devices: none -> 33.1 us  [fetch(): return lax.ppermute(block, axes[0], pairs)]
    ppermute x17 -> x3, starting transfers between devices: 39.6 us -> 9.97 us  [fetch(): return lax.ppermute(block, tuple(axes), pairs)]
    ppermute x17 -> x3, waiting for transfers between devices: 21.4 us -> 3.51 us  [fetch(): return lax.ppermute(block, tuple(axes), pairs)]
    ppermute x0 -> x6, starting transfers between devices: none -> 13.3 us  [fetch(): return lax.ppermute(block, axes[0], pairs)]
    unnamed x43 -> x25, local copies, waits for them, and re-layouts: 20.3 us -> 10.3 us
    ppermute x0 -> x2, local copies, waits for them, and re-layouts: none -> 2.91 us  [fetch(): return lax.ppermute(block, axes[0], pairs)]
    concatenate x0 -> x2, other arithmetic: none -> 2.76 us  [extend_y(): return jnp.concatenate([low, block, high], axis=-1)]
    squeeze x12 -> x4, local copies, waits for them, and re-layouts: 4.2 us -> 1.52 us  [flat_extended(): segments.append(pieces[dx][..., r, :])]
  transfers between devices with their start and end apart: 17 -> 9, of which waited for: 4 -> 4; matrix products, arithmetic and copies ran while one was open for 21% -> 13% of each run, Pallas kernels for 0% -> 0%
where the time goes in v4:
time: 139 us; the launch traced here: 138 us
  local copies, waits for them, and re-layouts  39.9 us (29%)
  waiting for transfers between devices  36.6 us (26%)
  Pallas kernels  30.3 us (22%)
  starting transfers between devices  23.2 us (17%)
  other arithmetic  7.04 us (5%)
    ppermute x6, waiting for transfers between devices, fetch(): return lax.ppermute(block, axes[0], pairs)  33.1 us
    pallas_call x2, Pallas kernels, run_tick(): pl.pallas_call(functools.partial(tick_kernel, tick=tick, row=row, depth=d...  30.3 us
    ppermute x6, starting transfers between devices, fetch(): return lax.ppermute(block, axes[0], pairs)  13.3 us
    unnamed x25, local copies, waits for them, and re-layouts  10.3 us
    ppermute x3, starting transfers between devices, fetch(): return lax.ppermute(block, tuple(axes), pairs)  9.97 us
    concatenate x2, local copies, waits for them, and re-layouts, flat_extended(): return jnp.concatenate(segments, axis=-1)  6.02 us
    slice x3, local copies, waits for them, and re-layouts, flat_extended(): block[..., :width, :]  4.13 us
    ppermute x3, waiting for transfers between devices, fetch(): return lax.ppermute(block, tuple(axes), pairs)  3.51 us
  transfers between devices with their start and end apart: 9, of which 4 were waited for; matrix products, arithmetic and copies ran while one was open for 13% of the time, Pallas kernels for 0%

profile of v4, /device:TPU:12, one launch (start us, length us, event | category | flops | bytes accessed | tf_op | source)
XLA Modules:
  0.0 138.0 jit_solution(17000015534341948386)
XLA Ops:
  0.7 1.4 %copy.19 = f32[2,2,2,64,4,128]{5,3,2,1,0,4:T(8,128)S(1)} copy(f32[2,2,2,64,4,128]{5,4,3,2,1,0:T(4,128)} %param.6) | data formatting | bytes 2097152 | tf_op args[0]
  2.1 0.0 copy-start.1
  2.2 0.6 copy-done.1
  2.8 0.1 pad_maximum_fusion.1
  2.9 0.4 fusion.3
  3.2 0.4 copy.23
  3.6 1.7 %collective-permute-start = (f32[581,4,3]{0,1,2:T(4,128)S(1)}, f32[581,4,3]{0,1,2:T(4,128)S(1)}, u32[]{:S(2)}, u32[]{:S(2)}) collective-permute-start(f32[581,4,3]{0,1,2:T(4,128)S(1)} %copy.23), channel_id=1, source_target_pairs={{0,1},{2,3},{4,5},{6,7},{8,9},{10,11},{12,13},{14,15},{16,17},{18,... | collective-permute-start | bytes 83672 | tf_op jit(solution)/shard_map/ppermute | solution.py:39
  5.4 0.4 copy.24
  5.8 1.3 collective-permute-start.1
  7.1 1.0 copy.46
  8.1 0.1 maximum_maximum_fusion
  8.2 0.7 slice_bitcast_fusion.9
  8.9 0.5 compare_and_fusion
  9.4 0.0 collective-permute-done
  9.5 1.4 %copy.25 = f32[581,4,3]{2,0,1:T(8,128)} copy(f32[581,4,3]{0,1,2:T(4,128)S(1)} %collective-permute-done) | data formatting | bytes 55776 | tf_op jit(solution)/shard_map/ppermute | solution.py:39
  10.9 0.0 collective-permute-done.1
  10.9 1.5 %copy.26 = f32[581,4,3]{2,0,1:T(8,128)} copy(f32[581,4,3]{0,1,2:T(4,128)S(1)} %collective-permute-done.1) | data formatting | bytes 55776 | tf_op jit(solution)/shard_map/ppermute | solution.py:39
  12.4 2.7 %pad_maximum_fusion = f32[581,4,134]{2,0,1:T(8,128)S(1)} fusion(f32[581,4,3]{2,0,1:T(8,128)} %copy.26, f32[1,4,128]{2,0,1:T(1,128)S(1)} %bitcast.76, f32[4,4,128]{2,0,1:T(4,128)S(1)} %bitcast.74, f32[64,4,128]{2,0,1:T(8,128)} %copy-done.1, f32[512,4,128]{2,0,1:T(8,128)S(1)} %bitcast.62, f32[581,4,3]{2,0,1:T(8,128)} %copy.25), kind=kLoop, calls=%fused_computation | loop fusion | flops 1557080 | bytes 2491328 | tf_op jit(solution)/shard_map/concatenate | solution.py:47
  15.0 2.1 %fusion.2 = (f32[581,3,134]{2,0,1:T(8,128)}, f32[581,3,134]{2,0,1:T(8,128)}) fusion(f32[581,4,134]{2,0,1:T(8,128)S(1)} %pad_maximum_fusion), kind=kLoop, calls=%fused_computation.38 | loop fusion | bytes 3736992 | tf_op jit(solution)/shard_map/slice | solution.py:54
  17.1 2.0 %copy.31 = f32[581,3,134]{0,2,1:T(8,128)S(1)} copy(f32[581,3,134]{2,0,1:T(8,128)} %get-tuple-element.2) | data formatting | bytes 1868496 | tf_op jit(solution)/shard_map/slice | solution.py:54
  19.2 3.5 %collective-permute-start.3 = (f32[581,3,134]{0,2,1:T(8,128)S(1)}, f32[581,3,134]{0,2,1:T(8,128)}, u32[]{:S(2)}, u32[]{:S(2)}) collective-permute-start(f32[581,3,134]{0,2,1:T(8,128)S(1)} %copy.31), channel_id=1, source_target_pairs={{2,0},{4,2},{6,4},{3,1},{5,3},{7,5},{10,8},{12,10},{14,12},{11,9},... | collective-permute-start | bytes 2802752 | tf_op jit(solution)/shard_map/ppermute | solution.py:39
  22.7 0.1 broadcast_and_fusion
  22.7 3.0 %copy.27 = f32[581,3,134]{0,2,1:T(8,128)} copy(f32[581,3,134]{2,0,1:T(8,128)} %get-tuple-element.3) | data formatting | bytes 1868496 | tf_op jit(solution)/shard_map/slice | solution.py:53
  25.7 3.4 %collective-permute-start.2 = (f32[581,3,134]{0,2,1:T(8,128)}, f32[581,3,134]{0,2,1:T(8,128)}, u32[]{:S(2)}, u32[]{:S(2)}) collective-permute-start(f32[581,3,134]{0,2,1:T(8,128)} %copy.27), channel_id=1, source_target_pairs={{0,2},{2,4},{4,6},{1,3},{3,5},{5,7},{8,10},{10,12},{12,14},{9,11},... | collective-permute-start | bytes 2802752 | tf_op jit(solution)/shard_map/ppermute | solution.py:39
  29.2 0.6 slice_bitcast_fusion.21
  29.8 0.1 convert_element_type.24
  29.9 1.6 %fusion = (bf16[128,512]{1,0:T(8,128)(2,1)}, bf16[128,512]{1,0:T(8,128)(2,1)}) fusion(f32[128,128]{1,0:T(8,128)} %get-tuple-element.19, f32[128,128]{1,0:T(8,128)} %get-tuple-element.20, f32[128,128]{1,0:T(8,128)} %get-tuple-element.21, f32[128,128]{1,0:T(8,128)S(1)} %get-tuple-element.18), kind=kLoop, calls=%fused_computation.9 | loop fusion | flops 458752 | bytes 524288 | tf_op jit(solution)/shard_map/convert_element_type | solution.py:194
  31.5 0.6 pad_convert_fusion.ins_ref
  32.1 1.5 %slice_bitcast_fusion = (f32[581,134]{1,0:T(8,128)}, f32[581,134]{1,0:T(8,128)}, f32[581,134]{1,0:T(8,128)}, f32[581,134]{1,0:T(8,128)}) fusion(f32[581,4,134]{2,0,1:T(8,128)S(1)} %pad_maximum_fusion), kind=kLoop, calls=%fused_computation.3 | loop fusion | bytes 2491328 | tf_op jit(solution)/shard_map/squeeze | solution.py:64
  33.6 13.5 %collective-permute-done.3 = f32[581,3,134]{0,2,1:T(8,128)} collective-permute-done((f32[581,3,134]{0,2,1:T(8,128)S(1)}, f32[581,3,134]{0,2,1:T(8,128)}, u32[]{:S(2)}, u32[]{:S(2)}) %collective-permute-start.3) | collective-permute-done | bytes 934280 | tf_op jit(solution)/shard_map/ppermute | solution.py:39
  47.1 1.3 fusion.4
  48.4 1.0 copy.40
  49.4 1.1 copy.41
  50.5 1.1 copy.42
  51.5 17.9 %collective-permute-done.2 = f32[581,3,134]{0,2,1:T(8,128)} collective-permute-done((f32[581,3,134]{0,2,1:T(8,128)}, f32[581,3,134]{0,2,1:T(8,128)}, u32[]{:S(2)}, u32[]{:S(2)}) %collective-permute-start.2) | collective-permute-done | bytes 934280 | tf_op jit(solution)/shard_map/ppermute | solution.py:39
  69.4 1.3 fusion.5
  70.7 1.0 copy.37
  71.7 1.0 copy.38
  72.8 1.0 copy.39
  73.8 0.7 broadcast_in_dim.8
  74.5 5.3 %concatenate.29.pk_ref = f32[581,1408]{1,0:T(8,128)S(1)} concatenate(f32[581,134]{1,0:T(8,128)} %bitcast.66, f32[581,134]{1,0:T(8,128)} %bitcast.67, f32[581,134]{1,0:T(8,128)} %bitcast.68, f32[581,134]{1,0:T(8,128)} %get-tuple-element.7, f32[581,134]{1,0:T(8,128)} %get-tuple-element.6, f32[581,134]{1,0:T(8,128)} %get-tuple-element.5, f32[581,134]{1,0:T(8,128)} %get-tuple-element.4, ...), dimensions={1} | concatenate | bytes 6544384 | tf_op jit(solution)/shard_map/concatenate | solution.py:68
  79.8 0.7 reshape.67.inc_ref
  80.5 1.0 copy-done
  81.5 15.1 %shard_map.77 = f32[2,128,512]{2,1,0:T(8,128)} custom-call(s32[2]{0:T(128)} %get-tuple-element.38.order_ref, f32[581,1408]{1,0:T(8,128)} %copy-done, f32[2,2,1408]{2,1,0:T(2,128)} %reshape.67.inc_ref, f32[1,1408]{1,0:T(1,128)} %pad_convert_fusion.ins_ref, bf16[128,512]{1,0:T(8,128)(2,1)} %get-tuple-element.17.bhi_ref, bf16[128,512]{1,0:T(8,128)(2,1)} %get-tuple-element.16.blo_ref), custom_call_target="tpu_custom_call" | custom-call | flops 4429185024 | bytes 2160384 | tf_op jit(solution)/shard_map/pallas_call | solution.py:143
  96.6 1.2 reshape.68
  97.9 0.1 fusion.7
  97.9 2.0 %collective-permute-start.4 = (f32[2,2,4,3]{3,1,0,2:T(2,128)S(1)}, f32[2,2,4,3]{3,1,0,2:T(2,128)S(1)}, u32[]{:S(2)}, u32[]{:S(2)}) collective-permute-start(f32[2,2,4,3]{3,1,0,2:T(2,128)S(1)} %get-tuple-element.36), channel_id=1, source_target_pairs={{0,1},{2,3},{4,5},{6,7},{8,9},{10,11},{12,13},{14,15},{16,17},{18,... | collective-permute-start | bytes 584 | tf_op jit(solution)/shard_map/ppermute | solution.py:39
  100.0 1.3 collective-permute-start.5
  101.3 0.0 collective-permute-done.4
  101.3 1.8 %collective-permute-done.5 = f32[2,2,4,3]{3,1,0,2:T(2,128)S(1)} collective-permute-done((f32[2,2,4,3]{3,1,0,2:T(2,128)S(1)}, f32[2,2,4,3]{3,1,0,2:T(2,128)S(1)}, u32[]{:S(2)}, u32[]{:S(2)}) %collective-permute-start.5) | collective-permute-done | bytes 224 | tf_op jit(solution)/shard_map/ppermute | solution.py:39
  103.0 0.1 pad_maximum_fusion.4
  103.1 2.6 %collective-permute-start.8 = (f32[2,2,3,134]{3,1,0,2:T(2,128)S(1)}, f32[2,2,3,134]{3,1,0,2:T(2,128)S(1)}, u32[]{:S(2)}, u32[]{:S(2)}) collective-permute-start(f32[2,2,3,134]{3,1,0,2:T(2,128)S(1)} %get-tuple-element.24), channel_id=1, source_target_pairs={{2,8},{4,10},{6,12},{10,16},{12,18},{14,20},{18,24},{20,26},{22,28... | collective-permute-start | bytes 19304 | tf_op jit(solution)/shard_map/ppermute | solution.py:40
  105.8 1.2 stack_reshape.6
  107.0 3.5 %collective-permute-start.7 = (f32[2,2,4,134]{3,1,0,2:T(2,128)S(1)}, f32[2,2,4,134]{3,1,0,2:T(2,128)S(1)}, u32[]{:S(2)}, u32[]{:S(2)}) collective-permute-start(f32[2,2,4,134]{3,1,0,2:T(2,128)S(1)} %pad_maximum_fusion.4), channel_id=1, source_target_pairs={{0,8},{2,10},{4,12},{6,14},{8,16},{10,18},{12,20},{14,22},{16,24},... | collective-permute-start | bytes 25736 | tf_op jit(solution)/shard_map/ppermute | solution.py:40
  110.5 3.9 %collective-permute-start.6 = (f32[2,2,3,134]{3,1,0,2:T(2,128)S(1)}, f32[2,2,3,134]{3,1,0,2:T(2,128)S(1)}, u32[]{:S(2)}, u32[]{:S(2)}) collective-permute-start(f32[2,2,3,134]{3,1,0,2:T(2,128)S(1)} %get-tuple-element.25), channel_id=1, source_target_pairs={{0,10},{2,12},{4,14},{8,18},{10,20},{12,22},{16,26},{18,28},{20,30... | collective-permute-start | bytes 19304 | tf_op jit(solution)/shard_map/ppermute | solution.py:40
  114.4 0.0 collective-permute-done.8
  114.4 3.5 %collective-permute-done.6 = f32[2,2,3,134]{3,1,0,2:T(2,128)S(1)} collective-permute-done((f32[2,2,3,134]{3,1,0,2:T(2,128)S(1)}, f32[2,2,3,134]{3,1,0,2:T(2,128)S(1)}, u32[]{:S(2)}, u32[]{:S(2)}) %collective-permute-start.6) | collective-permute-done | bytes 6464 | tf_op jit(solution)/shard_map/ppermute | solution.py:40
  117.9 0.0 collective-permute-done.7
  117.9 0.8 concatenate.35.inc_ref
  118.7 15.1 %shard_map.78 = f32[2,128,512]{2,1,0:T(8,128)} custom-call(s32[2]{0:T(128)} %get-tuple-element.39.order_ref, f32[581,1408]{1,0:T(8,128)} %copy-done, f32[2,2,1408]{2,1,0:T(2,128)} %concatenate.35.inc_ref, f32[1,1408]{1,0:T(1,128)} %pad_convert_fusion.ins_ref, bf16[128,512]{1,0:T(8,128)(2,1)} %get-tuple-element.17.bhi_ref, ...), custom_call_target="tpu_custom_call" | custom-call | flops 4429185024 | bytes 2160384 | tf_op jit(solution)/shard_map/pallas_call | solution.py:143
  133.8 1.2 stack_reshape.7
  135.0 1.2 reshape.69
  136.2 0.6 slice.194
  136.8 1.2 pad_maximum_fusion.2
  (25 shorter events, 0.1 us)
Async XLA Ops:
  0.6 1.4 %copy-start.2 = (f32[64,4,128]{2,1,0:T(4,128)S(1)}, f32[64,4,128]{2,1,0:T(4,128)}, u32[]{:S(2)}) copy-start(f32[64,4,128]{2,1,0:T(4,128)} %param.7) | copy-start | bytes 393220
  0.6 1.5 %copy-start.3 = (f32[2,2,1,4,128]{4,3,2,1,0:T(4,128)S(1)}, f32[2,2,1,4,128]{4,3,2,1,0:T(4,128)}, u32[]{:S(2)}) copy-start(f32[2,2,1,4,128]{4,3,2,1,0:T(4,128)} %param.11) | copy-start | bytes 24580
  0.7 1.5 %copy-start.4 = (s32[1,4,128]{2,1,0:T(4,128)S(1)}, s32[1,4,128]{2,1,0:T(4,128)}, u32[]{:S(2)}) copy-start(s32[1,4,128]{2,1,0:T(4,128)} %param.9) | copy-start | bytes 6148
  2.1 0.7 copy-start.1
  3.6 5.8 %collective-permute-start = (f32[581,4,3]{0,1,2:T(4,128)S(1)}, f32[581,4,3]{0,1,2:T(4,128)S(1)}, u32[]{:S(2)}, u32[]{:S(2)}) collective-permute-start(f32[581,4,3]{0,1,2:T(4,128)S(1)} %copy.23), channel_id=1, source_target_pairs={{0,1},{2,3},{4,5},{6,7},{8,9},{10,11},{12,13},{14,15},{16,17},{18,... | collective-permute-start | bytes 83672 | tf_op jit(solution)/shard_map/ppermute | solution.py:39
  5.8 5.1 %collective-permute-start.1 = (f32[581,4,3]{0,1,2:T(4,128)S(1)}, f32[581,4,3]{0,1,2:T(4,128)S(1)}, u32[]{:S(2)}, u32[]{:S(2)}) collective-permute-start(f32[581,4,3]{0,1,2:T(4,128)S(1)} %copy.24), channel_id=1, source_target_pairs={{1,0},{3,2},{5,4},{7,6},{9,8},{11,10},{13,12},{15,14},{17,16},{19,... | collective-permute-start | bytes 83672 | tf_op jit(solution)/shard_map/ppermute | solution.py:39
  17.1 5.5 %copy-start.6 = (pred[134]{0:T(512)(128)(4,1)S(1)}, pred[134]{0:T(512)(128)(4,1)}, u32[]{:S(2)}) copy-start(pred[134]{0:T(512)(128)(4,1)} %compare_and_fusion) | copy-start | bytes 406
  19.2 10.0 %copy-start.5 = (s32[2,1,2]{2,1,0:T(1,128)S(1)}, s32[2,1,2]{2,1,0:T(1,128)}, u32[]{:S(2)}) copy-start(s32[2,1,2]{2,1,0:T(1,128)} %param.10) | copy-start | bytes 52
  19.2 27.9 %collective-permute-start.3 = (f32[581,3,134]{0,2,1:T(8,128)S(1)}, f32[581,3,134]{0,2,1:T(8,128)}, u32[]{:S(2)}, u32[]{:S(2)}) collective-permute-start(f32[581,3,134]{0,2,1:T(8,128)S(1)} %copy.31), channel_id=1, source_target_pairs={{2,0},{4,2},{6,4},{3,1},{5,3},{7,5},{10,8},{12,10},{14,12},{11,9},... | collective-permute-start | bytes 2802752 | tf_op jit(solution)/shard_map/ppermute | solution.py:39
  25.7 43.7 %collective-permute-start.2 = (f32[581,3,134]{0,2,1:T(8,128)}, f32[581,3,134]{0,2,1:T(8,128)}, u32[]{:S(2)}, u32[]{:S(2)}) collective-permute-start(f32[581,3,134]{0,2,1:T(8,128)} %copy.27), channel_id=1, source_target_pairs={{0,2},{2,4},{4,6},{1,3},{3,5},{5,7},{8,10},{10,12},{12,14},{9,11},... | collective-permute-start | bytes 2802752 | tf_op jit(solution)/shard_map/ppermute | solution.py:39
  79.8 1.7 %copy-start = (f32[581,1408]{1,0:T(8,128)}, f32[581,1408]{1,0:T(8,128)S(1)}, u32[]{:S(2)}) copy-start(f32[581,1408]{1,0:T(8,128)S(1)} %concatenate.29.pk_ref) | copy-start | bytes 9816580
  97.9 3.3 %collective-permute-start.4 = (f32[2,2,4,3]{3,1,0,2:T(2,128)S(1)}, f32[2,2,4,3]{3,1,0,2:T(2,128)S(1)}, u32[]{:S(2)}, u32[]{:S(2)}) collective-permute-start(f32[2,2,4,3]{3,1,0,2:T(2,128)S(1)} %get-tuple-element.36), channel_id=1, source_target_pairs={{0,1},{2,3},{4,5},{6,7},{8,9},{10,11},{12,13},{14,15},{16,17},{18,... | collective-permute-start | bytes 584 | tf_op jit(solution)/shard_map/ppermute | solution.py:39
  100.0 3.1 %collective-permute-start.5 = (f32[2,2,4,3]{3,1,0,2:T(2,128)S(1)}, f32[2,2,4,3]{3,1,0,2:T(2,128)S(1)}, u32[]{:S(2)}, u32[]{:S(2)}) collective-permute-start(f32[2,2,4,3]{3,1,0,2:T(2,128)S(1)} %get-tuple-element.37), channel_id=1, source_target_pairs={{1,0},{3,2},{5,4},{7,6},{9,8},{11,10},{13,12},{15,14},{17,16},{19,... | collective-permute-start | bytes 584 | tf_op jit(solution)/shard_map/ppermute | solution.py:39
  103.1 11.2 %collective-permute-start.8 = (f32[2,2,3,134]{3,1,0,2:T(2,128)S(1)}, f32[2,2,3,134]{3,1,0,2:T(2,128)S(1)}, u32[]{:S(2)}, u32[]{:S(2)}) collective-permute-start(f32[2,2,3,134]{3,1,0,2:T(2,128)S(1)} %get-tuple-element.24), channel_id=1, source_target_pairs={{2,8},{4,10},{6,12},{10,16},{12,18},{14,20},{18,24},{20,26},{22,28... | collective-permute-start | bytes 19304 | tf_op jit(solution)/shard_map/ppermute | solution.py:40
  107.0 10.9 %collective-permute-start.7 = (f32[2,2,4,134]{3,1,0,2:T(2,128)S(1)}, f32[2,2,4,134]{3,1,0,2:T(2,128)S(1)}, u32[]{:S(2)}, u32[]{:S(2)}) collective-permute-start(f32[2,2,4,134]{3,1,0,2:T(2,128)S(1)} %pad_maximum_fusion.4), channel_id=1, source_target_pairs={{0,8},{2,10},{4,12},{6,14},{8,16},{10,18},{12,20},{14,22},{16,24},... | collective-permute-start | bytes 25736 | tf_op jit(solution)/shard_map/ppermute | solution.py:40
  110.5 7.4 %collective-permute-start.6 = (f32[2,2,3,134]{3,1,0,2:T(2,128)S(1)}, f32[2,2,3,134]{3,1,0,2:T(2,128)S(1)}, u32[]{:S(2)}, u32[]{:S(2)}) collective-permute-start(f32[2,2,3,134]{3,1,0,2:T(2,128)S(1)} %get-tuple-element.25), channel_id=1, source_target_pairs={{0,10},{2,12},{4,14},{8,18},{10,20},{12,22},{16,26},{18,28},{20,30... | collective-permute-start | bytes 19304 | tf_op jit(solution)/shard_map/ppermute | solution.py:40

commit v5 on v4

--- a/solution.py
+++ b/solution.py
@@ -40,28 +40,22 @@
     return lax.ppermute(block, tuple(axes), pairs)
 
 
-def extend_y(block, width):
+def extend_x(block, width, lead_axes=(), lead_offsets=()):
+    nx = block.shape[-2]
+    axes = tuple(lead_axes) + ("tx",)
+    low = fetch(block[..., nx - width :, :], axes, tuple(lead_offsets) + (-1,))
+    high = fetch(block[..., :width, :], axes, tuple(lead_offsets) + (1,))
+    middle = fetch(block, axes, tuple(lead_offsets) + (0,)) if lead_axes else block
+    return jnp.concatenate([low, middle, high], axis=-2)
+
+
+def flat_extended(block, width, padded):
     ny = block.shape[-1]
     low = fetch(block[..., ny - width :], ("ty",), (-1,))
     high = fetch(block[..., :width], ("ty",), (1,))
-    return jnp.concatenate([low, block, high], axis=-1)
-
-
-def flat_extended(block, width, padded, lead_axes=(), lead_offsets=()):
-    nx = block.shape[-2]
-    pieces = {
-        -1: fetch(block[..., nx - width :, :], tuple(lead_axes) + ("tx",), tuple(lead_offsets) + (-1,)),
-        1: fetch(block[..., :width, :], tuple(lead_axes) + ("tx",), tuple(lead_offsets) + (1,)),
-    }
-    if lead_axes:
-        pieces[0] = fetch(block, tuple(lead_axes) + ("tx",), tuple(lead_offsets) + (0,))
-    else:
-        pieces[0] = block
     segments = []
-    for ix in range(nx + 2 * width):
-        dx = -1 if ix < width else (0 if ix < width + nx else 1)
-        r = ix - (0 if dx == -1 else (width if dx == 0 else width + nx))
-        segments.append(pieces[dx][..., r, :])
+    for ix in range(block.shape[-2]):
+        segments += [low[..., ix, :], block[..., ix, :], high[..., ix, :]]
     used = sum(s.shape[-1] for s in segments)
     lead = segments[0].shape[:-1]
     segments.append(jnp.zeros(lead + (padded - used,), segments[0].dtype))
@@ -179,7 +173,7 @@
         ],
         axis=0,
     )
-    packed = flat_extended(extend_y(packed, width), width, padded)
+    packed = flat_extended(extend_x(packed, width), width, padded)
     first_pending = ticks * nsrc * two * depth + depth
 
     gx = lax.axis_index("tx") * nx - width + jnp.arange(ex)
@@ -205,7 +199,7 @@
         solutions.append(tile)
         trace = tile[:, :, depth - 1]
         if tick + 1 < ticks:
-            incoming = flat_extended(extend_y(trace, width), width, padded, ("slab",), (-1,))
+            incoming = flat_extended(extend_x(trace, width, ("slab",), (-1,)), width, padded)
     return (jnp.stack(solutions, axis=0), trace[:, :, None])
 
 

time: 139 us -> 151 us (1.086)
  local copies, waits for them, and re-layouts: 39.9 us -> 52.1 us
  starting transfers between devices: 23.2 us -> 25.4 us
  waiting for transfers between devices: 36.6 us -> 34.5 us
    unnamed x25 -> x33, local copies, waits for them, and re-layouts: 10.3 us -> 21.8 us
    ppermute x6, waiting for transfers between devices: 33.1 us -> 29.1 us  [fetch(): return lax.ppermute(block, axes[0], pairs)]
    squeeze x4 -> x8, local copies, waits for them, and re-layouts: 1.52 us -> 5.32 us  [flat_extended(): segments += [low[..., ix, :], block[..., ix, :], high[..., ix, :]]]
    slice x10 -> x8, local copies, waits for them, and re-layouts: 10.9 us -> 7.71 us  [the longest x3 3.91 us: flat_extended(): high = fetch(block[..., :width], ('ty',), (1,))]
    ppermute x2 -> x0, local copies, waits for them, and re-layouts: 2.91 us -> none  [fetch(): return lax.ppermute(block, axes[0], pairs)]
    ppermute x3, waiting for transfers between devices: 3.51 us -> 5.38 us  [fetch(): return lax.ppermute(block, tuple(axes), pairs)]
    ppermute x3, starting transfers between devices: 9.97 us -> 11.7 us  [fetch(): return lax.ppermute(block, tuple(axes), pairs)]
    concatenate x2, local copies, waits for them, and re-layouts: 6.02 us -> 7.66 us  [flat_extended(): return jnp.concatenate(segments, axis=-1)]
  transfers between devices with their start and end apart: 9 -> 9, of which waited for: 4 -> 4; matrix products, arithmetic and copies ran while one was open for 13% -> 10% of each run, Pallas kernels for 0% -> 0%
where the time goes in v5:
time: 151 us; the launch traced here: 150 us
  local copies, waits for them, and re-layouts  52.1 us (35%)
  waiting for transfers between devices  34.5 us (23%)
  Pallas kernels  30.3 us (20%)
  starting transfers between devices  25.4 us (17%)
  other arithmetic  6.49 us (4%)
    pallas_call x2, Pallas kernels, run_tick(): pl.pallas_call(functools.partial(tick_kernel, tick=tick, row=row, depth=d...  30.3 us
    ppermute x6, waiting for transfers between devices, fetch(): return lax.ppermute(block, axes[0], pairs)  29.1 us
    unnamed x33, local copies, waits for them, and re-layouts  21.8 us
    ppermute x6, starting transfers between devices, fetch(): return lax.ppermute(block, axes[0], pairs)  13.7 us
    ppermute x3, starting transfers between devices, fetch(): return lax.ppermute(block, tuple(axes), pairs)  11.7 us
    concatenate x2, local copies, waits for them, and re-layouts, flat_extended(): return jnp.concatenate(segments, axis=-1)  7.66 us
    ppermute x3, waiting for transfers between devices, fetch(): return lax.ppermute(block, tuple(axes), pairs)  5.38 us
    squeeze x8, local copies, waits for them, and re-layouts, flat_extended(): segments += [low[..., ix, :], block[..., ix, :], high[..., ix, :]]  5.32 us
  transfers between devices with their start and end apart: 9, of which 4 were waited for; matrix products, arithmetic and copies ran while one was open for 10% of the time, Pallas kernels for 0%

profile of v5, /device:TPU:12, one launch (start us, length us, event | category | flops | bytes accessed | tf_op | source)
XLA Modules:
  0.0 149.7 jit_solution(12517140989532491606)
XLA Ops:
  0.6 1.3 copy.19
  2.0 0.9 copy.21
  2.9 0.7 copy.20
  3.6 0.7 convert_element_type.23
  4.4 1.4 fusion.3
  5.7 3.4 %collective-permute-start = (f32[581,3,128]{2,0,1:T(8,128)}, f32[581,3,128]{2,0,1:T(8,128)S(1)}, u32[]{:S(2)}, u32[]{:S(2)}) collective-permute-start(f32[581,3,128]{2,0,1:T(8,128)} %get-tuple-element.8), channel_id=1, source_target_pairs={{0,2},{2,4},{4,6},{1,3},{3,5},{5,7},{8,10},{10,12},{12,14},{9,11},... | collective-permute-start | bytes 2677256 | tf_op jit(solution)/shard_map/ppermute | solution.py:39
  9.1 3.3 %collective-permute-start.1 = (f32[581,3,128]{2,0,1:T(8,128)}, f32[581,3,128]{2,0,1:T(8,128)}, u32[]{:S(2)}, u32[]{:S(2)}) collective-permute-start(f32[581,3,128]{2,0,1:T(8,128)} %get-tuple-element.9), channel_id=1, source_target_pairs={{2,0},{4,2},{6,4},{3,1},{5,3},{7,5},{10,8},{12,10},{14,12},{11,9},... | collective-permute-start | bytes 2677256 | tf_op jit(solution)/shard_map/ppermute | solution.py:39
  12.5 0.7 slice_bitcast_fusion.10
  13.2 1.1 maximum_maximum_fusion
  14.4 0.7 broadcast_and_fusion
  15.1 0.8 convert_element_type.24
  15.9 0.7 fusion
  16.6 1.3 slice_bitcast_fusion.47
  17.8 0.6 pad_convert_fusion.ins_ref
  18.4 1.1 slice_bitcast_fusion.3
  19.5 12.0 %collective-permute-done = f32[581,3,128]{2,0,1:T(8,128)S(1)} collective-permute-done((f32[581,3,128]{2,0,1:T(8,128)}, f32[581,3,128]{2,0,1:T(8,128)S(1)}, u32[]{:S(2)}, u32[]{:S(2)}) %collective-permute-start) | collective-permute-done | bytes 892448 | tf_op jit(solution)/shard_map/ppermute | solution.py:39
  31.5 16.3 %collective-permute-done.1 = f32[581,3,128]{2,0,1:T(8,128)} collective-permute-done((f32[581,3,128]{2,0,1:T(8,128)}, f32[581,3,128]{2,0,1:T(8,128)}, u32[]{:S(2)}, u32[]{:S(2)}) %collective-permute-start.1) | collective-permute-done | bytes 892448 | tf_op jit(solution)/shard_map/ppermute | solution.py:39
  47.8 1.4 pad_maximum_fusion
  49.2 2.6 %fusion.2 = (f32[581,10,3]{2,0,1:T(8,128)S(1)}, f32[581,10,3]{2,0,1:T(8,128)}) fusion(f32[581,10,128]{2,0,1:T(8,128)S(1)} %pad_maximum_fusion), kind=kLoop, calls=%fused_computation.66 | loop fusion | bytes 278880 | tf_op jit(solution)/shard_map/slice | solution.py:55
  51.8 2.4 %copy.23 = f32[581,10,3]{0,2,1:T(4,128)S(1)} copy(f32[581,10,3]{2,0,1:T(8,128)} %get-tuple-element.3) | data formatting | bytes 139440 | tf_op jit(solution)/shard_map/slice | solution.py:54
  54.2 1.3 collective-permute-start.2
  55.5 1.2 copy.25
  56.8 1.3 collective-permute-start.3
  58.1 2.1 %slice_bitcast_fusion = (f32[581,128]{1,0:T(8,128)}, f32[581,128]{1,0:T(8,128)}, f32[581,128]{1,0:T(8,128)}) fusion(f32[581,3,128]{2,0,1:T(8,128)} %collective-permute-done.1), kind=kLoop, calls=%fused_computation.5 | loop fusion | bytes 1784832 | tf_op jit(solution)/shard_map/squeeze | solution.py:58
  60.2 2.1 %slice_bitcast_fusion.7 = (f32[581,128]{1,0:T(8,128)}, f32[581,128]{1,0:T(8,128)}, f32[581,128]{1,0:T(8,128)}) fusion(f32[581,3,128]{2,0,1:T(8,128)} %copy-done), kind=kLoop, calls=%fused_computation.12 | loop fusion | bytes 1784832 | tf_op jit(solution)/shard_map/squeeze | solution.py:58
  62.3 0.9 copy.51
  63.2 0.9 copy.52
  64.1 0.9 copy.53
  65.0 0.9 copy.54
  65.9 0.9 copy.55
  66.8 0.9 copy.56
  67.7 0.9 copy.57
  68.5 0.9 copy.58
  69.4 0.9 copy.59
  70.3 0.9 copy.60
  71.2 0.9 copy.61
  72.1 0.9 copy.62
  73.0 0.9 copy.63
  73.9 0.9 copy.64
  74.8 0.9 copy.65
  75.8 0.9 copy.66
  76.6 0.9 copy.47
  77.5 0.9 copy.48
  78.4 0.9 copy.49
  79.3 0.9 copy.50
  80.2 0.7 broadcast_in_dim.8
  80.9 6.9 %concatenate.29.pk_ref = f32[581,1408]{1,0:T(8,128)S(1)} concatenate(f32[581,3]{1,0:T(8,128)} %bitcast.147, f32[581,128]{1,0:T(8,128)} %get-tuple-element.15, f32[581,3]{1,0:T(8,128)} %bitcast.148, f32[581,3]{1,0:T(8,128)} %bitcast.149, f32[581,128]{1,0:T(8,128)} %get-tuple-element.14, f32[581,3]{1,0:T(8,128)} %bitcast.150, f32[581,3]{1,0:T(8,128)} %bitcast.131, ...), dimensions={1} | concatenate | bytes 6544384 | tf_op jit(solution)/shard_map/concatenate | solution.py:62
  87.8 0.7 reshape.67.inc_ref
  88.5 1.0 copy-done.1
  89.5 15.1 %shard_map.77 = f32[2,128,512]{2,1,0:T(8,128)} custom-call(s32[2]{0:T(128)} %get-tuple-element.78.order_ref, f32[581,1408]{1,0:T(8,128)} %copy-done.1, f32[2,2,1408]{2,1,0:T(2,128)} %reshape.67.inc_ref, f32[1,1408]{1,0:T(1,128)} %pad_convert_fusion.ins_ref, bf16[128,512]{1,0:T(8,128)(2,1)} %get-tuple-element.17.bhi_ref, ...), custom_call_target="tpu_custom_call" | custom-call | flops 4429185024 | bytes 2160384 | tf_op jit(solution)/shard_map/pallas_call | solution.py:137
  104.6 1.2 reshape.68
  105.9 6.3 %collective-permute-start.6 = (f32[2,2,3,128]{3,1,0,2:T(2,128)S(1)}, f32[2,2,3,128]{3,1,0,2:T(2,128)S(1)}, u32[]{:S(2)}, u32[]{:S(2)}) collective-permute-start(f32[2,2,3,128]{3,1,0,2:T(2,128)S(1)} %get-tuple-element.70), channel_id=1, source_target_pairs={{2,8},{4,10},{6,12},{10,16},{12,18},{14,20},{18,24},{20,26},{22,28... | collective-permute-start | bytes 18440 | tf_op jit(solution)/shard_map/ppermute | solution.py:40
  112.2 3.5 %collective-permute-start.5 = (f32[2,2,4,128]{3,1,0,2:T(2,128)S(1)}, f32[2,2,4,128]{3,1,0,2:T(2,128)S(1)}, u32[]{:S(2)}, u32[]{:S(2)}) collective-permute-start(f32[2,2,4,128]{3,1,0,2:T(2,128)S(1)} %bitcast.154), channel_id=1, source_target_pairs={{0,8},{2,10},{4,12},{6,14},{8,16},{10,18},{12,20},{14,22},{16,24},... | collective-permute-start | bytes 24584 | tf_op jit(solution)/shard_map/ppermute | solution.py:40
  115.7 1.2 stack_reshape.6
  116.9 1.9 %collective-permute-start.4 = (f32[2,2,3,128]{3,1,0,2:T(2,128)S(1)}, f32[2,2,3,128]{3,1,0,2:T(2,128)S(1)}, u32[]{:S(2)}, u32[]{:S(2)}) collective-permute-start(f32[2,2,3,128]{3,1,0,2:T(2,128)S(1)} %get-tuple-element.71), channel_id=1, source_target_pairs={{0,10},{2,12},{4,14},{8,18},{10,20},{12,22},{16,26},{18,28},{20,30... | collective-permute-start | bytes 18440 | tf_op jit(solution)/shard_map/ppermute | solution.py:40
  118.9 5.4 %collective-permute-done.4 = f32[2,2,3,128]{3,1,0,2:T(2,128)S(1)} collective-permute-done((f32[2,2,3,128]{3,1,0,2:T(2,128)S(1)}, f32[2,2,3,128]{3,1,0,2:T(2,128)S(1)}, u32[]{:S(2)}, u32[]{:S(2)}) %collective-permute-start.4) | collective-permute-done | bytes 6176 | tf_op jit(solution)/shard_map/ppermute | solution.py:40
  124.3 1.3 collective-permute-start.8
  125.6 3.0 %collective-permute-start.7 = (f32[2,2,10,3]{3,1,0,2:T(2,128)S(1)}, f32[2,2,10,3]{3,1,0,2:T(2,128)S(1)}, u32[]{:S(2)}, u32[]{:S(2)}) collective-permute-start(f32[2,2,10,3]{3,1,0,2:T(2,128)S(1)} %get-tuple-element.65), channel_id=1, source_target_pairs={{0,1},{2,3},{4,5},{6,7},{8,9},{10,11},{12,13},{14,15},{16,17},{18,... | collective-permute-start | bytes 1448 | tf_op jit(solution)/shard_map/ppermute | solution.py:39
  128.7 0.8 collective-permute-done.7
  129.5 0.8 concatenate.35.inc_ref
  130.3 15.1 %shard_map.78 = f32[2,128,512]{2,1,0:T(8,128)} custom-call(s32[2]{0:T(128)} %get-tuple-element.79.order_ref, f32[581,1408]{1,0:T(8,128)} %copy-done.1, f32[2,2,1408]{2,1,0:T(2,128)} %concatenate.35.inc_ref, f32[1,1408]{1,0:T(1,128)} %pad_convert_fusion.ins_ref, bf16[128,512]{1,0:T(8,128)(2,1)} %get-tuple-element.17.bhi_ref, ...), custom_call_target="tpu_custom_call" | custom-call | flops 4429185024 | bytes 2160384 | tf_op jit(solution)/shard_map/pallas_call | solution.py:137
  145.4 1.2 stack_reshape.7
  146.7 1.2 reshape.69
  148.5 1.2 pad_maximum_fusion.2
  (33 shorter events, 1.0 us)
Async XLA Ops:
  4.3 8.2 %copy-start.2 = (f32[1,4,2,64,64]{4,3,2,1,0:T(8,128)S(1)}, f32[1,4,2,64,64]{4,3,2,1,0:T(8,128)}, u32[]{:S(2)}) copy-start(f32[1,4,2,64,64]{4,3,2,1,0:T(8,128)} %param.8) | copy-start | bytes 393220
  5.7 25.8 %collective-permute-start = (f32[581,3,128]{2,0,1:T(8,128)}, f32[581,3,128]{2,0,1:T(8,128)S(1)}, u32[]{:S(2)}, u32[]{:S(2)}) collective-permute-start(f32[581,3,128]{2,0,1:T(8,128)} %get-tuple-element.8), channel_id=1, source_target_pairs={{0,2},{2,4},{4,6},{1,3},{3,5},{5,7},{8,10},{10,12},{12,14},{9,11},... | collective-permute-start | bytes 2677256 | tf_op jit(solution)/shard_map/ppermute | solution.py:39
  9.1 38.7 %collective-permute-start.1 = (f32[581,3,128]{2,0,1:T(8,128)}, f32[581,3,128]{2,0,1:T(8,128)}, u32[]{:S(2)}, u32[]{:S(2)}) collective-permute-start(f32[581,3,128]{2,0,1:T(8,128)} %get-tuple-element.9), channel_id=1, source_target_pairs={{2,0},{4,2},{6,4},{3,1},{5,3},{7,5},{10,8},{12,10},{14,12},{11,9},... | collective-permute-start | bytes 2677256 | tf_op jit(solution)/shard_map/ppermute | solution.py:39
  31.5 16.3 %copy-start = (f32[581,3,128]{2,0,1:T(8,128)}, f32[581,3,128]{2,0,1:T(8,128)S(1)}, u32[]{:S(2)}) copy-start(f32[581,3,128]{2,0,1:T(8,128)S(1)} %collective-permute-done) | copy-start | bytes 2677252
  54.2 8.1 %collective-permute-start.2 = (f32[581,10,3]{0,2,1:T(4,128)S(1)}, f32[581,10,3]{0,2,1:T(4,128)S(1)}, u32[]{:S(2)}, u32[]{:S(2)}) collective-permute-start(f32[581,10,3]{0,2,1:T(4,128)S(1)} %copy.23), channel_id=1, source_target_pairs={{0,1},{2,3},{4,5},{6,7},{8,9},{10,11},{12,13},{14,15},{16,17},{18,... | collective-permute-start | bytes 209168 | tf_op jit(solution)/shard_map/ppermute | solution.py:39
  56.8 6.5 %collective-permute-start.3 = (f32[581,10,3]{0,2,1:T(4,128)S(1)}, f32[581,10,3]{0,2,1:T(4,128)S(1)}, u32[]{:S(2)}, u32[]{:S(2)}) collective-permute-start(f32[581,10,3]{0,2,1:T(4,128)S(1)} %copy.25), channel_id=1, source_target_pairs={{1,0},{3,2},{5,4},{7,6},{9,8},{11,10},{13,12},{15,14},{17,16},{19,... | collective-permute-start | bytes 209168 | tf_op jit(solution)/shard_map/ppermute | solution.py:39
  87.8 1.7 %copy-start.1 = (f32[581,1408]{1,0:T(8,128)}, f32[581,1408]{1,0:T(8,128)S(1)}, u32[]{:S(2)}) copy-start(f32[581,1408]{1,0:T(8,128)S(1)} %concatenate.29.pk_ref) | copy-start | bytes 9816580
  105.9 12.9 %collective-permute-start.6 = (f32[2,2,3,128]{3,1,0,2:T(2,128)S(1)}, f32[2,2,3,128]{3,1,0,2:T(2,128)S(1)}, u32[]{:S(2)}, u32[]{:S(2)}) collective-permute-start(f32[2,2,3,128]{3,1,0,2:T(2,128)S(1)} %get-tuple-element.70), channel_id=1, source_target_pairs={{2,8},{4,10},{6,12},{10,16},{12,18},{14,20},{18,24},{20,26},{22,28... | collective-permute-start | bytes 18440 | tf_op jit(solution)/shard_map/ppermute | solution.py:40
  112.2 12.0 %collective-permute-start.5 = (f32[2,2,4,128]{3,1,0,2:T(2,128)S(1)}, f32[2,2,4,128]{3,1,0,2:T(2,128)S(1)}, u32[]{:S(2)}, u32[]{:S(2)}) collective-permute-start(f32[2,2,4,128]{3,1,0,2:T(2,128)S(1)} %bitcast.154), channel_id=1, source_target_pairs={{0,8},{2,10},{4,12},{6,14},{8,16},{10,18},{12,20},{14,22},{16,24},... | collective-permute-start | bytes 24584 | tf_op jit(solution)/shard_map/ppermute | solution.py:40
  116.9 7.3 %collective-permute-start.4 = (f32[2,2,3,128]{3,1,0,2:T(2,128)S(1)}, f32[2,2,3,128]{3,1,0,2:T(2,128)S(1)}, u32[]{:S(2)}, u32[]{:S(2)}) collective-permute-start(f32[2,2,3,128]{3,1,0,2:T(2,128)S(1)} %get-tuple-element.71), channel_id=1, source_target_pairs={{0,10},{2,12},{4,14},{8,18},{10,20},{12,22},{16,26},{18,28},{20,30... | collective-permute-start | bytes 18440 | tf_op jit(solution)/shard_map/ppermute | solution.py:40
  124.3 4.4 %collective-permute-start.8 = (f32[2,2,10,3]{3,1,0,2:T(2,128)S(1)}, f32[2,2,10,3]{3,1,0,2:T(2,128)S(1)}, u32[]{:S(2)}, u32[]{:S(2)}) collective-permute-start(f32[2,2,10,3]{3,1,0,2:T(2,128)S(1)} %get-tuple-element.64), channel_id=1, source_target_pairs={{1,0},{3,2},{5,4},{7,6},{9,8},{11,10},{13,12},{15,14},{17,16},{19,... | collective-permute-start | bytes 1448 | tf_op jit(solution)/shard_map/ppermute | solution.py:39
  125.6 3.9 %collective-permute-start.7 = (f32[2,2,10,3]{3,1,0,2:T(2,128)S(1)}, f32[2,2,10,3]{3,1,0,2:T(2,128)S(1)}, u32[]{:S(2)}, u32[]{:S(2)}) collective-permute-start(f32[2,2,10,3]{3,1,0,2:T(2,128)S(1)} %get-tuple-element.65), channel_id=1, source_target_pairs={{0,1},{2,3},{4,5},{6,7},{8,9},{10,11},{12,13},{14,15},{16,17},{18,... | collective-permute-start | bytes 1448 | tf_op jit(solution)/shard_map/ppermute | solution.py:39

commit v6 on v4

--- a/solution.py
+++ b/solution.py
@@ -68,12 +68,11 @@
     return jnp.concatenate(segments, axis=-1)
 
 
-def tick_kernel(order_ref, pk_ref, inc_ref, ins_ref, bhi_ref, blo_ref, out_ref, *, tick, row, depth, width):
+def tick_kernel(order_ref, frc_ref, pk_ref, inc_ref, ins_ref, bhi_ref, blo_ref, out_ref, *, row, depth, width):
     nsrc, rows, owned = out_ref.shape
     cols = pk_ref.shape[1]
     classes = bhi_ref.shape[1] // rows
     lanes = 128
-    waves = tick * nsrc * rows
     wave0 = pk_ref.shape[0] - depth - 2 * nsrc - 1
     zrow = lax.broadcasted_iota(jnp.int32, (rows, cols), 0) % depth
     top = zrow == 0
@@ -110,8 +109,8 @@
         return diagonal - beside
 
     def one_source(s, carry):
-        first = pl.multiple_of(waves + order_ref[s] * rows, rows)
-        forcing = pk_ref[pl.ds(first, rows), :]
+        first = pl.multiple_of(order_ref[s] * rows, rows)
+        forcing = frc_ref[pl.ds(first, rows), :]
         incoming = inc_ref[s]
         layer = jnp.concatenate(
             [
@@ -134,21 +133,23 @@
     lax.fori_loop(0, nsrc, one_source, 0)
 
 
-def run_tick(order, packed, incoming, ins, bhi, blo, tick, row, depth, width, owned):
+def run_tick(order, forcing, packed, incoming, ins, bhi, blo, row, depth, width, owned):
     nsrc = incoming.shape[0]
     rows, stacked = bhi.shape
     cols = packed.shape[1]
     flops = nsrc * (CORR + 1) * 3 * 2 * rows * stacked * cols
     vmem = pl.BlockSpec(memory_space=pltpu.VMEM)
     return pl.pallas_call(
-        functools.partial(tick_kernel, tick=tick, row=row, depth=depth, width=width),
+        functools.partial(tick_kernel, row=row, depth=depth, width=width),
         out_shape=jax.ShapeDtypeStruct((nsrc, rows, owned), jnp.float32),
-        in_specs=[pl.BlockSpec(memory_space=pltpu.SMEM)] + [vmem] * 5,
+        in_specs=[pl.BlockSpec(memory_space=pltpu.SMEM)] + [vmem] * 6,
         out_specs=vmem,
         cost_estimate=pl.CostEstimate(
-            flops=flops, transcendentals=0, bytes_accessed=4 * (packed.size // 2 + nsrc * rows * owned)
+            flops=flops,
+            transcendentals=0,
+            bytes_accessed=4 * (forcing.size + packed.size // 4 + nsrc * rows * owned),
         ),
-    )(order, packed, incoming, ins, bhi, blo)
+    )(order, forcing, packed, incoming, ins, bhi, blo)
 
 
 def block_matrix(inverse):
@@ -170,17 +171,25 @@
     padded = -(-cols // 128) * 128
     assert width <= nx and width <= ny
 
+    per_tick = forcing.reshape(ticks, -1, nx, ny)
     packed = jnp.concatenate(
         [
-            forcing.reshape(-1, nx, ny),
+            per_tick[0],
             wavenumber_sq,
             pending_trace.reshape(-1, nx, ny),
             column_class[0][None].astype(jnp.float32),
-        ],
+        ]
+        + [per_tick[t] for t in range(1, ticks)],
         axis=0,
     )
-    packed = flat_extended(extend_y(packed, width), width, padded)
-    first_pending = ticks * nsrc * two * depth + depth
+    packed = extend_y(packed, width)
+    rows_now = per_tick.shape[1] + depth + nsrc * two + 1
+    later = [
+        packed[rows_now + (t - 1) * per_tick.shape[1] : rows_now + t * per_tick.shape[1]]
+        for t in range(1, ticks)
+    ]
+    packed = flat_extended(packed[:rows_now], width, padded)
+    first_pending = nsrc * two * depth + depth
 
     gx = lax.axis_index("tx") * nx - width + jnp.arange(ex)
     gy = lax.axis_index("ty") * ny - width + jnp.arange(ey)
@@ -197,10 +206,14 @@
     incoming = packed[first_pending : first_pending + nsrc * two].reshape(nsrc, two, padded)
     solutions = []
     trace = None
+    forcing_f = packed
     for tick in range(ticks):
         field = run_tick(
-            orders[tick], packed, incoming, inside, bhi, blo, tick, ey, depth, width, nx * ny
+            orders[tick], forcing_f, packed, incoming, inside, bhi, blo, ey, depth, width, nx * ny
         )
+        if tick + 1 < ticks:
+            field, rows = lax.optimization_barrier((field, later[tick]))
+            forcing_f = flat_extended(rows, width, padded)
         tile = field.reshape(nsrc, two, depth, nx, ny)
         solutions.append(tile)
         trace = tile[:, :, depth - 1]

time: 139 us -> 139 us (level)
  the two profiles are of different devices: /device:TPU:12 before, /device:TPU:0 now
where the time goes in v6:
time: 139 us; the launch traced here: 138 us
  local copies, waits for them, and re-layouts  39.6 us (28%)
  starting transfers between devices  31.8 us (23%)
  Pallas kernels  30.3 us (22%)
  waiting for transfers between devices  26.4 us (19%)
  other arithmetic  8.5 us (6%)
    pallas_call x2, Pallas kernels, run_tick(): pl.pallas_call(functools.partial(tick_kernel, row=row, depth=depth, width...  30.3 us
    ppermute x8, waiting for transfers between devices, fetch(): return lax.ppermute(block, axes[0], pairs)  25.2 us
    ppermute x8, starting transfers between devices, fetch(): return lax.ppermute(block, axes[0], pairs)  21.5 us
    ppermute x3, starting transfers between devices, fetch(): return lax.ppermute(block, tuple(axes), pairs)  10.2 us
    unnamed x38, local copies, waits for them, and re-layouts  8.84 us
    concatenate x3, local copies, waits for them, and re-layouts, flat_extended(): return jnp.concatenate(segments, axis=-1)  5.99 us
    slice x5, local copies, waits for them, and re-layouts, flat_extended(): block[..., :width, :]  3.54 us
    slice x4, local copies, waits for them, and re-layouts, flat_extended(): segments.append(pieces[dx][..., r, :])  3.44 us
  transfers between devices with their start and end apart: 11, of which 5 were waited for; matrix products, arithmetic and copies ran while one was open for 12% of the time, Pallas kernels for 0%

profile of v6, /device:TPU:0, one launch (start us, length us, event | category | flops | bytes accessed | tf_op | source)
XLA Modules:
  0.0 137.7 jit_solution(6565543951098050605)
XLA Ops:
  0.6 0.7 convert_element_type.23
  1.3 0.7 copy.22
  2.0 0.9 copy.24
  2.9 1.3 fusion.5
  4.3 0.5 concatenate.30
  4.9 1.4 %fusion.3 = (f32[581,4,3]{2,0,1:T(8,128)S(1)}, f32[581,4,3]{2,0,1:T(8,128)}) fusion(f32[581,4,128]{2,0,1:T(8,128)S(1)} %concatenate.30), kind=kLoop, calls=%fused_computation.42 | loop fusion | bytes 111552 | tf_op jit(solution)/shard_map/slice | solution.py:45
  6.3 1.7 %copy.27 = f32[581,4,3]{0,1,2:T(4,128)S(1)} copy(f32[581,4,3]{2,0,1:T(8,128)} %get-tuple-element.13) | data formatting | bytes 55776 | tf_op jit(solution)/shard_map/slice | solution.py:46
  8.0 1.3 collective-permute-start.1
  9.3 0.4 copy.26
  9.7 3.0 %collective-permute-start = (f32[581,4,3]{0,1,2:T(4,128)S(1)}, f32[581,4,3]{0,1,2:T(4,128)S(1)}, u32[]{:S(2)}, u32[]{:S(2)}) collective-permute-start(f32[581,4,3]{0,1,2:T(4,128)S(1)} %copy.26), channel_id=1, source_target_pairs={{0,1},{2,3},{4,5},{6,7},{8,9},{10,11},{12,13},{14,15},{16,17},{18,... | collective-permute-start | bytes 83672 | tf_op jit(solution)/shard_map/ppermute | solution.py:39
  12.8 0.1 maximum_maximum_fusion
  13.0 0.7 slice_bitcast_fusion.9
  13.9 0.4 copy.28
  14.3 1.4 %copy.29 = f32[581,4,3]{2,0,1:T(8,128)} copy(f32[581,4,3]{0,1,2:T(4,128)S(1)} %collective-permute-done.1) | data formatting | bytes 55776 | tf_op jit(solution)/shard_map/ppermute | solution.py:39
  15.7 2.3 %pad_maximum_fusion = f32[581,4,134]{2,0,1:T(8,128)S(1)} fusion(f32[581,4,3]{2,0,1:T(8,128)} %copy.29, f32[581,4,128]{2,0,1:T(8,128)S(1)} %concatenate.30, f32[581,4,3]{2,0,1:T(8,128)S(1)} %copy.28), kind=kLoop, calls=%fused_computation | loop fusion | flops 622832 | bytes 2491328 | tf_op jit(solution)/shard_map/concatenate | solution.py:47
  18.0 1.2 fusion.2
  19.2 0.5 copy-done
  19.7 2.4 %copy.30 = f32[325,3,134]{0,2,1:T(8,128)} copy(f32[325,3,134]{2,0,1:T(8,128)} %get-tuple-element.11) | data formatting | bytes 1045200 | tf_op jit(solution)/shard_map/slice | solution.py:53
  22.1 5.8 %collective-permute-start.2 = (f32[325,3,134]{0,2,1:T(8,128)}, f32[325,3,134]{0,2,1:T(8,128)}, u32[]{:S(2)}, u32[]{:S(2)}) collective-permute-start(f32[325,3,134]{0,2,1:T(8,128)} %copy.30), channel_id=1, source_target_pairs={{0,2},{2,4},{4,6},{1,3},{3,5},{5,7},{8,10},{10,12},{12,14},{9,11},... | collective-permute-start | bytes 1567808 | tf_op jit(solution)/shard_map/ppermute | solution.py:39
  27.9 0.6 pad_convert_fusion.ins_ref
  28.5 1.2 copy.34
  29.7 1.3 collective-permute-start.3
  31.0 0.6 slice_bitcast_fusion.21
  31.6 1.7 %fusion = (bf16[128,512]{1,0:T(8,128)(2,1)}, bf16[128,512]{1,0:T(8,128)(2,1)}) fusion(f32[128,128]{1,0:T(8,128)} %get-tuple-element.37, f32[128,128]{1,0:T(8,128)} %get-tuple-element.38, f32[128,128]{1,0:T(8,128)} %get-tuple-element.39, f32[128,128]{1,0:T(8,128)S(1)} %get-tuple-element.36), kind=kLoop, calls=%fused_computation.8 | loop fusion | flops 458752 | bytes 524288 | tf_op jit(solution)/shard_map/convert_element_type | solution.py:203
  33.3 1.3 slice.244
  34.6 1.7 %maximum_bitcast_fusion = (f32[325,134]{1,0:T(8,128)}, f32[325,134]{1,0:T(8,128)}, f32[325,134]{1,0:T(8,128)}, f32[325,134]{1,0:T(8,128)}) fusion(f32[581,4,3]{2,0,1:T(8,128)S(1)} %copy-done.1, f32[581,4,128]{2,0,1:T(8,128)S(1)} %concatenate.30, f32[581,4,3]{2,0,1:T(8,128)S(1)} %copy.28), kind=kLoop, calls=%fused_computation.4 | loop fusion | flops 348400 | bytes 1942464 | tf_op jit(solution)/shard_map/squeeze | solution.py:64
  36.3 4.7 %collective-permute-done.2 = f32[325,3,134]{0,2,1:T(8,128)} collective-permute-done((f32[325,3,134]{0,2,1:T(8,128)}, f32[325,3,134]{0,2,1:T(8,128)}, u32[]{:S(2)}, u32[]{:S(2)}) %collective-permute-start.2) | collective-permute-done | bytes 522632 | tf_op jit(solution)/shard_map/ppermute | solution.py:39
  41.0 1.2 fusion.7
  42.1 0.9 copy.50
  43.0 0.9 copy.49
  43.9 0.9 copy.48
  44.9 11.5 %collective-permute-done.3 = f32[325,3,134]{0,2,1:T(8,128)} collective-permute-done((f32[325,3,134]{0,2,1:T(8,128)}, f32[325,3,134]{0,2,1:T(8,128)}, u32[]{:S(2)}, u32[]{:S(2)}) %collective-permute-start.3) | collective-permute-done | bytes 522632 | tf_op jit(solution)/shard_map/ppermute | solution.py:39
  56.3 1.2 fusion.6
  57.5 0.9 copy.53
  58.4 0.9 copy.52
  59.3 0.9 copy.51
  60.2 3.4 %concatenate.32.frc_ref.pk_ref = f32[325,1408]{1,0:T(8,128)S(1)} concatenate(f32[325,134]{1,0:T(8,128)} %bitcast.82, f32[325,134]{1,0:T(8,128)} %bitcast.81, f32[325,134]{1,0:T(8,128)} %bitcast.80, f32[325,134]{1,0:T(8,128)} %get-tuple-element.9, f32[325,134]{1,0:T(8,128)} %get-tuple-element.8, f32[325,134]{1,0:T(8,128)} %get-tuple-element.7, f32[325,134]{1,0:T(8,128)S(1)} %copy-done.5, ...), dimensions={1} | concatenate | bytes 3660800 | tf_op jit(solution)/shard_map/concatenate | solution.py:68
  63.7 0.7 reshape.68.inc_ref
  64.4 0.5 copy-done.4
  64.9 15.3 %shard_map.77 = f32[2,128,512]{2,1,0:T(8,128)} custom-call(s32[2]{0:T(128)} %get-tuple-element.56.order_ref, f32[325,1408]{1,0:T(8,128)} %copy-done.4, f32[325,1408]{1,0:T(8,128)} %copy-done.4, f32[2,2,1408]{2,1,0:T(2,128)} %reshape.68.inc_ref, f32[1,1408]{1,0:T(1,128)} %pad_convert_fusion.ins_ref, bf16[128,512]{1,0:T(8,128)(2,1)} %get-tuple-element.35.bhi_ref, ...), custom_call_target="tpu_custom_call" | custom-call | flops 4429185024 | bytes 2812288 | tf_op jit(solution)/shard_map/pallas_call | solution.py:142
  80.2 1.2 reshape.69
  81.5 1.3 collective-permute-start.6
  82.8 1.3 collective-permute-start.7
  84.1 0.1 fusion.4
  84.2 1.6 %collective-permute-done.7 = f32[2,2,4,3]{3,1,0,2:T(2,128)S(1)} collective-permute-done((f32[2,2,4,3]{3,1,0,2:T(2,128)S(1)}, f32[2,2,4,3]{3,1,0,2:T(2,128)S(1)}, u32[]{:S(2)}, u32[]{:S(2)}) %collective-permute-start.7) | collective-permute-done | bytes 224 | tf_op jit(solution)/shard_map/ppermute | solution.py:39
  85.9 0.7 collective-permute-start.10
  86.6 0.9 slice_bitcast_fusion
  87.5 0.2 stack_reshape.6
  87.7 1.0 copy.43
  88.7 0.2 copy.39
  88.9 6.2 %collective-permute-start.4 = (f32[256,3,134]{0,2,1:T(8,128)S(1)}, f32[256,3,134]{0,2,1:T(8,128)S(1)}, u32[]{:S(2)}, u32[]{:S(2)}) collective-permute-start(f32[256,3,134]{0,2,1:T(8,128)S(1)} %copy.39), channel_id=1, source_target_pairs={{0,2},{2,4},{4,6},{1,3},{3,5},{5,7},{8,10},{10,12},{12,14},{9,11},... | collective-permute-start | bytes 1234952 | tf_op jit(solution)/shard_map/ppermute | solution.py:39
  95.2 1.3 collective-permute-start.5
  96.5 3.5 %collective-permute-start.9 = (f32[2,2,4,134]{3,1,0,2:T(2,128)S(1)}, f32[2,2,4,134]{3,1,0,2:T(2,128)S(1)}, u32[]{:S(2)}, u32[]{:S(2)}) collective-permute-start(f32[2,2,4,134]{3,1,0,2:T(2,128)S(1)} %pad_maximum_fusion.3), channel_id=1, source_target_pairs={{0,8},{2,10},{4,12},{6,14},{8,16},{10,18},{12,20},{14,22},{16,24},... | collective-permute-start | bytes 25736 | tf_op jit(solution)/shard_map/ppermute | solution.py:40
  100.0 6.1 %collective-permute-start.8 = (f32[2,2,3,134]{3,1,0,2:T(2,128)S(1)}, f32[2,2,3,134]{3,1,0,2:T(2,128)S(1)}, u32[]{:S(2)}, u32[]{:S(2)}) collective-permute-start(f32[2,2,3,134]{3,1,0,2:T(2,128)S(1)} %get-tuple-element.43), channel_id=1, source_target_pairs={{0,10},{2,12},{4,14},{8,18},{10,20},{12,22},{16,26},{18,28},{20,30... | collective-permute-start | bytes 19304 | tf_op jit(solution)/shard_map/ppermute | solution.py:40
  106.1 1.2 collective-permute-done.8
  107.3 0.7 concatenate.39.inc_ref
  108.5 7.5 %collective-permute-done.5 = f32[256,3,134]{0,2,1:T(8,128)} collective-permute-done((f32[256,3,134]{0,2,1:T(8,128)}, f32[256,3,134]{0,2,1:T(8,128)}, u32[]{:S(2)}, u32[]{:S(2)}) %collective-permute-start.5) | collective-permute-done | bytes 411680 | tf_op jit(solution)/shard_map/ppermute | solution.py:39
  116.0 1.1 fusion.8
  117.5 1.8 %concatenate.37.frc_ref = f32[256,1408]{1,0:T(8,128)} concatenate(f32[256,134]{1,0:T(8,128)S(1)} %bitcast.88, f32[256,134]{1,0:T(8,128)S(1)} %bitcast.87, f32[256,134]{1,0:T(8,128)S(1)} %bitcast.86, f32[256,134]{1,0:T(8,128)S(1)} %copy-done.8, f32[256,134]{1,0:T(8,128)S(1)} %copy-done.7, f32[256,134]{1,0:T(8,128)S(1)} %copy-done.6, f32[256,134]{1,0:T(8,128)S(1)} %get-tuple-element.16, ...), dimensions={1} | concatenate | bytes 2883584 | tf_op jit(solution)/shard_map/concatenate | solution.py:68
  119.3 15.1 %shard_map.78 = f32[2,128,512]{2,1,0:T(8,128)} custom-call(s32[2]{0:T(128)} %get-tuple-element.57.order_ref, f32[256,1408]{1,0:T(8,128)} %concatenate.37.frc_ref, f32[325,1408]{1,0:T(8,128)} %copy-done.4, f32[2,2,1408]{2,1,0:T(2,128)} %concatenate.39.inc_ref, f32[1,1408]{1,0:T(1,128)} %pad_convert_fusion.ins_ref, ...), custom_call_target="tpu_custom_call" | custom-call | flops 4429185024 | bytes 2423680 | tf_op jit(solution)/shard_map/pallas_call | solution.py:142
  134.4 1.3 reshape.70
  135.7 0.2 stack_reshape.7
  135.9 0.6 slice.266
  136.5 1.2 pad_maximum_fusion.1
  (54 shorter events, 1.4 us)
Async XLA Ops:
  6.3 6.5 %copy-start.9 = (f32[1,4,2,64,64]{4,3,2,1,0:T(8,128)S(1)}, f32[1,4,2,64,64]{4,3,2,1,0:T(8,128)}, u32[]{:S(2)}) copy-start(f32[1,4,2,64,64]{4,3,2,1,0:T(8,128)} %param.8) | copy-start | bytes 393220
  8.0 6.3 %collective-permute-start.1 = (f32[581,4,3]{0,1,2:T(4,128)S(1)}, f32[581,4,3]{0,1,2:T(4,128)S(1)}, u32[]{:S(2)}, u32[]{:S(2)}) collective-permute-start(f32[581,4,3]{0,1,2:T(4,128)S(1)} %copy.27), channel_id=1, source_target_pairs={{1,0},{3,2},{5,4},{7,6},{9,8},{11,10},{13,12},{15,14},{17,16},{19,... | collective-permute-start | bytes 83672 | tf_op jit(solution)/shard_map/ppermute | solution.py:39
  9.7 4.2 %collective-permute-start = (f32[581,4,3]{0,1,2:T(4,128)S(1)}, f32[581,4,3]{0,1,2:T(4,128)S(1)}, u32[]{:S(2)}, u32[]{:S(2)}) collective-permute-start(f32[581,4,3]{0,1,2:T(4,128)S(1)} %copy.26), channel_id=1, source_target_pairs={{0,1},{2,3},{4,5},{6,7},{8,9},{10,11},{12,13},{14,15},{16,17},{18,... | collective-permute-start | bytes 83672 | tf_op jit(solution)/shard_map/ppermute | solution.py:39
  18.0 1.7 %copy-start = (f32[581,4,134]{2,0,1:T(8,128)}, f32[581,4,134]{2,0,1:T(8,128)S(1)}, u32[]{:S(2)}) copy-start(f32[581,4,134]{2,0,1:T(8,128)S(1)} %pad_maximum_fusion) | copy-start | bytes 3736996
  22.1 8.9 %copy-start.10 = (s32[2,1,2]{2,1,0:T(1,128)S(1)}, s32[2,1,2]{2,1,0:T(1,128)}, u32[]{:S(2)}) copy-start(s32[2,1,2]{2,1,0:T(1,128)} %param.10) | copy-start | bytes 52
  22.1 18.9 %collective-permute-start.2 = (f32[325,3,134]{0,2,1:T(8,128)}, f32[325,3,134]{0,2,1:T(8,128)}, u32[]{:S(2)}, u32[]{:S(2)}) collective-permute-start(f32[325,3,134]{0,2,1:T(8,128)} %copy.30), channel_id=1, source_target_pairs={{0,2},{2,4},{4,6},{1,3},{3,5},{5,7},{8,10},{10,12},{12,14},{9,11},... | collective-permute-start | bytes 1567808 | tf_op jit(solution)/shard_map/ppermute | solution.py:39
  29.7 26.6 %collective-permute-start.3 = (f32[325,3,134]{0,2,1:T(8,128)}, f32[325,3,134]{0,2,1:T(8,128)}, u32[]{:S(2)}, u32[]{:S(2)}) collective-permute-start(f32[325,3,134]{0,2,1:T(8,128)} %copy.34), channel_id=1, source_target_pairs={{2,0},{4,2},{6,4},{3,1},{5,3},{7,5},{10,8},{12,10},{14,12},{11,9},... | collective-permute-start | bytes 1567808 | tf_op jit(solution)/shard_map/ppermute | solution.py:39
  31.6 3.1 %copy-start.1 = (f32[581,4,3]{2,0,1:T(8,128)S(1)}, f32[581,4,3]{2,0,1:T(8,128)}, u32[]{:S(2)}) copy-start(f32[581,4,3]{2,0,1:T(8,128)} %copy.29) | copy-start | bytes 83668
  57.5 2.7 %copy-start.5 = (f32[325,134]{1,0:T(8,128)S(1)}, f32[325,134]{1,0:T(8,128)}, u32[]{:S(2)}) copy-start(f32[325,134]{1,0:T(8,128)} %get-tuple-element.6) | copy-start | bytes 522604
  63.6 1.3 copy-start.4
  81.5 2.7 %collective-permute-start.6 = (f32[2,2,4,3]{3,1,0,2:T(2,128)S(1)}, f32[2,2,4,3]{3,1,0,2:T(2,128)S(1)}, u32[]{:S(2)}, u32[]{:S(2)}) collective-permute-start(f32[2,2,4,3]{3,1,0,2:T(2,128)S(1)} %get-tuple-element.54), channel_id=1, source_target_pairs={{0,1},{2,3},{4,5},{6,7},{8,9},{10,11},{12,13},{14,15},{16,17},{18,... | collective-permute-start | bytes 584 | tf_op jit(solution)/shard_map/ppermute | solution.py:39
  82.8 3.1 %collective-permute-start.7 = (f32[2,2,4,3]{3,1,0,2:T(2,128)S(1)}, f32[2,2,4,3]{3,1,0,2:T(2,128)S(1)}, u32[]{:S(2)}, u32[]{:S(2)}) collective-permute-start(f32[2,2,4,3]{3,1,0,2:T(2,128)S(1)} %get-tuple-element.55), channel_id=1, source_target_pairs={{1,0},{3,2},{5,4},{7,6},{9,8},{11,10},{13,12},{15,14},{17,16},{19,... | collective-permute-start | bytes 584 | tf_op jit(solution)/shard_map/ppermute | solution.py:39
  84.2 3.3 %copy-start.2 = (f32[2,128,512]{2,1,0:T(8,128)S(1)}, f32[2,128,512]{2,1,0:T(8,128)}, u32[]{:S(2)}) copy-start(f32[2,128,512]{2,1,0:T(8,128)} %shard_map.77) | copy-start | bytes 1572868
  85.9 20.1 %collective-permute-start.10 = (f32[2,2,3,134]{3,1,0,2:T(2,128)S(1)}, f32[2,2,3,134]{3,1,0,2:T(2,128)S(1)}, u32[]{:S(2)}, u32[]{:S(2)}) collective-permute-start(f32[2,2,3,134]{3,1,0,2:T(2,128)S(1)} %get-tuple-element.42), channel_id=1, source_target_pairs={{2,8},{4,10},{6,12},{10,16},{12,18},{14,20},{18,24},{20,26},{22,28... | collective-permute-start | bytes 19304 | tf_op jit(solution)/shard_map/ppermute | solution.py:40
  88.9 19.1 %collective-permute-start.4 = (f32[256,3,134]{0,2,1:T(8,128)S(1)}, f32[256,3,134]{0,2,1:T(8,128)S(1)}, u32[]{:S(2)}, u32[]{:S(2)}) collective-permute-start(f32[256,3,134]{0,2,1:T(8,128)S(1)} %copy.39), channel_id=1, source_target_pairs={{0,2},{2,4},{4,6},{1,3},{3,5},{5,7},{8,10},{10,12},{12,14},{9,11},... | collective-permute-start | bytes 1234952 | tf_op jit(solution)/shard_map/ppermute | solution.py:39
  95.2 20.8 %collective-permute-start.5 = (f32[256,3,134]{0,2,1:T(8,128)}, f32[256,3,134]{0,2,1:T(8,128)}, u32[]{:S(2)}, u32[]{:S(2)}) collective-permute-start(f32[256,3,134]{0,2,1:T(8,128)} %copy.43), channel_id=1, source_target_pairs={{2,0},{4,2},{6,4},{3,1},{5,3},{7,5},{10,8},{12,10},{14,12},{11,9},... | collective-permute-start | bytes 1234952 | tf_op jit(solution)/shard_map/ppermute | solution.py:39
  96.5 10.8 %collective-permute-start.9 = (f32[2,2,4,134]{3,1,0,2:T(2,128)S(1)}, f32[2,2,4,134]{3,1,0,2:T(2,128)S(1)}, u32[]{:S(2)}, u32[]{:S(2)}) collective-permute-start(f32[2,2,4,134]{3,1,0,2:T(2,128)S(1)} %pad_maximum_fusion.3), channel_id=1, source_target_pairs={{0,8},{2,10},{4,12},{6,14},{8,16},{10,18},{12,20},{14,22},{16,24},... | collective-permute-start | bytes 25736 | tf_op jit(solution)/shard_map/ppermute | solution.py:40
  100.0 7.3 %collective-permute-start.8 = (f32[2,2,3,134]{3,1,0,2:T(2,128)S(1)}, f32[2,2,3,134]{3,1,0,2:T(2,128)S(1)}, u32[]{:S(2)}, u32[]{:S(2)}) collective-permute-start(f32[2,2,3,134]{3,1,0,2:T(2,128)S(1)} %get-tuple-element.43), channel_id=1, source_target_pairs={{0,10},{2,12},{4,14},{8,18},{10,20},{12,22},{16,26},{18,28},{20,30... | collective-permute-start | bytes 19304 | tf_op jit(solution)/shard_map/ppermute | solution.py:40
  108.5 9.0 %copy-start.6 = (f32[256,134]{1,0:T(8,128)S(1)}, f32[256,134]{1,0:T(8,128)}, u32[]{:S(2)}) copy-start(f32[256,134]{1,0:T(8,128)} %get-tuple-element.17) | copy-start | bytes 411652
  108.5 9.0 %copy-start.7 = (f32[256,134]{1,0:T(8,128)S(1)}, f32[256,134]{1,0:T(8,128)}, u32[]{:S(2)}) copy-start(f32[256,134]{1,0:T(8,128)} %get-tuple-element.18) | copy-start | bytes 411652
  108.5 9.0 %copy-start.8 = (f32[256,134]{1,0:T(8,128)S(1)}, f32[256,134]{1,0:T(8,128)}, u32[]{:S(2)}) copy-start(f32[256,134]{1,0:T(8,128)} %get-tuple-element.19) | copy-start | bytes 411652
  134.4 1.3 copy-start.3

commit v7 on v6

--- a/solution.py
+++ b/solution.py
@@ -68,21 +68,26 @@
     return jnp.concatenate(segments, axis=-1)
 
 
-def tick_kernel(order_ref, frc_ref, pk_ref, inc_ref, ins_ref, bhi_ref, blo_ref, out_ref, *, row, depth, width):
+def tick_kernel(
+    order_ref, frc_ref, pk_ref, inc_ref, ins_ref, bhi_ref, blo_ref, out_ref, field_ref, *, row, depth, width
+):
     nsrc, rows, owned = out_ref.shape
     cols = pk_ref.shape[1]
     classes = bhi_ref.shape[1] // rows
     lanes = 128
     wave0 = pk_ref.shape[0] - depth - 2 * nsrc - 1
-    zrow = lax.broadcasted_iota(jnp.int32, (rows, cols), 0) % depth
-    top = zrow == 0
-    bottom = zrow == depth - 1
-
-    def precond(x):
+    label_row = wave0 + depth + 2 * nsrc
+    extent = owned // lanes + 2 * width
+
+    def edges(lo, hi):
+        zrow = lax.broadcasted_iota(jnp.int32, (rows, hi - lo), 0) % depth
+        return zrow == 0, zrow == depth - 1
+
+    def precond(x, lo, hi):
         scaled = x * SPLIT
         high = scaled - (scaled - x)
         low = x - high
-        label = pk_ref[pl.ds(wave0 + depth + 2 * nsrc, 1), :]
+        label = pk_ref[pl.ds(label_row, 1), lo:hi]
         hots = [(label == float(k)).astype(jnp.float32) for k in range(classes)]
         high = jnp.concatenate([high * h for h in hots], axis=0).astype(jnp.bfloat16)
         low = jnp.concatenate([low * h for h in hots], axis=0).astype(jnp.bfloat16)
@@ -92,8 +97,10 @@
         out = out + jnp.dot(blo, high, preferred_element_type=jnp.float32)
         return out + jnp.dot(bhi, high, preferred_element_type=jnp.float32)
 
-    def apply_a(u):
-        wave = pk_ref[pl.ds(wave0, depth), :]
+    def apply_a(u, lo, hi):
+        span = hi - lo
+        top, bottom = edges(lo, hi)
+        wave = pk_ref[pl.ds(wave0, depth), lo:hi]
         dr = 6.0 - wave
         di = -DAMPING * wave
         real = u[:depth]
@@ -104,8 +111,8 @@
         down = jnp.where(top, 0.0, pltpu.roll(u, 1, 0))
         up = jnp.where(bottom, 0.0, pltpu.roll(u, rows - 1, 0))
         beside = up + down
-        beside = beside + pltpu.roll(u, cols - row, 1) + pltpu.roll(u, row, 1)
-        beside = beside + pltpu.roll(u, cols - 1, 1) + pltpu.roll(u, 1, 1)
+        beside = beside + pltpu.roll(u, span - row, 1) + pltpu.roll(u, row, 1)
+        beside = beside + pltpu.roll(u, span - 1, 1) + pltpu.roll(u, 1, 1)
         return diagonal - beside
 
     def one_source(s, carry):
@@ -119,12 +126,18 @@
             ],
             axis=0,
         )
+        top, _ = edges(0, cols)
         rhs = jnp.where(top, forcing + layer, forcing)
-
-        def correct(i, u):
-            return u + precond(ins_ref[...] * (rhs - apply_a(u)))
-
-        u = lax.fori_loop(0, CORR, correct, precond(rhs))
+        field_ref[...] = precond(rhs, 0, cols)
+        for step in range(1, CORR + 1):
+            a = (step * row) // lanes * lanes
+            b = min(-(-((extent - step) * row) // lanes) * lanes, cols)
+            lo = max(a - 2 * lanes, 0)
+            hi = min(b + 2 * lanes, cols)
+            stencil = apply_a(field_ref[:, lo:hi], lo, hi)[:, a - lo : b - lo]
+            residual = ins_ref[:, a:b] * (rhs[:, a:b] - stencil)
+            field_ref[:, a:b] = field_ref[:, a:b] + precond(residual, a, b)
+        u = field_ref[...]
         for x in range(owned // lanes):
             begin = (x + width) * row + width
             out_ref[s, :, x * lanes : (x + 1) * lanes] = pltpu.roll(u, cols - begin, 1)[:, :lanes]
@@ -144,6 +157,7 @@
         out_shape=jax.ShapeDtypeStruct((nsrc, rows, owned), jnp.float32),
         in_specs=[pl.BlockSpec(memory_space=pltpu.SMEM)] + [vmem] * 6,
         out_specs=vmem,
+        scratch_shapes=[pltpu.VMEM((rows, cols), jnp.float32)],
         cost_estimate=pl.CostEstimate(
             flops=flops,
             transcendentals=0,

time: 139 us -> 131 us (0.942)
  Pallas kernels: 30.3 us -> 23 us
    pallas_call x2, Pallas kernels: 30.3 us -> 23 us  [run_tick(): pl.pallas_call(functools.partial(tick_kernel, row=row, depth=depth, width...]
  transfers between devices with their start and end apart: 11 -> 11, of which waited for: 5 -> 5; matrix products, arithmetic and copies ran while one was open for 12% -> 13% of each run, Pallas kernels for 0% -> 0%
where the time goes in v7:
time: 131 us; the launch traced here: 130 us
  local copies, waits for them, and re-layouts  39.6 us (30%)
  starting transfers between devices  31.8 us (24%)
  waiting for transfers between devices  26.4 us (20%)
  Pallas kernels  23 us (18%)
  other arithmetic  8.5 us (6%)
    ppermute x8, waiting for transfers between devices, fetch(): return lax.ppermute(block, axes[0], pairs)  25.2 us
    pallas_call x2, Pallas kernels, run_tick(): pl.pallas_call(functools.partial(tick_kernel, row=row, depth=depth, width...  23 us
    ppermute x8, starting transfers between devices, fetch(): return lax.ppermute(block, axes[0], pairs)  21.5 us
    ppermute x3, starting transfers between devices, fetch(): return lax.ppermute(block, tuple(axes), pairs)  10.2 us
    unnamed x38, local copies, waits for them, and re-layouts  8.84 us
    concatenate x3, local copies, waits for them, and re-layouts, flat_extended(): return jnp.concatenate(segments, axis=-1)  5.99 us
    slice x5, local copies, waits for them, and re-layouts, flat_extended(): block[..., :width, :]  3.54 us
    slice x4, local copies, waits for them, and re-layouts, flat_extended(): segments.append(pieces[dx][..., r, :])  3.44 us
  transfers between devices with their start and end apart: 11, of which 5 were waited for; matrix products, arithmetic and copies ran while one was open for 13% of the time, Pallas kernels for 0%

profile of v7, /device:TPU:0, one launch (start us, length us, event | category | flops | bytes accessed | tf_op | source)
XLA Modules:
  0.0 130.4 jit_solution(4194672913738434431)
XLA Ops:
  0.6 0.7 convert_element_type.23
  1.3 0.7 copy.22
  2.0 0.9 copy.24
  2.9 1.3 fusion.5
  4.3 0.5 concatenate.30
  4.9 1.4 %fusion.3 = (f32[581,4,3]{2,0,1:T(8,128)S(1)}, f32[581,4,3]{2,0,1:T(8,128)}) fusion(f32[581,4,128]{2,0,1:T(8,128)S(1)} %concatenate.30), kind=kLoop, calls=%fused_computation.42 | loop fusion | bytes 111552 | tf_op jit(solution)/shard_map/slice | solution.py:45
  6.3 1.7 %copy.27 = f32[581,4,3]{0,1,2:T(4,128)S(1)} copy(f32[581,4,3]{2,0,1:T(8,128)} %get-tuple-element.13) | data formatting | bytes 55776 | tf_op jit(solution)/shard_map/slice | solution.py:46
  8.0 1.3 collective-permute-start.1
  9.3 0.4 copy.26
  9.7 3.0 %collective-permute-start = (f32[581,4,3]{0,1,2:T(4,128)S(1)}, f32[581,4,3]{0,1,2:T(4,128)S(1)}, u32[]{:S(2)}, u32[]{:S(2)}) collective-permute-start(f32[581,4,3]{0,1,2:T(4,128)S(1)} %copy.26), channel_id=1, source_target_pairs={{0,1},{2,3},{4,5},{6,7},{8,9},{10,11},{12,13},{14,15},{16,17},{18,... | collective-permute-start | bytes 83672 | tf_op jit(solution)/shard_map/ppermute | solution.py:39
  12.8 0.1 maximum_maximum_fusion
  13.0 0.7 slice_bitcast_fusion.9
  13.9 0.4 copy.28
  14.3 1.4 %copy.29 = f32[581,4,3]{2,0,1:T(8,128)} copy(f32[581,4,3]{0,1,2:T(4,128)S(1)} %collective-permute-done.1) | data formatting | bytes 55776 | tf_op jit(solution)/shard_map/ppermute | solution.py:39
  15.7 2.3 %pad_maximum_fusion = f32[581,4,134]{2,0,1:T(8,128)S(1)} fusion(f32[581,4,3]{2,0,1:T(8,128)} %copy.29, f32[581,4,128]{2,0,1:T(8,128)S(1)} %concatenate.30, f32[581,4,3]{2,0,1:T(8,128)S(1)} %copy.28), kind=kLoop, calls=%fused_computation | loop fusion | flops 622832 | bytes 2491328 | tf_op jit(solution)/shard_map/concatenate | solution.py:47
  18.0 1.2 fusion.2
  19.2 0.5 copy-done
  19.7 2.4 %copy.30 = f32[325,3,134]{0,2,1:T(8,128)} copy(f32[325,3,134]{2,0,1:T(8,128)} %get-tuple-element.11) | data formatting | bytes 1045200 | tf_op jit(solution)/shard_map/slice | solution.py:53
  22.1 5.8 %collective-permute-start.2 = (f32[325,3,134]{0,2,1:T(8,128)}, f32[325,3,134]{0,2,1:T(8,128)}, u32[]{:S(2)}, u32[]{:S(2)}) collective-permute-start(f32[325,3,134]{0,2,1:T(8,128)} %copy.30), channel_id=1, source_target_pairs={{0,2},{2,4},{4,6},{1,3},{3,5},{5,7},{8,10},{10,12},{12,14},{9,11},... | collective-permute-start | bytes 1567808 | tf_op jit(solution)/shard_map/ppermute | solution.py:39
  27.9 0.6 pad_convert_fusion.ins_ref
  28.5 1.2 copy.34
  29.7 1.3 collective-permute-start.3
  31.0 0.6 slice_bitcast_fusion.21
  31.6 1.7 %fusion = (bf16[128,512]{1,0:T(8,128)(2,1)}, bf16[128,512]{1,0:T(8,128)(2,1)}) fusion(f32[128,128]{1,0:T(8,128)} %get-tuple-element.37, f32[128,128]{1,0:T(8,128)} %get-tuple-element.38, f32[128,128]{1,0:T(8,128)} %get-tuple-element.39, f32[128,128]{1,0:T(8,128)S(1)} %get-tuple-element.36), kind=kLoop, calls=%fused_computation.8 | loop fusion | flops 458752 | bytes 524288 | tf_op jit(solution)/shard_map/convert_element_type | solution.py:217
  33.3 1.3 %slice.244 = f32[256,4,134]{2,0,1:T(8,128)S(1)} slice(f32[581,4,134]{2,0,1:T(8,128)} %copy-done), slice={[325:581], [0:4], [0:134]} | slice | bytes 1097728 | tf_op jit(solution)/shard_map/slice | solution.py:202
  34.6 1.7 %maximum_bitcast_fusion = (f32[325,134]{1,0:T(8,128)}, f32[325,134]{1,0:T(8,128)}, f32[325,134]{1,0:T(8,128)}, f32[325,134]{1,0:T(8,128)}) fusion(f32[581,4,3]{2,0,1:T(8,128)S(1)} %copy-done.1, f32[581,4,128]{2,0,1:T(8,128)S(1)} %concatenate.30, f32[581,4,3]{2,0,1:T(8,128)S(1)} %copy.28), kind=kLoop, calls=%fused_computation.4 | loop fusion | flops 348400 | bytes 1942464 | tf_op jit(solution)/shard_map/squeeze | solution.py:64
  36.3 4.7 %collective-permute-done.2 = f32[325,3,134]{0,2,1:T(8,128)} collective-permute-done((f32[325,3,134]{0,2,1:T(8,128)}, f32[325,3,134]{0,2,1:T(8,128)}, u32[]{:S(2)}, u32[]{:S(2)}) %collective-permute-start.2) | collective-permute-done | bytes 522632 | tf_op jit(solution)/shard_map/ppermute | solution.py:39
  41.0 1.2 fusion.7
  42.1 0.9 copy.50
  43.0 0.9 copy.49
  43.9 0.9 copy.48
  44.9 11.5 %collective-permute-done.3 = f32[325,3,134]{0,2,1:T(8,128)} collective-permute-done((f32[325,3,134]{0,2,1:T(8,128)}, f32[325,3,134]{0,2,1:T(8,128)}, u32[]{:S(2)}, u32[]{:S(2)}) %collective-permute-start.3) | collective-permute-done | bytes 522632 | tf_op jit(solution)/shard_map/ppermute | solution.py:39
  56.3 1.2 fusion.6
  57.5 0.9 copy.53
  58.4 0.9 copy.52
  59.3 0.9 copy.51
  60.2 3.4 %concatenate.32.frc_ref.pk_ref = f32[325,1408]{1,0:T(8,128)S(1)} concatenate(f32[325,134]{1,0:T(8,128)} %bitcast.82, f32[325,134]{1,0:T(8,128)} %bitcast.81, f32[325,134]{1,0:T(8,128)} %bitcast.80, f32[325,134]{1,0:T(8,128)} %get-tuple-element.9, f32[325,134]{1,0:T(8,128)} %get-tuple-element.8, f32[325,134]{1,0:T(8,128)} %get-tuple-element.7, f32[325,134]{1,0:T(8,128)S(1)} %copy-done.5, ...), dimensions={1} | concatenate | bytes 3660800 | tf_op jit(solution)/shard_map/concatenate | solution.py:68
  63.7 0.7 reshape.68.inc_ref
  64.4 0.5 copy-done.4
  64.9 11.6 %shard_map.77 = f32[2,128,512]{2,1,0:T(8,128)} custom-call(s32[2]{0:T(128)} %get-tuple-element.56.order_ref, f32[325,1408]{1,0:T(8,128)} %copy-done.4, f32[325,1408]{1,0:T(8,128)} %copy-done.4, f32[2,2,1408]{2,1,0:T(2,128)} %reshape.68.inc_ref, f32[1,1408]{1,0:T(1,128)} %pad_convert_fusion.ins_ref, bf16[128,512]{1,0:T(8,128)(2,1)} %get-tuple-element.35.bhi_ref, ...), custom_call_target="tpu_custom_call" | custom-call | flops 4429185024 | bytes 2812288 | tf_op jit(solution)/shard_map/pallas_call | solution.py:155
  76.5 1.2 reshape.69
  77.8 1.3 collective-permute-start.6
  79.1 1.3 collective-permute-start.7
  80.4 0.1 fusion.4
  80.5 1.6 %collective-permute-done.7 = f32[2,2,4,3]{3,1,0,2:T(2,128)S(1)} collective-permute-done((f32[2,2,4,3]{3,1,0,2:T(2,128)S(1)}, f32[2,2,4,3]{3,1,0,2:T(2,128)S(1)}, u32[]{:S(2)}, u32[]{:S(2)}) %collective-permute-start.7) | collective-permute-done | bytes 224 | tf_op jit(solution)/shard_map/ppermute | solution.py:39
  82.3 0.7 collective-permute-start.10
  82.9 0.9 slice_bitcast_fusion
  83.9 0.2 stack_reshape.6
  84.0 1.0 copy.43
  85.0 0.2 copy.39
  85.3 6.2 %collective-permute-start.4 = (f32[256,3,134]{0,2,1:T(8,128)S(1)}, f32[256,3,134]{0,2,1:T(8,128)S(1)}, u32[]{:S(2)}, u32[]{:S(2)}) collective-permute-start(f32[256,3,134]{0,2,1:T(8,128)S(1)} %copy.39), channel_id=1, source_target_pairs={{0,2},{2,4},{4,6},{1,3},{3,5},{5,7},{8,10},{10,12},{12,14},{9,11},... | collective-permute-start | bytes 1234952 | tf_op jit(solution)/shard_map/ppermute | solution.py:39
  91.5 1.3 collective-permute-start.5
  92.8 3.5 %collective-permute-start.9 = (f32[2,2,4,134]{3,1,0,2:T(2,128)S(1)}, f32[2,2,4,134]{3,1,0,2:T(2,128)S(1)}, u32[]{:S(2)}, u32[]{:S(2)}) collective-permute-start(f32[2,2,4,134]{3,1,0,2:T(2,128)S(1)} %pad_maximum_fusion.3), channel_id=1, source_target_pairs={{0,8},{2,10},{4,12},{6,14},{8,16},{10,18},{12,20},{14,22},{16,24},... | collective-permute-start | bytes 25736 | tf_op jit(solution)/shard_map/ppermute | solution.py:40
  96.3 6.1 %collective-permute-start.8 = (f32[2,2,3,134]{3,1,0,2:T(2,128)S(1)}, f32[2,2,3,134]{3,1,0,2:T(2,128)S(1)}, u32[]{:S(2)}, u32[]{:S(2)}) collective-permute-start(f32[2,2,3,134]{3,1,0,2:T(2,128)S(1)} %get-tuple-element.43), channel_id=1, source_target_pairs={{0,10},{2,12},{4,14},{8,18},{10,20},{12,22},{16,26},{18,28},{20,30... | collective-permute-start | bytes 19304 | tf_op jit(solution)/shard_map/ppermute | solution.py:40
  102.4 1.2 collective-permute-done.8
  103.6 0.7 concatenate.39.inc_ref
  104.8 7.5 %collective-permute-done.5 = f32[256,3,134]{0,2,1:T(8,128)} collective-permute-done((f32[256,3,134]{0,2,1:T(8,128)}, f32[256,3,134]{0,2,1:T(8,128)}, u32[]{:S(2)}, u32[]{:S(2)}) %collective-permute-start.5) | collective-permute-done | bytes 411680 | tf_op jit(solution)/shard_map/ppermute | solution.py:39
  112.3 1.1 fusion.8
  113.8 1.8 %concatenate.37.frc_ref = f32[256,1408]{1,0:T(8,128)} concatenate(f32[256,134]{1,0:T(8,128)S(1)} %bitcast.88, f32[256,134]{1,0:T(8,128)S(1)} %bitcast.87, f32[256,134]{1,0:T(8,128)S(1)} %bitcast.86, f32[256,134]{1,0:T(8,128)S(1)} %copy-done.8, f32[256,134]{1,0:T(8,128)S(1)} %copy-done.7, f32[256,134]{1,0:T(8,128)S(1)} %copy-done.6, f32[256,134]{1,0:T(8,128)S(1)} %get-tuple-element.16, ...), dimensions={1} | concatenate | bytes 2883584 | tf_op jit(solution)/shard_map/concatenate | solution.py:68
  115.7 11.4 %shard_map.78 = f32[2,128,512]{2,1,0:T(8,128)} custom-call(s32[2]{0:T(128)} %get-tuple-element.57.order_ref, f32[256,1408]{1,0:T(8,128)} %concatenate.37.frc_ref, f32[325,1408]{1,0:T(8,128)} %copy-done.4, f32[2,2,1408]{2,1,0:T(2,128)} %concatenate.39.inc_ref, f32[1,1408]{1,0:T(1,128)} %pad_convert_fusion.ins_ref, ...), custom_call_target="tpu_custom_call" | custom-call | flops 4429185024 | bytes 2423680 | tf_op jit(solution)/shard_map/pallas_call | solution.py:155
  127.1 1.3 reshape.70
  128.4 0.2 stack_reshape.7
  128.6 0.6 slice.266
  129.2 1.2 pad_maximum_fusion.1
  (54 shorter events, 1.4 us)
Async XLA Ops:
  6.3 6.5 %copy-start.9 = (f32[1,4,2,64,64]{4,3,2,1,0:T(8,128)S(1)}, f32[1,4,2,64,64]{4,3,2,1,0:T(8,128)}, u32[]{:S(2)}) copy-start(f32[1,4,2,64,64]{4,3,2,1,0:T(8,128)} %param.8) | copy-start | bytes 393220
  8.0 6.3 %collective-permute-start.1 = (f32[581,4,3]{0,1,2:T(4,128)S(1)}, f32[581,4,3]{0,1,2:T(4,128)S(1)}, u32[]{:S(2)}, u32[]{:S(2)}) collective-permute-start(f32[581,4,3]{0,1,2:T(4,128)S(1)} %copy.27), channel_id=1, source_target_pairs={{1,0},{3,2},{5,4},{7,6},{9,8},{11,10},{13,12},{15,14},{17,16},{19,... | collective-permute-start | bytes 83672 | tf_op jit(solution)/shard_map/ppermute | solution.py:39
  9.7 4.2 %collective-permute-start = (f32[581,4,3]{0,1,2:T(4,128)S(1)}, f32[581,4,3]{0,1,2:T(4,128)S(1)}, u32[]{:S(2)}, u32[]{:S(2)}) collective-permute-start(f32[581,4,3]{0,1,2:T(4,128)S(1)} %copy.26), channel_id=1, source_target_pairs={{0,1},{2,3},{4,5},{6,7},{8,9},{10,11},{12,13},{14,15},{16,17},{18,... | collective-permute-start | bytes 83672 | tf_op jit(solution)/shard_map/ppermute | solution.py:39
  18.0 1.7 %copy-start = (f32[581,4,134]{2,0,1:T(8,128)}, f32[581,4,134]{2,0,1:T(8,128)S(1)}, u32[]{:S(2)}) copy-start(f32[581,4,134]{2,0,1:T(8,128)S(1)} %pad_maximum_fusion) | copy-start | bytes 3736996
  22.1 8.9 %copy-start.10 = (s32[2,1,2]{2,1,0:T(1,128)S(1)}, s32[2,1,2]{2,1,0:T(1,128)}, u32[]{:S(2)}) copy-start(s32[2,1,2]{2,1,0:T(1,128)} %param.10) | copy-start | bytes 52
  22.1 18.9 %collective-permute-start.2 = (f32[325,3,134]{0,2,1:T(8,128)}, f32[325,3,134]{0,2,1:T(8,128)}, u32[]{:S(2)}, u32[]{:S(2)}) collective-permute-start(f32[325,3,134]{0,2,1:T(8,128)} %copy.30), channel_id=1, source_target_pairs={{0,2},{2,4},{4,6},{1,3},{3,5},{5,7},{8,10},{10,12},{12,14},{9,11},... | collective-permute-start | bytes 1567808 | tf_op jit(solution)/shard_map/ppermute | solution.py:39
  29.7 26.6 %collective-permute-start.3 = (f32[325,3,134]{0,2,1:T(8,128)}, f32[325,3,134]{0,2,1:T(8,128)}, u32[]{:S(2)}, u32[]{:S(2)}) collective-permute-start(f32[325,3,134]{0,2,1:T(8,128)} %copy.34), channel_id=1, source_target_pairs={{2,0},{4,2},{6,4},{3,1},{5,3},{7,5},{10,8},{12,10},{14,12},{11,9},... | collective-permute-start | bytes 1567808 | tf_op jit(solution)/shard_map/ppermute | solution.py:39
  31.6 3.1 %copy-start.1 = (f32[581,4,3]{2,0,1:T(8,128)S(1)}, f32[581,4,3]{2,0,1:T(8,128)}, u32[]{:S(2)}) copy-start(f32[581,4,3]{2,0,1:T(8,128)} %copy.29) | copy-start | bytes 83668
  57.5 2.7 %copy-start.5 = (f32[325,134]{1,0:T(8,128)S(1)}, f32[325,134]{1,0:T(8,128)}, u32[]{:S(2)}) copy-start(f32[325,134]{1,0:T(8,128)} %get-tuple-element.6) | copy-start | bytes 522604
  63.6 1.3 copy-start.4
  77.8 2.7 %collective-permute-start.6 = (f32[2,2,4,3]{3,1,0,2:T(2,128)S(1)}, f32[2,2,4,3]{3,1,0,2:T(2,128)S(1)}, u32[]{:S(2)}, u32[]{:S(2)}) collective-permute-start(f32[2,2,4,3]{3,1,0,2:T(2,128)S(1)} %get-tuple-element.54), channel_id=1, source_target_pairs={{0,1},{2,3},{4,5},{6,7},{8,9},{10,11},{12,13},{14,15},{16,17},{18,... | collective-permute-start | bytes 584 | tf_op jit(solution)/shard_map/ppermute | solution.py:39
  79.1 3.1 %collective-permute-start.7 = (f32[2,2,4,3]{3,1,0,2:T(2,128)S(1)}, f32[2,2,4,3]{3,1,0,2:T(2,128)S(1)}, u32[]{:S(2)}, u32[]{:S(2)}) collective-permute-start(f32[2,2,4,3]{3,1,0,2:T(2,128)S(1)} %get-tuple-element.55), channel_id=1, source_target_pairs={{1,0},{3,2},{5,4},{7,6},{9,8},{11,10},{13,12},{15,14},{17,16},{19,... | collective-permute-start | bytes 584 | tf_op jit(solution)/shard_map/ppermute | solution.py:39
  80.5 3.3 %copy-start.2 = (f32[2,128,512]{2,1,0:T(8,128)S(1)}, f32[2,128,512]{2,1,0:T(8,128)}, u32[]{:S(2)}) copy-start(f32[2,128,512]{2,1,0:T(8,128)} %shard_map.77) | copy-start | bytes 1572868
  82.3 20.1 %collective-permute-start.10 = (f32[2,2,3,134]{3,1,0,2:T(2,128)S(1)}, f32[2,2,3,134]{3,1,0,2:T(2,128)S(1)}, u32[]{:S(2)}, u32[]{:S(2)}) collective-permute-start(f32[2,2,3,134]{3,1,0,2:T(2,128)S(1)} %get-tuple-element.42), channel_id=1, source_target_pairs={{2,8},{4,10},{6,12},{10,16},{12,18},{14,20},{18,24},{20,26},{22,28... | collective-permute-start | bytes 19304 | tf_op jit(solution)/shard_map/ppermute | solution.py:40
  85.3 19.1 %collective-permute-start.4 = (f32[256,3,134]{0,2,1:T(8,128)S(1)}, f32[256,3,134]{0,2,1:T(8,128)S(1)}, u32[]{:S(2)}, u32[]{:S(2)}) collective-permute-start(f32[256,3,134]{0,2,1:T(8,128)S(1)} %copy.39), channel_id=1, source_target_pairs={{0,2},{2,4},{4,6},{1,3},{3,5},{5,7},{8,10},{10,12},{12,14},{9,11},... | collective-permute-start | bytes 1234952 | tf_op jit(solution)/shard_map/ppermute | solution.py:39
  91.5 20.8 %collective-permute-start.5 = (f32[256,3,134]{0,2,1:T(8,128)}, f32[256,3,134]{0,2,1:T(8,128)}, u32[]{:S(2)}, u32[]{:S(2)}) collective-permute-start(f32[256,3,134]{0,2,1:T(8,128)} %copy.43), channel_id=1, source_target_pairs={{2,0},{4,2},{6,4},{3,1},{5,3},{7,5},{10,8},{12,10},{14,12},{11,9},... | collective-permute-start | bytes 1234952 | tf_op jit(solution)/shard_map/ppermute | solution.py:39
  92.8 10.8 %collective-permute-start.9 = (f32[2,2,4,134]{3,1,0,2:T(2,128)S(1)}, f32[2,2,4,134]{3,1,0,2:T(2,128)S(1)}, u32[]{:S(2)}, u32[]{:S(2)}) collective-permute-start(f32[2,2,4,134]{3,1,0,2:T(2,128)S(1)} %pad_maximum_fusion.3), channel_id=1, source_target_pairs={{0,8},{2,10},{4,12},{6,14},{8,16},{10,18},{12,20},{14,22},{16,24},... | collective-permute-start | bytes 25736 | tf_op jit(solution)/shard_map/ppermute | solution.py:40
  96.3 7.3 %collective-permute-start.8 = (f32[2,2,3,134]{3,1,0,2:T(2,128)S(1)}, f32[2,2,3,134]{3,1,0,2:T(2,128)S(1)}, u32[]{:S(2)}, u32[]{:S(2)}) collective-permute-start(f32[2,2,3,134]{3,1,0,2:T(2,128)S(1)} %get-tuple-element.43), channel_id=1, source_target_pairs={{0,10},{2,12},{4,14},{8,18},{10,20},{12,22},{16,26},{18,28},{20,30... | collective-permute-start | bytes 19304 | tf_op jit(solution)/shard_map/ppermute | solution.py:40
  104.8 9.0 %copy-start.6 = (f32[256,134]{1,0:T(8,128)S(1)}, f32[256,134]{1,0:T(8,128)}, u32[]{:S(2)}) copy-start(f32[256,134]{1,0:T(8,128)} %get-tuple-element.17) | copy-start | bytes 411652
  104.8 9.0 %copy-start.7 = (f32[256,134]{1,0:T(8,128)S(1)}, f32[256,134]{1,0:T(8,128)}, u32[]{:S(2)}) copy-start(f32[256,134]{1,0:T(8,128)} %get-tuple-element.18) | copy-start | bytes 411652
  104.8 9.0 %copy-start.8 = (f32[256,134]{1,0:T(8,128)S(1)}, f32[256,134]{1,0:T(8,128)}, u32[]{:S(2)}) copy-start(f32[256,134]{1,0:T(8,128)} %get-tuple-element.19) | copy-start | bytes 411652
  127.1 1.3 copy-start.3

commit v8 on v7

--- a/solution.py
+++ b/solution.py
@@ -196,13 +196,32 @@
         + [per_tick[t] for t in range(1, ticks)],
         axis=0,
     )
-    packed = extend_y(packed, width)
     rows_now = per_tick.shape[1] + depth + nsrc * two + 1
+    now = packed[:rows_now]
+    low_x = fetch(now[:, nx - width :, :], ("tx",), (-1,))
+    high_x = fetch(now[:, :width, :], ("tx",), (1,))
+    widened = extend_y(packed, width)
     later = [
-        packed[rows_now + (t - 1) * per_tick.shape[1] : rows_now + t * per_tick.shape[1]]
+        widened[rows_now + (t - 1) * per_tick.shape[1] : rows_now + t * per_tick.shape[1]]
         for t in range(1, ticks)
     ]
-    packed = flat_extended(packed[:rows_now], width, padded)
+    low_y = widened[:rows_now, :, :width]
+    high_y = widened[:rows_now, :, width + ny :]
+    rims = jnp.concatenate([low_x, high_x], axis=1)
+    corner_low = fetch(rims[..., ny - width :], ("ty",), (-1,))
+    corner_high = fetch(rims[..., :width], ("ty",), (1,))
+    segments = []
+    for ix in range(ex):
+        if ix < width:
+            segments += [corner_low[:, ix], low_x[:, ix], corner_high[:, ix]]
+        elif ix < width + nx:
+            r = ix - width
+            segments += [low_y[:, r], now[:, r], high_y[:, r]]
+        else:
+            r = ix - width - nx
+            segments += [corner_low[:, width + r], high_x[:, r], corner_high[:, width + r]]
+    segments.append(jnp.zeros((rows_now, padded - cols), jnp.float32))
+    packed = jnp.concatenate(segments, axis=-1)
     first_pending = nsrc * two * depth + depth
 
     gx = lax.axis_index("tx") * nx - width + jnp.arange(ex)

time: 131 us -> 123 us (0.939)
  waiting for transfers between devices: 26.4 us -> 10.3 us
  local copies, waits for them, and re-layouts: 39.6 us -> 45.5 us
  starting transfers between devices: 31.8 us -> 37.2 us
  other arithmetic: 8.5 us -> 5.21 us
    ppermute x8 -> x10, waiting for transfers between devices: 25.2 us -> 9.09 us  [fetch(): return lax.ppermute(block, axes[0], pairs)]
    squeeze x0 -> x5, local copies, waits for them, and re-layouts: none -> 6.41 us  [the longest x3 2.63 us: per_device(): segments += [low_y[:, r], now[:, r], high_y[:, r]]]
    ppermute x8 -> x10, starting transfers between devices: 21.5 us -> 26.8 us  [fetch(): return lax.ppermute(block, axes[0], pairs)]
    concatenate x0 -> x2, local copies, waits for them, and re-layouts: none -> 5.12 us  [the longest x1 4.05 us: per_device(): packed = jnp.concatenate(segments, axis=-1)]
    unnamed x38 -> x39, local copies, waits for them, and re-layouts: 8.84 us -> 12.8 us
    concatenate x3 -> x2, local copies, waits for them, and re-layouts: 5.99 us -> 2.6 us  [flat_extended(): return jnp.concatenate(segments, axis=-1)]
    slice x5 -> x3, local copies, waits for them, and re-layouts: 3.54 us -> 1.13 us  [flat_extended(): block[..., :width, :]]
    slice x2 -> x1, local copies, waits for them, and re-layouts: 2.62 us -> 0.23 us  [flat_extended(): block[..., nx - width:, :]]
  transfers between devices with their start and end apart: 11 -> 13, of which waited for: 5 -> 3; matrix products, arithmetic and copies ran while one was open for 13% -> 18% of each run, Pallas kernels for 0% -> 0%
where the time goes in v8:
time: 123 us; the launch traced here: 122 us
  local copies, waits for them, and re-layouts  45.5 us (37%)
  starting transfers between devices  37.2 us (30%)
  Pallas kernels  22.9 us (19%)
  waiting for transfers between devices  10.3 us (8%)
  other arithmetic  5.21 us (4%)
    ppermute x10, starting transfers between devices, fetch(): return lax.ppermute(block, axes[0], pairs)  26.8 us
    pallas_call x2, Pallas kernels, run_tick(): pl.pallas_call(functools.partial(tick_kernel, row=row, depth=depth, width...  22.9 us
    unnamed x39, local copies, waits for them, and re-layouts  12.8 us
    ppermute x3, starting transfers between devices, fetch(): return lax.ppermute(block, tuple(axes), pairs)  10.4 us
    ppermute x10, waiting for transfers between devices, fetch(): return lax.ppermute(block, axes[0], pairs)  9.09 us
    concatenate x1, local copies, waits for them, and re-layouts, per_device(): packed = jnp.concatenate(segments, axis=-1)  4.05 us
    squeeze x3, local copies, waits for them, and re-layouts, per_device(): segments += [low_y[:, r], now[:, r], high_y[:, r]]  2.63 us
    concatenate x2, local copies, waits for them, and re-layouts, flat_extended(): return jnp.concatenate(segments, axis=-1)  2.6 us
  transfers between devices with their start and end apart: 13, of which 3 were waited for; matrix products, arithmetic and copies ran while one was open for 18% of the time, Pallas kernels for 0%

profile of v8, /device:TPU:0, one launch (start us, length us, event | category | flops | bytes accessed | tf_op | source)
XLA Modules:
  0.0 122.3 jit_solution(15898857701610176381)
XLA Ops:
  0.6 0.7 convert_element_type.23
  1.3 0.7 copy.24
  2.0 0.9 copy.26
  2.9 1.3 %fusion.4 = (f32[1,2,2,64,4,128]{5,4,3,2,1,0:T(4,128)S(1)}, f32[1,2,2,64,4,128]{5,4,3,2,1,0:T(4,128)S(1)}) fusion(f32[2,2,2,64,4,128]{5,4,3,2,1,0:T(4,128)} %param.6), kind=kLoop, calls=%fused_computation.61 | loop fusion | bytes 2097152 | tf_op jit(solution)/shard_map/slice | solution.py:196
  4.3 1.0 fusion.6
  5.4 1.3 %collective-permute-start.1 = (f32[325,3,128]{2,0,1:T(8,128)}, f32[325,3,128]{2,0,1:T(8,128)}, u32[]{:S(2)}, u32[]{:S(2)}) collective-permute-start(f32[325,3,128]{2,0,1:T(8,128)} %get-tuple-element.30), channel_id=1, source_target_pairs={{2,0},{4,2},{6,4},{3,1},{5,3},{7,5},{10,8},{12,10},{14,12},{11,9},... | collective-permute-start | bytes 1497608 | tf_op jit(solution)/shard_map/ppermute | solution.py:39
  6.6 6.3 %collective-permute-start = (f32[325,3,128]{2,0,1:T(8,128)}, f32[325,3,128]{2,0,1:T(8,128)}, u32[]{:S(2)}, u32[]{:S(2)}) collective-permute-start(f32[325,3,128]{2,0,1:T(8,128)} %get-tuple-element.31), channel_id=1, source_target_pairs={{0,2},{2,4},{4,6},{1,3},{3,5},{5,7},{8,10},{10,12},{12,14},{9,11},... | collective-permute-start | bytes 1497608 | tf_op jit(solution)/shard_map/ppermute | solution.py:39
  13.0 0.5 concatenate.38
  13.5 1.4 %fusion.2 = (f32[581,4,3]{2,0,1:T(8,128)S(1)}, f32[581,4,3]{2,0,1:T(8,128)}) fusion(f32[581,4,128]{2,0,1:T(8,128)S(1)} %concatenate.38), kind=kLoop, calls=%fused_computation.59 | loop fusion | bytes 111552 | tf_op jit(solution)/shard_map/slice | solution.py:46
  14.9 1.7 %copy.37 = f32[581,4,3]{0,1,2:T(4,128)S(1)} copy(f32[581,4,3]{2,0,1:T(8,128)} %get-tuple-element.15) | data formatting | bytes 55776 | tf_op jit(solution)/shard_map/slice | solution.py:45
  16.6 1.5 %collective-permute-start.4 = (f32[581,4,3]{0,1,2:T(4,128)S(1)}, f32[581,4,3]{0,1,2:T(4,128)S(1)}, u32[]{:S(2)}, u32[]{:S(2)}) collective-permute-start(f32[581,4,3]{0,1,2:T(4,128)S(1)} %copy.37), channel_id=1, source_target_pairs={{0,1},{2,3},{4,5},{6,7},{8,9},{10,11},{12,13},{14,15},{16,17},{18,... | collective-permute-start | bytes 83672 | tf_op jit(solution)/shard_map/ppermute | solution.py:39
  18.4 1.3 %collective-permute-start.5 = (f32[581,4,3]{0,1,2:T(4,128)S(1)}, f32[581,4,3]{0,1,2:T(4,128)S(1)}, u32[]{:S(2)}, u32[]{:S(2)}) collective-permute-start(f32[581,4,3]{0,1,2:T(4,128)S(1)} %copy.39), channel_id=1, source_target_pairs={{1,0},{3,2},{5,4},{7,6},{9,8},{11,10},{13,12},{15,14},{17,16},{19,... | collective-permute-start | bytes 83672 | tf_op jit(solution)/shard_map/ppermute | solution.py:39
  19.7 1.0 copy.86
  20.8 0.9 slice_bitcast_fusion.8
  21.7 0.5 slice_bitcast_fusion.39
  22.4 0.6 pad_convert_fusion.ins_ref
  23.1 0.7 fusion
  23.9 0.4 copy.40
  24.3 0.9 slice_bitcast_fusion.7
  25.2 1.5 %copy.38 = f32[581,4,3]{2,0,1:T(8,128)} copy(f32[581,4,3]{0,1,2:T(4,128)S(1)} %collective-permute-done.4) | data formatting | bytes 55776 | tf_op jit(solution)/shard_map/ppermute | solution.py:39
  26.7 1.6 %pad_maximum_fusion = f32[256,4,134]{2,0,1:T(8,128)S(1)} fusion(f32[581,4,3]{2,0,1:T(8,128)S(1)} %copy.40, f32[581,4,128]{2,0,1:T(8,128)S(1)} %concatenate.38, f32[581,4,3]{2,0,1:T(8,128)} %copy.38), kind=kLoop, calls=%fused_computation | loop fusion | flops 274432 | bytes 1794528 | tf_op jit(solution)/shard_map/concatenate | solution.py:47
  28.3 0.9 slice_bitcast_fusion.9
  29.2 1.1 constant_dynamic-update-slice_fusion.1
  30.2 1.1 constant_dynamic-update-slice_fusion
  31.6 0.5 copy.29
  32.1 0.5 copy.27
  32.6 3.0 %collective-permute-start.2 = (f32[325,6,3]{0,1,2:T(8,128)S(1)}, f32[325,6,3]{0,1,2:T(8,128)S(1)}, u32[]{:S(2)}, u32[]{:S(2)}) collective-permute-start(f32[325,6,3]{0,1,2:T(8,128)S(1)} %copy.27), channel_id=1, source_target_pairs={{0,1},{2,3},{4,5},{6,7},{8,9},{10,11},{12,13},{14,15},{16,17},{18,... | collective-permute-start | bytes 70208 | tf_op jit(solution)/shard_map/ppermute | solution.py:39
  35.6 1.3 %collective-permute-start.3 = (f32[325,6,3]{0,1,2:T(8,128)S(1)}, f32[325,6,3]{0,1,2:T(8,128)S(1)}, u32[]{:S(2)}, u32[]{:S(2)}) collective-permute-start(f32[325,6,3]{0,1,2:T(8,128)S(1)} %copy.29), channel_id=1, source_target_pairs={{1,0},{3,2},{5,4},{7,6},{9,8},{11,10},{13,12},{15,14},{17,16},{19,... | collective-permute-start | bytes 70208 | tf_op jit(solution)/shard_map/ppermute | solution.py:39
  36.9 1.9 %slice_bitcast_fusion.4 = (f32[325,128]{1,0:T(8,128)}, f32[325,128]{1,0:T(8,128)}, f32[325,128]{1,0:T(8,128)}) fusion(f32[325,3,128]{2,0,1:T(8,128)} %collective-permute-done.1), kind=kLoop, calls=%fused_computation.14 | loop fusion | bytes 998400 | tf_op jit(solution)/shard_map/squeeze | solution.py:222
  38.8 1.9 %slice_bitcast_fusion.19 = (f32[325,128]{1,0:T(8,128)}, f32[325,128]{1,0:T(8,128)}, f32[325,128]{1,0:T(8,128)}) fusion(f32[325,3,128]{2,0,1:T(8,128)} %collective-permute-done), kind=kLoop, calls=%fused_computation.29 | loop fusion | bytes 998400 | tf_op jit(solution)/shard_map/squeeze | solution.py:216
  41.2 0.8 copy.72
  42.1 0.8 copy.70
  42.9 0.8 copy.68
  43.7 0.8 copy.66
  44.5 0.8 copy.73
  45.3 0.8 copy.71
  46.1 0.8 copy.69
  47.0 0.8 copy.67
  47.8 0.8 copy.65
  48.6 0.7 broadcast_in_dim.11
  49.3 4.1 %concatenate.39.frc_ref.pk_ref = f32[325,1408]{1,0:T(8,128)S(1)} concatenate(f32[325,3]{1,0:T(8,128)} %bitcast.132, f32[325,128]{1,0:T(8,128)} %get-tuple-element.37, f32[325,3]{1,0:T(8,128)} %bitcast.127, f32[325,3]{1,0:T(8,128)} %bitcast.131, f32[325,128]{1,0:T(8,128)} %get-tuple-element.36, f32[325,3]{1,0:T(8,128)} %bitcast.126, f32[325,3]{1,0:T(8,128)} %bitcast.130, ...), dimensions={1} | concatenate | bytes 3660800 | tf_op jit(solution)/shard_map/concatenate | solution.py:224
  53.4 0.7 reshape.68.inc_ref
  54.1 0.5 copy-done.3
  54.6 11.5 %shard_map.77 = f32[2,128,512]{2,1,0:T(8,128)} custom-call(s32[2]{0:T(128)} %get-tuple-element.78.order_ref, f32[325,1408]{1,0:T(8,128)} %copy-done.3, f32[325,1408]{1,0:T(8,128)} %copy-done.3, f32[2,2,1408]{2,1,0:T(2,128)} %reshape.68.inc_ref, f32[1,1408]{1,0:T(1,128)} %pad_convert_fusion.ins_ref, bf16[128,512]{1,0:T(8,128)(2,1)} %get-tuple-element.45.bhi_ref, ...), custom_call_target="tpu_custom_call" | custom-call | flops 4429185024 | bytes 2812288 | tf_op jit(solution)/shard_map/pallas_call | solution.py:155
  66.1 1.2 reshape.69
  67.4 3.0 %collective-permute-start.8 = (f32[2,2,4,3]{3,1,0,2:T(2,128)S(1)}, f32[2,2,4,3]{3,1,0,2:T(2,128)S(1)}, u32[]{:S(2)}, u32[]{:S(2)}) collective-permute-start(f32[2,2,4,3]{3,1,0,2:T(2,128)S(1)} %get-tuple-element.76), channel_id=1, source_target_pairs={{0,1},{2,3},{4,5},{6,7},{8,9},{10,11},{12,13},{14,15},{16,17},{18,... | collective-permute-start | bytes 584 | tf_op jit(solution)/shard_map/ppermute | solution.py:39
  70.5 1.3 %collective-permute-start.9 = (f32[2,2,4,3]{3,1,0,2:T(2,128)S(1)}, f32[2,2,4,3]{3,1,0,2:T(2,128)S(1)}, u32[]{:S(2)}, u32[]{:S(2)}) collective-permute-start(f32[2,2,4,3]{3,1,0,2:T(2,128)S(1)} %get-tuple-element.77), channel_id=1, source_target_pairs={{1,0},{3,2},{5,4},{7,6},{9,8},{11,10},{13,12},{15,14},{17,16},{19,... | collective-permute-start | bytes 584 | tf_op jit(solution)/shard_map/ppermute | solution.py:39
  71.9 1.6 %collective-permute-done.9 = f32[2,2,4,3]{3,1,0,2:T(2,128)S(1)} collective-permute-done((f32[2,2,4,3]{3,1,0,2:T(2,128)S(1)}, f32[2,2,4,3]{3,1,0,2:T(2,128)S(1)}, u32[]{:S(2)}, u32[]{:S(2)}) %collective-permute-start.9) | collective-permute-done | bytes 224 | tf_op jit(solution)/shard_map/ppermute | solution.py:39
  73.6 0.7 collective-permute-start.12
  74.3 0.9 slice_bitcast_fusion
  75.4 1.0 copy.60
  76.7 6.6 %collective-permute-start.6 = (f32[256,3,134]{0,2,1:T(8,128)S(1)}, f32[256,3,134]{0,2,1:T(8,128)S(1)}, u32[]{:S(2)}, u32[]{:S(2)}) collective-permute-start(f32[256,3,134]{0,2,1:T(8,128)S(1)} %copy.56), channel_id=1, source_target_pairs={{0,2},{2,4},{4,6},{1,3},{3,5},{5,7},{8,10},{10,12},{12,14},{9,11},... | collective-permute-start | bytes 1234952 | tf_op jit(solution)/shard_map/ppermute | solution.py:39
  83.2 1.3 %collective-permute-start.7 = (f32[256,3,134]{0,2,1:T(8,128)}, f32[256,3,134]{0,2,1:T(8,128)}, u32[]{:S(2)}, u32[]{:S(2)}) collective-permute-start(f32[256,3,134]{0,2,1:T(8,128)} %copy.60), channel_id=1, source_target_pairs={{2,0},{4,2},{6,4},{3,1},{5,3},{7,5},{10,8},{12,10},{14,12},{11,9},... | collective-permute-start | bytes 1234952 | tf_op jit(solution)/shard_map/ppermute | solution.py:39
  84.5 3.5 %collective-permute-start.11 = (f32[2,2,4,134]{3,1,0,2:T(2,128)S(1)}, f32[2,2,4,134]{3,1,0,2:T(2,128)S(1)}, u32[]{:S(2)}, u32[]{:S(2)}) collective-permute-start(f32[2,2,4,134]{3,1,0,2:T(2,128)S(1)} %pad_maximum_fusion.5), channel_id=1, source_target_pairs={{0,8},{2,10},{4,12},{6,14},{8,16},{10,18},{12,20},{14,22},{16,24},... | collective-permute-start | bytes 25736 | tf_op jit(solution)/shard_map/ppermute | solution.py:40
  88.0 6.2 %collective-permute-start.10 = (f32[2,2,3,134]{3,1,0,2:T(2,128)S(1)}, f32[2,2,3,134]{3,1,0,2:T(2,128)S(1)}, u32[]{:S(2)}, u32[]{:S(2)}) collective-permute-start(f32[2,2,3,134]{3,1,0,2:T(2,128)S(1)} %get-tuple-element.65), channel_id=1, source_target_pairs={{0,10},{2,12},{4,14},{8,18},{10,20},{12,22},{16,26},{18,28},{20,30... | collective-permute-start | bytes 19304 | tf_op jit(solution)/shard_map/ppermute | solution.py:40
  94.3 1.2 collective-permute-done.10
  95.5 0.7 concatenate.47.inc_ref
  96.7 7.5 %collective-permute-done.7 = f32[256,3,134]{0,2,1:T(8,128)} collective-permute-done((f32[256,3,134]{0,2,1:T(8,128)}, f32[256,3,134]{0,2,1:T(8,128)}, u32[]{:S(2)}, u32[]{:S(2)}) %collective-permute-start.7) | collective-permute-done | bytes 411680 | tf_op jit(solution)/shard_map/ppermute | solution.py:39
  104.2 1.1 fusion.7
  105.7 1.9 %concatenate.45.frc_ref = f32[256,1408]{1,0:T(8,128)} concatenate(f32[256,134]{1,0:T(8,128)S(1)} %bitcast.117, f32[256,134]{1,0:T(8,128)S(1)} %bitcast.116, f32[256,134]{1,0:T(8,128)S(1)} %bitcast.115, f32[256,134]{1,0:T(8,128)S(1)} %copy-done.6, f32[256,134]{1,0:T(8,128)S(1)} %copy-done.5, f32[256,134]{1,0:T(8,128)S(1)} %copy-done.4, f32[256,134]{1,0:T(8,128)S(1)} %get-tuple-element.18, ...), dimensions={1} | concatenate | bytes 2883584 | tf_op jit(solution)/shard_map/concatenate | solution.py:68
  107.6 11.4 %shard_map.78 = f32[2,128,512]{2,1,0:T(8,128)} custom-call(s32[2]{0:T(128)} %get-tuple-element.79.order_ref, f32[256,1408]{1,0:T(8,128)} %concatenate.45.frc_ref, f32[325,1408]{1,0:T(8,128)} %copy-done.3, f32[2,2,1408]{2,1,0:T(2,128)} %concatenate.47.inc_ref, f32[1,1408]{1,0:T(1,128)} %pad_convert_fusion.ins_ref, ...), custom_call_target="tpu_custom_call" | custom-call | flops 4429185024 | bytes 2423680 | tf_op jit(solution)/shard_map/pallas_call | solution.py:155
  119.0 1.3 %reshape.70 = f32[2,2,64,4,128]{4,3,2,1,0:T(4,128)S(1)} reshape(f32[2,128,512]{2,1,0:T(8,128)} %shard_map.78) | data formatting | bytes 1048576 | tf_op jit(solution)/shard_map/reshape | solution.py:250
  120.5 0.6 slice.385
  121.1 1.2 pad_maximum_fusion.2
  (65 shorter events, 3.5 us)
Async XLA Ops:
  5.4 24.9 %collective-permute-start.1 = (f32[325,3,128]{2,0,1:T(8,128)}, f32[325,3,128]{2,0,1:T(8,128)}, u32[]{:S(2)}, u32[]{:S(2)}) collective-permute-start(f32[325,3,128]{2,0,1:T(8,128)} %get-tuple-element.30), channel_id=1, source_target_pairs={{2,0},{4,2},{6,4},{3,1},{5,3},{7,5},{10,8},{12,10},{14,12},{11,9},... | collective-permute-start | bytes 1497608 | tf_op jit(solution)/shard_map/ppermute | solution.py:39
  6.6 22.5 %collective-permute-start = (f32[325,3,128]{2,0,1:T(8,128)}, f32[325,3,128]{2,0,1:T(8,128)}, u32[]{:S(2)}, u32[]{:S(2)}) collective-permute-start(f32[325,3,128]{2,0,1:T(8,128)} %get-tuple-element.31), channel_id=1, source_target_pairs={{0,2},{2,4},{4,6},{1,3},{3,5},{5,7},{8,10},{10,12},{12,14},{9,11},... | collective-permute-start | bytes 1497608 | tf_op jit(solution)/shard_map/ppermute | solution.py:39
  16.6 8.6 %collective-permute-start.4 = (f32[581,4,3]{0,1,2:T(4,128)S(1)}, f32[581,4,3]{0,1,2:T(4,128)S(1)}, u32[]{:S(2)}, u32[]{:S(2)}) collective-permute-start(f32[581,4,3]{0,1,2:T(4,128)S(1)} %copy.37), channel_id=1, source_target_pairs={{0,1},{2,3},{4,5},{6,7},{8,9},{10,11},{12,13},{14,15},{16,17},{18,... | collective-permute-start | bytes 83672 | tf_op jit(solution)/shard_map/ppermute | solution.py:39
  18.4 5.4 %collective-permute-start.5 = (f32[581,4,3]{0,1,2:T(4,128)S(1)}, f32[581,4,3]{0,1,2:T(4,128)S(1)}, u32[]{:S(2)}, u32[]{:S(2)}) collective-permute-start(f32[581,4,3]{0,1,2:T(4,128)S(1)} %copy.39), channel_id=1, source_target_pairs={{1,0},{3,2},{5,4},{7,6},{9,8},{11,10},{13,12},{15,14},{17,16},{19,... | collective-permute-start | bytes 83672 | tf_op jit(solution)/shard_map/ppermute | solution.py:39
  20.7 0.9 copy-start.7
  26.6 1.6 %copy-start = (f32[581,4,3]{2,0,1:T(8,128)S(1)}, f32[581,4,3]{2,0,1:T(8,128)}, u32[]{:S(2)}) copy-start(f32[581,4,3]{2,0,1:T(8,128)} %copy.38) | copy-start | bytes 83668
  32.6 8.3 %collective-permute-start.2 = (f32[325,6,3]{0,1,2:T(8,128)S(1)}, f32[325,6,3]{0,1,2:T(8,128)S(1)}, u32[]{:S(2)}, u32[]{:S(2)}) collective-permute-start(f32[325,6,3]{0,1,2:T(8,128)S(1)} %copy.27), channel_id=1, source_target_pairs={{0,1},{2,3},{4,5},{6,7},{8,9},{10,11},{12,13},{14,15},{16,17},{18,... | collective-permute-start | bytes 70208 | tf_op jit(solution)/shard_map/ppermute | solution.py:39
  35.6 5.1 %collective-permute-start.3 = (f32[325,6,3]{0,1,2:T(8,128)S(1)}, f32[325,6,3]{0,1,2:T(8,128)S(1)}, u32[]{:S(2)}, u32[]{:S(2)}) collective-permute-start(f32[325,6,3]{0,1,2:T(8,128)S(1)} %copy.29), channel_id=1, source_target_pairs={{1,0},{3,2},{5,4},{7,6},{9,8},{11,10},{13,12},{15,14},{17,16},{19,... | collective-permute-start | bytes 70208 | tf_op jit(solution)/shard_map/ppermute | solution.py:39
  53.4 1.3 %copy-start.3 = (f32[325,1408]{1,0:T(8,128)}, f32[325,1408]{1,0:T(8,128)S(1)}, u32[]{:S(2)}) copy-start(f32[325,1408]{1,0:T(8,128)S(1)} %concatenate.39.frc_ref.pk_ref) | copy-start | bytes 5491204
  67.4 4.5 %collective-permute-start.8 = (f32[2,2,4,3]{3,1,0,2:T(2,128)S(1)}, f32[2,2,4,3]{3,1,0,2:T(2,128)S(1)}, u32[]{:S(2)}, u32[]{:S(2)}) collective-permute-start(f32[2,2,4,3]{3,1,0,2:T(2,128)S(1)} %get-tuple-element.76), channel_id=1, source_target_pairs={{0,1},{2,3},{4,5},{6,7},{8,9},{10,11},{12,13},{14,15},{16,17},{18,... | collective-permute-start | bytes 584 | tf_op jit(solution)/shard_map/ppermute | solution.py:39
  70.5 3.1 %collective-permute-start.9 = (f32[2,2,4,3]{3,1,0,2:T(2,128)S(1)}, f32[2,2,4,3]{3,1,0,2:T(2,128)S(1)}, u32[]{:S(2)}, u32[]{:S(2)}) collective-permute-start(f32[2,2,4,3]{3,1,0,2:T(2,128)S(1)} %get-tuple-element.77), channel_id=1, source_target_pairs={{1,0},{3,2},{5,4},{7,6},{9,8},{11,10},{13,12},{15,14},{17,16},{19,... | collective-permute-start | bytes 584 | tf_op jit(solution)/shard_map/ppermute | solution.py:39
  71.9 3.3 %copy-start.1 = (f32[2,128,512]{2,1,0:T(8,128)S(1)}, f32[2,128,512]{2,1,0:T(8,128)}, u32[]{:S(2)}) copy-start(f32[2,128,512]{2,1,0:T(8,128)} %shard_map.77) | copy-start | bytes 1572868
  73.6 20.6 %collective-permute-start.12 = (f32[2,2,3,134]{3,1,0,2:T(2,128)S(1)}, f32[2,2,3,134]{3,1,0,2:T(2,128)S(1)}, u32[]{:S(2)}, u32[]{:S(2)}) collective-permute-start(f32[2,2,3,134]{3,1,0,2:T(2,128)S(1)} %get-tuple-element.64), channel_id=1, source_target_pairs={{2,8},{4,10},{6,12},{10,16},{12,18},{14,20},{18,24},{20,26},{22,28... | collective-permute-start | bytes 19304 | tf_op jit(solution)/shard_map/ppermute | solution.py:40
  76.7 19.6 %collective-permute-start.6 = (f32[256,3,134]{0,2,1:T(8,128)S(1)}, f32[256,3,134]{0,2,1:T(8,128)S(1)}, u32[]{:S(2)}, u32[]{:S(2)}) collective-permute-start(f32[256,3,134]{0,2,1:T(8,128)S(1)} %copy.56), channel_id=1, source_target_pairs={{0,2},{2,4},{4,6},{1,3},{3,5},{5,7},{8,10},{10,12},{12,14},{9,11},... | collective-permute-start | bytes 1234952 | tf_op jit(solution)/shard_map/ppermute | solution.py:39
  83.2 20.9 %collective-permute-start.7 = (f32[256,3,134]{0,2,1:T(8,128)}, f32[256,3,134]{0,2,1:T(8,128)}, u32[]{:S(2)}, u32[]{:S(2)}) collective-permute-start(f32[256,3,134]{0,2,1:T(8,128)} %copy.60), channel_id=1, source_target_pairs={{2,0},{4,2},{6,4},{3,1},{5,3},{7,5},{10,8},{12,10},{14,12},{11,9},... | collective-permute-start | bytes 1234952 | tf_op jit(solution)/shard_map/ppermute | solution.py:39
  84.5 10.9 %collective-permute-start.11 = (f32[2,2,4,134]{3,1,0,2:T(2,128)S(1)}, f32[2,2,4,134]{3,1,0,2:T(2,128)S(1)}, u32[]{:S(2)}, u32[]{:S(2)}) collective-permute-start(f32[2,2,4,134]{3,1,0,2:T(2,128)S(1)} %pad_maximum_fusion.5), channel_id=1, source_target_pairs={{0,8},{2,10},{4,12},{6,14},{8,16},{10,18},{12,20},{14,22},{16,24},... | collective-permute-start | bytes 25736 | tf_op jit(solution)/shard_map/ppermute | solution.py:40
  88.0 7.4 %collective-permute-start.10 = (f32[2,2,3,134]{3,1,0,2:T(2,128)S(1)}, f32[2,2,3,134]{3,1,0,2:T(2,128)S(1)}, u32[]{:S(2)}, u32[]{:S(2)}) collective-permute-start(f32[2,2,3,134]{3,1,0,2:T(2,128)S(1)} %get-tuple-element.65), channel_id=1, source_target_pairs={{0,10},{2,12},{4,14},{8,18},{10,20},{12,22},{16,26},{18,28},{20,30... | collective-permute-start | bytes 19304 | tf_op jit(solution)/shard_map/ppermute | solution.py:40
  96.7 9.0 %copy-start.4 = (f32[256,134]{1,0:T(8,128)S(1)}, f32[256,134]{1,0:T(8,128)}, u32[]{:S(2)}) copy-start(f32[256,134]{1,0:T(8,128)} %get-tuple-element.19) | copy-start | bytes 411652
  96.7 9.0 %copy-start.5 = (f32[256,134]{1,0:T(8,128)S(1)}, f32[256,134]{1,0:T(8,128)}, u32[]{:S(2)}) copy-start(f32[256,134]{1,0:T(8,128)} %get-tuple-element.20) | copy-start | bytes 411652
  96.7 9.0 %copy-start.6 = (f32[256,134]{1,0:T(8,128)S(1)}, f32[256,134]{1,0:T(8,128)}, u32[]{:S(2)}) copy-start(f32[256,134]{1,0:T(8,128)} %get-tuple-element.21) | copy-start | bytes 411652
  119.0 1.3 %copy-start.2 = (f32[2,128,512]{2,1,0:T(8,128)S(1)}, f32[2,128,512]{2,1,0:T(8,128)}, u32[]{:S(2)}) copy-start(f32[2,128,512]{2,1,0:T(8,128)} %shard_map.78) | copy-start | bytes 1572868

commit v9 on v8

--- a/solution.py
+++ b/solution.py
@@ -205,21 +205,18 @@
         widened[rows_now + (t - 1) * per_tick.shape[1] : rows_now + t * per_tick.shape[1]]
         for t in range(1, ticks)
     ]
-    low_y = widened[:rows_now, :, :width]
-    high_y = widened[:rows_now, :, width + ny :]
     rims = jnp.concatenate([low_x, high_x], axis=1)
     corner_low = fetch(rims[..., ny - width :], ("ty",), (-1,))
     corner_high = fetch(rims[..., :width], ("ty",), (1,))
+    rims = jnp.concatenate([corner_low, rims, corner_high], axis=-1)
     segments = []
     for ix in range(ex):
         if ix < width:
-            segments += [corner_low[:, ix], low_x[:, ix], corner_high[:, ix]]
+            segments.append(rims[:, ix])
         elif ix < width + nx:
-            r = ix - width
-            segments += [low_y[:, r], now[:, r], high_y[:, r]]
+            segments.append(widened[:rows_now, ix - width])
         else:
-            r = ix - width - nx
-            segments += [corner_low[:, width + r], high_x[:, r], corner_high[:, width + r]]
+            segments.append(rims[:, ix - nx])
     segments.append(jnp.zeros((rows_now, padded - cols), jnp.float32))
     packed = jnp.concatenate(segments, axis=-1)
     first_pending = nsrc * two * depth + depth

time: 123 us -> 121 us (0.984)
  local copies, waits for them, and re-layouts: 45.5 us -> 35.8 us
  other arithmetic: 5.21 us -> 10.2 us
  starting transfers between devices: 37.2 us -> 39.1 us
    unnamed x39 -> x43, local copies, waits for them, and re-layouts: 12.8 us -> 4.14 us
    squeeze x5 -> x1, local copies, waits for them, and re-layouts: 6.41 us -> 1.11 us  [per_device(): segments.append(rims[:, ix - nx])]
    squeeze x0 -> x1, other arithmetic: none -> 2.81 us  [per_device(): segments.append(widened[:rows_now, ix - width])]
    slice x1 -> x2, local copies, waits for them, and re-layouts: 0.48 us -> 2.96 us  [per_device(): corner_low = fetch(rims[..., ny - width:], ('ty',), (-1,))]
    concatenate x0 -> x1, other arithmetic: none -> 2.05 us  [per_device(): rims = jnp.concatenate([corner_low, rims, corner_high], axis=-1)]
    ppermute x2 -> x4, local copies, waits for them, and re-layouts: 1.88 us -> 3.52 us  [fetch(): return lax.ppermute(block, axes[0], pairs)]
    ppermute x3, starting transfers between devices: 10.4 us -> 12 us  [fetch(): return lax.ppermute(block, tuple(axes), pairs)]
  transfers between devices with their start and end apart: 13 -> 13, of which waited for: 3 -> 3; matrix products, arithmetic and copies ran while one was open for 18% -> 15% of each run, Pallas kernels for 0% -> 0%
where the time goes in v9:
time: 121 us; the launch traced here: 120 us
  starting transfers between devices  39.1 us (32%)
  local copies, waits for them, and re-layouts  35.8 us (30%)
  Pallas kernels  22.9 us (19%)
  waiting for transfers between devices  10.3 us (9%)
  other arithmetic  10.2 us (8%)
  between operations  1.26 us (1%)
    ppermute x10, starting transfers between devices, fetch(): return lax.ppermute(block, axes[0], pairs)  27.1 us
    pallas_call x2, Pallas kernels, run_tick(): pl.pallas_call(functools.partial(tick_kernel, row=row, depth=depth, width...  22.9 us
    ppermute x3, starting transfers between devices, fetch(): return lax.ppermute(block, tuple(axes), pairs)  12 us
    ppermute x10, waiting for transfers between devices, fetch(): return lax.ppermute(block, axes[0], pairs)  9.64 us
    unnamed x43, local copies, waits for them, and re-layouts  4.14 us
    concatenate x1, local copies, waits for them, and re-layouts, per_device(): packed = jnp.concatenate(segments, axis=-1)  3.93 us
    ppermute x4, local copies, waits for them, and re-layouts, fetch(): return lax.ppermute(block, axes[0], pairs)  3.52 us
    slice x2, local copies, waits for them, and re-layouts, per_device(): corner_low = fetch(rims[..., ny - width:], ('ty',), (-1,))  2.96 us
  transfers between devices with their start and end apart: 13, of which 3 were waited for; matrix products, arithmetic and copies ran while one was open for 15% of the time, Pallas kernels for 0%

profile of v9, /device:TPU:0, one launch (start us, length us, event | category | flops | bytes accessed | tf_op | source)
XLA Modules:
  0.0 119.6 jit_solution(9390657664912627941)
XLA Ops:
  0.6 0.7 convert_element_type.23
  1.3 0.7 copy.24
  2.0 0.9 copy.26
  2.9 1.3 %fusion.4 = (f32[1,2,2,64,4,128]{5,4,3,2,1,0:T(4,128)S(1)}, f32[1,2,2,64,4,128]{5,4,3,2,1,0:T(4,128)S(1)}) fusion(f32[2,2,2,64,4,128]{5,4,3,2,1,0:T(4,128)} %param.6), kind=kLoop, calls=%fused_computation.54 | loop fusion | bytes 2097152 | tf_op jit(solution)/shard_map/slice | solution.py:196
  4.3 0.8 fusion.6
  5.2 1.3 %collective-permute-start.1 = (f32[325,3,128]{2,0,1:T(8,128)}, f32[325,3,128]{2,0,1:T(8,128)}, u32[]{:S(2)}, u32[]{:S(2)}) collective-permute-start(f32[325,3,128]{2,0,1:T(8,128)} %get-tuple-element.28), channel_id=1, source_target_pairs={{2,0},{4,2},{6,4},{3,1},{5,3},{7,5},{10,8},{12,10},{14,12},{11,9},... | collective-permute-start | bytes 1497608 | tf_op jit(solution)/shard_map/ppermute | solution.py:39
  6.5 6.3 %collective-permute-start = (f32[325,3,128]{2,0,1:T(8,128)S(1)}, f32[325,3,128]{2,0,1:T(8,128)}, u32[]{:S(2)}, u32[]{:S(2)}) collective-permute-start(f32[325,3,128]{2,0,1:T(8,128)S(1)} %get-tuple-element.29), channel_id=1, source_target_pairs={{0,2},{2,4},{4,6},{1,3},{3,5},{5,7},{8,10},{10,12},{12,14},{9,11},... | collective-permute-start | bytes 1497608 | tf_op jit(solution)/shard_map/ppermute | solution.py:39
  12.8 0.5 concatenate.42
  13.3 1.4 %fusion.2 = (f32[581,4,3]{2,0,1:T(8,128)S(1)}, f32[581,4,3]{2,0,1:T(8,128)}) fusion(f32[581,4,128]{2,0,1:T(8,128)S(1)} %concatenate.42), kind=kLoop, calls=%fused_computation.52 | loop fusion | bytes 111552 | tf_op jit(solution)/shard_map/slice | solution.py:45
  14.8 1.7 %copy.34 = f32[581,4,3]{0,1,2:T(4,128)S(1)} copy(f32[581,4,3]{2,0,1:T(8,128)} %get-tuple-element.17) | data formatting | bytes 55776 | tf_op jit(solution)/shard_map/slice | solution.py:46
  16.5 1.3 %collective-permute-start.5 = (f32[581,4,3]{0,1,2:T(4,128)S(1)}, f32[581,4,3]{0,1,2:T(4,128)S(1)}, u32[]{:S(2)}, u32[]{:S(2)}) collective-permute-start(f32[581,4,3]{0,1,2:T(4,128)S(1)} %copy.34), channel_id=1, source_target_pairs={{1,0},{3,2},{5,4},{7,6},{9,8},{11,10},{13,12},{15,14},{17,16},{19,... | collective-permute-start | bytes 83672 | tf_op jit(solution)/shard_map/ppermute | solution.py:39
  17.8 0.4 copy.33
  18.2 3.0 %collective-permute-start.4 = (f32[581,4,3]{0,1,2:T(4,128)S(1)}, f32[581,4,3]{0,1,2:T(4,128)S(1)}, u32[]{:S(2)}, u32[]{:S(2)}) collective-permute-start(f32[581,4,3]{0,1,2:T(4,128)S(1)} %copy.33), channel_id=1, source_target_pairs={{0,1},{2,3},{4,5},{6,7},{8,9},{10,11},{12,13},{14,15},{16,17},{18,... | collective-permute-start | bytes 83672 | tf_op jit(solution)/shard_map/ppermute | solution.py:39
  21.5 0.1 maximum_maximum_fusion
  21.7 0.6 pad_convert_fusion.ins_ref
  22.3 0.6 slice_bitcast_fusion.27
  22.9 0.8 fusion
  23.6 0.4 copy.35
  24.1 1.5 %copy.36 = f32[581,4,3]{2,0,1:T(8,128)} copy(f32[581,4,3]{0,1,2:T(4,128)S(1)} %collective-permute-done.5) | data formatting | bytes 55776 | tf_op jit(solution)/shard_map/ppermute | solution.py:39
  25.5 2.8 %maximum_bitcast_fusion = (f32[325,134]{1,0:T(8,128)}, f32[325,134]{1,0:T(8,128)}, f32[325,134]{1,0:T(8,128)}, f32[325,134]{1,0:T(8,128)}) fusion(f32[581,4,3]{2,0,1:T(8,128)} %copy.36, f32[581,4,128]{2,0,1:T(8,128)S(1)} %concatenate.42, f32[581,4,3]{2,0,1:T(8,128)S(1)} %copy.35), kind=kLoop, calls=%fused_computation.10 | loop fusion | flops 348400 | bytes 1942464 | tf_op jit(solution)/shard_map/squeeze | solution.py:217
  28.3 1.1 constant_dynamic-update-slice_fusion.1
  29.4 1.1 constant_dynamic-update-slice_fusion
  30.5 1.3 %fusion.5 = (f32[325,6,3]{2,0,1:T(8,128)}, f32[325,6,3]{2,0,1:T(8,128)S(1)}) fusion(f32[325,6,128]{2,0,1:T(8,128)S(1)} %constant_dynamic-update-slice_fusion), kind=kLoop, calls=%fused_computation.55 | loop fusion | bytes 93600 | tf_op jit(solution)/shard_map/slice | solution.py:209
  31.8 1.7 %copy.27 = f32[325,6,3]{0,1,2:T(8,128)S(1)} copy(f32[325,6,3]{2,0,1:T(8,128)} %get-tuple-element.26) | data formatting | bytes 46800 | tf_op jit(solution)/shard_map/slice | solution.py:209
  33.5 0.5 copy.28
  33.9 1.3 %collective-permute-start.3 = (f32[325,6,3]{0,1,2:T(8,128)S(1)}, f32[325,6,3]{0,1,2:T(8,128)S(1)}, u32[]{:S(2)}, u32[]{:S(2)}) collective-permute-start(f32[325,6,3]{0,1,2:T(8,128)S(1)} %copy.28), channel_id=1, source_target_pairs={{1,0},{3,2},{5,4},{7,6},{9,8},{11,10},{13,12},{15,14},{17,16},{19,... | collective-permute-start | bytes 70208 | tf_op jit(solution)/shard_map/ppermute | solution.py:39
  35.2 3.0 %collective-permute-start.2 = (f32[325,6,3]{0,1,2:T(8,128)S(1)}, f32[325,6,3]{0,1,2:T(8,128)S(1)}, u32[]{:S(2)}, u32[]{:S(2)}) collective-permute-start(f32[325,6,3]{0,1,2:T(8,128)S(1)} %copy.27), channel_id=1, source_target_pairs={{0,1},{2,3},{4,5},{6,7},{8,9},{10,11},{12,13},{14,15},{16,17},{18,... | collective-permute-start | bytes 70208 | tf_op jit(solution)/shard_map/ppermute | solution.py:39
  38.3 1.7 %pad_maximum_fusion.1 = f32[256,4,134]{2,0,1:T(8,128)S(1)} fusion(f32[581,4,3]{2,0,1:T(8,128)} %copy.36, f32[581,4,128]{2,0,1:T(8,128)S(1)} %concatenate.42, f32[581,4,3]{2,0,1:T(8,128)} %copy-done), kind=kLoop, calls=%fused_computation.1 | loop fusion | flops 274432 | bytes 1794528 | tf_op jit(solution)/shard_map/concatenate | solution.py:47
  40.0 0.3 copy.29
  40.4 1.3 %copy.30 = f32[325,6,3]{2,0,1:T(8,128)} copy(f32[325,6,3]{0,1,2:T(8,128)S(1)} %collective-permute-done.3) | data formatting | bytes 46800 | tf_op jit(solution)/shard_map/ppermute | solution.py:39
  41.7 2.1 %pad_maximum_fusion = f32[325,6,134]{2,0,1:T(8,128)S(1)} fusion(f32[325,6,3]{2,0,1:T(8,128)} %copy.30, f32[325,6,128]{2,0,1:T(8,128)S(1)} %constant_dynamic-update-slice_fusion, f32[325,6,3]{2,0,1:T(8,128)S(1)} %copy.29), kind=kLoop, calls=%fused_computation | loop fusion | flops 522600 | bytes 2090400 | tf_op jit(solution)/shard_map/concatenate | solution.py:211
  43.8 1.1 slice_bitcast_fusion
  44.9 0.2 copy-done.4
  45.1 0.3 copy-done.5
  45.5 3.9 %concatenate.44.frc_ref.pk_ref = f32[325,1408]{1,0:T(8,128)} concatenate(f32[325,134]{1,0:T(8,128)} %get-tuple-element.15, f32[325,134]{1,0:T(8,128)} %get-tuple-element.14, f32[325,134]{1,0:T(8,128)} %get-tuple-element.13, f32[325,134]{1,0:T(8,128)S(1)} %copy-done.6, f32[325,134]{1,0:T(8,128)S(1)} %copy-done.5, f32[325,134]{1,0:T(8,128)S(1)} %copy-done.4, ...), dimensions={1} | concatenate | bytes 3660800 | tf_op jit(solution)/shard_map/concatenate | solution.py:221
  49.4 0.8 slice.243
  50.2 0.6 reshape.68.inc_ref
  50.9 11.5 %shard_map.77 = f32[2,128,512]{2,1,0:T(8,128)} custom-call(s32[2]{0:T(128)} %get-tuple-element.58.order_ref, f32[325,1408]{1,0:T(8,128)} %concatenate.44.frc_ref.pk_ref, f32[325,1408]{1,0:T(8,128)} %concatenate.44.frc_ref.pk_ref, f32[2,2,1408]{2,1,0:T(2,128)} %reshape.68.inc_ref, f32[1,1408]{1,0:T(1,128)} %pad_convert_fusion.ins_ref, ...), custom_call_target="tpu_custom_call" | custom-call | flops 4429185024 | bytes 2812288 | tf_op jit(solution)/shard_map/pallas_call | solution.py:155
  62.4 1.2 %reshape.69 = f32[2,2,64,4,128]{4,3,2,1,0:T(4,128)S(1)} reshape(f32[2,128,512]{2,1,0:T(8,128)} %shard_map.77) | data formatting | bytes 1048576 | tf_op jit(solution)/shard_map/reshape | solution.py:247
  63.7 1.4 %collective-permute-start.8 = (f32[2,2,4,3]{3,1,0,2:T(2,128)S(1)}, f32[2,2,4,3]{3,1,0,2:T(2,128)S(1)}, u32[]{:S(2)}, u32[]{:S(2)}) collective-permute-start(f32[2,2,4,3]{3,1,0,2:T(2,128)S(1)} %get-tuple-element.56), channel_id=1, source_target_pairs={{0,1},{2,3},{4,5},{6,7},{8,9},{10,11},{12,13},{14,15},{16,17},{18,... | collective-permute-start | bytes 584 | tf_op jit(solution)/shard_map/ppermute | solution.py:39
  65.1 1.3 %collective-permute-start.9 = (f32[2,2,4,3]{3,1,0,2:T(2,128)S(1)}, f32[2,2,4,3]{3,1,0,2:T(2,128)S(1)}, u32[]{:S(2)}, u32[]{:S(2)}) collective-permute-start(f32[2,2,4,3]{3,1,0,2:T(2,128)S(1)} %get-tuple-element.57), channel_id=1, source_target_pairs={{1,0},{3,2},{5,4},{7,6},{9,8},{11,10},{13,12},{15,14},{17,16},{19,... | collective-permute-start | bytes 584 | tf_op jit(solution)/shard_map/ppermute | solution.py:39
  66.4 0.1 fusion.3
  66.5 1.6 %collective-permute-done.9 = f32[2,2,4,3]{3,1,0,2:T(2,128)S(1)} collective-permute-done((f32[2,2,4,3]{3,1,0,2:T(2,128)S(1)}, f32[2,2,4,3]{3,1,0,2:T(2,128)S(1)}, u32[]{:S(2)}, u32[]{:S(2)}) %collective-permute-start.9) | collective-permute-done | bytes 224 | tf_op jit(solution)/shard_map/ppermute | solution.py:39
  68.2 0.6 fusion.9
  68.8 1.2 %collective-permute-start.12 = (f32[2,2,3,134]{3,1,0,2:T(2,128)}, f32[2,2,3,134]{3,1,0,2:T(2,128)}, u32[]{:S(2)}, u32[]{:S(2)}) collective-permute-start(f32[2,2,3,134]{3,1,0,2:T(2,128)} %get-tuple-element.44), channel_id=1, source_target_pairs={{2,8},{4,10},{6,12},{10,16},{12,18},{14,20},{18,24},{20,26},{22,28... | collective-permute-start | bytes 19304 | tf_op jit(solution)/shard_map/ppermute | solution.py:40
  70.1 1.0 slice_bitcast_fusion.6
  71.1 0.2 stack_reshape.6
  71.3 0.2 copy.42
  71.5 0.2 copy.38
  71.8 6.9 %collective-permute-start.6 = (f32[256,3,134]{0,2,1:T(8,128)S(1)}, f32[256,3,134]{0,2,1:T(8,128)S(1)}, u32[]{:S(2)}, u32[]{:S(2)}) collective-permute-start(f32[256,3,134]{0,2,1:T(8,128)S(1)} %copy.38), channel_id=1, source_target_pairs={{0,2},{2,4},{4,6},{1,3},{3,5},{5,7},{8,10},{10,12},{12,14},{9,11},... | collective-permute-start | bytes 1234952 | tf_op jit(solution)/shard_map/ppermute | solution.py:39
  78.7 1.3 %collective-permute-start.7 = (f32[256,3,134]{0,2,1:T(8,128)S(1)}, f32[256,3,134]{0,2,1:T(8,128)}, u32[]{:S(2)}, u32[]{:S(2)}) collective-permute-start(f32[256,3,134]{0,2,1:T(8,128)S(1)} %copy.42), channel_id=1, source_target_pairs={{2,0},{4,2},{6,4},{3,1},{5,3},{7,5},{10,8},{12,10},{14,12},{11,9},... | collective-permute-start | bytes 1234952 | tf_op jit(solution)/shard_map/ppermute | solution.py:39
  80.0 3.3 %collective-permute-start.11 = (f32[2,2,4,134]{3,1,0,2:T(2,128)S(1)}, f32[2,2,4,134]{3,1,0,2:T(2,128)S(1)}, u32[]{:S(2)}, u32[]{:S(2)}) collective-permute-start(f32[2,2,4,134]{3,1,0,2:T(2,128)S(1)} %copy-done.13), channel_id=1, source_target_pairs={{0,8},{2,10},{4,12},{6,14},{8,16},{10,18},{12,20},{14,22},{16,24},... | collective-permute-start | bytes 25736 | tf_op jit(solution)/shard_map/ppermute | solution.py:40
  83.3 7.4 %collective-permute-start.10 = (f32[2,2,3,134]{3,1,0,2:T(2,128)S(1)}, f32[2,2,3,134]{3,1,0,2:T(2,128)S(1)}, u32[]{:S(2)}, u32[]{:S(2)}) collective-permute-start(f32[2,2,3,134]{3,1,0,2:T(2,128)S(1)} %copy-done.14), channel_id=1, source_target_pairs={{0,10},{2,12},{4,14},{8,18},{10,20},{12,22},{16,26},{18,28},{20,30... | collective-permute-start | bytes 19304 | tf_op jit(solution)/shard_map/ppermute | solution.py:40
  90.8 0.7 slice_bitcast_fusion.16
  91.5 0.7 collective-permute-done.10
  92.2 0.7 concatenate.51.inc_ref
  93.4 8.0 %collective-permute-done.7 = f32[256,3,134]{0,2,1:T(8,128)} collective-permute-done((f32[256,3,134]{0,2,1:T(8,128)S(1)}, f32[256,3,134]{0,2,1:T(8,128)}, u32[]{:S(2)}, u32[]{:S(2)}) %collective-permute-start.7) | collective-permute-done | bytes 411680 | tf_op jit(solution)/shard_map/ppermute | solution.py:39
  101.4 1.1 fusion.7
  103.0 1.9 %concatenate.49.frc_ref = f32[256,1408]{1,0:T(8,128)} concatenate(f32[256,134]{1,0:T(8,128)S(1)} %bitcast.89, f32[256,134]{1,0:T(8,128)S(1)} %bitcast.88, f32[256,134]{1,0:T(8,128)S(1)} %bitcast.87, f32[256,134]{1,0:T(8,128)S(1)} %copy-done.10, f32[256,134]{1,0:T(8,128)S(1)} %copy-done.9, f32[256,134]{1,0:T(8,128)S(1)} %copy-done.8, f32[256,134]{1,0:T(8,128)S(1)} %copy-done.7, ...), dimensions={1} | concatenate | bytes 2883584 | tf_op jit(solution)/shard_map/concatenate | solution.py:68
  104.9 11.4 %shard_map.78 = f32[2,128,512]{2,1,0:T(8,128)} custom-call(s32[2]{0:T(128)} %get-tuple-element.59.order_ref, f32[256,1408]{1,0:T(8,128)} %concatenate.49.frc_ref, f32[325,1408]{1,0:T(8,128)} %concatenate.44.frc_ref.pk_ref, f32[2,2,1408]{2,1,0:T(2,128)} %concatenate.51.inc_ref, f32[1,1408]{1,0:T(1,128)} %pad_convert_fusion.ins_ref, ...), custom_call_target="tpu_custom_call" | custom-call | flops 4429185024 | bytes 2423680 | tf_op jit(solution)/shard_map/pallas_call | solution.py:155
  116.3 1.3 %reshape.70 = f32[2,2,64,4,128]{4,3,2,1,0:T(4,128)S(1)} reshape(f32[2,128,512]{2,1,0:T(8,128)} %shard_map.78) | data formatting | bytes 1048576 | tf_op jit(solution)/shard_map/reshape | solution.py:247
  117.6 0.2 stack_reshape.7
  117.8 0.6 slice.271
  118.4 1.2 %pad_maximum_fusion.3 = f32[2,2,2,64,4,128]{5,4,3,2,1,0:T(4,128)} fusion(f32[1,2,2,64,4,128]{5,4,3,2,1,0:T(4,128)S(1)} %stack_reshape.7, f32[1,2,2,64,4,128]{5,4,3,2,1,0:T(4,128)S(1)} %stack_reshape.6), kind=kLoop, calls=%fused_computation.3 | loop fusion | flops 262144 | bytes 2097152 | tf_op jit(solution)/shard_map/stack | solution.py:252
  (67 shorter events, 1.6 us)
Async XLA Ops:
  5.2 24.2 %collective-permute-start.1 = (f32[325,3,128]{2,0,1:T(8,128)}, f32[325,3,128]{2,0,1:T(8,128)}, u32[]{:S(2)}, u32[]{:S(2)}) collective-permute-start(f32[325,3,128]{2,0,1:T(8,128)} %get-tuple-element.28), channel_id=1, source_target_pairs={{2,0},{4,2},{6,4},{3,1},{5,3},{7,5},{10,8},{12,10},{14,12},{11,9},... | collective-permute-start | bytes 1497608 | tf_op jit(solution)/shard_map/ppermute | solution.py:39
  6.5 21.9 %collective-permute-start = (f32[325,3,128]{2,0,1:T(8,128)S(1)}, f32[325,3,128]{2,0,1:T(8,128)}, u32[]{:S(2)}, u32[]{:S(2)}) collective-permute-start(f32[325,3,128]{2,0,1:T(8,128)S(1)} %get-tuple-element.29), channel_id=1, source_target_pairs={{0,2},{2,4},{4,6},{1,3},{3,5},{5,7},{8,10},{10,12},{12,14},{9,11},... | collective-permute-start | bytes 1497608 | tf_op jit(solution)/shard_map/ppermute | solution.py:39
  14.8 6.5 %copy-start.11 = (f32[1,4,2,64,64]{4,3,2,1,0:T(8,128)S(1)}, f32[1,4,2,64,64]{4,3,2,1,0:T(8,128)}, u32[]{:S(2)}) copy-start(f32[1,4,2,64,64]{4,3,2,1,0:T(8,128)} %param.8) | copy-start | bytes 393220
  16.5 7.6 %collective-permute-start.5 = (f32[581,4,3]{0,1,2:T(4,128)S(1)}, f32[581,4,3]{0,1,2:T(4,128)S(1)}, u32[]{:S(2)}, u32[]{:S(2)}) collective-permute-start(f32[581,4,3]{0,1,2:T(4,128)S(1)} %copy.34), channel_id=1, source_target_pairs={{1,0},{3,2},{5,4},{7,6},{9,8},{11,10},{13,12},{15,14},{17,16},{19,... | collective-permute-start | bytes 83672 | tf_op jit(solution)/shard_map/ppermute | solution.py:39
  18.2 5.5 %collective-permute-start.4 = (f32[581,4,3]{0,1,2:T(4,128)S(1)}, f32[581,4,3]{0,1,2:T(4,128)S(1)}, u32[]{:S(2)}, u32[]{:S(2)}) collective-permute-start(f32[581,4,3]{0,1,2:T(4,128)S(1)} %copy.33), channel_id=1, source_target_pairs={{0,1},{2,3},{4,5},{6,7},{8,9},{10,11},{12,13},{14,15},{16,17},{18,... | collective-permute-start | bytes 83672 | tf_op jit(solution)/shard_map/ppermute | solution.py:39
  21.2 1.1 copy-start.15
  24.1 4.3 %copy-start = (f32[581,4,3]{2,0,1:T(8,128)}, f32[581,4,3]{2,0,1:T(8,128)S(1)}, u32[]{:S(2)}) copy-start(f32[581,4,3]{2,0,1:T(8,128)S(1)} %copy.35) | copy-start | bytes 83668
  33.9 6.4 %collective-permute-start.3 = (f32[325,6,3]{0,1,2:T(8,128)S(1)}, f32[325,6,3]{0,1,2:T(8,128)S(1)}, u32[]{:S(2)}, u32[]{:S(2)}) collective-permute-start(f32[325,6,3]{0,1,2:T(8,128)S(1)} %copy.28), channel_id=1, source_target_pairs={{1,0},{3,2},{5,4},{7,6},{9,8},{11,10},{13,12},{15,14},{17,16},{19,... | collective-permute-start | bytes 70208 | tf_op jit(solution)/shard_map/ppermute | solution.py:39
  35.2 4.7 %collective-permute-start.2 = (f32[325,6,3]{0,1,2:T(8,128)S(1)}, f32[325,6,3]{0,1,2:T(8,128)S(1)}, u32[]{:S(2)}, u32[]{:S(2)}) collective-permute-start(f32[325,6,3]{0,1,2:T(8,128)S(1)} %copy.27), channel_id=1, source_target_pairs={{0,1},{2,3},{4,5},{6,7},{8,9},{10,11},{12,13},{14,15},{16,17},{18,... | collective-permute-start | bytes 70208 | tf_op jit(solution)/shard_map/ppermute | solution.py:39
  43.7 1.2 copy-start.3
  43.7 1.4 %copy-start.4 = (f32[325,134]{1,0:T(8,128)S(1)}, f32[325,134]{1,0:T(8,128)}, u32[]{:S(2)}) copy-start(f32[325,134]{1,0:T(8,128)} %get-tuple-element.7) | copy-start | bytes 522604
  43.7 1.6 %copy-start.5 = (f32[325,134]{1,0:T(8,128)S(1)}, f32[325,134]{1,0:T(8,128)}, u32[]{:S(2)}) copy-start(f32[325,134]{1,0:T(8,128)} %get-tuple-element.8) | copy-start | bytes 522604
  43.8 1.7 %copy-start.6 = (f32[325,134]{1,0:T(8,128)S(1)}, f32[325,134]{1,0:T(8,128)}, u32[]{:S(2)}) copy-start(f32[325,134]{1,0:T(8,128)} %get-tuple-element.9) | copy-start | bytes 522604
  63.7 2.8 %collective-permute-start.8 = (f32[2,2,4,3]{3,1,0,2:T(2,128)S(1)}, f32[2,2,4,3]{3,1,0,2:T(2,128)S(1)}, u32[]{:S(2)}, u32[]{:S(2)}) collective-permute-start(f32[2,2,4,3]{3,1,0,2:T(2,128)S(1)} %get-tuple-element.56), channel_id=1, source_target_pairs={{0,1},{2,3},{4,5},{6,7},{8,9},{10,11},{12,13},{14,15},{16,17},{18,... | collective-permute-start | bytes 584 | tf_op jit(solution)/shard_map/ppermute | solution.py:39
  65.1 3.1 %collective-permute-start.9 = (f32[2,2,4,3]{3,1,0,2:T(2,128)S(1)}, f32[2,2,4,3]{3,1,0,2:T(2,128)S(1)}, u32[]{:S(2)}, u32[]{:S(2)}) collective-permute-start(f32[2,2,4,3]{3,1,0,2:T(2,128)S(1)} %get-tuple-element.57), channel_id=1, source_target_pairs={{1,0},{3,2},{5,4},{7,6},{9,8},{11,10},{13,12},{15,14},{17,16},{19,... | collective-permute-start | bytes 584 | tf_op jit(solution)/shard_map/ppermute | solution.py:39
  66.5 4.6 %copy-start.1 = (f32[2,128,512]{2,1,0:T(8,128)S(1)}, f32[2,128,512]{2,1,0:T(8,128)}, u32[]{:S(2)}) copy-start(f32[2,128,512]{2,1,0:T(8,128)} %shard_map.77) | copy-start | bytes 1572868
  68.2 1.9 %copy-start.12 = (f32[2,2,4,134]{3,1,0,2:T(2,128)}, f32[2,2,4,134]{3,1,0,2:T(2,128)S(1)}, u32[]{:S(2)}) copy-start(f32[2,2,4,134]{3,1,0,2:T(2,128)S(1)} %pad_maximum_fusion.6) | copy-start | bytes 25732
  68.8 21.9 %collective-permute-start.12 = (f32[2,2,3,134]{3,1,0,2:T(2,128)}, f32[2,2,3,134]{3,1,0,2:T(2,128)}, u32[]{:S(2)}, u32[]{:S(2)}) collective-permute-start(f32[2,2,3,134]{3,1,0,2:T(2,128)} %get-tuple-element.44), channel_id=1, source_target_pairs={{2,8},{4,10},{6,12},{10,16},{12,18},{14,20},{18,24},{20,26},{22,28... | collective-permute-start | bytes 19304 | tf_op jit(solution)/shard_map/ppermute | solution.py:40
  71.3 8.7 %copy-start.13 = (f32[2,2,4,134]{3,1,0,2:T(2,128)S(1)}, f32[2,2,4,134]{3,1,0,2:T(2,128)}, u32[]{:S(2)}) copy-start(f32[2,2,4,134]{3,1,0,2:T(2,128)} %copy-done.12) | copy-start | bytes 25732
  71.3 12.0 %copy-start.14 = (f32[2,2,3,134]{3,1,0,2:T(2,128)S(1)}, f32[2,2,3,134]{3,1,0,2:T(2,128)}, u32[]{:S(2)}) copy-start(f32[2,2,3,134]{3,1,0,2:T(2,128)} %get-tuple-element.45) | copy-start | bytes 19300
  71.8 21.1 %collective-permute-start.6 = (f32[256,3,134]{0,2,1:T(8,128)S(1)}, f32[256,3,134]{0,2,1:T(8,128)S(1)}, u32[]{:S(2)}, u32[]{:S(2)}) collective-permute-start(f32[256,3,134]{0,2,1:T(8,128)S(1)} %copy.38), channel_id=1, source_target_pairs={{0,2},{2,4},{4,6},{1,3},{3,5},{5,7},{8,10},{10,12},{12,14},{9,11},... | collective-permute-start | bytes 1234952 | tf_op jit(solution)/shard_map/ppermute | solution.py:39
  78.7 22.7 %collective-permute-start.7 = (f32[256,3,134]{0,2,1:T(8,128)S(1)}, f32[256,3,134]{0,2,1:T(8,128)}, u32[]{:S(2)}, u32[]{:S(2)}) collective-permute-start(f32[256,3,134]{0,2,1:T(8,128)S(1)} %copy.42), channel_id=1, source_target_pairs={{2,0},{4,2},{6,4},{3,1},{5,3},{7,5},{10,8},{12,10},{14,12},{11,9},... | collective-permute-start | bytes 1234952 | tf_op jit(solution)/shard_map/ppermute | solution.py:39
  80.0 12.2 %collective-permute-start.11 = (f32[2,2,4,134]{3,1,0,2:T(2,128)S(1)}, f32[2,2,4,134]{3,1,0,2:T(2,128)S(1)}, u32[]{:S(2)}, u32[]{:S(2)}) collective-permute-start(f32[2,2,4,134]{3,1,0,2:T(2,128)S(1)} %copy-done.13), channel_id=1, source_target_pairs={{0,8},{2,10},{4,12},{6,14},{8,16},{10,18},{12,20},{14,22},{16,24},... | collective-permute-start | bytes 25736 | tf_op jit(solution)/shard_map/ppermute | solution.py:40
  83.3 8.8 %collective-permute-start.10 = (f32[2,2,3,134]{3,1,0,2:T(2,128)S(1)}, f32[2,2,3,134]{3,1,0,2:T(2,128)S(1)}, u32[]{:S(2)}, u32[]{:S(2)}) collective-permute-start(f32[2,2,3,134]{3,1,0,2:T(2,128)S(1)} %copy-done.14), channel_id=1, source_target_pairs={{0,10},{2,12},{4,14},{8,18},{10,20},{12,22},{16,26},{18,28},{20,30... | collective-permute-start | bytes 19304 | tf_op jit(solution)/shard_map/ppermute | solution.py:40
  93.4 9.6 %copy-start.7 = (f32[256,134]{1,0:T(8,128)S(1)}, f32[256,134]{1,0:T(8,128)}, u32[]{:S(2)}) copy-start(f32[256,134]{1,0:T(8,128)} %get-tuple-element.20) | copy-start | bytes 411652
  93.4 9.6 %copy-start.8 = (f32[256,134]{1,0:T(8,128)S(1)}, f32[256,134]{1,0:T(8,128)}, u32[]{:S(2)}) copy-start(f32[256,134]{1,0:T(8,128)} %get-tuple-element.21) | copy-start | bytes 411652
  93.4 9.6 %copy-start.9 = (f32[256,134]{1,0:T(8,128)S(1)}, f32[256,134]{1,0:T(8,128)}, u32[]{:S(2)}) copy-start(f32[256,134]{1,0:T(8,128)} %get-tuple-element.22) | copy-start | bytes 411652
  93.4 9.6 %copy-start.10 = (f32[256,134]{1,0:T(8,128)S(1)}, f32[256,134]{1,0:T(8,128)}, u32[]{:S(2)}) copy-start(f32[256,134]{1,0:T(8,128)} %get-tuple-element.23) | copy-start | bytes 411652
  116.3 1.3 %copy-start.2 = (f32[2,128,512]{2,1,0:T(8,128)S(1)}, f32[2,128,512]{2,1,0:T(8,128)}, u32[]{:S(2)}) copy-start(f32[2,128,512]{2,1,0:T(8,128)} %shard_map.78) | copy-start | bytes 1572868

commit v10 on v9

--- a/solution.py
+++ b/solution.py
@@ -205,18 +205,20 @@
         widened[rows_now + (t - 1) * per_tick.shape[1] : rows_now + t * per_tick.shape[1]]
         for t in range(1, ticks)
     ]
-    rims = jnp.concatenate([low_x, high_x], axis=1)
-    corner_low = fetch(rims[..., ny - width :], ("ty",), (-1,))
-    corner_high = fetch(rims[..., :width], ("ty",), (1,))
-    rims = jnp.concatenate([corner_low, rims, corner_high], axis=-1)
+    corner = {}
+    for dx, rows in ((-1, slice(nx - width, nx)), (1, slice(0, width))):
+        for dy, lanes in ((-1, slice(ny - width, ny)), (1, slice(0, width))):
+            corner[dx, dy] = fetch(now[:, rows, lanes], ("tx", "ty"), (dx, dy))
+    rims_low = jnp.concatenate([corner[-1, -1], low_x, corner[-1, 1]], axis=-1)
+    rims_high = jnp.concatenate([corner[1, -1], high_x, corner[1, 1]], axis=-1)
     segments = []
     for ix in range(ex):
         if ix < width:
-            segments.append(rims[:, ix])
+            segments.append(rims_low[:, ix])
         elif ix < width + nx:
             segments.append(widened[:rows_now, ix - width])
         else:
-            segments.append(rims[:, ix - nx])
+            segments.append(rims_high[:, ix - width - nx])
     segments.append(jnp.zeros((rows_now, padded - cols), jnp.float32))
     packed = jnp.concatenate(segments, axis=-1)
     first_pending = nsrc * two * depth + depth

time: 121 us -> 129 us (1.066)
  starting transfers between devices: 39.1 us -> 50.1 us
  local copies, waits for them, and re-layouts: 35.8 us -> 29.8 us
  waiting for transfers between devices: 10.3 us -> 13.9 us
    ppermute x3 -> x7, starting transfers between devices: 12 us -> 28.1 us  [fetch(): return lax.ppermute(block, tuple(axes), pairs)]
    ppermute x10 -> x8, starting transfers between devices: 27.1 us -> 21.9 us  [fetch(): return lax.ppermute(block, axes[0], pairs)]
    ppermute x3 -> x7, waiting for transfers between devices: 0.69 us -> 4.82 us  [fetch(): return lax.ppermute(block, tuple(axes), pairs)]
    slice x3 -> x1, local copies, waits for them, and re-layouts: 3.44 us -> 1.57 us  [per_device(): corner[dx, dy] = fetch(now[:, rows, lanes], ('tx', 'ty'), (dx, dy))]
    ppermute x4 -> x2, local copies, waits for them, and re-layouts: 3.52 us -> 1.85 us  [fetch(): return lax.ppermute(block, axes[0], pairs)]
    concatenate x1 -> x2, other arithmetic: 2.05 us -> 3.44 us  [the longest x1 1.79 us: per_device(): rims_high = jnp.concatenate([corner[1, -1], high_x, corner[1, 1]], axis=-1)]
    ppermute x10 -> x8, waiting for transfers between devices: 9.64 us -> 9.08 us  [fetch(): return lax.ppermute(block, axes[0], pairs)]
    unnamed x43 -> x32, local copies, waits for them, and re-layouts: 4.14 us -> 3.63 us
  transfers between devices with their start and end apart: 13 -> 15, of which waited for: 3 -> 4; matrix products, arithmetic and copies ran while one was open for 15% -> 15% of each run, Pallas kernels for 0% -> 0%
where the time goes in v10:
time: 129 us; the launch traced here: 128 us
  starting transfers between devices  50.1 us (39%)
  local copies, waits for them, and re-layouts  29.8 us (23%)
  Pallas kernels  22.9 us (18%)
  waiting for transfers between devices  13.9 us (11%)
  other arithmetic  10.4 us (8%)
    ppermute x7, starting transfers between devices, fetch(): return lax.ppermute(block, tuple(axes), pairs)  28.1 us
    pallas_call x2, Pallas kernels, run_tick(): pl.pallas_call(functools.partial(tick_kernel, row=row, depth=depth, width...  22.9 us
    ppermute x8, starting transfers between devices, fetch(): return lax.ppermute(block, axes[0], pairs)  21.9 us
    ppermute x8, waiting for transfers between devices, fetch(): return lax.ppermute(block, axes[0], pairs)  9.08 us
    ppermute x7, waiting for transfers between devices, fetch(): return lax.ppermute(block, tuple(axes), pairs)  4.82 us
    unnamed x32, local copies, waits for them, and re-layouts  3.63 us
    concatenate x1, local copies, waits for them, and re-layouts, per_device(): packed = jnp.concatenate(segments, axis=-1)  3.39 us
    squeeze x1, other arithmetic, per_device(): segments.append(widened[:rows_now, ix - width])  2.9 us
  transfers between devices with their start and end apart: 15, of which 4 were waited for; matrix products, arithmetic and copies ran while one was open for 15% of the time, Pallas kernels for 0%

profile of v10, /device:TPU:0, one launch (start us, length us, event | category | flops | bytes accessed | tf_op | source)
XLA Modules:
  0.0 128.3 jit_solution(13939685728489889)
XLA Ops:
  0.6 0.7 convert_element_type.23
  1.3 0.7 copy.24
  2.0 0.9 copy.26
  2.9 1.3 fusion.4
  4.3 1.0 fusion.6
  5.4 1.3 collective-permute-start.6
  6.6 6.3 %collective-permute-start.1 = (f32[325,3,128]{2,0,1:T(8,128)}, f32[325,3,128]{2,0,1:T(8,128)}, u32[]{:S(2)}, u32[]{:S(2)}) collective-permute-start(f32[325,3,128]{2,0,1:T(8,128)} %get-tuple-element.31), channel_id=1, source_target_pairs={{0,2},{2,4},{4,6},{1,3},{3,5},{5,7},{8,10},{10,12},{12,14},{9,11},... | collective-permute-start | bytes 1497608 | tf_op jit(solution)/shard_map/ppermute | solution.py:39
  12.9 1.6 %fusion.5 = (f32[325,3,3]{2,0,1:T(8,128)}, f32[325,3,3]{2,0,1:T(8,128)}, f32[325,3,3]{2,0,1:T(8,128)}, f32[325,3,3]{2,0,1:T(8,128)}) fusion(f32[325,4,128]{2,0,1:T(8,128)S(1)} %pad_maximum_fusion.5), kind=kLoop, calls=%fused_computation.54 | loop fusion | bytes 93600 | tf_op jit(solution)/shard_map/slice | solution.py:211
  14.5 1.5 %collective-permute-start.5 = (f32[325,3,3]{2,0,1:T(8,128)}, f32[325,3,3]{2,0,1:T(8,128)}, u32[]{:S(2)}, u32[]{:S(2)}) collective-permute-start(f32[325,3,3]{2,0,1:T(8,128)} %get-tuple-element.26), channel_id=1, source_target_pairs={{2,1},{4,3},{6,5},{10,9},{12,11},{14,13},{18,17},{20,19},{22,21},{... | collective-permute-start | bytes 35108 | tf_op jit(solution)/shard_map/ppermute | solution.py:40
  16.0 0.5 concatenate.41
  16.5 1.4 %fusion.2 = (f32[581,4,3]{2,0,1:T(8,128)S(1)}, f32[581,4,3]{2,0,1:T(8,128)}) fusion(f32[581,4,128]{2,0,1:T(8,128)S(1)} %concatenate.41), kind=kLoop, calls=%fused_computation.51 | loop fusion | bytes 111552 | tf_op jit(solution)/shard_map/slice | solution.py:45
  17.9 1.7 %copy.30 = f32[581,4,3]{0,1,2:T(4,128)S(1)} copy(f32[581,4,3]{2,0,1:T(8,128)} %get-tuple-element.11) | data formatting | bytes 55776 | tf_op jit(solution)/shard_map/slice | solution.py:46
  19.6 1.3 %collective-permute-start.4 = (f32[581,4,3]{0,1,2:T(4,128)S(1)}, f32[581,4,3]{0,1,2:T(4,128)S(1)}, u32[]{:S(2)}, u32[]{:S(2)}) collective-permute-start(f32[581,4,3]{0,1,2:T(4,128)S(1)} %copy.30), channel_id=1, source_target_pairs={{1,0},{3,2},{5,4},{7,6},{9,8},{11,10},{13,12},{15,14},{17,16},{19,... | collective-permute-start | bytes 83672 | tf_op jit(solution)/shard_map/ppermute | solution.py:39
  20.9 0.4 copy.29
  21.3 3.0 %collective-permute-start.3 = (f32[581,4,3]{0,1,2:T(4,128)S(1)}, f32[581,4,3]{0,1,2:T(4,128)S(1)}, u32[]{:S(2)}, u32[]{:S(2)}) collective-permute-start(f32[581,4,3]{0,1,2:T(4,128)S(1)} %copy.29), channel_id=1, source_target_pairs={{0,1},{2,3},{4,5},{6,7},{8,9},{10,11},{12,13},{14,15},{16,17},{18,... | collective-permute-start | bytes 83672 | tf_op jit(solution)/shard_map/ppermute | solution.py:39
  24.7 0.6 pad_convert_fusion.ins_ref
  25.3 0.1 maximum_maximum_fusion
  25.5 0.5 slice_bitcast_fusion.27
  26.0 0.8 fusion
  26.8 1.3 collective-permute-start.7
  28.1 0.4 copy.31
  28.5 1.5 %collective-permute-start.2 = (f32[325,3,3]{2,0,1:T(8,128)}, f32[325,3,3]{2,0,1:T(8,128)}, u32[]{:S(2)}, u32[]{:S(2)}) collective-permute-start(f32[325,3,3]{2,0,1:T(8,128)} %get-tuple-element.28), channel_id=1, source_target_pairs={{1,2},{3,4},{5,6},{9,10},{11,12},{13,14},{17,18},{19,20},{21,22},{... | collective-permute-start | bytes 35108 | tf_op jit(solution)/shard_map/ppermute | solution.py:40
  29.9 1.4 %copy.32 = f32[581,4,3]{2,0,1:T(8,128)} copy(f32[581,4,3]{0,1,2:T(4,128)S(1)} %collective-permute-done.4) | data formatting | bytes 55776 | tf_op jit(solution)/shard_map/ppermute | solution.py:39
  31.4 2.9 %maximum_bitcast_fusion = (f32[325,134]{1,0:T(8,128)}, f32[325,134]{1,0:T(8,128)}, f32[325,134]{1,0:T(8,128)}, f32[325,134]{1,0:T(8,128)}) fusion(f32[581,4,3]{2,0,1:T(8,128)} %copy.32, f32[581,4,128]{2,0,1:T(8,128)S(1)} %concatenate.41, f32[581,4,3]{2,0,1:T(8,128)S(1)} %copy.31), kind=kLoop, calls=%fused_computation.11 | loop fusion | flops 348400 | bytes 1942464 | tf_op jit(solution)/shard_map/squeeze | solution.py:219
  34.3 0.5 pad_maximum_fusion
  34.8 0.5 copy-done.8
  35.3 12.3 %collective-permute-start = (f32[325,3,3]{2,0,1:T(8,128)S(1)}, f32[325,3,3]{2,0,1:T(8,128)S(1)}, u32[]{:S(2)}, u32[]{:S(2)}) collective-permute-start(f32[325,3,3]{2,0,1:T(8,128)S(1)} %copy-done.8), channel_id=1, source_target_pairs={{0,3},{2,5},{4,7},{8,11},{10,13},{12,15},{16,19},{18,21},{20,23},{... | collective-permute-start | bytes 35108 | tf_op jit(solution)/shard_map/ppermute | solution.py:40
  47.6 1.8 %pad_maximum_fusion.4 = f32[325,3,134]{2,0,1:T(8,128)S(1)} fusion(f32[325,3,3]{2,0,1:T(8,128)} %collective-permute-done.7, f32[325,3,128]{2,0,1:T(8,128)} %collective-permute-done.6, f32[325,3,3]{2,0,1:T(8,128)} %collective-permute-done.5), kind=kLoop, calls=%fused_computation.4 | loop fusion | flops 261300 | bytes 1045200 | tf_op jit(solution)/shard_map/concatenate | solution.py:213
  49.4 1.0 slice_bitcast_fusion
  50.4 3.6 %collective-permute-done = f32[325,3,3]{2,0,1:T(8,128)S(1)} collective-permute-done((f32[325,3,3]{2,0,1:T(8,128)S(1)}, f32[325,3,3]{2,0,1:T(8,128)S(1)}, u32[]{:S(2)}, u32[]{:S(2)}) %collective-permute-start) | collective-permute-done | bytes 11732 | tf_op jit(solution)/shard_map/ppermute | solution.py:40
  54.0 1.6 %pad_maximum_fusion.3 = f32[325,3,134]{2,0,1:T(8,128)S(1)} fusion(f32[325,3,3]{2,0,1:T(8,128)} %collective-permute-done.2, f32[325,3,128]{2,0,1:T(8,128)} %collective-permute-done.1, f32[325,3,3]{2,0,1:T(8,128)S(1)} %collective-permute-done), kind=kLoop, calls=%fused_computation.3 | loop fusion | flops 261300 | bytes 1045200 | tf_op jit(solution)/shard_map/concatenate | solution.py:212
  55.7 1.0 slice_bitcast_fusion.3
  56.8 3.4 %concatenate.44.frc_ref.pk_ref = f32[325,1408]{1,0:T(8,128)S(1)} concatenate(f32[325,134]{1,0:T(8,128)} %get-tuple-element.25, f32[325,134]{1,0:T(8,128)} %get-tuple-element.24, f32[325,134]{1,0:T(8,128)} %get-tuple-element.23, f32[325,134]{1,0:T(8,128)} %get-tuple-element.9, f32[325,134]{1,0:T(8,128)} %get-tuple-element.8, f32[325,134]{1,0:T(8,128)} %get-tuple-element.7, ...), dimensions={1} | concatenate | bytes 3660800 | tf_op jit(solution)/shard_map/concatenate | solution.py:223
  60.2 0.7 reshape.68.inc_ref
  60.9 0.5 copy-done.3
  61.5 11.5 %shard_map.77 = f32[2,128,512]{2,1,0:T(8,128)} custom-call(s32[2]{0:T(128)} %get-tuple-element.60.order_ref, f32[325,1408]{1,0:T(8,128)} %copy-done.3, f32[325,1408]{1,0:T(8,128)} %copy-done.3, f32[2,2,1408]{2,1,0:T(2,128)} %reshape.68.inc_ref, f32[1,1408]{1,0:T(1,128)} %pad_convert_fusion.ins_ref, bf16[128,512]{1,0:T(8,128)(2,1)} %get-tuple-element.39.bhi_ref, ...), custom_call_target="tpu_custom_call" | custom-call | flops 4429185024 | bytes 2812288 | tf_op jit(solution)/shard_map/pallas_call | solution.py:155
  73.0 1.2 reshape.69
  74.3 1.3 collective-permute-start.10
  75.6 1.3 %collective-permute-start.11 = (f32[2,2,4,3]{3,1,0,2:T(2,128)S(1)}, f32[2,2,4,3]{3,1,0,2:T(2,128)S(1)}, u32[]{:S(2)}, u32[]{:S(2)}) collective-permute-start(f32[2,2,4,3]{3,1,0,2:T(2,128)S(1)} %get-tuple-element.59), channel_id=1, source_target_pairs={{1,0},{3,2},{5,4},{7,6},{9,8},{11,10},{13,12},{15,14},{17,16},{19,... | collective-permute-start | bytes 584 | tf_op jit(solution)/shard_map/ppermute | solution.py:39
  76.9 0.1 fusion.3
  77.0 1.6 %collective-permute-done.11 = f32[2,2,4,3]{3,1,0,2:T(2,128)S(1)} collective-permute-done((f32[2,2,4,3]{3,1,0,2:T(2,128)S(1)}, f32[2,2,4,3]{3,1,0,2:T(2,128)S(1)}, u32[]{:S(2)}, u32[]{:S(2)}) %collective-permute-start.11) | collective-permute-done | bytes 224 | tf_op jit(solution)/shard_map/ppermute | solution.py:39
  78.7 0.7 collective-permute-start.14
  79.4 0.9 slice_bitcast_fusion.6
  80.3 0.2 stack_reshape.6
  80.5 1.0 copy.38
  81.5 0.2 copy.34
  81.8 6.2 %collective-permute-start.8 = (f32[256,3,134]{0,2,1:T(8,128)S(1)}, f32[256,3,134]{0,2,1:T(8,128)S(1)}, u32[]{:S(2)}, u32[]{:S(2)}) collective-permute-start(f32[256,3,134]{0,2,1:T(8,128)S(1)} %copy.34), channel_id=1, source_target_pairs={{0,2},{2,4},{4,6},{1,3},{3,5},{5,7},{8,10},{10,12},{12,14},{9,11},... | collective-permute-start | bytes 1234952 | tf_op jit(solution)/shard_map/ppermute | solution.py:39
  88.0 1.3 %collective-permute-start.9 = (f32[256,3,134]{0,2,1:T(8,128)}, f32[256,3,134]{0,2,1:T(8,128)}, u32[]{:S(2)}, u32[]{:S(2)}) collective-permute-start(f32[256,3,134]{0,2,1:T(8,128)} %copy.38), channel_id=1, source_target_pairs={{2,0},{4,2},{6,4},{3,1},{5,3},{7,5},{10,8},{12,10},{14,12},{11,9},... | collective-permute-start | bytes 1234952 | tf_op jit(solution)/shard_map/ppermute | solution.py:39
  89.3 3.5 %collective-permute-start.13 = (f32[2,2,4,134]{3,1,0,2:T(2,128)S(1)}, f32[2,2,4,134]{3,1,0,2:T(2,128)S(1)}, u32[]{:S(2)}, u32[]{:S(2)}) collective-permute-start(f32[2,2,4,134]{3,1,0,2:T(2,128)S(1)} %pad_maximum_fusion.7), channel_id=1, source_target_pairs={{0,8},{2,10},{4,12},{6,14},{8,16},{10,18},{12,20},{14,22},{16,24},... | collective-permute-start | bytes 25736 | tf_op jit(solution)/shard_map/ppermute | solution.py:40
  92.8 7.5 %collective-permute-start.12 = (f32[2,2,3,134]{3,1,0,2:T(2,128)S(1)}, f32[2,2,3,134]{3,1,0,2:T(2,128)S(1)}, u32[]{:S(2)}, u32[]{:S(2)}) collective-permute-start(f32[2,2,3,134]{3,1,0,2:T(2,128)S(1)} %get-tuple-element.47), channel_id=1, source_target_pairs={{0,10},{2,12},{4,14},{8,18},{10,20},{12,22},{16,26},{18,28},{20,30... | collective-permute-start | bytes 19304 | tf_op jit(solution)/shard_map/ppermute | solution.py:40
  100.3 1.2 collective-permute-done.12
  101.5 0.7 concatenate.51.inc_ref
  102.3 0.1 copy.45
  102.4 0.1 copy.44
  102.6 0.1 copy.43
  102.7 7.5 %collective-permute-done.9 = f32[256,3,134]{0,2,1:T(8,128)} collective-permute-done((f32[256,3,134]{0,2,1:T(8,128)}, f32[256,3,134]{0,2,1:T(8,128)}, u32[]{:S(2)}, u32[]{:S(2)}) %collective-permute-start.9) | collective-permute-done | bytes 411680 | tf_op jit(solution)/shard_map/ppermute | solution.py:39
  110.2 1.1 fusion.7
  111.3 0.1 copy.48
  111.8 1.9 %concatenate.49.frc_ref = f32[256,1408]{1,0:T(8,128)} concatenate(f32[256,134]{1,0:T(8,128)S(1)} %bitcast.89, f32[256,134]{1,0:T(8,128)S(1)} %bitcast.88, f32[256,134]{1,0:T(8,128)S(1)} %bitcast.87, f32[256,134]{1,0:T(8,128)S(1)} %copy-done.7, f32[256,134]{1,0:T(8,128)S(1)} %copy-done.6, f32[256,134]{1,0:T(8,128)S(1)} %copy-done.5, f32[256,134]{1,0:T(8,128)S(1)} %get-tuple-element.14, ...), dimensions={1} | concatenate | bytes 2883584 | tf_op jit(solution)/shard_map/concatenate | solution.py:68
  113.6 11.4 %shard_map.78 = f32[2,128,512]{2,1,0:T(8,128)} custom-call(s32[2]{0:T(128)} %get-tuple-element.61.order_ref, f32[256,1408]{1,0:T(8,128)} %concatenate.49.frc_ref, f32[325,1408]{1,0:T(8,128)} %copy-done.3, f32[2,2,1408]{2,1,0:T(2,128)} %concatenate.51.inc_ref, f32[1,1408]{1,0:T(1,128)} %pad_convert_fusion.ins_ref, ...), custom_call_target="tpu_custom_call" | custom-call | flops 4429185024 | bytes 2423680 | tf_op jit(solution)/shard_map/pallas_call | solution.py:155
  125.0 1.3 reshape.70
  126.3 0.2 stack_reshape.7
  126.5 0.6 slice.281
  127.1 1.2 pad_maximum_fusion.2
  (57 shorter events, 1.1 us)
Async XLA Ops:
  5.4 42.2 %collective-permute-start.6 = (f32[325,3,128]{2,0,1:T(8,128)}, f32[325,3,128]{2,0,1:T(8,128)}, u32[]{:S(2)}, u32[]{:S(2)}) collective-permute-start(f32[325,3,128]{2,0,1:T(8,128)} %get-tuple-element.30), channel_id=1, source_target_pairs={{2,0},{4,2},{6,4},{3,1},{5,3},{7,5},{10,8},{12,10},{14,12},{11,9},... | collective-permute-start | bytes 1497608 | tf_op jit(solution)/shard_map/ppermute | solution.py:39
  6.6 47.4 %collective-permute-start.1 = (f32[325,3,128]{2,0,1:T(8,128)}, f32[325,3,128]{2,0,1:T(8,128)}, u32[]{:S(2)}, u32[]{:S(2)}) collective-permute-start(f32[325,3,128]{2,0,1:T(8,128)} %get-tuple-element.31), channel_id=1, source_target_pairs={{0,2},{2,4},{4,6},{1,3},{3,5},{5,7},{8,10},{10,12},{12,14},{9,11},... | collective-permute-start | bytes 1497608 | tf_op jit(solution)/shard_map/ppermute | solution.py:39
  14.5 20.3 %collective-permute-start.5 = (f32[325,3,3]{2,0,1:T(8,128)}, f32[325,3,3]{2,0,1:T(8,128)}, u32[]{:S(2)}, u32[]{:S(2)}) collective-permute-start(f32[325,3,3]{2,0,1:T(8,128)} %get-tuple-element.26), channel_id=1, source_target_pairs={{2,1},{4,3},{6,5},{10,9},{12,11},{14,13},{18,17},{20,19},{22,21},{... | collective-permute-start | bytes 35108 | tf_op jit(solution)/shard_map/ppermute | solution.py:40
  17.9 6.5 %copy-start.9 = (f32[1,4,2,64,64]{4,3,2,1,0:T(8,128)S(1)}, f32[1,4,2,64,64]{4,3,2,1,0:T(8,128)}, u32[]{:S(2)}) copy-start(f32[1,4,2,64,64]{4,3,2,1,0:T(8,128)} %param.8) | copy-start | bytes 393220
  19.6 8.8 %collective-permute-start.4 = (f32[581,4,3]{0,1,2:T(4,128)S(1)}, f32[581,4,3]{0,1,2:T(4,128)S(1)}, u32[]{:S(2)}, u32[]{:S(2)}) collective-permute-start(f32[581,4,3]{0,1,2:T(4,128)S(1)} %copy.30), channel_id=1, source_target_pairs={{1,0},{3,2},{5,4},{7,6},{9,8},{11,10},{13,12},{15,14},{17,16},{19,... | collective-permute-start | bytes 83672 | tf_op jit(solution)/shard_map/ppermute | solution.py:39
  21.3 5.4 %collective-permute-start.3 = (f32[581,4,3]{0,1,2:T(4,128)S(1)}, f32[581,4,3]{0,1,2:T(4,128)S(1)}, u32[]{:S(2)}, u32[]{:S(2)}) collective-permute-start(f32[581,4,3]{0,1,2:T(4,128)S(1)} %copy.29), channel_id=1, source_target_pairs={{0,1},{2,3},{4,5},{6,7},{8,9},{10,11},{12,13},{14,15},{16,17},{18,... | collective-permute-start | bytes 83672 | tf_op jit(solution)/shard_map/ppermute | solution.py:39
  24.4 1.1 copy-start.10
  26.8 20.8 %collective-permute-start.7 = (f32[325,3,3]{2,0,1:T(8,128)}, f32[325,3,3]{2,0,1:T(8,128)}, u32[]{:S(2)}, u32[]{:S(2)}) collective-permute-start(f32[325,3,3]{2,0,1:T(8,128)} %get-tuple-element.27), channel_id=1, source_target_pairs={{3,0},{5,2},{7,4},{11,8},{13,10},{15,12},{19,16},{21,18},{23,20},{... | collective-permute-start | bytes 35108 | tf_op jit(solution)/shard_map/ppermute | solution.py:40
  28.5 21.9 %collective-permute-start.2 = (f32[325,3,3]{2,0,1:T(8,128)}, f32[325,3,3]{2,0,1:T(8,128)}, u32[]{:S(2)}, u32[]{:S(2)}) collective-permute-start(f32[325,3,3]{2,0,1:T(8,128)} %get-tuple-element.28), channel_id=1, source_target_pairs={{1,2},{3,4},{5,6},{9,10},{11,12},{13,14},{17,18},{19,20},{21,22},{... | collective-permute-start | bytes 35108 | tf_op jit(solution)/shard_map/ppermute | solution.py:40
  31.4 2.9 %copy-start = (f32[581,4,3]{2,0,1:T(8,128)S(1)}, f32[581,4,3]{2,0,1:T(8,128)}, u32[]{:S(2)}) copy-start(f32[581,4,3]{2,0,1:T(8,128)} %copy.32) | copy-start | bytes 83668
  34.3 1.0 copy-start.8
  35.3 18.7 %collective-permute-start = (f32[325,3,3]{2,0,1:T(8,128)S(1)}, f32[325,3,3]{2,0,1:T(8,128)S(1)}, u32[]{:S(2)}, u32[]{:S(2)}) collective-permute-start(f32[325,3,3]{2,0,1:T(8,128)S(1)} %copy-done.8), channel_id=1, source_target_pairs={{0,3},{2,5},{4,7},{8,11},{10,13},{12,15},{16,19},{18,21},{20,23},{... | collective-permute-start | bytes 35108 | tf_op jit(solution)/shard_map/ppermute | solution.py:40
  55.7 1.1 copy-start.4
  60.2 1.3 copy-start.3
  74.3 2.7 %collective-permute-start.10 = (f32[2,2,4,3]{3,1,0,2:T(2,128)S(1)}, f32[2,2,4,3]{3,1,0,2:T(2,128)S(1)}, u32[]{:S(2)}, u32[]{:S(2)}) collective-permute-start(f32[2,2,4,3]{3,1,0,2:T(2,128)S(1)} %get-tuple-element.58), channel_id=1, source_target_pairs={{0,1},{2,3},{4,5},{6,7},{8,9},{10,11},{12,13},{14,15},{16,17},{18,... | collective-permute-start | bytes 584 | tf_op jit(solution)/shard_map/ppermute | solution.py:39
  75.6 3.1 %collective-permute-start.11 = (f32[2,2,4,3]{3,1,0,2:T(2,128)S(1)}, f32[2,2,4,3]{3,1,0,2:T(2,128)S(1)}, u32[]{:S(2)}, u32[]{:S(2)}) collective-permute-start(f32[2,2,4,3]{3,1,0,2:T(2,128)S(1)} %get-tuple-element.59), channel_id=1, source_target_pairs={{1,0},{3,2},{5,4},{7,6},{9,8},{11,10},{13,12},{15,14},{17,16},{19,... | collective-permute-start | bytes 584 | tf_op jit(solution)/shard_map/ppermute | solution.py:39
  77.0 3.3 %copy-start.1 = (f32[2,128,512]{2,1,0:T(8,128)S(1)}, f32[2,128,512]{2,1,0:T(8,128)}, u32[]{:S(2)}) copy-start(f32[2,128,512]{2,1,0:T(8,128)} %shard_map.77) | copy-start | bytes 1572868
  78.7 21.6 %collective-permute-start.14 = (f32[2,2,3,134]{3,1,0,2:T(2,128)S(1)}, f32[2,2,3,134]{3,1,0,2:T(2,128)S(1)}, u32[]{:S(2)}, u32[]{:S(2)}) collective-permute-start(f32[2,2,3,134]{3,1,0,2:T(2,128)S(1)} %get-tuple-element.46), channel_id=1, source_target_pairs={{2,8},{4,10},{6,12},{10,16},{12,18},{14,20},{18,24},{20,26},{22,28... | collective-permute-start | bytes 19304 | tf_op jit(solution)/shard_map/ppermute | solution.py:40
  81.8 20.5 %collective-permute-start.8 = (f32[256,3,134]{0,2,1:T(8,128)S(1)}, f32[256,3,134]{0,2,1:T(8,128)S(1)}, u32[]{:S(2)}, u32[]{:S(2)}) collective-permute-start(f32[256,3,134]{0,2,1:T(8,128)S(1)} %copy.34), channel_id=1, source_target_pairs={{0,2},{2,4},{4,6},{1,3},{3,5},{5,7},{8,10},{10,12},{12,14},{9,11},... | collective-permute-start | bytes 1234952 | tf_op jit(solution)/shard_map/ppermute | solution.py:39
  88.0 22.2 %collective-permute-start.9 = (f32[256,3,134]{0,2,1:T(8,128)}, f32[256,3,134]{0,2,1:T(8,128)}, u32[]{:S(2)}, u32[]{:S(2)}) collective-permute-start(f32[256,3,134]{0,2,1:T(8,128)} %copy.38), channel_id=1, source_target_pairs={{2,0},{4,2},{6,4},{3,1},{5,3},{7,5},{10,8},{12,10},{14,12},{11,9},... | collective-permute-start | bytes 1234952 | tf_op jit(solution)/shard_map/ppermute | solution.py:39
  89.3 12.2 %collective-permute-start.13 = (f32[2,2,4,134]{3,1,0,2:T(2,128)S(1)}, f32[2,2,4,134]{3,1,0,2:T(2,128)S(1)}, u32[]{:S(2)}, u32[]{:S(2)}) collective-permute-start(f32[2,2,4,134]{3,1,0,2:T(2,128)S(1)} %pad_maximum_fusion.7), channel_id=1, source_target_pairs={{0,8},{2,10},{4,12},{6,14},{8,16},{10,18},{12,20},{14,22},{16,24},... | collective-permute-start | bytes 25736 | tf_op jit(solution)/shard_map/ppermute | solution.py:40
  92.8 8.7 %collective-permute-start.12 = (f32[2,2,3,134]{3,1,0,2:T(2,128)S(1)}, f32[2,2,3,134]{3,1,0,2:T(2,128)S(1)}, u32[]{:S(2)}, u32[]{:S(2)}) collective-permute-start(f32[2,2,3,134]{3,1,0,2:T(2,128)S(1)} %get-tuple-element.47), channel_id=1, source_target_pairs={{0,10},{2,12},{4,14},{8,18},{10,20},{12,22},{16,26},{18,28},{20,30... | collective-permute-start | bytes 19304 | tf_op jit(solution)/shard_map/ppermute | solution.py:40
  102.7 9.0 %copy-start.5 = (f32[256,134]{1,0:T(8,128)S(1)}, f32[256,134]{1,0:T(8,128)}, u32[]{:S(2)}) copy-start(f32[256,134]{1,0:T(8,128)} %get-tuple-element.15) | copy-start | bytes 411652
  102.7 9.0 %copy-start.6 = (f32[256,134]{1,0:T(8,128)S(1)}, f32[256,134]{1,0:T(8,128)}, u32[]{:S(2)}) copy-start(f32[256,134]{1,0:T(8,128)} %get-tuple-element.16) | copy-start | bytes 411652
  102.7 9.0 %copy-start.7 = (f32[256,134]{1,0:T(8,128)S(1)}, f32[256,134]{1,0:T(8,128)}, u32[]{:S(2)}) copy-start(f32[256,134]{1,0:T(8,128)} %get-tuple-element.17) | copy-start | bytes 411652
  125.0 1.3 %copy-start.2 = (f32[2,128,512]{2,1,0:T(8,128)S(1)}, f32[2,128,512]{2,1,0:T(8,128)}, u32[]{:S(2)}) copy-start(f32[2,128,512]{2,1,0:T(8,128)} %shard_map.78) | copy-start | bytes 1572868

commit v11 on v9

--- a/solution.py
+++ b/solution.py
@@ -88,9 +88,11 @@
         high = scaled - (scaled - x)
         low = x - high
         label = pk_ref[pl.ds(label_row, 1), lo:hi]
-        hots = [(label == float(k)).astype(jnp.float32) for k in range(classes)]
-        high = jnp.concatenate([high * h for h in hots], axis=0).astype(jnp.bfloat16)
-        low = jnp.concatenate([low * h for h in hots], axis=0).astype(jnp.bfloat16)
+        hots = [(label == float(k)).astype(jnp.bfloat16) for k in range(classes)]
+        high = high.astype(jnp.bfloat16)
+        low = low.astype(jnp.bfloat16)
+        high = jnp.concatenate([high * h for h in hots], axis=0)
+        low = jnp.concatenate([low * h for h in hots], axis=0)
         bhi = bhi_ref[...]
         blo = blo_ref[...]
         out = jnp.dot(bhi, low, preferred_element_type=jnp.float32)

time: 121 us -> 119 us (0.983)
  no operation moved by 1% of the time
where the time goes in v11:
time: 119 us; the launch traced here: 118 us
  starting transfers between devices  39.1 us (33%)
  local copies, waits for them, and re-layouts  35.8 us (30%)
  Pallas kernels  21.9 us (18%)
  other arithmetic  10.2 us (9%)
  waiting for transfers between devices  10.1 us (8%)
  between operations  1.26 us (1%)
    ppermute x10, starting transfers between devices, fetch(): return lax.ppermute(block, axes[0], pairs)  26.9 us
    pallas_call x2, Pallas kernels, run_tick(): pl.pallas_call(functools.partial(tick_kernel, row=row, depth=depth, width...  21.9 us
    ppermute x3, starting transfers between devices, fetch(): return lax.ppermute(block, tuple(axes), pairs)  12.2 us
    ppermute x10, waiting for transfers between devices, fetch(): return lax.ppermute(block, axes[0], pairs)  9.63 us
    unnamed x43, local copies, waits for them, and re-layouts  4.14 us
    concatenate x1, local copies, waits for them, and re-layouts, per_device(): packed = jnp.concatenate(segments, axis=-1)  3.93 us
    ppermute x4, local copies, waits for them, and re-layouts, fetch(): return lax.ppermute(block, axes[0], pairs)  3.52 us
    slice x2, local copies, waits for them, and re-layouts, per_device(): corner_low = fetch(rims[..., ny - width:], ('ty',), (-1,))  2.96 us
  transfers between devices with their start and end apart: 13, of which 3 were waited for; matrix products, arithmetic and copies ran while one was open for 15% of the time, Pallas kernels for 0%

profile of v11, /device:TPU:0, one launch (start us, length us, event | category | flops | bytes accessed | tf_op | source)
XLA Modules:
  0.0 118.4 jit_solution(3842054357446643939)
XLA Ops:
  0.6 0.7 convert_element_type.23
  1.3 0.7 copy.24
  2.0 0.9 copy.26
  2.9 1.3 %fusion.4 = (f32[1,2,2,64,4,128]{5,4,3,2,1,0:T(4,128)S(1)}, f32[1,2,2,64,4,128]{5,4,3,2,1,0:T(4,128)S(1)}) fusion(f32[2,2,2,64,4,128]{5,4,3,2,1,0:T(4,128)} %param.6), kind=kLoop, calls=%fused_computation.54 | loop fusion | bytes 2097152 | tf_op jit(solution)/shard_map/slice | solution.py:198
  4.3 0.8 fusion.6
  5.2 1.3 %collective-permute-start.1 = (f32[325,3,128]{2,0,1:T(8,128)}, f32[325,3,128]{2,0,1:T(8,128)}, u32[]{:S(2)}, u32[]{:S(2)}) collective-permute-start(f32[325,3,128]{2,0,1:T(8,128)} %get-tuple-element.28), channel_id=1, source_target_pairs={{2,0},{4,2},{6,4},{3,1},{5,3},{7,5},{10,8},{12,10},{14,12},{11,9},... | collective-permute-start | bytes 1497608 | tf_op jit(solution)/shard_map/ppermute | solution.py:39
  6.5 6.3 %collective-permute-start = (f32[325,3,128]{2,0,1:T(8,128)S(1)}, f32[325,3,128]{2,0,1:T(8,128)}, u32[]{:S(2)}, u32[]{:S(2)}) collective-permute-start(f32[325,3,128]{2,0,1:T(8,128)S(1)} %get-tuple-element.29), channel_id=1, source_target_pairs={{0,2},{2,4},{4,6},{1,3},{3,5},{5,7},{8,10},{10,12},{12,14},{9,11},... | collective-permute-start | bytes 1497608 | tf_op jit(solution)/shard_map/ppermute | solution.py:39
  12.8 0.5 concatenate.42
  13.3 1.4 %fusion.2 = (f32[581,4,3]{2,0,1:T(8,128)S(1)}, f32[581,4,3]{2,0,1:T(8,128)}) fusion(f32[581,4,128]{2,0,1:T(8,128)S(1)} %concatenate.42), kind=kLoop, calls=%fused_computation.52 | loop fusion | bytes 111552 | tf_op jit(solution)/shard_map/slice | solution.py:45
  14.8 1.7 %copy.34 = f32[581,4,3]{0,1,2:T(4,128)S(1)} copy(f32[581,4,3]{2,0,1:T(8,128)} %get-tuple-element.17) | data formatting | bytes 55776 | tf_op jit(solution)/shard_map/slice | solution.py:46
  16.5 1.3 %collective-permute-start.5 = (f32[581,4,3]{0,1,2:T(4,128)S(1)}, f32[581,4,3]{0,1,2:T(4,128)S(1)}, u32[]{:S(2)}, u32[]{:S(2)}) collective-permute-start(f32[581,4,3]{0,1,2:T(4,128)S(1)} %copy.34), channel_id=1, source_target_pairs={{1,0},{3,2},{5,4},{7,6},{9,8},{11,10},{13,12},{15,14},{17,16},{19,... | collective-permute-start | bytes 83672 | tf_op jit(solution)/shard_map/ppermute | solution.py:39
  17.8 0.4 copy.33
  18.2 3.0 %collective-permute-start.4 = (f32[581,4,3]{0,1,2:T(4,128)S(1)}, f32[581,4,3]{0,1,2:T(4,128)S(1)}, u32[]{:S(2)}, u32[]{:S(2)}) collective-permute-start(f32[581,4,3]{0,1,2:T(4,128)S(1)} %copy.33), channel_id=1, source_target_pairs={{0,1},{2,3},{4,5},{6,7},{8,9},{10,11},{12,13},{14,15},{16,17},{18,... | collective-permute-start | bytes 83672 | tf_op jit(solution)/shard_map/ppermute | solution.py:39
  21.5 0.1 maximum_maximum_fusion
  21.7 0.6 pad_convert_fusion.ins_ref
  22.3 0.6 slice_bitcast_fusion.27
  22.9 0.8 fusion
  23.6 0.4 copy.35
  24.1 1.5 %copy.36 = f32[581,4,3]{2,0,1:T(8,128)} copy(f32[581,4,3]{0,1,2:T(4,128)S(1)} %collective-permute-done.5) | data formatting | bytes 55776 | tf_op jit(solution)/shard_map/ppermute | solution.py:39
  25.5 2.8 %maximum_bitcast_fusion = (f32[325,134]{1,0:T(8,128)}, f32[325,134]{1,0:T(8,128)}, f32[325,134]{1,0:T(8,128)}, f32[325,134]{1,0:T(8,128)}) fusion(f32[581,4,3]{2,0,1:T(8,128)} %copy.36, f32[581,4,128]{2,0,1:T(8,128)S(1)} %concatenate.42, f32[581,4,3]{2,0,1:T(8,128)S(1)} %copy.35), kind=kLoop, calls=%fused_computation.10 | loop fusion | flops 348400 | bytes 1942464 | tf_op jit(solution)/shard_map/squeeze | solution.py:219
  28.3 1.1 constant_dynamic-update-slice_fusion.1
  29.4 1.1 constant_dynamic-update-slice_fusion
  30.5 1.3 %fusion.5 = (f32[325,6,3]{2,0,1:T(8,128)}, f32[325,6,3]{2,0,1:T(8,128)S(1)}) fusion(f32[325,6,128]{2,0,1:T(8,128)S(1)} %constant_dynamic-update-slice_fusion), kind=kLoop, calls=%fused_computation.55 | loop fusion | bytes 93600 | tf_op jit(solution)/shard_map/slice | solution.py:211
  31.8 1.7 %copy.27 = f32[325,6,3]{0,1,2:T(8,128)S(1)} copy(f32[325,6,3]{2,0,1:T(8,128)} %get-tuple-element.26) | data formatting | bytes 46800 | tf_op jit(solution)/shard_map/slice | solution.py:211
  33.5 0.5 copy.28
  33.9 1.3 %collective-permute-start.3 = (f32[325,6,3]{0,1,2:T(8,128)S(1)}, f32[325,6,3]{0,1,2:T(8,128)S(1)}, u32[]{:S(2)}, u32[]{:S(2)}) collective-permute-start(f32[325,6,3]{0,1,2:T(8,128)S(1)} %copy.28), channel_id=1, source_target_pairs={{1,0},{3,2},{5,4},{7,6},{9,8},{11,10},{13,12},{15,14},{17,16},{19,... | collective-permute-start | bytes 70208 | tf_op jit(solution)/shard_map/ppermute | solution.py:39
  35.2 3.0 %collective-permute-start.2 = (f32[325,6,3]{0,1,2:T(8,128)S(1)}, f32[325,6,3]{0,1,2:T(8,128)S(1)}, u32[]{:S(2)}, u32[]{:S(2)}) collective-permute-start(f32[325,6,3]{0,1,2:T(8,128)S(1)} %copy.27), channel_id=1, source_target_pairs={{0,1},{2,3},{4,5},{6,7},{8,9},{10,11},{12,13},{14,15},{16,17},{18,... | collective-permute-start | bytes 70208 | tf_op jit(solution)/shard_map/ppermute | solution.py:39
  38.3 1.7 %pad_maximum_fusion.1 = f32[256,4,134]{2,0,1:T(8,128)S(1)} fusion(f32[581,4,3]{2,0,1:T(8,128)} %copy.36, f32[581,4,128]{2,0,1:T(8,128)S(1)} %concatenate.42, f32[581,4,3]{2,0,1:T(8,128)} %copy-done), kind=kLoop, calls=%fused_computation.1 | loop fusion | flops 274432 | bytes 1794528 | tf_op jit(solution)/shard_map/concatenate | solution.py:47
  40.0 0.3 copy.29
  40.4 1.3 %copy.30 = f32[325,6,3]{2,0,1:T(8,128)} copy(f32[325,6,3]{0,1,2:T(8,128)S(1)} %collective-permute-done.3) | data formatting | bytes 46800 | tf_op jit(solution)/shard_map/ppermute | solution.py:39
  41.7 2.1 %pad_maximum_fusion = f32[325,6,134]{2,0,1:T(8,128)S(1)} fusion(f32[325,6,3]{2,0,1:T(8,128)} %copy.30, f32[325,6,128]{2,0,1:T(8,128)S(1)} %constant_dynamic-update-slice_fusion, f32[325,6,3]{2,0,1:T(8,128)S(1)} %copy.29), kind=kLoop, calls=%fused_computation | loop fusion | flops 522600 | bytes 2090400 | tf_op jit(solution)/shard_map/concatenate | solution.py:213
  43.8 1.1 slice_bitcast_fusion
  44.9 0.2 copy-done.4
  45.1 0.3 copy-done.5
  45.5 3.9 %concatenate.44.frc_ref.pk_ref = f32[325,1408]{1,0:T(8,128)} concatenate(f32[325,134]{1,0:T(8,128)} %get-tuple-element.15, f32[325,134]{1,0:T(8,128)} %get-tuple-element.14, f32[325,134]{1,0:T(8,128)} %get-tuple-element.13, f32[325,134]{1,0:T(8,128)S(1)} %copy-done.6, f32[325,134]{1,0:T(8,128)S(1)} %copy-done.5, f32[325,134]{1,0:T(8,128)S(1)} %copy-done.4, ...), dimensions={1} | concatenate | bytes 3660800 | tf_op jit(solution)/shard_map/concatenate | solution.py:223
  49.4 0.8 slice.243
  50.2 0.6 reshape.68.inc_ref
  50.9 11.0 %shard_map.77 = f32[2,128,512]{2,1,0:T(8,128)} custom-call(s32[2]{0:T(128)} %get-tuple-element.58.order_ref, f32[325,1408]{1,0:T(8,128)} %concatenate.44.frc_ref.pk_ref, f32[325,1408]{1,0:T(8,128)} %concatenate.44.frc_ref.pk_ref, f32[2,2,1408]{2,1,0:T(2,128)} %reshape.68.inc_ref, f32[1,1408]{1,0:T(1,128)} %pad_convert_fusion.ins_ref, ...), custom_call_target="tpu_custom_call" | custom-call | flops 4429185024 | bytes 2812288 | tf_op jit(solution)/shard_map/pallas_call | solution.py:157
  61.9 1.2 %reshape.69 = f32[2,2,64,4,128]{4,3,2,1,0:T(4,128)S(1)} reshape(f32[2,128,512]{2,1,0:T(8,128)} %shard_map.77) | data formatting | bytes 1048576 | tf_op jit(solution)/shard_map/reshape | solution.py:249
  63.2 1.4 %collective-permute-start.8 = (f32[2,2,4,3]{3,1,0,2:T(2,128)S(1)}, f32[2,2,4,3]{3,1,0,2:T(2,128)S(1)}, u32[]{:S(2)}, u32[]{:S(2)}) collective-permute-start(f32[2,2,4,3]{3,1,0,2:T(2,128)S(1)} %get-tuple-element.56), channel_id=1, source_target_pairs={{0,1},{2,3},{4,5},{6,7},{8,9},{10,11},{12,13},{14,15},{16,17},{18,... | collective-permute-start | bytes 584 | tf_op jit(solution)/shard_map/ppermute | solution.py:39
  64.6 1.3 %collective-permute-start.9 = (f32[2,2,4,3]{3,1,0,2:T(2,128)S(1)}, f32[2,2,4,3]{3,1,0,2:T(2,128)S(1)}, u32[]{:S(2)}, u32[]{:S(2)}) collective-permute-start(f32[2,2,4,3]{3,1,0,2:T(2,128)S(1)} %get-tuple-element.57), channel_id=1, source_target_pairs={{1,0},{3,2},{5,4},{7,6},{9,8},{11,10},{13,12},{15,14},{17,16},{19,... | collective-permute-start | bytes 584 | tf_op jit(solution)/shard_map/ppermute | solution.py:39
  65.9 0.1 fusion.3
  66.1 1.6 %collective-permute-done.9 = f32[2,2,4,3]{3,1,0,2:T(2,128)S(1)} collective-permute-done((f32[2,2,4,3]{3,1,0,2:T(2,128)S(1)}, f32[2,2,4,3]{3,1,0,2:T(2,128)S(1)}, u32[]{:S(2)}, u32[]{:S(2)}) %collective-permute-start.9) | collective-permute-done | bytes 224 | tf_op jit(solution)/shard_map/ppermute | solution.py:39
  67.8 0.6 fusion.9
  68.4 1.2 %collective-permute-start.12 = (f32[2,2,3,134]{3,1,0,2:T(2,128)}, f32[2,2,3,134]{3,1,0,2:T(2,128)}, u32[]{:S(2)}, u32[]{:S(2)}) collective-permute-start(f32[2,2,3,134]{3,1,0,2:T(2,128)} %get-tuple-element.44), channel_id=1, source_target_pairs={{2,8},{4,10},{6,12},{10,16},{12,18},{14,20},{18,24},{20,26},{22,28... | collective-permute-start | bytes 19304 | tf_op jit(solution)/shard_map/ppermute | solution.py:40
  69.6 1.0 slice_bitcast_fusion.6
  70.6 0.2 stack_reshape.6
  70.8 0.2 copy.42
  71.1 0.2 copy.38
  71.3 6.7 %collective-permute-start.6 = (f32[256,3,134]{0,2,1:T(8,128)S(1)}, f32[256,3,134]{0,2,1:T(8,128)S(1)}, u32[]{:S(2)}, u32[]{:S(2)}) collective-permute-start(f32[256,3,134]{0,2,1:T(8,128)S(1)} %copy.38), channel_id=1, source_target_pairs={{0,2},{2,4},{4,6},{1,3},{3,5},{5,7},{8,10},{10,12},{12,14},{9,11},... | collective-permute-start | bytes 1234952 | tf_op jit(solution)/shard_map/ppermute | solution.py:39
  78.1 1.3 %collective-permute-start.7 = (f32[256,3,134]{0,2,1:T(8,128)S(1)}, f32[256,3,134]{0,2,1:T(8,128)}, u32[]{:S(2)}, u32[]{:S(2)}) collective-permute-start(f32[256,3,134]{0,2,1:T(8,128)S(1)} %copy.42), channel_id=1, source_target_pairs={{2,0},{4,2},{6,4},{3,1},{5,3},{7,5},{10,8},{12,10},{14,12},{11,9},... | collective-permute-start | bytes 1234952 | tf_op jit(solution)/shard_map/ppermute | solution.py:39
  79.4 3.3 %collective-permute-start.11 = (f32[2,2,4,134]{3,1,0,2:T(2,128)S(1)}, f32[2,2,4,134]{3,1,0,2:T(2,128)S(1)}, u32[]{:S(2)}, u32[]{:S(2)}) collective-permute-start(f32[2,2,4,134]{3,1,0,2:T(2,128)S(1)} %copy-done.13), channel_id=1, source_target_pairs={{0,8},{2,10},{4,12},{6,14},{8,16},{10,18},{12,20},{14,22},{16,24},... | collective-permute-start | bytes 25736 | tf_op jit(solution)/shard_map/ppermute | solution.py:40
  82.7 7.6 %collective-permute-start.10 = (f32[2,2,3,134]{3,1,0,2:T(2,128)S(1)}, f32[2,2,3,134]{3,1,0,2:T(2,128)S(1)}, u32[]{:S(2)}, u32[]{:S(2)}) collective-permute-start(f32[2,2,3,134]{3,1,0,2:T(2,128)S(1)} %copy-done.14), channel_id=1, source_target_pairs={{0,10},{2,12},{4,14},{8,18},{10,20},{12,22},{16,26},{18,28},{20,30... | collective-permute-start | bytes 19304 | tf_op jit(solution)/shard_map/ppermute | solution.py:40
  90.3 0.7 slice_bitcast_fusion.16
  91.0 0.5 collective-permute-done.10
  91.5 0.7 concatenate.51.inc_ref
  92.8 8.0 %collective-permute-done.7 = f32[256,3,134]{0,2,1:T(8,128)} collective-permute-done((f32[256,3,134]{0,2,1:T(8,128)S(1)}, f32[256,3,134]{0,2,1:T(8,128)}, u32[]{:S(2)}, u32[]{:S(2)}) %collective-permute-start.7) | collective-permute-done | bytes 411680 | tf_op jit(solution)/shard_map/ppermute | solution.py:39
  100.8 1.1 fusion.7
  102.3 1.9 %concatenate.49.frc_ref = f32[256,1408]{1,0:T(8,128)} concatenate(f32[256,134]{1,0:T(8,128)S(1)} %bitcast.89, f32[256,134]{1,0:T(8,128)S(1)} %bitcast.88, f32[256,134]{1,0:T(8,128)S(1)} %bitcast.87, f32[256,134]{1,0:T(8,128)S(1)} %copy-done.10, f32[256,134]{1,0:T(8,128)S(1)} %copy-done.9, f32[256,134]{1,0:T(8,128)S(1)} %copy-done.8, f32[256,134]{1,0:T(8,128)S(1)} %copy-done.7, ...), dimensions={1} | concatenate | bytes 2883584 | tf_op jit(solution)/shard_map/concatenate | solution.py:68
  104.2 10.9 %shard_map.78 = f32[2,128,512]{2,1,0:T(8,128)} custom-call(s32[2]{0:T(128)} %get-tuple-element.59.order_ref, f32[256,1408]{1,0:T(8,128)} %concatenate.49.frc_ref, f32[325,1408]{1,0:T(8,128)} %concatenate.44.frc_ref.pk_ref, f32[2,2,1408]{2,1,0:T(2,128)} %concatenate.51.inc_ref, f32[1,1408]{1,0:T(1,128)} %pad_convert_fusion.ins_ref, ...), custom_call_target="tpu_custom_call" | custom-call | flops 4429185024 | bytes 2423680 | tf_op jit(solution)/shard_map/pallas_call | solution.py:157
  115.1 1.3 %reshape.70 = f32[2,2,64,4,128]{4,3,2,1,0:T(4,128)S(1)} reshape(f32[2,128,512]{2,1,0:T(8,128)} %shard_map.78) | data formatting | bytes 1048576 | tf_op jit(solution)/shard_map/reshape | solution.py:249
  116.4 0.2 stack_reshape.7
  116.6 0.6 slice.271
  117.2 1.2 %pad_maximum_fusion.3 = f32[2,2,2,64,4,128]{5,4,3,2,1,0:T(4,128)} fusion(f32[1,2,2,64,4,128]{5,4,3,2,1,0:T(4,128)S(1)} %stack_reshape.7, f32[1,2,2,64,4,128]{5,4,3,2,1,0:T(4,128)S(1)} %stack_reshape.6), kind=kLoop, calls=%fused_computation.3 | loop fusion | flops 262144 | bytes 2097152 | tf_op jit(solution)/shard_map/stack | solution.py:254
  (67 shorter events, 1.6 us)
Async XLA Ops:
  5.2 24.2 %collective-permute-start.1 = (f32[325,3,128]{2,0,1:T(8,128)}, f32[325,3,128]{2,0,1:T(8,128)}, u32[]{:S(2)}, u32[]{:S(2)}) collective-permute-start(f32[325,3,128]{2,0,1:T(8,128)} %get-tuple-element.28), channel_id=1, source_target_pairs={{2,0},{4,2},{6,4},{3,1},{5,3},{7,5},{10,8},{12,10},{14,12},{11,9},... | collective-permute-start | bytes 1497608 | tf_op jit(solution)/shard_map/ppermute | solution.py:39
  6.5 21.9 %collective-permute-start = (f32[325,3,128]{2,0,1:T(8,128)S(1)}, f32[325,3,128]{2,0,1:T(8,128)}, u32[]{:S(2)}, u32[]{:S(2)}) collective-permute-start(f32[325,3,128]{2,0,1:T(8,128)S(1)} %get-tuple-element.29), channel_id=1, source_target_pairs={{0,2},{2,4},{4,6},{1,3},{3,5},{5,7},{8,10},{10,12},{12,14},{9,11},... | collective-permute-start | bytes 1497608 | tf_op jit(solution)/shard_map/ppermute | solution.py:39
  14.8 6.5 %copy-start.11 = (f32[1,4,2,64,64]{4,3,2,1,0:T(8,128)S(1)}, f32[1,4,2,64,64]{4,3,2,1,0:T(8,128)}, u32[]{:S(2)}) copy-start(f32[1,4,2,64,64]{4,3,2,1,0:T(8,128)} %param.8) | copy-start | bytes 393220
  16.5 7.6 %collective-permute-start.5 = (f32[581,4,3]{0,1,2:T(4,128)S(1)}, f32[581,4,3]{0,1,2:T(4,128)S(1)}, u32[]{:S(2)}, u32[]{:S(2)}) collective-permute-start(f32[581,4,3]{0,1,2:T(4,128)S(1)} %copy.34), channel_id=1, source_target_pairs={{1,0},{3,2},{5,4},{7,6},{9,8},{11,10},{13,12},{15,14},{17,16},{19,... | collective-permute-start | bytes 83672 | tf_op jit(solution)/shard_map/ppermute | solution.py:39
  18.2 5.5 %collective-permute-start.4 = (f32[581,4,3]{0,1,2:T(4,128)S(1)}, f32[581,4,3]{0,1,2:T(4,128)S(1)}, u32[]{:S(2)}, u32[]{:S(2)}) collective-permute-start(f32[581,4,3]{0,1,2:T(4,128)S(1)} %copy.33), channel_id=1, source_target_pairs={{0,1},{2,3},{4,5},{6,7},{8,9},{10,11},{12,13},{14,15},{16,17},{18,... | collective-permute-start | bytes 83672 | tf_op jit(solution)/shard_map/ppermute | solution.py:39
  21.2 1.1 copy-start.15
  24.1 4.3 %copy-start = (f32[581,4,3]{2,0,1:T(8,128)}, f32[581,4,3]{2,0,1:T(8,128)S(1)}, u32[]{:S(2)}) copy-start(f32[581,4,3]{2,0,1:T(8,128)S(1)} %copy.35) | copy-start | bytes 83668
  33.9 6.4 %collective-permute-start.3 = (f32[325,6,3]{0,1,2:T(8,128)S(1)}, f32[325,6,3]{0,1,2:T(8,128)S(1)}, u32[]{:S(2)}, u32[]{:S(2)}) collective-permute-start(f32[325,6,3]{0,1,2:T(8,128)S(1)} %copy.28), channel_id=1, source_target_pairs={{1,0},{3,2},{5,4},{7,6},{9,8},{11,10},{13,12},{15,14},{17,16},{19,... | collective-permute-start | bytes 70208 | tf_op jit(solution)/shard_map/ppermute | solution.py:39
  35.2 4.7 %collective-permute-start.2 = (f32[325,6,3]{0,1,2:T(8,128)S(1)}, f32[325,6,3]{0,1,2:T(8,128)S(1)}, u32[]{:S(2)}, u32[]{:S(2)}) collective-permute-start(f32[325,6,3]{0,1,2:T(8,128)S(1)} %copy.27), channel_id=1, source_target_pairs={{0,1},{2,3},{4,5},{6,7},{8,9},{10,11},{12,13},{14,15},{16,17},{18,... | collective-permute-start | bytes 70208 | tf_op jit(solution)/shard_map/ppermute | solution.py:39
  43.7 1.2 copy-start.3
  43.7 1.4 %copy-start.4 = (f32[325,134]{1,0:T(8,128)S(1)}, f32[325,134]{1,0:T(8,128)}, u32[]{:S(2)}) copy-start(f32[325,134]{1,0:T(8,128)} %get-tuple-element.7) | copy-start | bytes 522604
  43.7 1.6 %copy-start.5 = (f32[325,134]{1,0:T(8,128)S(1)}, f32[325,134]{1,0:T(8,128)}, u32[]{:S(2)}) copy-start(f32[325,134]{1,0:T(8,128)} %get-tuple-element.8) | copy-start | bytes 522604
  43.8 1.7 %copy-start.6 = (f32[325,134]{1,0:T(8,128)S(1)}, f32[325,134]{1,0:T(8,128)}, u32[]{:S(2)}) copy-start(f32[325,134]{1,0:T(8,128)} %get-tuple-element.9) | copy-start | bytes 522604
  63.2 2.9 %collective-permute-start.8 = (f32[2,2,4,3]{3,1,0,2:T(2,128)S(1)}, f32[2,2,4,3]{3,1,0,2:T(2,128)S(1)}, u32[]{:S(2)}, u32[]{:S(2)}) collective-permute-start(f32[2,2,4,3]{3,1,0,2:T(2,128)S(1)} %get-tuple-element.56), channel_id=1, source_target_pairs={{0,1},{2,3},{4,5},{6,7},{8,9},{10,11},{12,13},{14,15},{16,17},{18,... | collective-permute-start | bytes 584 | tf_op jit(solution)/shard_map/ppermute | solution.py:39
  64.6 3.1 %collective-permute-start.9 = (f32[2,2,4,3]{3,1,0,2:T(2,128)S(1)}, f32[2,2,4,3]{3,1,0,2:T(2,128)S(1)}, u32[]{:S(2)}, u32[]{:S(2)}) collective-permute-start(f32[2,2,4,3]{3,1,0,2:T(2,128)S(1)} %get-tuple-element.57), channel_id=1, source_target_pairs={{1,0},{3,2},{5,4},{7,6},{9,8},{11,10},{13,12},{15,14},{17,16},{19,... | collective-permute-start | bytes 584 | tf_op jit(solution)/shard_map/ppermute | solution.py:39
  66.0 4.6 %copy-start.1 = (f32[2,128,512]{2,1,0:T(8,128)S(1)}, f32[2,128,512]{2,1,0:T(8,128)}, u32[]{:S(2)}) copy-start(f32[2,128,512]{2,1,0:T(8,128)} %shard_map.77) | copy-start | bytes 1572868
  67.8 1.9 %copy-start.12 = (f32[2,2,4,134]{3,1,0,2:T(2,128)}, f32[2,2,4,134]{3,1,0,2:T(2,128)S(1)}, u32[]{:S(2)}) copy-start(f32[2,2,4,134]{3,1,0,2:T(2,128)S(1)} %pad_maximum_fusion.6) | copy-start | bytes 25732
  68.4 22.0 %collective-permute-start.12 = (f32[2,2,3,134]{3,1,0,2:T(2,128)}, f32[2,2,3,134]{3,1,0,2:T(2,128)}, u32[]{:S(2)}, u32[]{:S(2)}) collective-permute-start(f32[2,2,3,134]{3,1,0,2:T(2,128)} %get-tuple-element.44), channel_id=1, source_target_pairs={{2,8},{4,10},{6,12},{10,16},{12,18},{14,20},{18,24},{20,26},{22,28... | collective-permute-start | bytes 19304 | tf_op jit(solution)/shard_map/ppermute | solution.py:40
  70.8 8.5 %copy-start.13 = (f32[2,2,4,134]{3,1,0,2:T(2,128)S(1)}, f32[2,2,4,134]{3,1,0,2:T(2,128)}, u32[]{:S(2)}) copy-start(f32[2,2,4,134]{3,1,0,2:T(2,128)} %copy-done.12) | copy-start | bytes 25732
  70.8 11.8 %copy-start.14 = (f32[2,2,3,134]{3,1,0,2:T(2,128)S(1)}, f32[2,2,3,134]{3,1,0,2:T(2,128)}, u32[]{:S(2)}) copy-start(f32[2,2,3,134]{3,1,0,2:T(2,128)} %get-tuple-element.45) | copy-start | bytes 19300
  71.3 21.0 %collective-permute-start.6 = (f32[256,3,134]{0,2,1:T(8,128)S(1)}, f32[256,3,134]{0,2,1:T(8,128)S(1)}, u32[]{:S(2)}, u32[]{:S(2)}) collective-permute-start(f32[256,3,134]{0,2,1:T(8,128)S(1)} %copy.38), channel_id=1, source_target_pairs={{0,2},{2,4},{4,6},{1,3},{3,5},{5,7},{8,10},{10,12},{12,14},{9,11},... | collective-permute-start | bytes 1234952 | tf_op jit(solution)/shard_map/ppermute | solution.py:39
  78.1 22.7 %collective-permute-start.7 = (f32[256,3,134]{0,2,1:T(8,128)S(1)}, f32[256,3,134]{0,2,1:T(8,128)}, u32[]{:S(2)}, u32[]{:S(2)}) collective-permute-start(f32[256,3,134]{0,2,1:T(8,128)S(1)} %copy.42), channel_id=1, source_target_pairs={{2,0},{4,2},{6,4},{3,1},{5,3},{7,5},{10,8},{12,10},{14,12},{11,9},... | collective-permute-start | bytes 1234952 | tf_op jit(solution)/shard_map/ppermute | solution.py:39
  79.4 12.2 %collective-permute-start.11 = (f32[2,2,4,134]{3,1,0,2:T(2,128)S(1)}, f32[2,2,4,134]{3,1,0,2:T(2,128)S(1)}, u32[]{:S(2)}, u32[]{:S(2)}) collective-permute-start(f32[2,2,4,134]{3,1,0,2:T(2,128)S(1)} %copy-done.13), channel_id=1, source_target_pairs={{0,8},{2,10},{4,12},{6,14},{8,16},{10,18},{12,20},{14,22},{16,24},... | collective-permute-start | bytes 25736 | tf_op jit(solution)/shard_map/ppermute | solution.py:40
  82.7 8.9 %collective-permute-start.10 = (f32[2,2,3,134]{3,1,0,2:T(2,128)S(1)}, f32[2,2,3,134]{3,1,0,2:T(2,128)S(1)}, u32[]{:S(2)}, u32[]{:S(2)}) collective-permute-start(f32[2,2,3,134]{3,1,0,2:T(2,128)S(1)} %copy-done.14), channel_id=1, source_target_pairs={{0,10},{2,12},{4,14},{8,18},{10,20},{12,22},{16,26},{18,28},{20,30... | collective-permute-start | bytes 19304 | tf_op jit(solution)/shard_map/ppermute | solution.py:40
  92.7 9.6 %copy-start.7 = (f32[256,134]{1,0:T(8,128)S(1)}, f32[256,134]{1,0:T(8,128)}, u32[]{:S(2)}) copy-start(f32[256,134]{1,0:T(8,128)} %get-tuple-element.20) | copy-start | bytes 411652
  92.8 9.6 %copy-start.8 = (f32[256,134]{1,0:T(8,128)S(1)}, f32[256,134]{1,0:T(8,128)}, u32[]{:S(2)}) copy-start(f32[256,134]{1,0:T(8,128)} %get-tuple-element.21) | copy-start | bytes 411652
  92.8 9.6 %copy-start.9 = (f32[256,134]{1,0:T(8,128)S(1)}, f32[256,134]{1,0:T(8,128)}, u32[]{:S(2)}) copy-start(f32[256,134]{1,0:T(8,128)} %get-tuple-element.22) | copy-start | bytes 411652
  92.8 9.6 %copy-start.10 = (f32[256,134]{1,0:T(8,128)S(1)}, f32[256,134]{1,0:T(8,128)}, u32[]{:S(2)}) copy-start(f32[256,134]{1,0:T(8,128)} %get-tuple-element.23) | copy-start | bytes 411652
  115.1 1.3 %copy-start.2 = (f32[2,128,512]{2,1,0:T(8,128)S(1)}, f32[2,128,512]{2,1,0:T(8,128)}, u32[]{:S(2)}) copy-start(f32[2,128,512]{2,1,0:T(8,128)} %shard_map.78) | copy-start | bytes 1572868

commit v12 on v11

--- a/solution.py
+++ b/solution.py
@@ -236,6 +236,8 @@
     orders = batch_order[:, 0]
 
     incoming = packed[first_pending : first_pending + nsrc * two].reshape(nsrc, two, padded)
+    low_later = [fetch(r[:, nx - width :, :], ("tx",), (-1,)) for r in later]
+    high_later = [fetch(r[:, :width, :], ("tx",), (1,)) for r in later]
     solutions = []
     trace = None
     forcing_f = packed
@@ -244,8 +246,13 @@
             orders[tick], forcing_f, packed, incoming, inside, bhi, blo, ey, depth, width, nx * ny
         )
         if tick + 1 < ticks:
-            field, rows = lax.optimization_barrier((field, later[tick]))
-            forcing_f = flat_extended(rows, width, padded)
+            rows = later[tick]
+            field, low, high = lax.optimization_barrier((field, low_later[tick], high_later[tick]))
+            segments = [low[:, ix] for ix in range(width)]
+            segments += [rows[:, r] for r in range(nx)]
+            segments += [high[:, r] for r in range(width)]
+            segments.append(jnp.zeros((rows.shape[0], padded - cols), jnp.float32))
+            forcing_f = jnp.concatenate(segments, axis=-1)
         tile = field.reshape(nsrc, two, depth, nx, ny)
         solutions.append(tile)
         trace = tile[:, :, depth - 1]

time: 119 us -> 115 us (0.966)
  the two profiles are of different devices: /device:TPU:0 before, /device:TPU:12 now
where the time goes in v12:
time: 115 us; the launch traced here: 114 us
  local copies, waits for them, and re-layouts  41.4 us (36%)
  starting transfers between devices  33.9 us (29%)
  Pallas kernels  22 us (19%)
  waiting for transfers between devices  7.76 us (7%)
  other arithmetic  7.55 us (7%)
  between operations  1.2 us (1%)
    ppermute x10, starting transfers between devices, fetch(): return lax.ppermute(block, axes[0], pairs)  23.1 us
    pallas_call x2, Pallas kernels, run_tick(): pl.pallas_call(functools.partial(tick_kernel, row=row, depth=depth, width...  22 us
    ppermute x3, starting transfers between devices, fetch(): return lax.ppermute(block, tuple(axes), pairs)  10.8 us
    ppermute x3, waiting for transfers between devices, fetch(): return lax.ppermute(block, tuple(axes), pairs)  5.44 us
    ppermute x4, local copies, waits for them, and re-layouts, fetch(): return lax.ppermute(block, axes[0], pairs)  4.5 us
    slice x2, local copies, waits for them, and re-layouts, per_device(): high_later = [fetch(r[:, :width, :], ('tx',), (1,)) for r in later]  3.59 us
    slice x2, local copies, waits for them, and re-layouts, per_device(): corner_low = fetch(rims[..., ny - width:], ('ty',), (-1,))  3.27 us
    concatenate x1, local copies, waits for them, and re-layouts, per_device(): packed = jnp.concatenate(segments, axis=-1)  3.24 us
  transfers between devices with their start and end apart: 13, of which 2 were waited for; matrix products, arithmetic and copies ran while one was open for 31% of the time, Pallas kernels for 10%

profile of v12, /device:TPU:12, one launch (start us, length us, event | category | flops | bytes accessed | tf_op | source)
XLA Modules:
  0.0 113.9 jit_solution(16796019334323712316)
XLA Ops:
  0.7 1.3 %fusion.4 = (f32[1,2,2,64,4,128]{5,4,3,2,1,0:T(4,128)S(1)}, f32[1,2,2,64,4,128]{5,4,3,2,1,0:T(4,128)S(1)}) fusion(f32[2,2,2,64,4,128]{5,4,3,2,1,0:T(4,128)} %param.6), kind=kLoop, calls=%fused_computation.59 | loop fusion | bytes 2097152 | tf_op jit(solution)/shard_map/slice | solution.py:198
  2.2 1.0 fusion.6
  3.2 3.4 %collective-permute-start = (f32[325,3,128]{2,0,1:T(8,128)}, f32[325,3,128]{2,0,1:T(8,128)S(1)}, u32[]{:S(2)}, u32[]{:S(2)}) collective-permute-start(f32[325,3,128]{2,0,1:T(8,128)} %get-tuple-element.37), channel_id=1, source_target_pairs={{0,2},{2,4},{4,6},{1,3},{3,5},{5,7},{8,10},{10,12},{12,14},{9,11},... | collective-permute-start | bytes 1497608 | tf_op jit(solution)/shard_map/ppermute | solution.py:39
  6.6 3.3 %collective-permute-start.1 = (f32[325,3,128]{2,0,1:T(8,128)}, f32[325,3,128]{2,0,1:T(8,128)S(1)}, u32[]{:S(2)}, u32[]{:S(2)}) collective-permute-start(f32[325,3,128]{2,0,1:T(8,128)} %get-tuple-element.36), channel_id=1, source_target_pairs={{2,0},{4,2},{6,4},{3,1},{5,3},{7,5},{10,8},{12,10},{14,12},{11,9},... | collective-permute-start | bytes 1497608 | tf_op jit(solution)/shard_map/ppermute | solution.py:39
  10.0 0.5 concatenate.42
  10.5 1.4 %fusion.3 = (f32[581,4,3]{2,0,1:T(8,128)}, f32[581,4,3]{2,0,1:T(8,128)S(1)}) fusion(f32[581,4,128]{2,0,1:T(8,128)S(1)} %concatenate.42), kind=kLoop, calls=%fused_computation.58 | loop fusion | bytes 111552 | tf_op jit(solution)/shard_map/slice | solution.py:45
  12.0 1.7 %copy.33 = f32[581,4,3]{0,1,2:T(4,128)S(1)} copy(f32[581,4,3]{2,0,1:T(8,128)} %get-tuple-element.24) | data formatting | bytes 55776 | tf_op jit(solution)/shard_map/slice | solution.py:45
  13.6 1.4 %collective-permute-start.4 = (f32[581,4,3]{0,1,2:T(4,128)S(1)}, f32[581,4,3]{0,1,2:T(4,128)S(1)}, u32[]{:S(2)}, u32[]{:S(2)}) collective-permute-start(f32[581,4,3]{0,1,2:T(4,128)S(1)} %copy.33), channel_id=1, source_target_pairs={{0,1},{2,3},{4,5},{6,7},{8,9},{10,11},{12,13},{14,15},{16,17},{18,... | collective-permute-start | bytes 83672 | tf_op jit(solution)/shard_map/ppermute | solution.py:39
  15.1 0.4 copy.34
  15.5 1.3 %collective-permute-start.5 = (f32[581,4,3]{0,1,2:T(4,128)S(1)}, f32[581,4,3]{0,1,2:T(4,128)S(1)}, u32[]{:S(2)}, u32[]{:S(2)}) collective-permute-start(f32[581,4,3]{0,1,2:T(4,128)S(1)} %copy.34), channel_id=1, source_target_pairs={{1,0},{3,2},{5,4},{7,6},{9,8},{11,10},{13,12},{15,14},{17,16},{19,... | collective-permute-start | bytes 83672 | tf_op jit(solution)/shard_map/ppermute | solution.py:39
  16.8 1.0 copy.50
  17.8 0.1 maximum_maximum_fusion
  18.0 0.1 broadcast_and_fusion
  18.1 0.1 convert_element_type.24
  18.2 0.6 pad_convert_fusion.ins_ref
  18.8 0.5 slice_bitcast_fusion.37
  19.3 0.7 fusion
  20.1 0.0 collective-permute-done.4
  20.1 0.4 copy.35
  20.5 1.5 %copy.36 = f32[581,4,3]{2,0,1:T(8,128)} copy(f32[581,4,3]{0,1,2:T(4,128)S(1)} %collective-permute-done.5) | data formatting | bytes 55776 | tf_op jit(solution)/shard_map/ppermute | solution.py:39
  21.9 2.3 %pad_maximum_fusion = f32[581,4,134]{2,0,1:T(8,128)S(1)} fusion(f32[581,4,3]{2,0,1:T(8,128)} %copy.36, f32[581,4,128]{2,0,1:T(8,128)S(1)} %concatenate.42, f32[581,4,3]{2,0,1:T(8,128)S(1)} %copy.35), kind=kLoop, calls=%fused_computation | loop fusion | flops 622832 | bytes 2491328 | tf_op jit(solution)/shard_map/concatenate | solution.py:47
  24.2 1.5 %fusion.2 = (f32[256,3,134]{2,0,1:T(8,128)}, f32[256,3,134]{2,0,1:T(8,128)}) fusion(f32[581,4,134]{2,0,1:T(8,128)S(1)} %pad_maximum_fusion), kind=kLoop, calls=%fused_computation.57 | loop fusion | bytes 1646592 | tf_op jit(solution)/shard_map/slice | solution.py:240
  25.7 0.4 copy-done
  26.1 2.3 %collective-permute-done.1 = f32[325,3,128]{2,0,1:T(8,128)S(1)} collective-permute-done((f32[325,3,128]{2,0,1:T(8,128)}, f32[325,3,128]{2,0,1:T(8,128)S(1)}, u32[]{:S(2)}, u32[]{:S(2)}) %collective-permute-start.1) | collective-permute-done | bytes 499232 | tf_op jit(solution)/shard_map/ppermute | solution.py:39
  28.5 1.6 %fusion.5 = (f32[325,6,3]{2,0,1:T(8,128)}, f32[325,6,3]{2,0,1:T(8,128)}) fusion(f32[325,6,128]{2,0,1:T(8,128)S(1)} %constant_dynamic-update-slice_fusion), kind=kLoop, calls=%fused_computation.60 | loop fusion | bytes 93600 | tf_op jit(solution)/shard_map/slice | solution.py:211
  30.1 1.7 %copy.27 = f32[325,6,3]{0,1,2:T(8,128)S(1)} copy(f32[325,6,3]{2,0,1:T(8,128)} %get-tuple-element.28) | data formatting | bytes 46800 | tf_op jit(solution)/shard_map/slice | solution.py:211
  31.8 1.3 %collective-permute-start.2 = (f32[325,6,3]{0,1,2:T(8,128)S(1)}, f32[325,6,3]{0,1,2:T(8,128)S(1)}, u32[]{:S(2)}, u32[]{:S(2)}) collective-permute-start(f32[325,6,3]{0,1,2:T(8,128)S(1)} %copy.27), channel_id=1, source_target_pairs={{0,1},{2,3},{4,5},{6,7},{8,9},{10,11},{12,13},{14,15},{16,17},{18,... | collective-permute-start | bytes 70208 | tf_op jit(solution)/shard_map/ppermute | solution.py:39
  33.1 1.7 %copy.28 = f32[325,6,3]{0,1,2:T(8,128)S(1)} copy(f32[325,6,3]{2,0,1:T(8,128)} %get-tuple-element.29) | data formatting | bytes 46800 | tf_op jit(solution)/shard_map/slice | solution.py:212
  34.7 1.3 %collective-permute-start.3 = (f32[325,6,3]{0,1,2:T(8,128)S(1)}, f32[325,6,3]{0,1,2:T(8,128)S(1)}, u32[]{:S(2)}, u32[]{:S(2)}) collective-permute-start(f32[325,6,3]{0,1,2:T(8,128)S(1)} %copy.28), channel_id=1, source_target_pairs={{1,0},{3,2},{5,4},{7,6},{9,8},{11,10},{13,12},{15,14},{17,16},{19,... | collective-permute-start | bytes 70208 | tf_op jit(solution)/shard_map/ppermute | solution.py:39
  36.1 1.0 slice_bitcast_fusion.13
  37.1 2.1 %copy.38 = f32[256,3,134]{0,2,1:T(8,128)} copy(f32[256,3,134]{2,0,1:T(8,128)} %get-tuple-element.13) | data formatting | bytes 823296 | tf_op jit(solution)/shard_map/slice | solution.py:239
  39.2 2.0 %collective-permute-start.6 = (f32[256,3,134]{0,2,1:T(8,128)}, f32[256,3,134]{0,2,1:T(8,128)}, u32[]{:S(2)}, u32[]{:S(2)}) collective-permute-start(f32[256,3,134]{0,2,1:T(8,128)} %copy.38), channel_id=1, source_target_pairs={{0,2},{2,4},{4,6},{1,3},{3,5},{5,7},{8,10},{10,12},{12,14},{9,11},... | collective-permute-start | bytes 1234952 | tf_op jit(solution)/shard_map/ppermute | solution.py:39
  41.2 2.1 %copy.39 = f32[256,3,134]{0,2,1:T(8,128)} copy(f32[256,3,134]{2,0,1:T(8,128)} %get-tuple-element.12) | data formatting | bytes 823296 | tf_op jit(solution)/shard_map/slice | solution.py:240
  43.3 5.1 %collective-permute-start.7 = (f32[256,3,134]{0,2,1:T(8,128)}, f32[256,3,134]{0,2,1:T(8,128)}, u32[]{:S(2)}, u32[]{:S(2)}) collective-permute-start(f32[256,3,134]{0,2,1:T(8,128)} %copy.39), channel_id=1, source_target_pairs={{2,0},{4,2},{6,4},{3,1},{5,3},{7,5},{10,8},{12,10},{14,12},{11,9},... | collective-permute-start | bytes 1234952 | tf_op jit(solution)/shard_map/ppermute | solution.py:39
  48.5 1.3 %copy.29 = f32[325,6,3]{2,0,1:T(8,128)} copy(f32[325,6,3]{0,1,2:T(8,128)S(1)} %collective-permute-done.2) | data formatting | bytes 46800 | tf_op jit(solution)/shard_map/ppermute | solution.py:39
  49.8 1.3 %copy.30 = f32[325,6,3]{2,0,1:T(8,128)} copy(f32[325,6,3]{0,1,2:T(8,128)S(1)} %collective-permute-done.3) | data formatting | bytes 46800 | tf_op jit(solution)/shard_map/ppermute | solution.py:39
  51.1 2.4 %pad_maximum_fusion.1 = f32[325,6,134]{2,0,1:T(8,128)S(1)} fusion(f32[325,6,3]{2,0,1:T(8,128)} %copy.30, f32[325,6,128]{2,0,1:T(8,128)S(1)} %constant_dynamic-update-slice_fusion, f32[325,6,3]{2,0,1:T(8,128)} %copy.29), kind=kLoop, calls=%fused_computation.1 | loop fusion | flops 522600 | bytes 2090400 | tf_op jit(solution)/shard_map/concatenate | solution.py:213
  53.5 1.4 %slice_bitcast_fusion = (f32[325,134]{1,0:T(8,128)S(1)}, f32[325,134]{1,0:T(8,128)S(1)}, f32[325,134]{1,0:T(8,128)S(1)}, f32[325,134]{1,0:T(8,128)}, f32[325,134...) fusion(f32[325,6,134]{2,0,1:T(8,128)S(1)} %pad_maximum_fusion.1, ...), kind=kLoop, calls=%fused_computation.6 | loop fusion | bytes 3484000 | tf_op jit(solution)/shard_map/squeeze | solution.py:221
  54.9 3.2 %concatenate.44.frc_ref.pk_ref = f32[325,1408]{1,0:T(8,128)S(1)} concatenate(f32[325,134]{1,0:T(8,128)} %get-tuple-element.23, f32[325,134]{1,0:T(8,128)} %get-tuple-element.22, f32[325,134]{1,0:T(8,128)} %get-tuple-element.21, f32[325,134]{1,0:T(8,128)} %get-tuple-element.62, f32[325,134]{1,0:T(8,128)} %get-tuple-element.63, f32[325,134]{1,0:T(8,128)} %get-tuple-element.64, ...), dimensions={1} | concatenate | bytes 3660800 | tf_op jit(solution)/shard_map/concatenate | solution.py:223
  58.2 0.7 reshape.68.inc_ref
  58.9 0.5 copy-done.3
  59.4 11.1 %shard_map.77 = f32[2,128,512]{2,1,0:T(8,128)} custom-call(s32[2]{0:T(128)} %get-tuple-element.60.order_ref, f32[325,1408]{1,0:T(8,128)} %copy-done.3, f32[325,1408]{1,0:T(8,128)} %copy-done.3, f32[2,2,1408]{2,1,0:T(2,128)} %reshape.68.inc_ref, f32[1,1408]{1,0:T(1,128)} %pad_convert_fusion.ins_ref, bf16[128,512]{1,0:T(8,128)(2,1)} %get-tuple-element.39.bhi_ref, ...), custom_call_target="tpu_custom_call" | custom-call | flops 4429185024 | bytes 2812288 | tf_op jit(solution)/shard_map/pallas_call | solution.py:157
  70.5 1.2 %reshape.69 = f32[2,2,64,4,128]{4,3,2,1,0:T(4,128)S(1)} reshape(f32[2,128,512]{2,1,0:T(8,128)} %shard_map.77) | data formatting | bytes 1048576 | tf_op jit(solution)/shard_map/reshape | solution.py:256
  71.8 0.1 fusion.8
  71.8 2.7 %collective-permute-start.8 = (f32[2,2,4,3]{3,1,0,2:T(2,128)S(1)}, f32[2,2,4,3]{3,1,0,2:T(2,128)S(1)}, u32[]{:S(2)}, u32[]{:S(2)}) collective-permute-start(f32[2,2,4,3]{3,1,0,2:T(2,128)S(1)} %get-tuple-element.58), channel_id=1, source_target_pairs={{0,1},{2,3},{4,5},{6,7},{8,9},{10,11},{12,13},{14,15},{16,17},{18,... | collective-permute-start | bytes 584 | tf_op jit(solution)/shard_map/ppermute | solution.py:39
  74.6 1.3 %collective-permute-start.9 = (f32[2,2,4,3]{3,1,0,2:T(2,128)S(1)}, f32[2,2,4,3]{3,1,0,2:T(2,128)S(1)}, u32[]{:S(2)}, u32[]{:S(2)}) collective-permute-start(f32[2,2,4,3]{3,1,0,2:T(2,128)S(1)} %get-tuple-element.59), channel_id=1, source_target_pairs={{1,0},{3,2},{5,4},{7,6},{9,8},{11,10},{13,12},{15,14},{17,16},{19,... | collective-permute-start | bytes 584 | tf_op jit(solution)/shard_map/ppermute | solution.py:39
  75.9 1.3 %copy.43 = f32[256,3,134]{2,0,1:T(8,128)S(1)} copy(f32[256,3,134]{0,2,1:T(8,128)} %collective-permute-done.7) | data formatting | bytes 823296 | tf_op jit(solution)/shard_map/optimization_barrier | solution.py:250
  77.2 0.0 copy-start.2
  77.2 0.1 slice_bitcast_fusion.10
  77.2 1.3 %copy.40 = f32[256,3,134]{2,0,1:T(8,128)S(1)} copy(f32[256,3,134]{0,2,1:T(8,128)} %collective-permute-done.6) | data formatting | bytes 823296 | tf_op jit(solution)/shard_map/optimization_barrier | solution.py:250
  78.6 0.1 pad_maximum_fusion.5
  78.7 5.4 %collective-permute-start.12 = (f32[2,2,3,134]{3,1,0,2:T(2,128)S(1)}, f32[2,2,3,134]{3,1,0,2:T(2,128)S(1)}, u32[]{:S(2)}, u32[]{:S(2)}) collective-permute-start(f32[2,2,3,134]{3,1,0,2:T(2,128)S(1)} %get-tuple-element.46), channel_id=1, source_target_pairs={{2,8},{4,10},{6,12},{10,16},{12,18},{14,20},{18,24},{20,26},{22,28... | collective-permute-start | bytes 19304 | tf_op jit(solution)/shard_map/ppermute | solution.py:40
  84.1 0.1 slice_bitcast_fusion.17
  84.2 0.2 stack_reshape.6
  84.4 2.6 %concatenate.49.frc_ref = f32[256,1408]{1,0:T(8,128)} concatenate(f32[256,134]{1,0:T(8,128)S(1)} %get-tuple-element.35, f32[256,134]{1,0:T(8,128)S(1)} %get-tuple-element.34, f32[256,134]{1,0:T(8,128)S(1)} %get-tuple-element.33, f32[256,134]{1,0:T(8,128)} %get-tuple-element.11, f32[256,134]{1,0:T(8,128)} %get-tuple-element.10, f32[256,134]{1,0:T(8,128)S(1)} %copy-done.5, ...), dimensions={1} | concatenate | bytes 2883584 | tf_op jit(solution)/shard_map/concatenate | solution.py:255
  87.1 3.5 %collective-permute-start.11 = (f32[2,2,4,134]{3,1,0,2:T(2,128)S(1)}, f32[2,2,4,134]{3,1,0,2:T(2,128)S(1)}, u32[]{:S(2)}, u32[]{:S(2)}) collective-permute-start(f32[2,2,4,134]{3,1,0,2:T(2,128)S(1)} %pad_maximum_fusion.5), channel_id=1, source_target_pairs={{0,8},{2,10},{4,12},{6,14},{8,16},{10,18},{12,20},{14,22},{16,24},... | collective-permute-start | bytes 25736 | tf_op jit(solution)/shard_map/ppermute | solution.py:40
  90.6 1.9 %collective-permute-start.10 = (f32[2,2,3,134]{3,1,0,2:T(2,128)S(1)}, f32[2,2,3,134]{3,1,0,2:T(2,128)S(1)}, u32[]{:S(2)}, u32[]{:S(2)}) collective-permute-start(f32[2,2,3,134]{3,1,0,2:T(2,128)S(1)} %get-tuple-element.47), channel_id=1, source_target_pairs={{0,10},{2,12},{4,14},{8,18},{10,20},{12,22},{16,26},{18,28},{20,30... | collective-permute-start | bytes 19304 | tf_op jit(solution)/shard_map/ppermute | solution.py:40
  92.5 5.4 %collective-permute-done.10 = f32[2,2,3,134]{3,1,0,2:T(2,128)S(1)} collective-permute-done((f32[2,2,3,134]{3,1,0,2:T(2,128)S(1)}, f32[2,2,3,134]{3,1,0,2:T(2,128)S(1)}, u32[]{:S(2)}, u32[]{:S(2)}) %collective-permute-start.10) | collective-permute-done | bytes 6464 | tf_op jit(solution)/shard_map/ppermute | solution.py:40
  98.0 0.7 concatenate.51.inc_ref
  98.7 10.9 %shard_map.78 = f32[2,128,512]{2,1,0:T(8,128)} custom-call(s32[2]{0:T(128)} %get-tuple-element.61.order_ref, f32[256,1408]{1,0:T(8,128)} %concatenate.49.frc_ref, f32[325,1408]{1,0:T(8,128)} %copy-done.3, f32[2,2,1408]{2,1,0:T(2,128)} %concatenate.51.inc_ref, f32[1,1408]{1,0:T(1,128)} %pad_convert_fusion.ins_ref, ...), custom_call_target="tpu_custom_call" | custom-call | flops 4429185024 | bytes 2423680 | tf_op jit(solution)/shard_map/pallas_call | solution.py:157
  109.6 1.2 %stack_reshape.7 = f32[1,2,2,64,4,128]{5,4,3,2,1,0:T(4,128)S(1)} reshape(f32[2,128,512]{2,1,0:T(8,128)} %shard_map.78) | data formatting | bytes 1048576 | tf_op jit(solution)/shard_map/stack;reshape | solution.py:261
  110.8 1.2 %reshape.70 = f32[2,2,64,4,128]{4,3,2,1,0:T(4,128)S(1)} reshape(f32[2,128,512]{2,1,0:T(8,128)} %shard_map.78) | data formatting | bytes 1048576 | tf_op jit(solution)/shard_map/reshape | solution.py:256
  112.1 0.6 slice.284
  112.7 1.2 %pad_maximum_fusion.2 = f32[2,2,2,64,4,128]{5,4,3,2,1,0:T(4,128)} fusion(f32[1,2,2,64,4,128]{5,4,3,2,1,0:T(4,128)S(1)} %stack_reshape.7, f32[1,2,2,64,4,128]{5,4,3,2,1,0:T(4,128)S(1)} %stack_reshape.6), kind=kLoop, calls=%fused_computation.2 | loop fusion | flops 262144 | bytes 2097152 | tf_op jit(solution)/shard_map/stack | solution.py:261
  (50 shorter events, 0.4 us)
Async XLA Ops:
  0.6 1.4 %copy-start.6 = (f32[64,4,128]{2,1,0:T(4,128)S(1)}, f32[64,4,128]{2,1,0:T(4,128)}, u32[]{:S(2)}) copy-start(f32[64,4,128]{2,1,0:T(4,128)} %param.7) | copy-start | bytes 393220
  0.6 1.4 %copy-start.7 = (f32[2,2,1,4,128]{4,3,2,1,0:T(4,128)S(1)}, f32[2,2,1,4,128]{4,3,2,1,0:T(4,128)}, u32[]{:S(2)}) copy-start(f32[2,2,1,4,128]{4,3,2,1,0:T(4,128)} %param.11) | copy-start | bytes 24580
  0.7 1.5 %copy-start.8 = (s32[1,4,128]{2,1,0:T(4,128)S(1)}, s32[1,4,128]{2,1,0:T(4,128)}, u32[]{:S(2)}) copy-start(s32[1,4,128]{2,1,0:T(4,128)} %param.9) | copy-start | bytes 6148
  3.2 22.5 %collective-permute-start = (f32[325,3,128]{2,0,1:T(8,128)}, f32[325,3,128]{2,0,1:T(8,128)S(1)}, u32[]{:S(2)}, u32[]{:S(2)}) collective-permute-start(f32[325,3,128]{2,0,1:T(8,128)} %get-tuple-element.37), channel_id=1, source_target_pairs={{0,2},{2,4},{4,6},{1,3},{3,5},{5,7},{8,10},{10,12},{12,14},{9,11},... | collective-permute-start | bytes 1497608 | tf_op jit(solution)/shard_map/ppermute | solution.py:39
  6.6 21.8 %collective-permute-start.1 = (f32[325,3,128]{2,0,1:T(8,128)}, f32[325,3,128]{2,0,1:T(8,128)S(1)}, u32[]{:S(2)}, u32[]{:S(2)}) collective-permute-start(f32[325,3,128]{2,0,1:T(8,128)} %get-tuple-element.36), channel_id=1, source_target_pairs={{2,0},{4,2},{6,4},{3,1},{5,3},{7,5},{10,8},{12,10},{14,12},{11,9},... | collective-permute-start | bytes 1497608 | tf_op jit(solution)/shard_map/ppermute | solution.py:39
  13.6 5.2 %copy-start.9 = (s32[2,1,2]{2,1,0:T(1,128)S(1)}, s32[2,1,2]{2,1,0:T(1,128)}, u32[]{:S(2)}) copy-start(s32[2,1,2]{2,1,0:T(1,128)} %param.10) | copy-start | bytes 52
  13.6 6.4 %collective-permute-start.4 = (f32[581,4,3]{0,1,2:T(4,128)S(1)}, f32[581,4,3]{0,1,2:T(4,128)S(1)}, u32[]{:S(2)}, u32[]{:S(2)}) collective-permute-start(f32[581,4,3]{0,1,2:T(4,128)S(1)} %copy.33), channel_id=1, source_target_pairs={{0,1},{2,3},{4,5},{6,7},{8,9},{10,11},{12,13},{14,15},{16,17},{18,... | collective-permute-start | bytes 83672 | tf_op jit(solution)/shard_map/ppermute | solution.py:39
  15.5 5.0 %collective-permute-start.5 = (f32[581,4,3]{0,1,2:T(4,128)S(1)}, f32[581,4,3]{0,1,2:T(4,128)S(1)}, u32[]{:S(2)}, u32[]{:S(2)}) collective-permute-start(f32[581,4,3]{0,1,2:T(4,128)S(1)} %copy.34), channel_id=1, source_target_pairs={{1,0},{3,2},{5,4},{7,6},{9,8},{11,10},{13,12},{15,14},{17,16},{19,... | collective-permute-start | bytes 83672 | tf_op jit(solution)/shard_map/ppermute | solution.py:39
  24.2 1.9 %copy-start = (f32[581,4,134]{2,0,1:T(8,128)}, f32[581,4,134]{2,0,1:T(8,128)S(1)}, u32[]{:S(2)}) copy-start(f32[581,4,134]{2,0,1:T(8,128)S(1)} %pad_maximum_fusion) | copy-start | bytes 3736996
  28.5 7.6 %copy-start.1 = (f32[581,4,134]{2,0,1:T(8,128)S(1)}, f32[581,4,134]{2,0,1:T(8,128)}, u32[]{:S(2)}) copy-start(f32[581,4,134]{2,0,1:T(8,128)} %copy-done) | copy-start | bytes 3736996
  31.8 16.7 %collective-permute-start.2 = (f32[325,6,3]{0,1,2:T(8,128)S(1)}, f32[325,6,3]{0,1,2:T(8,128)S(1)}, u32[]{:S(2)}, u32[]{:S(2)}) collective-permute-start(f32[325,6,3]{0,1,2:T(8,128)S(1)} %copy.27), channel_id=1, source_target_pairs={{0,1},{2,3},{4,5},{6,7},{8,9},{10,11},{12,13},{14,15},{16,17},{18,... | collective-permute-start | bytes 70208 | tf_op jit(solution)/shard_map/ppermute | solution.py:39
  34.7 15.1 %collective-permute-start.3 = (f32[325,6,3]{0,1,2:T(8,128)S(1)}, f32[325,6,3]{0,1,2:T(8,128)S(1)}, u32[]{:S(2)}, u32[]{:S(2)}) collective-permute-start(f32[325,6,3]{0,1,2:T(8,128)S(1)} %copy.28), channel_id=1, source_target_pairs={{1,0},{3,2},{5,4},{7,6},{9,8},{11,10},{13,12},{15,14},{17,16},{19,... | collective-permute-start | bytes 70208 | tf_op jit(solution)/shard_map/ppermute | solution.py:39
  39.2 31.3 %collective-permute-start.6 = (f32[256,3,134]{0,2,1:T(8,128)}, f32[256,3,134]{0,2,1:T(8,128)}, u32[]{:S(2)}, u32[]{:S(2)}) collective-permute-start(f32[256,3,134]{0,2,1:T(8,128)} %copy.38), channel_id=1, source_target_pairs={{0,2},{2,4},{4,6},{1,3},{3,5},{5,7},{8,10},{10,12},{12,14},{9,11},... | collective-permute-start | bytes 1234952 | tf_op jit(solution)/shard_map/ppermute | solution.py:39
  43.3 27.2 %collective-permute-start.7 = (f32[256,3,134]{0,2,1:T(8,128)}, f32[256,3,134]{0,2,1:T(8,128)}, u32[]{:S(2)}, u32[]{:S(2)}) collective-permute-start(f32[256,3,134]{0,2,1:T(8,128)} %copy.39), channel_id=1, source_target_pairs={{2,0},{4,2},{6,4},{3,1},{5,3},{7,5},{10,8},{12,10},{14,12},{11,9},... | collective-permute-start | bytes 1234952 | tf_op jit(solution)/shard_map/ppermute | solution.py:39
  58.1 1.3 %copy-start.3 = (f32[325,1408]{1,0:T(8,128)}, f32[325,1408]{1,0:T(8,128)S(1)}, u32[]{:S(2)}) copy-start(f32[325,1408]{1,0:T(8,128)S(1)} %concatenate.44.frc_ref.pk_ref) | copy-start | bytes 5491204
  71.8 6.8 %collective-permute-start.8 = (f32[2,2,4,3]{3,1,0,2:T(2,128)S(1)}, f32[2,2,4,3]{3,1,0,2:T(2,128)S(1)}, u32[]{:S(2)}, u32[]{:S(2)}) collective-permute-start(f32[2,2,4,3]{3,1,0,2:T(2,128)S(1)} %get-tuple-element.58), channel_id=1, source_target_pairs={{0,1},{2,3},{4,5},{6,7},{8,9},{10,11},{12,13},{14,15},{16,17},{18,... | collective-permute-start | bytes 584 | tf_op jit(solution)/shard_map/ppermute | solution.py:39
  74.6 4.0 %collective-permute-start.9 = (f32[2,2,4,3]{3,1,0,2:T(2,128)S(1)}, f32[2,2,4,3]{3,1,0,2:T(2,128)S(1)}, u32[]{:S(2)}, u32[]{:S(2)}) collective-permute-start(f32[2,2,4,3]{3,1,0,2:T(2,128)S(1)} %get-tuple-element.59), channel_id=1, source_target_pairs={{1,0},{3,2},{5,4},{7,6},{9,8},{11,10},{13,12},{15,14},{17,16},{19,... | collective-permute-start | bytes 584 | tf_op jit(solution)/shard_map/ppermute | solution.py:39
  77.2 7.1 %copy-start.2 = (f32[2,128,512]{2,1,0:T(8,128)S(1)}, f32[2,128,512]{2,1,0:T(8,128)}, u32[]{:S(2)}) copy-start(f32[2,128,512]{2,1,0:T(8,128)} %shard_map.77) | copy-start | bytes 1572868
  77.2 7.2 %copy-start.4 = (f32[256,134]{1,0:T(8,128)S(1)}, f32[256,134]{1,0:T(8,128)}, u32[]{:S(2)}) copy-start(f32[256,134]{1,0:T(8,128)} %get-tuple-element.8) | copy-start | bytes 411652
  77.2 7.2 %copy-start.5 = (f32[256,134]{1,0:T(8,128)S(1)}, f32[256,134]{1,0:T(8,128)}, u32[]{:S(2)}) copy-start(f32[256,134]{1,0:T(8,128)} %get-tuple-element.9) | copy-start | bytes 411652
  78.7 13.8 %collective-permute-start.12 = (f32[2,2,3,134]{3,1,0,2:T(2,128)S(1)}, f32[2,2,3,134]{3,1,0,2:T(2,128)S(1)}, u32[]{:S(2)}, u32[]{:S(2)}) collective-permute-start(f32[2,2,3,134]{3,1,0,2:T(2,128)S(1)} %get-tuple-element.46), channel_id=1, source_target_pairs={{2,8},{4,10},{6,12},{10,16},{12,18},{14,20},{18,24},{20,26},{22,28... | collective-permute-start | bytes 19304 | tf_op jit(solution)/shard_map/ppermute | solution.py:40
  87.1 10.9 %collective-permute-start.11 = (f32[2,2,4,134]{3,1,0,2:T(2,128)S(1)}, f32[2,2,4,134]{3,1,0,2:T(2,128)S(1)}, u32[]{:S(2)}, u32[]{:S(2)}) collective-permute-start(f32[2,2,4,134]{3,1,0,2:T(2,128)S(1)} %pad_maximum_fusion.5), channel_id=1, source_target_pairs={{0,8},{2,10},{4,12},{6,14},{8,16},{10,18},{12,20},{14,22},{16,24},... | collective-permute-start | bytes 25736 | tf_op jit(solution)/shard_map/ppermute | solution.py:40
  90.6 7.4 %collective-permute-start.10 = (f32[2,2,3,134]{3,1,0,2:T(2,128)S(1)}, f32[2,2,3,134]{3,1,0,2:T(2,128)S(1)}, u32[]{:S(2)}, u32[]{:S(2)}) collective-permute-start(f32[2,2,3,134]{3,1,0,2:T(2,128)S(1)} %get-tuple-element.47), channel_id=1, source_target_pairs={{0,10},{2,12},{4,14},{8,18},{10,20},{12,22},{16,26},{18,28},{20,30... | collective-permute-start | bytes 19304 | tf_op jit(solution)/shard_map/ppermute | solution.py:40

commit v13 on v12

--- a/solution.py
+++ b/solution.py
@@ -69,7 +69,8 @@
 
 
 def tick_kernel(
-    order_ref, frc_ref, pk_ref, inc_ref, ins_ref, bhi_ref, blo_ref, out_ref, field_ref, *, row, depth, width
+    order_ref, frc_ref, pk_ref, inc_ref, ins_ref, bhi_ref, blo_ref, out_ref, trace_ref, field_ref, *, row, depth,
+    width,
 ):
     nsrc, rows, owned = out_ref.shape
     cols = pk_ref.shape[1]
@@ -142,7 +143,11 @@
         u = field_ref[...]
         for x in range(owned // lanes):
             begin = (x + width) * row + width
-            out_ref[s, :, x * lanes : (x + 1) * lanes] = pltpu.roll(u, cols - begin, 1)[:, :lanes]
+            chunk = pltpu.roll(u, cols - begin, 1)[:, :lanes]
+            out_ref[s, :, x * lanes : (x + 1) * lanes] = chunk
+            for part in range(rows // depth):
+                bottom = (part + 1) * depth - 1
+                trace_ref[s, part, pl.ds(x, 1), :] = chunk[bottom : bottom + 1, :]
         return carry
 
     lax.fori_loop(0, nsrc, one_source, 0)
@@ -156,9 +161,12 @@
     vmem = pl.BlockSpec(memory_space=pltpu.VMEM)
     return pl.pallas_call(
         functools.partial(tick_kernel, row=row, depth=depth, width=width),
-        out_shape=jax.ShapeDtypeStruct((nsrc, rows, owned), jnp.float32),
+        out_shape=(
+            jax.ShapeDtypeStruct((nsrc, rows, owned), jnp.float32),
+            jax.ShapeDtypeStruct((nsrc, rows // depth, owned // 128, 128), jnp.float32),
+        ),
         in_specs=[pl.BlockSpec(memory_space=pltpu.SMEM)] + [vmem] * 6,
-        out_specs=vmem,
+        out_specs=(vmem, vmem),
         scratch_shapes=[pltpu.VMEM((rows, cols), jnp.float32)],
         cost_estimate=pl.CostEstimate(
             flops=flops,
@@ -242,7 +250,7 @@
     trace = None
     forcing_f = packed
     for tick in range(ticks):
-        field = run_tick(
+        field, trace = run_tick(
             orders[tick], forcing_f, packed, incoming, inside, bhi, blo, ey, depth, width, nx * ny
         )
         if tick + 1 < ticks:
@@ -255,7 +263,6 @@
             forcing_f = jnp.concatenate(segments, axis=-1)
         tile = field.reshape(nsrc, two, depth, nx, ny)
         solutions.append(tile)
-        trace = tile[:, :, depth - 1]
         if tick + 1 < ticks:
             incoming = flat_extended(extend_y(trace, width), width, padded, ("slab",), (-1,))
     return (jnp.stack(solutions, axis=0), trace[:, :, None])

time: 115 us -> 113 us (0.983)
  local copies, waits for them, and re-layouts: 41.4 us -> 39.5 us
    reshape x2 -> x0, local copies, waits for them, and re-layouts: 2.43 us -> none  [per_device(): tile = field.reshape(nsrc, two, depth, nx, ny)]
  transfers between devices with their start and end apart: 13 -> 13, of which waited for: 2 -> 2; matrix products, arithmetic and copies ran while one was open for 31% -> 33% of each run, Pallas kernels for 10% -> 10%
where the time goes in v13:
time: 113 us; the launch traced here: 112 us
  local copies, waits for them, and re-layouts  39.5 us (35%)
  starting transfers between devices  34.1 us (30%)
  Pallas kernels  22 us (19%)
  waiting for transfers between devices  7.76 us (7%)
  other arithmetic  7.54 us (7%)
  between operations  1.2 us (1%)
    ppermute x10, starting transfers between devices, fetch(): return lax.ppermute(block, axes[0], pairs)  23.1 us
    pallas_call x2, Pallas kernels, run_tick(): pl.pallas_call(functools.partial(tick_kernel, row=row, depth=depth, width...  22 us
    ppermute x3, starting transfers between devices, fetch(): return lax.ppermute(block, tuple(axes), pairs)  11 us
    ppermute x3, waiting for transfers between devices, fetch(): return lax.ppermute(block, tuple(axes), pairs)  5.44 us
    ppermute x4, local copies, waits for them, and re-layouts, fetch(): return lax.ppermute(block, axes[0], pairs)  4.5 us
    slice x2, local copies, waits for them, and re-layouts, per_device(): high_later = [fetch(r[:, :width, :], ('tx',), (1,)) for r in later]  3.58 us
    concatenate x1, local copies, waits for them, and re-layouts, per_device(): packed = jnp.concatenate(segments, axis=-1)  3.31 us
    slice x2, local copies, waits for them, and re-layouts, per_device(): corner_low = fetch(rims[..., ny - width:], ('ty',), (-1,))  3.27 us
  transfers between devices with their start and end apart: 13, of which 2 were waited for; matrix products, arithmetic and copies ran while one was open for 33% of the time, Pallas kernels for 10%

profile of v13, /device:TPU:12, one launch (start us, length us, event | category | flops | bytes accessed | tf_op | source)
XLA Modules:
  0.0 112.1 jit_solution(7545877142898073330)
XLA Ops:
  0.7 1.3 %fusion.4 = (f32[1,2,2,64,4,128]{5,4,3,2,1,0:T(4,128)S(1)}, f32[1,2,2,64,4,128]{5,4,3,2,1,0:T(4,128)S(1)}) fusion(f32[2,2,2,64,4,128]{5,4,3,2,1,0:T(4,128)} %param.6), kind=kLoop, calls=%fused_computation.58 | loop fusion | bytes 2097152 | tf_op jit(solution)/shard_map/slice | solution.py:206
  2.2 1.0 fusion.6
  3.2 3.4 %collective-permute-start = (f32[325,3,128]{2,0,1:T(8,128)}, f32[325,3,128]{2,0,1:T(8,128)S(1)}, u32[]{:S(2)}, u32[]{:S(2)}) collective-permute-start(f32[325,3,128]{2,0,1:T(8,128)} %get-tuple-element.49), channel_id=1, source_target_pairs={{0,2},{2,4},{4,6},{1,3},{3,5},{5,7},{8,10},{10,12},{12,14},{9,11},... | collective-permute-start | bytes 1497608 | tf_op jit(solution)/shard_map/ppermute | solution.py:39
  6.6 3.3 %collective-permute-start.1 = (f32[325,3,128]{2,0,1:T(8,128)}, f32[325,3,128]{2,0,1:T(8,128)S(1)}, u32[]{:S(2)}, u32[]{:S(2)}) collective-permute-start(f32[325,3,128]{2,0,1:T(8,128)} %get-tuple-element.48), channel_id=1, source_target_pairs={{2,0},{4,2},{6,4},{3,1},{5,3},{7,5},{10,8},{12,10},{14,12},{11,9},... | collective-permute-start | bytes 1497608 | tf_op jit(solution)/shard_map/ppermute | solution.py:39
  10.0 0.5 concatenate.42
  10.5 1.4 %fusion.3 = (f32[581,4,3]{2,0,1:T(8,128)}, f32[581,4,3]{2,0,1:T(8,128)S(1)}) fusion(f32[581,4,128]{2,0,1:T(8,128)S(1)} %concatenate.42), kind=kLoop, calls=%fused_computation.57 | loop fusion | bytes 111552 | tf_op jit(solution)/shard_map/slice | solution.py:45
  12.0 1.7 %copy.29 = f32[581,4,3]{0,1,2:T(4,128)S(1)} copy(f32[581,4,3]{2,0,1:T(8,128)} %get-tuple-element.36) | data formatting | bytes 55776 | tf_op jit(solution)/shard_map/slice | solution.py:45
  13.6 1.4 %collective-permute-start.4 = (f32[581,4,3]{0,1,2:T(4,128)S(1)}, f32[581,4,3]{0,1,2:T(4,128)S(1)}, u32[]{:S(2)}, u32[]{:S(2)}) collective-permute-start(f32[581,4,3]{0,1,2:T(4,128)S(1)} %copy.29), channel_id=1, source_target_pairs={{0,1},{2,3},{4,5},{6,7},{8,9},{10,11},{12,13},{14,15},{16,17},{18,... | collective-permute-start | bytes 83672 | tf_op jit(solution)/shard_map/ppermute | solution.py:39
  15.1 0.4 copy.30
  15.5 1.3 %collective-permute-start.5 = (f32[581,4,3]{0,1,2:T(4,128)S(1)}, f32[581,4,3]{0,1,2:T(4,128)S(1)}, u32[]{:S(2)}, u32[]{:S(2)}) collective-permute-start(f32[581,4,3]{0,1,2:T(4,128)S(1)} %copy.30), channel_id=1, source_target_pairs={{1,0},{3,2},{5,4},{7,6},{9,8},{11,10},{13,12},{15,14},{17,16},{19,... | collective-permute-start | bytes 83672 | tf_op jit(solution)/shard_map/ppermute | solution.py:39
  16.8 1.0 copy.47
  17.8 0.1 maximum_maximum_fusion
  18.0 0.1 broadcast_and_fusion
  18.1 0.1 convert_element_type.24
  18.2 0.6 pad_convert_fusion.ins_ref
  18.8 0.6 slice_bitcast_fusion.37
  19.4 0.7 fusion
  20.1 0.0 collective-permute-done.4
  20.1 0.4 copy.31
  20.5 0.0 collective-permute-done.5
  20.5 1.5 %copy.32 = f32[581,4,3]{2,0,1:T(8,128)} copy(f32[581,4,3]{0,1,2:T(4,128)S(1)} %collective-permute-done.5) | data formatting | bytes 55776 | tf_op jit(solution)/shard_map/ppermute | solution.py:39
  22.0 2.3 %pad_maximum_fusion = f32[581,4,134]{2,0,1:T(8,128)S(1)} fusion(f32[581,4,3]{2,0,1:T(8,128)} %copy.32, f32[581,4,128]{2,0,1:T(8,128)S(1)} %concatenate.42, f32[581,4,3]{2,0,1:T(8,128)S(1)} %copy.31), kind=kLoop, calls=%fused_computation | loop fusion | flops 622832 | bytes 2491328 | tf_op jit(solution)/shard_map/concatenate | solution.py:47
  24.2 1.4 %fusion.2 = (f32[256,3,134]{2,0,1:T(8,128)}, f32[256,3,134]{2,0,1:T(8,128)}) fusion(f32[581,4,134]{2,0,1:T(8,128)S(1)} %pad_maximum_fusion), kind=kLoop, calls=%fused_computation.56 | loop fusion | bytes 1646592 | tf_op jit(solution)/shard_map/slice | solution.py:248
  25.7 0.0 collective-permute-done
  25.7 0.4 copy-done
  26.1 2.3 %collective-permute-done.1 = f32[325,3,128]{2,0,1:T(8,128)S(1)} collective-permute-done((f32[325,3,128]{2,0,1:T(8,128)}, f32[325,3,128]{2,0,1:T(8,128)S(1)}, u32[]{:S(2)}, u32[]{:S(2)}) %collective-permute-start.1) | collective-permute-done | bytes 499232 | tf_op jit(solution)/shard_map/ppermute | solution.py:39
  28.5 1.6 %fusion.5 = (f32[325,6,3]{2,0,1:T(8,128)}, f32[325,6,3]{2,0,1:T(8,128)}) fusion(f32[325,6,128]{2,0,1:T(8,128)S(1)} %constant_dynamic-update-slice_fusion), kind=kLoop, calls=%fused_computation.59 | loop fusion | bytes 93600 | tf_op jit(solution)/shard_map/slice | solution.py:219
  30.1 1.7 %copy.23 = f32[325,6,3]{0,1,2:T(8,128)S(1)} copy(f32[325,6,3]{2,0,1:T(8,128)} %get-tuple-element.40) | data formatting | bytes 46800 | tf_op jit(solution)/shard_map/slice | solution.py:219
  31.8 1.3 %collective-permute-start.2 = (f32[325,6,3]{0,1,2:T(8,128)S(1)}, f32[325,6,3]{0,1,2:T(8,128)S(1)}, u32[]{:S(2)}, u32[]{:S(2)}) collective-permute-start(f32[325,6,3]{0,1,2:T(8,128)S(1)} %copy.23), channel_id=1, source_target_pairs={{0,1},{2,3},{4,5},{6,7},{8,9},{10,11},{12,13},{14,15},{16,17},{18,... | collective-permute-start | bytes 70208 | tf_op jit(solution)/shard_map/ppermute | solution.py:39
  33.1 1.7 %copy.24 = f32[325,6,3]{0,1,2:T(8,128)S(1)} copy(f32[325,6,3]{2,0,1:T(8,128)} %get-tuple-element.41) | data formatting | bytes 46800 | tf_op jit(solution)/shard_map/slice | solution.py:220
  34.7 1.3 %collective-permute-start.3 = (f32[325,6,3]{0,1,2:T(8,128)S(1)}, f32[325,6,3]{0,1,2:T(8,128)S(1)}, u32[]{:S(2)}, u32[]{:S(2)}) collective-permute-start(f32[325,6,3]{0,1,2:T(8,128)S(1)} %copy.24), channel_id=1, source_target_pairs={{1,0},{3,2},{5,4},{7,6},{9,8},{11,10},{13,12},{15,14},{17,16},{19,... | collective-permute-start | bytes 70208 | tf_op jit(solution)/shard_map/ppermute | solution.py:39
  36.1 1.0 slice_bitcast_fusion.13
  37.1 2.1 %copy.34 = f32[256,3,134]{0,2,1:T(8,128)} copy(f32[256,3,134]{2,0,1:T(8,128)} %get-tuple-element.25) | data formatting | bytes 823296 | tf_op jit(solution)/shard_map/slice | solution.py:247
  39.2 2.0 %collective-permute-start.6 = (f32[256,3,134]{0,2,1:T(8,128)}, f32[256,3,134]{0,2,1:T(8,128)}, u32[]{:S(2)}, u32[]{:S(2)}) collective-permute-start(f32[256,3,134]{0,2,1:T(8,128)} %copy.34), channel_id=1, source_target_pairs={{0,2},{2,4},{4,6},{1,3},{3,5},{5,7},{8,10},{10,12},{12,14},{9,11},... | collective-permute-start | bytes 1234952 | tf_op jit(solution)/shard_map/ppermute | solution.py:39
  41.2 2.1 %copy.35 = f32[256,3,134]{0,2,1:T(8,128)} copy(f32[256,3,134]{2,0,1:T(8,128)} %get-tuple-element.24) | data formatting | bytes 823296 | tf_op jit(solution)/shard_map/slice | solution.py:248
  43.4 5.1 %collective-permute-start.7 = (f32[256,3,134]{0,2,1:T(8,128)}, f32[256,3,134]{0,2,1:T(8,128)}, u32[]{:S(2)}, u32[]{:S(2)}) collective-permute-start(f32[256,3,134]{0,2,1:T(8,128)} %copy.35), channel_id=1, source_target_pairs={{2,0},{4,2},{6,4},{3,1},{5,3},{7,5},{10,8},{12,10},{14,12},{11,9},... | collective-permute-start | bytes 1234952 | tf_op jit(solution)/shard_map/ppermute | solution.py:39
  48.5 0.0 collective-permute-done.2
  48.5 1.3 %copy.25 = f32[325,6,3]{2,0,1:T(8,128)} copy(f32[325,6,3]{0,1,2:T(8,128)S(1)} %collective-permute-done.2) | data formatting | bytes 46800 | tf_op jit(solution)/shard_map/ppermute | solution.py:39
  49.8 1.3 %copy.26 = f32[325,6,3]{2,0,1:T(8,128)} copy(f32[325,6,3]{0,1,2:T(8,128)S(1)} %collective-permute-done.3) | data formatting | bytes 46800 | tf_op jit(solution)/shard_map/ppermute | solution.py:39
  51.1 2.4 %pad_maximum_fusion.1 = f32[325,6,134]{2,0,1:T(8,128)S(1)} fusion(f32[325,6,3]{2,0,1:T(8,128)} %copy.26, f32[325,6,128]{2,0,1:T(8,128)S(1)} %constant_dynamic-update-slice_fusion, f32[325,6,3]{2,0,1:T(8,128)} %copy.25), kind=kLoop, calls=%fused_computation.1 | loop fusion | flops 522600 | bytes 2090400 | tf_op jit(solution)/shard_map/concatenate | solution.py:221
  53.5 1.5 %slice_bitcast_fusion = (f32[325,134]{1,0:T(8,128)S(1)}, f32[325,134]{1,0:T(8,128)S(1)}, f32[325,134]{1,0:T(8,128)}, f32[325,134]{1,0:T(8,128)}, f32[325,134]{1,...) fusion(f32[325,6,134]{2,0,1:T(8,128)S(1)} %pad_maximum_fusion.1, ...), kind=kLoop, calls=%fused_computation.6 | loop fusion | bytes 3484000 | tf_op jit(solution)/shard_map/squeeze | solution.py:229
  55.0 3.3 %concatenate.44.frc_ref.pk_ref = f32[325,1408]{1,0:T(8,128)S(1)} concatenate(f32[325,134]{1,0:T(8,128)} %get-tuple-element.35, f32[325,134]{1,0:T(8,128)} %get-tuple-element.34, f32[325,134]{1,0:T(8,128)} %get-tuple-element.33, f32[325,134]{1,0:T(8,128)} %get-tuple-element.74, f32[325,134]{1,0:T(8,128)} %get-tuple-element.75, f32[325,134]{1,0:T(8,128)} %get-tuple-element.76, ...), dimensions={1} | concatenate | bytes 3660800 | tf_op jit(solution)/shard_map/concatenate | solution.py:231
  58.4 0.7 reshape.62.inc_ref
  59.1 0.5 copy-done.2
  59.6 11.0 %shard_map.77 = (f32[2,128,512]{2,1,0:T(8,128)}, f32[2,2,4,128]{3,2,1,0:T(4,128)}) custom-call(s32[2]{0:T(128)} %get-tuple-element.72.order_ref, f32[325,1408]{1,0:T(8,128)} %copy-done.2, f32[325,1408]{1,0:T(8,128)} %copy-done.2, f32[2,2,1408]{2,1,0:T(2,128)} %reshape.62.inc_ref, f32[1,1408]{1,0:T(1,128)} %pad_convert_fusion.ins_ref, ...), custom_call_target="tpu_custom_call" | custom-call | flops 4429185024 | bytes 2812288 | tf_op jit(solution)/shard_map/pallas_call | solution.py:162
  70.6 0.7 copy.42
  71.3 0.1 fusion.8
  71.4 2.7 %collective-permute-start.8 = (f32[2,2,4,3]{3,1,0,2:T(2,128)S(1)}, f32[2,2,4,3]{3,1,0,2:T(2,128)S(1)}, u32[]{:S(2)}, u32[]{:S(2)}) collective-permute-start(f32[2,2,4,3]{3,1,0,2:T(2,128)S(1)} %get-tuple-element.70), channel_id=1, source_target_pairs={{0,1},{2,3},{4,5},{6,7},{8,9},{10,11},{12,13},{14,15},{16,17},{18,... | collective-permute-start | bytes 584 | tf_op jit(solution)/shard_map/ppermute | solution.py:39
  74.2 1.3 %collective-permute-start.9 = (f32[2,2,4,3]{3,1,0,2:T(2,128)S(1)}, f32[2,2,4,3]{3,1,0,2:T(2,128)S(1)}, u32[]{:S(2)}, u32[]{:S(2)}) collective-permute-start(f32[2,2,4,3]{3,1,0,2:T(2,128)S(1)} %get-tuple-element.71), channel_id=1, source_target_pairs={{1,0},{3,2},{5,4},{7,6},{9,8},{11,10},{13,12},{15,14},{17,16},{19,... | collective-permute-start | bytes 584 | tf_op jit(solution)/shard_map/ppermute | solution.py:39
  75.5 1.3 %copy.39 = f32[256,3,134]{2,0,1:T(8,128)S(1)} copy(f32[256,3,134]{0,2,1:T(8,128)} %collective-permute-done.7) | data formatting | bytes 823296 | tf_op jit(solution)/shard_map/optimization_barrier | solution.py:258
  76.8 0.1 slice_bitcast_fusion.10
  76.9 1.3 %copy.36 = f32[256,3,134]{2,0,1:T(8,128)S(1)} copy(f32[256,3,134]{0,2,1:T(8,128)} %collective-permute-done.6) | data formatting | bytes 823296 | tf_op jit(solution)/shard_map/optimization_barrier | solution.py:258
  78.2 0.1 pad_maximum_fusion.5
  78.4 5.6 %collective-permute-start.12 = (f32[2,2,3,134]{3,1,0,2:T(2,128)S(1)}, f32[2,2,3,134]{3,1,0,2:T(2,128)S(1)}, u32[]{:S(2)}, u32[]{:S(2)}) collective-permute-start(f32[2,2,3,134]{3,1,0,2:T(2,128)S(1)} %get-tuple-element.58), channel_id=1, source_target_pairs={{2,8},{4,10},{6,12},{10,16},{12,18},{14,20},{18,24},{20,26},{22,28... | collective-permute-start | bytes 19304 | tf_op jit(solution)/shard_map/ppermute | solution.py:40
  84.0 0.1 slice_bitcast_fusion.17
  84.0 1.2 %stack_reshape.6 = f32[1,2,2,64,4,128]{5,4,3,2,1,0:T(4,128)S(1)} reshape(f32[2,128,512]{2,1,0:T(8,128)} %get-tuple-element.10) | data formatting | bytes 1048576 | tf_op jit(solution)/shard_map/stack;reshape | solution.py:268
  85.3 1.8 %concatenate.49.frc_ref = f32[256,1408]{1,0:T(8,128)} concatenate(f32[256,134]{1,0:T(8,128)S(1)} %get-tuple-element.47, f32[256,134]{1,0:T(8,128)S(1)} %get-tuple-element.46, f32[256,134]{1,0:T(8,128)S(1)} %get-tuple-element.45, f32[256,134]{1,0:T(8,128)S(1)} %copy-done.6, f32[256,134]{1,0:T(8,128)S(1)} %copy-done.5, f32[256,134]{1,0:T(8,128)S(1)} %copy-done.4, ...), dimensions={1} | concatenate | bytes 2883584 | tf_op jit(solution)/shard_map/concatenate | solution.py:263
  87.1 3.5 %collective-permute-start.11 = (f32[2,2,4,134]{3,1,0,2:T(2,128)S(1)}, f32[2,2,4,134]{3,1,0,2:T(2,128)S(1)}, u32[]{:S(2)}, u32[]{:S(2)}) collective-permute-start(f32[2,2,4,134]{3,1,0,2:T(2,128)S(1)} %pad_maximum_fusion.5), channel_id=1, source_target_pairs={{0,8},{2,10},{4,12},{6,14},{8,16},{10,18},{12,20},{14,22},{16,24},... | collective-permute-start | bytes 25736 | tf_op jit(solution)/shard_map/ppermute | solution.py:40
  90.6 1.9 %collective-permute-start.10 = (f32[2,2,3,134]{3,1,0,2:T(2,128)S(1)}, f32[2,2,3,134]{3,1,0,2:T(2,128)S(1)}, u32[]{:S(2)}, u32[]{:S(2)}) collective-permute-start(f32[2,2,3,134]{3,1,0,2:T(2,128)S(1)} %get-tuple-element.59), channel_id=1, source_target_pairs={{0,10},{2,12},{4,14},{8,18},{10,20},{12,22},{16,26},{18,28},{20,30... | collective-permute-start | bytes 19304 | tf_op jit(solution)/shard_map/ppermute | solution.py:40
  92.6 5.4 %collective-permute-done.10 = f32[2,2,3,134]{3,1,0,2:T(2,128)S(1)} collective-permute-done((f32[2,2,3,134]{3,1,0,2:T(2,128)S(1)}, f32[2,2,3,134]{3,1,0,2:T(2,128)S(1)}, u32[]{:S(2)}, u32[]{:S(2)}) %collective-permute-start.10) | collective-permute-done | bytes 6464 | tf_op jit(solution)/shard_map/ppermute | solution.py:40
  98.0 0.7 concatenate.51.inc_ref
  98.8 10.9 %shard_map.78 = (f32[2,128,512]{2,1,0:T(8,128)}, f32[2,2,4,128]{3,2,1,0:T(4,128)}) custom-call(s32[2]{0:T(128)} %get-tuple-element.73.order_ref, f32[256,1408]{1,0:T(8,128)} %concatenate.49.frc_ref, f32[325,1408]{1,0:T(8,128)} %copy-done.2, f32[2,2,1408]{2,1,0:T(2,128)} %concatenate.51.inc_ref, f32[1,1408]{1,0:T(1,128)} %pad_convert_fusion.ins_ref, ...), custom_call_target="tpu_custom_call" | custom-call | flops 4429185024 | bytes 2423680 | tf_op jit(solution)/shard_map/pallas_call | solution.py:162
  109.7 1.2 %stack_reshape.7 = f32[1,2,2,64,4,128]{5,4,3,2,1,0:T(4,128)S(1)} reshape(f32[2,128,512]{2,1,0:T(8,128)} %get-tuple-element.14) | data formatting | bytes 1048576 | tf_op jit(solution)/shard_map/stack;reshape | solution.py:268
  110.9 1.2 %pad_maximum_fusion.2 = f32[2,2,2,64,4,128]{5,4,3,2,1,0:T(4,128)} fusion(f32[1,2,2,64,4,128]{5,4,3,2,1,0:T(4,128)S(1)} %stack_reshape.7, f32[1,2,2,64,4,128]{5,4,3,2,1,0:T(4,128)S(1)} %stack_reshape.6), kind=kLoop, calls=%fused_computation.2 | loop fusion | flops 262144 | bytes 2097152 | tf_op jit(solution)/shard_map/stack | solution.py:268
  (48 shorter events, 0.4 us)
Async XLA Ops:
  0.6 1.4 %copy-start.7 = (f32[64,4,128]{2,1,0:T(4,128)S(1)}, f32[64,4,128]{2,1,0:T(4,128)}, u32[]{:S(2)}) copy-start(f32[64,4,128]{2,1,0:T(4,128)} %param.7) | copy-start | bytes 393220
  0.6 1.4 %copy-start.8 = (f32[2,2,1,4,128]{4,3,2,1,0:T(4,128)S(1)}, f32[2,2,1,4,128]{4,3,2,1,0:T(4,128)}, u32[]{:S(2)}) copy-start(f32[2,2,1,4,128]{4,3,2,1,0:T(4,128)} %param.11) | copy-start | bytes 24580
  0.7 1.5 %copy-start.9 = (s32[1,4,128]{2,1,0:T(4,128)S(1)}, s32[1,4,128]{2,1,0:T(4,128)}, u32[]{:S(2)}) copy-start(s32[1,4,128]{2,1,0:T(4,128)} %param.9) | copy-start | bytes 6148
  3.2 22.5 %collective-permute-start = (f32[325,3,128]{2,0,1:T(8,128)}, f32[325,3,128]{2,0,1:T(8,128)S(1)}, u32[]{:S(2)}, u32[]{:S(2)}) collective-permute-start(f32[325,3,128]{2,0,1:T(8,128)} %get-tuple-element.49), channel_id=1, source_target_pairs={{0,2},{2,4},{4,6},{1,3},{3,5},{5,7},{8,10},{10,12},{12,14},{9,11},... | collective-permute-start | bytes 1497608 | tf_op jit(solution)/shard_map/ppermute | solution.py:39
  6.6 21.8 %collective-permute-start.1 = (f32[325,3,128]{2,0,1:T(8,128)}, f32[325,3,128]{2,0,1:T(8,128)S(1)}, u32[]{:S(2)}, u32[]{:S(2)}) collective-permute-start(f32[325,3,128]{2,0,1:T(8,128)} %get-tuple-element.48), channel_id=1, source_target_pairs={{2,0},{4,2},{6,4},{3,1},{5,3},{7,5},{10,8},{12,10},{14,12},{11,9},... | collective-permute-start | bytes 1497608 | tf_op jit(solution)/shard_map/ppermute | solution.py:39
  13.6 5.2 %copy-start.10 = (s32[2,1,2]{2,1,0:T(1,128)S(1)}, s32[2,1,2]{2,1,0:T(1,128)}, u32[]{:S(2)}) copy-start(s32[2,1,2]{2,1,0:T(1,128)} %param.10) | copy-start | bytes 52
  13.6 6.5 %collective-permute-start.4 = (f32[581,4,3]{0,1,2:T(4,128)S(1)}, f32[581,4,3]{0,1,2:T(4,128)S(1)}, u32[]{:S(2)}, u32[]{:S(2)}) collective-permute-start(f32[581,4,3]{0,1,2:T(4,128)S(1)} %copy.29), channel_id=1, source_target_pairs={{0,1},{2,3},{4,5},{6,7},{8,9},{10,11},{12,13},{14,15},{16,17},{18,... | collective-permute-start | bytes 83672 | tf_op jit(solution)/shard_map/ppermute | solution.py:39
  15.5 5.0 %collective-permute-start.5 = (f32[581,4,3]{0,1,2:T(4,128)S(1)}, f32[581,4,3]{0,1,2:T(4,128)S(1)}, u32[]{:S(2)}, u32[]{:S(2)}) collective-permute-start(f32[581,4,3]{0,1,2:T(4,128)S(1)} %copy.30), channel_id=1, source_target_pairs={{1,0},{3,2},{5,4},{7,6},{9,8},{11,10},{13,12},{15,14},{17,16},{19,... | collective-permute-start | bytes 83672 | tf_op jit(solution)/shard_map/ppermute | solution.py:39
  24.2 1.9 %copy-start = (f32[581,4,134]{2,0,1:T(8,128)}, f32[581,4,134]{2,0,1:T(8,128)S(1)}, u32[]{:S(2)}) copy-start(f32[581,4,134]{2,0,1:T(8,128)S(1)} %pad_maximum_fusion) | copy-start | bytes 3736996
  28.5 7.6 %copy-start.1 = (f32[581,4,134]{2,0,1:T(8,128)S(1)}, f32[581,4,134]{2,0,1:T(8,128)}, u32[]{:S(2)}) copy-start(f32[581,4,134]{2,0,1:T(8,128)} %copy-done) | copy-start | bytes 3736996
  31.8 16.7 %collective-permute-start.2 = (f32[325,6,3]{0,1,2:T(8,128)S(1)}, f32[325,6,3]{0,1,2:T(8,128)S(1)}, u32[]{:S(2)}, u32[]{:S(2)}) collective-permute-start(f32[325,6,3]{0,1,2:T(8,128)S(1)} %copy.23), channel_id=1, source_target_pairs={{0,1},{2,3},{4,5},{6,7},{8,9},{10,11},{12,13},{14,15},{16,17},{18,... | collective-permute-start | bytes 70208 | tf_op jit(solution)/shard_map/ppermute | solution.py:39
  34.7 15.1 %collective-permute-start.3 = (f32[325,6,3]{0,1,2:T(8,128)S(1)}, f32[325,6,3]{0,1,2:T(8,128)S(1)}, u32[]{:S(2)}, u32[]{:S(2)}) collective-permute-start(f32[325,6,3]{0,1,2:T(8,128)S(1)} %copy.24), channel_id=1, source_target_pairs={{1,0},{3,2},{5,4},{7,6},{9,8},{11,10},{13,12},{15,14},{17,16},{19,... | collective-permute-start | bytes 70208 | tf_op jit(solution)/shard_map/ppermute | solution.py:39
  39.2 36.2 %collective-permute-start.6 = (f32[256,3,134]{0,2,1:T(8,128)}, f32[256,3,134]{0,2,1:T(8,128)}, u32[]{:S(2)}, u32[]{:S(2)}) collective-permute-start(f32[256,3,134]{0,2,1:T(8,128)} %copy.34), channel_id=1, source_target_pairs={{0,2},{2,4},{4,6},{1,3},{3,5},{5,7},{8,10},{10,12},{12,14},{9,11},... | collective-permute-start | bytes 1234952 | tf_op jit(solution)/shard_map/ppermute | solution.py:39
  43.4 32.1 %collective-permute-start.7 = (f32[256,3,134]{0,2,1:T(8,128)}, f32[256,3,134]{0,2,1:T(8,128)}, u32[]{:S(2)}, u32[]{:S(2)}) collective-permute-start(f32[256,3,134]{0,2,1:T(8,128)} %copy.35), channel_id=1, source_target_pairs={{2,0},{4,2},{6,4},{3,1},{5,3},{7,5},{10,8},{12,10},{14,12},{11,9},... | collective-permute-start | bytes 1234952 | tf_op jit(solution)/shard_map/ppermute | solution.py:39
  58.4 1.3 %copy-start.2 = (f32[325,1408]{1,0:T(8,128)}, f32[325,1408]{1,0:T(8,128)S(1)}, u32[]{:S(2)}) copy-start(f32[325,1408]{1,0:T(8,128)S(1)} %concatenate.44.frc_ref.pk_ref) | copy-start | bytes 5491204
  71.4 6.8 %collective-permute-start.8 = (f32[2,2,4,3]{3,1,0,2:T(2,128)S(1)}, f32[2,2,4,3]{3,1,0,2:T(2,128)S(1)}, u32[]{:S(2)}, u32[]{:S(2)}) collective-permute-start(f32[2,2,4,3]{3,1,0,2:T(2,128)S(1)} %get-tuple-element.70), channel_id=1, source_target_pairs={{0,1},{2,3},{4,5},{6,7},{8,9},{10,11},{12,13},{14,15},{16,17},{18,... | collective-permute-start | bytes 584 | tf_op jit(solution)/shard_map/ppermute | solution.py:39
  74.2 4.1 %collective-permute-start.9 = (f32[2,2,4,3]{3,1,0,2:T(2,128)S(1)}, f32[2,2,4,3]{3,1,0,2:T(2,128)S(1)}, u32[]{:S(2)}, u32[]{:S(2)}) collective-permute-start(f32[2,2,4,3]{3,1,0,2:T(2,128)S(1)} %get-tuple-element.71), channel_id=1, source_target_pairs={{1,0},{3,2},{5,4},{7,6},{9,8},{11,10},{13,12},{15,14},{17,16},{19,... | collective-permute-start | bytes 584 | tf_op jit(solution)/shard_map/ppermute | solution.py:39
  76.8 8.4 %copy-start.3 = (f32[256,134]{1,0:T(8,128)S(1)}, f32[256,134]{1,0:T(8,128)}, u32[]{:S(2)}) copy-start(f32[256,134]{1,0:T(8,128)} %get-tuple-element.20) | copy-start | bytes 411652
  76.8 8.4 %copy-start.4 = (f32[256,134]{1,0:T(8,128)S(1)}, f32[256,134]{1,0:T(8,128)}, u32[]{:S(2)}) copy-start(f32[256,134]{1,0:T(8,128)} %get-tuple-element.21) | copy-start | bytes 411652
  76.8 8.4 %copy-start.5 = (f32[256,134]{1,0:T(8,128)S(1)}, f32[256,134]{1,0:T(8,128)}, u32[]{:S(2)}) copy-start(f32[256,134]{1,0:T(8,128)} %get-tuple-element.22) | copy-start | bytes 411652
  76.9 8.4 %copy-start.6 = (f32[256,134]{1,0:T(8,128)S(1)}, f32[256,134]{1,0:T(8,128)}, u32[]{:S(2)}) copy-start(f32[256,134]{1,0:T(8,128)} %get-tuple-element.23) | copy-start | bytes 411652
  78.4 14.2 %collective-permute-start.12 = (f32[2,2,3,134]{3,1,0,2:T(2,128)S(1)}, f32[2,2,3,134]{3,1,0,2:T(2,128)S(1)}, u32[]{:S(2)}, u32[]{:S(2)}) collective-permute-start(f32[2,2,3,134]{3,1,0,2:T(2,128)S(1)} %get-tuple-element.58), channel_id=1, source_target_pairs={{2,8},{4,10},{6,12},{10,16},{12,18},{14,20},{18,24},{20,26},{22,28... | collective-permute-start | bytes 19304 | tf_op jit(solution)/shard_map/ppermute | solution.py:40
  87.1 10.9 %collective-permute-start.11 = (f32[2,2,4,134]{3,1,0,2:T(2,128)S(1)}, f32[2,2,4,134]{3,1,0,2:T(2,128)S(1)}, u32[]{:S(2)}, u32[]{:S(2)}) collective-permute-start(f32[2,2,4,134]{3,1,0,2:T(2,128)S(1)} %pad_maximum_fusion.5), channel_id=1, source_target_pairs={{0,8},{2,10},{4,12},{6,14},{8,16},{10,18},{12,20},{14,22},{16,24},... | collective-permute-start | bytes 25736 | tf_op jit(solution)/shard_map/ppermute | solution.py:40
  90.6 7.4 %collective-permute-start.10 = (f32[2,2,3,134]{3,1,0,2:T(2,128)S(1)}, f32[2,2,3,134]{3,1,0,2:T(2,128)S(1)}, u32[]{:S(2)}, u32[]{:S(2)}) collective-permute-start(f32[2,2,3,134]{3,1,0,2:T(2,128)S(1)} %get-tuple-element.59), channel_id=1, source_target_pairs={{0,10},{2,12},{4,14},{8,18},{10,20},{12,22},{16,26},{18,28},{20,30... | collective-permute-start | bytes 19304 | tf_op jit(solution)/shard_map/ppermute | solution.py:40

commit v14 on v13

--- a/solution.py
+++ b/solution.py
@@ -72,7 +72,7 @@
     order_ref, frc_ref, pk_ref, inc_ref, ins_ref, bhi_ref, blo_ref, out_ref, trace_ref, field_ref, *, row, depth,
     width,
 ):
-    nsrc, rows, owned = out_ref.shape
+    nsrc, rows, owned = trace_ref.shape[0], bhi_ref.shape[0], trace_ref.shape[2] * 128
     cols = pk_ref.shape[1]
     classes = bhi_ref.shape[1] // rows
     lanes = 128
@@ -144,7 +144,8 @@
         for x in range(owned // lanes):
             begin = (x + width) * row + width
             chunk = pltpu.roll(u, cols - begin, 1)[:, :lanes]
-            out_ref[s, :, x * lanes : (x + 1) * lanes] = chunk
+            for part in range(rows // depth):
+                out_ref[s, part, :, x, :] = chunk[part * depth : (part + 1) * depth, :]
             for part in range(rows // depth):
                 bottom = (part + 1) * depth - 1
                 trace_ref[s, part, pl.ds(x, 1), :] = chunk[bottom : bottom + 1, :]
@@ -162,7 +163,7 @@
     return pl.pallas_call(
         functools.partial(tick_kernel, row=row, depth=depth, width=width),
         out_shape=(
-            jax.ShapeDtypeStruct((nsrc, rows, owned), jnp.float32),
+            jax.ShapeDtypeStruct((nsrc, rows // depth, depth, owned // 128, 128), jnp.float32),
             jax.ShapeDtypeStruct((nsrc, rows // depth, owned // 128, 128), jnp.float32),
         ),
         in_specs=[pl.BlockSpec(memory_space=pltpu.SMEM)] + [vmem] * 6,
@@ -261,7 +262,7 @@
             segments += [high[:, r] for r in range(width)]
             segments.append(jnp.zeros((rows.shape[0], padded - cols), jnp.float32))
             forcing_f = jnp.concatenate(segments, axis=-1)
-        tile = field.reshape(nsrc, two, depth, nx, ny)
+        tile = field
         solutions.append(tile)
         if tick + 1 < ticks:
             incoming = flat_extended(extend_y(trace, width), width, padded, ("slab",), (-1,))

time: 113 us -> 112 us (level)
  local copies, waits for them, and re-layouts: 39.5 us -> 37.1 us
    another operation x2 -> x0, local copies, waits for them, and re-layouts: 2.42 us -> none  [per_device(): return (jnp.stack(solutions, axis=0), trace[:, :, None])]
  transfers between devices with their start and end apart: 13 -> 13, of which waited for: 2 -> 2; matrix products, arithmetic and copies ran while one was open for 33% -> 32% of each run, Pallas kernels for 10% -> 10%
where the time goes in v14:
time: 112 us; the launch traced here: 111 us
  local copies, waits for them, and re-layouts  37.1 us (33%)
  starting transfers between devices  34.1 us (30%)
  Pallas kernels  22.1 us (20%)
  other arithmetic  8.59 us (8%)
  waiting for transfers between devices  7.72 us (7%)
  between operations  1.2 us (1%)
    ppermute x10, starting transfers between devices, fetch(): return lax.ppermute(block, axes[0], pairs)  23.1 us
    pallas_call x2, Pallas kernels, run_tick(): pl.pallas_call(functools.partial(tick_kernel, row=row, depth=depth, width...  22.1 us
    ppermute x3, starting transfers between devices, fetch(): return lax.ppermute(block, tuple(axes), pairs)  11 us
    ppermute x3, waiting for transfers between devices, fetch(): return lax.ppermute(block, tuple(axes), pairs)  5.44 us
    ppermute x4, local copies, waits for them, and re-layouts, fetch(): return lax.ppermute(block, axes[0], pairs)  4.5 us
    slice x2, local copies, waits for them, and re-layouts, per_device(): high_later = [fetch(r[:, :width, :], ('tx',), (1,)) for r in later]  3.57 us
    concatenate x1, local copies, waits for them, and re-layouts, per_device(): packed = jnp.concatenate(segments, axis=-1)  3.31 us
    slice x2, local copies, waits for them, and re-layouts, per_device(): corner_low = fetch(rims[..., ny - width:], ('ty',), (-1,))  3.27 us
  transfers between devices with their start and end apart: 13, of which 2 were waited for; matrix products, arithmetic and copies ran while one was open for 32% of the time, Pallas kernels for 10%

profile of v14, /device:TPU:12, one launch (start us, length us, event | category | flops | bytes accessed | tf_op | source)
XLA Modules:
  0.0 110.9 jit_solution(4910023168364368639)
XLA Ops:
  0.7 1.3 %fusion.4 = (f32[1,2,2,64,4,128]{5,4,3,2,1,0:T(4,128)S(1)}, f32[1,2,2,64,4,128]{5,4,3,2,1,0:T(4,128)S(1)}) fusion(f32[2,2,2,64,4,128]{5,4,3,2,1,0:T(4,128)} %param.6), kind=kLoop, calls=%fused_computation.58 | loop fusion | bytes 2097152 | tf_op jit(solution)/shard_map/slice | solution.py:207
  2.2 1.0 fusion.6
  3.2 3.4 %collective-permute-start = (f32[325,3,128]{2,0,1:T(8,128)}, f32[325,3,128]{2,0,1:T(8,128)S(1)}, u32[]{:S(2)}, u32[]{:S(2)}) collective-permute-start(f32[325,3,128]{2,0,1:T(8,128)} %get-tuple-element.49), channel_id=1, source_target_pairs={{0,2},{2,4},{4,6},{1,3},{3,5},{5,7},{8,10},{10,12},{12,14},{9,11},... | collective-permute-start | bytes 1497608 | tf_op jit(solution)/shard_map/ppermute | solution.py:39
  6.6 3.3 %collective-permute-start.1 = (f32[325,3,128]{2,0,1:T(8,128)}, f32[325,3,128]{2,0,1:T(8,128)S(1)}, u32[]{:S(2)}, u32[]{:S(2)}) collective-permute-start(f32[325,3,128]{2,0,1:T(8,128)} %get-tuple-element.48), channel_id=1, source_target_pairs={{2,0},{4,2},{6,4},{3,1},{5,3},{7,5},{10,8},{12,10},{14,12},{11,9},... | collective-permute-start | bytes 1497608 | tf_op jit(solution)/shard_map/ppermute | solution.py:39
  10.0 0.5 concatenate.42
  10.5 1.4 %fusion.3 = (f32[581,4,3]{2,0,1:T(8,128)}, f32[581,4,3]{2,0,1:T(8,128)S(1)}) fusion(f32[581,4,128]{2,0,1:T(8,128)S(1)} %concatenate.42), kind=kLoop, calls=%fused_computation.57 | loop fusion | bytes 111552 | tf_op jit(solution)/shard_map/slice | solution.py:45
  12.0 1.7 %copy.29 = f32[581,4,3]{0,1,2:T(4,128)S(1)} copy(f32[581,4,3]{2,0,1:T(8,128)} %get-tuple-element.36) | data formatting | bytes 55776 | tf_op jit(solution)/shard_map/slice | solution.py:45
  13.6 1.4 %collective-permute-start.4 = (f32[581,4,3]{0,1,2:T(4,128)S(1)}, f32[581,4,3]{0,1,2:T(4,128)S(1)}, u32[]{:S(2)}, u32[]{:S(2)}) collective-permute-start(f32[581,4,3]{0,1,2:T(4,128)S(1)} %copy.29), channel_id=1, source_target_pairs={{0,1},{2,3},{4,5},{6,7},{8,9},{10,11},{12,13},{14,15},{16,17},{18,... | collective-permute-start | bytes 83672 | tf_op jit(solution)/shard_map/ppermute | solution.py:39
  15.1 0.4 copy.30
  15.5 1.3 %collective-permute-start.5 = (f32[581,4,3]{0,1,2:T(4,128)S(1)}, f32[581,4,3]{0,1,2:T(4,128)S(1)}, u32[]{:S(2)}, u32[]{:S(2)}) collective-permute-start(f32[581,4,3]{0,1,2:T(4,128)S(1)} %copy.30), channel_id=1, source_target_pairs={{1,0},{3,2},{5,4},{7,6},{9,8},{11,10},{13,12},{15,14},{17,16},{19,... | collective-permute-start | bytes 83672 | tf_op jit(solution)/shard_map/ppermute | solution.py:39
  16.8 1.0 copy.47
  17.8 0.1 maximum_maximum_fusion
  18.0 0.1 broadcast_and_fusion
  18.1 0.1 convert_element_type.24
  18.2 0.6 pad_convert_fusion.ins_ref
  18.8 0.6 slice_bitcast_fusion.37
  19.4 0.7 fusion
  20.1 0.0 collective-permute-done.4
  20.1 0.4 copy.31
  20.5 0.0 collective-permute-done.5
  20.5 1.5 %copy.32 = f32[581,4,3]{2,0,1:T(8,128)} copy(f32[581,4,3]{0,1,2:T(4,128)S(1)} %collective-permute-done.5) | data formatting | bytes 55776 | tf_op jit(solution)/shard_map/ppermute | solution.py:39
  22.0 2.3 %pad_maximum_fusion = f32[581,4,134]{2,0,1:T(8,128)S(1)} fusion(f32[581,4,3]{2,0,1:T(8,128)} %copy.32, f32[581,4,128]{2,0,1:T(8,128)S(1)} %concatenate.42, f32[581,4,3]{2,0,1:T(8,128)S(1)} %copy.31), kind=kLoop, calls=%fused_computation | loop fusion | flops 622832 | bytes 2491328 | tf_op jit(solution)/shard_map/concatenate | solution.py:47
  24.3 1.4 %fusion.2 = (f32[256,3,134]{2,0,1:T(8,128)}, f32[256,3,134]{2,0,1:T(8,128)}) fusion(f32[581,4,134]{2,0,1:T(8,128)S(1)} %pad_maximum_fusion), kind=kLoop, calls=%fused_computation.56 | loop fusion | bytes 1646592 | tf_op jit(solution)/shard_map/slice | solution.py:249
  25.7 0.0 collective-permute-done
  25.7 0.4 copy-done
  26.2 2.3 %collective-permute-done.1 = f32[325,3,128]{2,0,1:T(8,128)S(1)} collective-permute-done((f32[325,3,128]{2,0,1:T(8,128)}, f32[325,3,128]{2,0,1:T(8,128)S(1)}, u32[]{:S(2)}, u32[]{:S(2)}) %collective-permute-start.1) | collective-permute-done | bytes 499232 | tf_op jit(solution)/shard_map/ppermute | solution.py:39
  28.5 1.6 %fusion.5 = (f32[325,6,3]{2,0,1:T(8,128)}, f32[325,6,3]{2,0,1:T(8,128)}) fusion(f32[325,6,128]{2,0,1:T(8,128)S(1)} %constant_dynamic-update-slice_fusion), kind=kLoop, calls=%fused_computation.59 | loop fusion | bytes 93600 | tf_op jit(solution)/shard_map/slice | solution.py:220
  30.1 1.7 %copy.23 = f32[325,6,3]{0,1,2:T(8,128)S(1)} copy(f32[325,6,3]{2,0,1:T(8,128)} %get-tuple-element.40) | data formatting | bytes 46800 | tf_op jit(solution)/shard_map/slice | solution.py:220
  31.8 1.3 %collective-permute-start.2 = (f32[325,6,3]{0,1,2:T(8,128)S(1)}, f32[325,6,3]{0,1,2:T(8,128)S(1)}, u32[]{:S(2)}, u32[]{:S(2)}) collective-permute-start(f32[325,6,3]{0,1,2:T(8,128)S(1)} %copy.23), channel_id=1, source_target_pairs={{0,1},{2,3},{4,5},{6,7},{8,9},{10,11},{12,13},{14,15},{16,17},{18,... | collective-permute-start | bytes 70208 | tf_op jit(solution)/shard_map/ppermute | solution.py:39
  33.1 1.7 %copy.24 = f32[325,6,3]{0,1,2:T(8,128)S(1)} copy(f32[325,6,3]{2,0,1:T(8,128)} %get-tuple-element.41) | data formatting | bytes 46800 | tf_op jit(solution)/shard_map/slice | solution.py:221
  34.7 1.3 %collective-permute-start.3 = (f32[325,6,3]{0,1,2:T(8,128)S(1)}, f32[325,6,3]{0,1,2:T(8,128)S(1)}, u32[]{:S(2)}, u32[]{:S(2)}) collective-permute-start(f32[325,6,3]{0,1,2:T(8,128)S(1)} %copy.24), channel_id=1, source_target_pairs={{1,0},{3,2},{5,4},{7,6},{9,8},{11,10},{13,12},{15,14},{17,16},{19,... | collective-permute-start | bytes 70208 | tf_op jit(solution)/shard_map/ppermute | solution.py:39
  36.1 1.0 slice_bitcast_fusion.13
  37.1 2.1 %copy.34 = f32[256,3,134]{0,2,1:T(8,128)} copy(f32[256,3,134]{2,0,1:T(8,128)} %get-tuple-element.25) | data formatting | bytes 823296 | tf_op jit(solution)/shard_map/slice | solution.py:248
  39.2 2.0 %collective-permute-start.6 = (f32[256,3,134]{0,2,1:T(8,128)}, f32[256,3,134]{0,2,1:T(8,128)}, u32[]{:S(2)}, u32[]{:S(2)}) collective-permute-start(f32[256,3,134]{0,2,1:T(8,128)} %copy.34), channel_id=1, source_target_pairs={{0,2},{2,4},{4,6},{1,3},{3,5},{5,7},{8,10},{10,12},{12,14},{9,11},... | collective-permute-start | bytes 1234952 | tf_op jit(solution)/shard_map/ppermute | solution.py:39
  41.2 2.1 %copy.35 = f32[256,3,134]{0,2,1:T(8,128)} copy(f32[256,3,134]{2,0,1:T(8,128)} %get-tuple-element.24) | data formatting | bytes 823296 | tf_op jit(solution)/shard_map/slice | solution.py:249
  43.4 5.1 %collective-permute-start.7 = (f32[256,3,134]{0,2,1:T(8,128)}, f32[256,3,134]{0,2,1:T(8,128)}, u32[]{:S(2)}, u32[]{:S(2)}) collective-permute-start(f32[256,3,134]{0,2,1:T(8,128)} %copy.35), channel_id=1, source_target_pairs={{2,0},{4,2},{6,4},{3,1},{5,3},{7,5},{10,8},{12,10},{14,12},{11,9},... | collective-permute-start | bytes 1234952 | tf_op jit(solution)/shard_map/ppermute | solution.py:39
  48.5 0.0 collective-permute-done.2
  48.5 1.3 %copy.25 = f32[325,6,3]{2,0,1:T(8,128)} copy(f32[325,6,3]{0,1,2:T(8,128)S(1)} %collective-permute-done.2) | data formatting | bytes 46800 | tf_op jit(solution)/shard_map/ppermute | solution.py:39
  49.8 0.0 collective-permute-done.3
  49.8 1.3 %copy.26 = f32[325,6,3]{2,0,1:T(8,128)} copy(f32[325,6,3]{0,1,2:T(8,128)S(1)} %collective-permute-done.3) | data formatting | bytes 46800 | tf_op jit(solution)/shard_map/ppermute | solution.py:39
  51.1 2.4 %pad_maximum_fusion.1 = f32[325,6,134]{2,0,1:T(8,128)S(1)} fusion(f32[325,6,3]{2,0,1:T(8,128)} %copy.26, f32[325,6,128]{2,0,1:T(8,128)S(1)} %constant_dynamic-update-slice_fusion, f32[325,6,3]{2,0,1:T(8,128)} %copy.25), kind=kLoop, calls=%fused_computation.1 | loop fusion | flops 522600 | bytes 2090400 | tf_op jit(solution)/shard_map/concatenate | solution.py:222
  53.5 1.5 %slice_bitcast_fusion = (f32[325,134]{1,0:T(8,128)S(1)}, f32[325,134]{1,0:T(8,128)S(1)}, f32[325,134]{1,0:T(8,128)}, f32[325,134]{1,0:T(8,128)}, f32[325,134]{1,...) fusion(f32[325,6,134]{2,0,1:T(8,128)S(1)} %pad_maximum_fusion.1, ...), kind=kLoop, calls=%fused_computation.6 | loop fusion | bytes 3484000 | tf_op jit(solution)/shard_map/squeeze | solution.py:230
  55.0 3.3 %concatenate.44.frc_ref.pk_ref = f32[325,1408]{1,0:T(8,128)S(1)} concatenate(f32[325,134]{1,0:T(8,128)} %get-tuple-element.35, f32[325,134]{1,0:T(8,128)} %get-tuple-element.34, f32[325,134]{1,0:T(8,128)} %get-tuple-element.33, f32[325,134]{1,0:T(8,128)} %get-tuple-element.74, f32[325,134]{1,0:T(8,128)} %get-tuple-element.75, f32[325,134]{1,0:T(8,128)} %get-tuple-element.76, ...), dimensions={1} | concatenate | bytes 3660800 | tf_op jit(solution)/shard_map/concatenate | solution.py:232
  58.4 0.7 reshape.62.inc_ref
  59.1 0.6 copy-done.2
  59.6 11.1 %shard_map.77 = (f32[2,2,64,4,128]{4,3,2,1,0:T(4,128)}, f32[2,2,4,128]{3,2,1,0:T(4,128)}) custom-call(s32[2]{0:T(128)} %get-tuple-element.72.order_ref, f32[325,1408]{1,0:T(8,128)} %copy-done.2, f32[325,1408]{1,0:T(8,128)} %copy-done.2, f32[2,2,1408]{2,1,0:T(2,128)} %reshape.62.inc_ref, f32[1,1408]{1,0:T(1,128)} %pad_convert_fusion.ins_ref, ...), custom_call_target="tpu_custom_call" | custom-call | flops 4429185024 | bytes 2812288 | tf_op jit(solution)/shard_map/pallas_call | solution.py:163
  70.7 0.7 copy.42
  71.4 0.1 fusion.8
  71.5 2.7 %collective-permute-start.8 = (f32[2,2,4,3]{3,1,0,2:T(2,128)S(1)}, f32[2,2,4,3]{3,1,0,2:T(2,128)S(1)}, u32[]{:S(2)}, u32[]{:S(2)}) collective-permute-start(f32[2,2,4,3]{3,1,0,2:T(2,128)S(1)} %get-tuple-element.70), channel_id=1, source_target_pairs={{0,1},{2,3},{4,5},{6,7},{8,9},{10,11},{12,13},{14,15},{16,17},{18,... | collective-permute-start | bytes 584 | tf_op jit(solution)/shard_map/ppermute | solution.py:39
  74.3 1.3 %collective-permute-start.9 = (f32[2,2,4,3]{3,1,0,2:T(2,128)S(1)}, f32[2,2,4,3]{3,1,0,2:T(2,128)S(1)}, u32[]{:S(2)}, u32[]{:S(2)}) collective-permute-start(f32[2,2,4,3]{3,1,0,2:T(2,128)S(1)} %get-tuple-element.71), channel_id=1, source_target_pairs={{1,0},{3,2},{5,4},{7,6},{9,8},{11,10},{13,12},{15,14},{17,16},{19,... | collective-permute-start | bytes 584 | tf_op jit(solution)/shard_map/ppermute | solution.py:39
  75.6 0.0 collective-permute-done.6
  75.6 1.3 %copy.39 = f32[256,3,134]{2,0,1:T(8,128)S(1)} copy(f32[256,3,134]{0,2,1:T(8,128)} %collective-permute-done.7) | data formatting | bytes 823296 | tf_op jit(solution)/shard_map/optimization_barrier | solution.py:259
  76.9 0.1 slice_bitcast_fusion.10
  77.0 1.3 %copy.36 = f32[256,3,134]{2,0,1:T(8,128)S(1)} copy(f32[256,3,134]{0,2,1:T(8,128)} %collective-permute-done.6) | data formatting | bytes 823296 | tf_op jit(solution)/shard_map/optimization_barrier | solution.py:259
  78.3 0.1 pad_maximum_fusion.5
  78.4 5.6 %collective-permute-start.12 = (f32[2,2,3,134]{3,1,0,2:T(2,128)S(1)}, f32[2,2,3,134]{3,1,0,2:T(2,128)S(1)}, u32[]{:S(2)}, u32[]{:S(2)}) collective-permute-start(f32[2,2,3,134]{3,1,0,2:T(2,128)S(1)} %get-tuple-element.58), channel_id=1, source_target_pairs={{2,8},{4,10},{6,12},{10,16},{12,18},{14,20},{18,24},{20,26},{22,28... | collective-permute-start | bytes 19304 | tf_op jit(solution)/shard_map/ppermute | solution.py:40
  84.0 0.1 slice_bitcast_fusion.17
  84.2 1.8 %concatenate.49.frc_ref = f32[256,1408]{1,0:T(8,128)} concatenate(f32[256,134]{1,0:T(8,128)S(1)} %get-tuple-element.47, f32[256,134]{1,0:T(8,128)S(1)} %get-tuple-element.46, f32[256,134]{1,0:T(8,128)S(1)} %get-tuple-element.45, f32[256,134]{1,0:T(8,128)S(1)} %copy-done.6, f32[256,134]{1,0:T(8,128)S(1)} %copy-done.5, f32[256,134]{1,0:T(8,128)S(1)} %copy-done.4, ...), dimensions={1} | concatenate | bytes 2883584 | tf_op jit(solution)/shard_map/concatenate | solution.py:264
  86.0 3.5 %collective-permute-start.11 = (f32[2,2,4,134]{3,1,0,2:T(2,128)S(1)}, f32[2,2,4,134]{3,1,0,2:T(2,128)S(1)}, u32[]{:S(2)}, u32[]{:S(2)}) collective-permute-start(f32[2,2,4,134]{3,1,0,2:T(2,128)S(1)} %pad_maximum_fusion.5), channel_id=1, source_target_pairs={{0,8},{2,10},{4,12},{6,14},{8,16},{10,18},{12,20},{14,22},{16,24},... | collective-permute-start | bytes 25736 | tf_op jit(solution)/shard_map/ppermute | solution.py:40
  89.5 1.9 %collective-permute-start.10 = (f32[2,2,3,134]{3,1,0,2:T(2,128)S(1)}, f32[2,2,3,134]{3,1,0,2:T(2,128)S(1)}, u32[]{:S(2)}, u32[]{:S(2)}) collective-permute-start(f32[2,2,3,134]{3,1,0,2:T(2,128)S(1)} %get-tuple-element.59), channel_id=1, source_target_pairs={{0,10},{2,12},{4,14},{8,18},{10,20},{12,22},{16,26},{18,28},{20,30... | collective-permute-start | bytes 19304 | tf_op jit(solution)/shard_map/ppermute | solution.py:40
  91.4 5.4 %collective-permute-done.10 = f32[2,2,3,134]{3,1,0,2:T(2,128)S(1)} collective-permute-done((f32[2,2,3,134]{3,1,0,2:T(2,128)S(1)}, f32[2,2,3,134]{3,1,0,2:T(2,128)S(1)}, u32[]{:S(2)}, u32[]{:S(2)}) %collective-permute-start.10) | collective-permute-done | bytes 6464 | tf_op jit(solution)/shard_map/ppermute | solution.py:40
  96.9 0.7 concatenate.51.inc_ref
  97.6 11.0 %shard_map.78 = (f32[2,2,64,4,128]{4,3,2,1,0:T(4,128)}, f32[2,2,4,128]{3,2,1,0:T(4,128)}) custom-call(s32[2]{0:T(128)} %get-tuple-element.73.order_ref, f32[256,1408]{1,0:T(8,128)} %concatenate.49.frc_ref, f32[325,1408]{1,0:T(8,128)} %copy-done.2, f32[2,2,1408]{2,1,0:T(2,128)} %concatenate.51.inc_ref, f32[1,1408]{1,0:T(1,128)} %pad_convert_fusion.ins_ref, ...), custom_call_target="tpu_custom_call" | custom-call | flops 4429185024 | bytes 2423680 | tf_op jit(solution)/shard_map/pallas_call | solution.py:163
  108.7 2.2 %pad_maximum_fusion.2 = f32[2,2,2,64,4,128]{5,4,3,2,1,0:T(4,128)} fusion(f32[1,2,2,64,4,128]{5,4,3,2,1,0:T(4,128)} %bitcast.96, f32[1,2,2,64,4,128]{5,4,3,2,1,0:T(4,128)S(1)} %bitcast.95), kind=kLoop, calls=%fused_computation.2 | loop fusion | flops 262144 | bytes 2097152 | tf_op jit(solution)/shard_map/stack | solution.py:269
  (48 shorter events, 0.4 us)
Async XLA Ops:
  0.6 1.4 %copy-start.8 = (f32[64,4,128]{2,1,0:T(4,128)S(1)}, f32[64,4,128]{2,1,0:T(4,128)}, u32[]{:S(2)}) copy-start(f32[64,4,128]{2,1,0:T(4,128)} %param.7) | copy-start | bytes 393220
  0.6 1.4 %copy-start.9 = (f32[2,2,1,4,128]{4,3,2,1,0:T(4,128)S(1)}, f32[2,2,1,4,128]{4,3,2,1,0:T(4,128)}, u32[]{:S(2)}) copy-start(f32[2,2,1,4,128]{4,3,2,1,0:T(4,128)} %param.11) | copy-start | bytes 24580
  0.7 1.5 %copy-start.10 = (s32[1,4,128]{2,1,0:T(4,128)S(1)}, s32[1,4,128]{2,1,0:T(4,128)}, u32[]{:S(2)}) copy-start(s32[1,4,128]{2,1,0:T(4,128)} %param.9) | copy-start | bytes 6148
  3.2 22.5 %collective-permute-start = (f32[325,3,128]{2,0,1:T(8,128)}, f32[325,3,128]{2,0,1:T(8,128)S(1)}, u32[]{:S(2)}, u32[]{:S(2)}) collective-permute-start(f32[325,3,128]{2,0,1:T(8,128)} %get-tuple-element.49), channel_id=1, source_target_pairs={{0,2},{2,4},{4,6},{1,3},{3,5},{5,7},{8,10},{10,12},{12,14},{9,11},... | collective-permute-start | bytes 1497608 | tf_op jit(solution)/shard_map/ppermute | solution.py:39
  6.6 21.8 %collective-permute-start.1 = (f32[325,3,128]{2,0,1:T(8,128)}, f32[325,3,128]{2,0,1:T(8,128)S(1)}, u32[]{:S(2)}, u32[]{:S(2)}) collective-permute-start(f32[325,3,128]{2,0,1:T(8,128)} %get-tuple-element.48), channel_id=1, source_target_pairs={{2,0},{4,2},{6,4},{3,1},{5,3},{7,5},{10,8},{12,10},{14,12},{11,9},... | collective-permute-start | bytes 1497608 | tf_op jit(solution)/shard_map/ppermute | solution.py:39
  13.6 5.2 %copy-start.11 = (s32[2,1,2]{2,1,0:T(1,128)S(1)}, s32[2,1,2]{2,1,0:T(1,128)}, u32[]{:S(2)}) copy-start(s32[2,1,2]{2,1,0:T(1,128)} %param.10) | copy-start | bytes 52
  13.6 6.5 %collective-permute-start.4 = (f32[581,4,3]{0,1,2:T(4,128)S(1)}, f32[581,4,3]{0,1,2:T(4,128)S(1)}, u32[]{:S(2)}, u32[]{:S(2)}) collective-permute-start(f32[581,4,3]{0,1,2:T(4,128)S(1)} %copy.29), channel_id=1, source_target_pairs={{0,1},{2,3},{4,5},{6,7},{8,9},{10,11},{12,13},{14,15},{16,17},{18,... | collective-permute-start | bytes 83672 | tf_op jit(solution)/shard_map/ppermute | solution.py:39
  15.5 5.1 %collective-permute-start.5 = (f32[581,4,3]{0,1,2:T(4,128)S(1)}, f32[581,4,3]{0,1,2:T(4,128)S(1)}, u32[]{:S(2)}, u32[]{:S(2)}) collective-permute-start(f32[581,4,3]{0,1,2:T(4,128)S(1)} %copy.30), channel_id=1, source_target_pairs={{1,0},{3,2},{5,4},{7,6},{9,8},{11,10},{13,12},{15,14},{17,16},{19,... | collective-permute-start | bytes 83672 | tf_op jit(solution)/shard_map/ppermute | solution.py:39
  24.3 1.9 %copy-start = (f32[581,4,134]{2,0,1:T(8,128)}, f32[581,4,134]{2,0,1:T(8,128)S(1)}, u32[]{:S(2)}) copy-start(f32[581,4,134]{2,0,1:T(8,128)S(1)} %pad_maximum_fusion) | copy-start | bytes 3736996
  28.5 7.6 %copy-start.1 = (f32[581,4,134]{2,0,1:T(8,128)S(1)}, f32[581,4,134]{2,0,1:T(8,128)}, u32[]{:S(2)}) copy-start(f32[581,4,134]{2,0,1:T(8,128)} %copy-done) | copy-start | bytes 3736996
  31.8 16.7 %collective-permute-start.2 = (f32[325,6,3]{0,1,2:T(8,128)S(1)}, f32[325,6,3]{0,1,2:T(8,128)S(1)}, u32[]{:S(2)}, u32[]{:S(2)}) collective-permute-start(f32[325,6,3]{0,1,2:T(8,128)S(1)} %copy.23), channel_id=1, source_target_pairs={{0,1},{2,3},{4,5},{6,7},{8,9},{10,11},{12,13},{14,15},{16,17},{18,... | collective-permute-start | bytes 70208 | tf_op jit(solution)/shard_map/ppermute | solution.py:39
  34.7 15.1 %collective-permute-start.3 = (f32[325,6,3]{0,1,2:T(8,128)S(1)}, f32[325,6,3]{0,1,2:T(8,128)S(1)}, u32[]{:S(2)}, u32[]{:S(2)}) collective-permute-start(f32[325,6,3]{0,1,2:T(8,128)S(1)} %copy.24), channel_id=1, source_target_pairs={{1,0},{3,2},{5,4},{7,6},{9,8},{11,10},{13,12},{15,14},{17,16},{19,... | collective-permute-start | bytes 70208 | tf_op jit(solution)/shard_map/ppermute | solution.py:39
  39.2 36.3 %collective-permute-start.6 = (f32[256,3,134]{0,2,1:T(8,128)}, f32[256,3,134]{0,2,1:T(8,128)}, u32[]{:S(2)}, u32[]{:S(2)}) collective-permute-start(f32[256,3,134]{0,2,1:T(8,128)} %copy.34), channel_id=1, source_target_pairs={{0,2},{2,4},{4,6},{1,3},{3,5},{5,7},{8,10},{10,12},{12,14},{9,11},... | collective-permute-start | bytes 1234952 | tf_op jit(solution)/shard_map/ppermute | solution.py:39
  43.4 32.2 %collective-permute-start.7 = (f32[256,3,134]{0,2,1:T(8,128)}, f32[256,3,134]{0,2,1:T(8,128)}, u32[]{:S(2)}, u32[]{:S(2)}) collective-permute-start(f32[256,3,134]{0,2,1:T(8,128)} %copy.35), channel_id=1, source_target_pairs={{2,0},{4,2},{6,4},{3,1},{5,3},{7,5},{10,8},{12,10},{14,12},{11,9},... | collective-permute-start | bytes 1234952 | tf_op jit(solution)/shard_map/ppermute | solution.py:39
  58.4 1.3 %copy-start.2 = (f32[325,1408]{1,0:T(8,128)}, f32[325,1408]{1,0:T(8,128)S(1)}, u32[]{:S(2)}) copy-start(f32[325,1408]{1,0:T(8,128)S(1)} %concatenate.44.frc_ref.pk_ref) | copy-start | bytes 5491204
  71.5 6.8 %collective-permute-start.8 = (f32[2,2,4,3]{3,1,0,2:T(2,128)S(1)}, f32[2,2,4,3]{3,1,0,2:T(2,128)S(1)}, u32[]{:S(2)}, u32[]{:S(2)}) collective-permute-start(f32[2,2,4,3]{3,1,0,2:T(2,128)S(1)} %get-tuple-element.70), channel_id=1, source_target_pairs={{0,1},{2,3},{4,5},{6,7},{8,9},{10,11},{12,13},{14,15},{16,17},{18,... | collective-permute-start | bytes 584 | tf_op jit(solution)/shard_map/ppermute | solution.py:39
  74.3 4.1 %collective-permute-start.9 = (f32[2,2,4,3]{3,1,0,2:T(2,128)S(1)}, f32[2,2,4,3]{3,1,0,2:T(2,128)S(1)}, u32[]{:S(2)}, u32[]{:S(2)}) collective-permute-start(f32[2,2,4,3]{3,1,0,2:T(2,128)S(1)} %get-tuple-element.71), channel_id=1, source_target_pairs={{1,0},{3,2},{5,4},{7,6},{9,8},{11,10},{13,12},{15,14},{17,16},{19,... | collective-permute-start | bytes 584 | tf_op jit(solution)/shard_map/ppermute | solution.py:39
  76.9 7.3 %copy-start.3 = (f32[256,134]{1,0:T(8,128)S(1)}, f32[256,134]{1,0:T(8,128)}, u32[]{:S(2)}) copy-start(f32[256,134]{1,0:T(8,128)} %get-tuple-element.20) | copy-start | bytes 411652
  76.9 7.3 %copy-start.4 = (f32[256,134]{1,0:T(8,128)S(1)}, f32[256,134]{1,0:T(8,128)}, u32[]{:S(2)}) copy-start(f32[256,134]{1,0:T(8,128)} %get-tuple-element.21) | copy-start | bytes 411652
  76.9 7.3 %copy-start.5 = (f32[256,134]{1,0:T(8,128)S(1)}, f32[256,134]{1,0:T(8,128)}, u32[]{:S(2)}) copy-start(f32[256,134]{1,0:T(8,128)} %get-tuple-element.22) | copy-start | bytes 411652
  76.9 7.3 %copy-start.6 = (f32[256,134]{1,0:T(8,128)S(1)}, f32[256,134]{1,0:T(8,128)}, u32[]{:S(2)}) copy-start(f32[256,134]{1,0:T(8,128)} %get-tuple-element.23) | copy-start | bytes 411652
  78.4 13.0 %collective-permute-start.12 = (f32[2,2,3,134]{3,1,0,2:T(2,128)S(1)}, f32[2,2,3,134]{3,1,0,2:T(2,128)S(1)}, u32[]{:S(2)}, u32[]{:S(2)}) collective-permute-start(f32[2,2,3,134]{3,1,0,2:T(2,128)S(1)} %get-tuple-element.58), channel_id=1, source_target_pairs={{2,8},{4,10},{6,12},{10,16},{12,18},{14,20},{18,24},{20,26},{22,28... | collective-permute-start | bytes 19304 | tf_op jit(solution)/shard_map/ppermute | solution.py:40
  86.0 10.9 %collective-permute-start.11 = (f32[2,2,4,134]{3,1,0,2:T(2,128)S(1)}, f32[2,2,4,134]{3,1,0,2:T(2,128)S(1)}, u32[]{:S(2)}, u32[]{:S(2)}) collective-permute-start(f32[2,2,4,134]{3,1,0,2:T(2,128)S(1)} %pad_maximum_fusion.5), channel_id=1, source_target_pairs={{0,8},{2,10},{4,12},{6,14},{8,16},{10,18},{12,20},{14,22},{16,24},... | collective-permute-start | bytes 25736 | tf_op jit(solution)/shard_map/ppermute | solution.py:40
  89.5 7.4 %collective-permute-start.10 = (f32[2,2,3,134]{3,1,0,2:T(2,128)S(1)}, f32[2,2,3,134]{3,1,0,2:T(2,128)S(1)}, u32[]{:S(2)}, u32[]{:S(2)}) collective-permute-start(f32[2,2,3,134]{3,1,0,2:T(2,128)S(1)} %get-tuple-element.59), channel_id=1, source_target_pairs={{0,10},{2,12},{4,14},{8,18},{10,20},{12,22},{16,26},{18,28},{20,30... | collective-permute-start | bytes 19304 | tf_op jit(solution)/shard_map/ppermute | solution.py:40
  97.6 11.0 %copy-start.7 = (f32[2,2,64,4,128]{4,3,2,1,0:T(4,128)S(1)}, f32[2,2,64,4,128]{4,3,2,1,0:T(4,128)}, u32[]{:S(2)}) copy-start(f32[2,2,64,4,128]{4,3,2,1,0:T(4,128)} %get-tuple-element.10) | copy-start | bytes 1572868

commit v15 on v14

--- a/solution.py
+++ b/solution.py
@@ -69,9 +69,11 @@
 
 
 def tick_kernel(
-    order_ref, frc_ref, pk_ref, inc_ref, ins_ref, bhi_ref, blo_ref, out_ref, trace_ref, field_ref, *, row, depth,
-    width,
+    order_ref, frc_ref, pk_ref, inc_ref, ins_ref, bhi_ref, blo_ref, *rest, row, depth, width, tick
 ):
+    out_ref, trace_ref, field_ref = rest[-3:]
+    if tick:
+        out_ref[:tick] = rest[0][...]
     nsrc, rows, owned = trace_ref.shape[0], bhi_ref.shape[0], trace_ref.shape[2] * 128
     cols = pk_ref.shape[1]
     classes = bhi_ref.shape[1] // rows
@@ -145,7 +147,7 @@
             begin = (x + width) * row + width
             chunk = pltpu.roll(u, cols - begin, 1)[:, :lanes]
             for part in range(rows // depth):
-                out_ref[s, part, :, x, :] = chunk[part * depth : (part + 1) * depth, :]
+                out_ref[tick, s, part, :, x, :] = chunk[part * depth : (part + 1) * depth, :]
             for part in range(rows // depth):
                 bottom = (part + 1) * depth - 1
                 trace_ref[s, part, pl.ds(x, 1), :] = chunk[bottom : bottom + 1, :]
@@ -154,19 +156,19 @@
     lax.fori_loop(0, nsrc, one_source, 0)
 
 
-def run_tick(order, forcing, packed, incoming, ins, bhi, blo, row, depth, width, owned):
+def run_tick(order, forcing, packed, incoming, ins, bhi, blo, row, depth, width, owned, tick, done):
     nsrc = incoming.shape[0]
     rows, stacked = bhi.shape
     cols = packed.shape[1]
     flops = nsrc * (CORR + 1) * 3 * 2 * rows * stacked * cols
     vmem = pl.BlockSpec(memory_space=pltpu.VMEM)
     return pl.pallas_call(
-        functools.partial(tick_kernel, row=row, depth=depth, width=width),
+        functools.partial(tick_kernel, row=row, depth=depth, width=width, tick=tick),
         out_shape=(
-            jax.ShapeDtypeStruct((nsrc, rows // depth, depth, owned // 128, 128), jnp.float32),
+            jax.ShapeDtypeStruct((tick + 1, nsrc, rows // depth, depth, owned // 128, 128), jnp.float32),
             jax.ShapeDtypeStruct((nsrc, rows // depth, owned // 128, 128), jnp.float32),
         ),
-        in_specs=[pl.BlockSpec(memory_space=pltpu.SMEM)] + [vmem] * 6,
+        in_specs=[pl.BlockSpec(memory_space=pltpu.SMEM)] + [vmem] * (6 + (tick > 0)),
         out_specs=(vmem, vmem),
         scratch_shapes=[pltpu.VMEM((rows, cols), jnp.float32)],
         cost_estimate=pl.CostEstimate(
@@ -174,7 +176,7 @@
             transcendentals=0,
             bytes_accessed=4 * (forcing.size + packed.size // 4 + nsrc * rows * owned),
         ),
-    )(order, forcing, packed, incoming, ins, bhi, blo)
+    )(*([order, forcing, packed, incoming, ins, bhi, blo] + ([done] if tick else [])))
 
 
 def block_matrix(inverse):
@@ -247,12 +249,13 @@
     incoming = packed[first_pending : first_pending + nsrc * two].reshape(nsrc, two, padded)
     low_later = [fetch(r[:, nx - width :, :], ("tx",), (-1,)) for r in later]
     high_later = [fetch(r[:, :width, :], ("tx",), (1,)) for r in later]
-    solutions = []
     trace = None
+    field = None
     forcing_f = packed
     for tick in range(ticks):
         field, trace = run_tick(
-            orders[tick], forcing_f, packed, incoming, inside, bhi, blo, ey, depth, width, nx * ny
+            orders[tick], forcing_f, packed, incoming, inside, bhi, blo, ey, depth, width, nx * ny,
+            tick, field,
         )
         if tick + 1 < ticks:
             rows = later[tick]
@@ -262,11 +265,9 @@
             segments += [high[:, r] for r in range(width)]
             segments.append(jnp.zeros((rows.shape[0], padded - cols), jnp.float32))
             forcing_f = jnp.concatenate(segments, axis=-1)
-        tile = field
-        solutions.append(tile)
         if tick + 1 < ticks:
             incoming = flat_extended(extend_y(trace, width), width, padded, ("slab",), (-1,))
-    return (jnp.stack(solutions, axis=0), trace[:, :, None])
+    return (field, trace[:, :, None])
 
 
 def solution(mesh):

time: 112 us -> 110 us (0.982)
  other arithmetic: 8.59 us -> 6.33 us
    another operation x1 -> x0, other arithmetic: 2.25 us -> none  [per_device(): return (jnp.stack(solutions, axis=0), trace[:, :, None])]
  transfers between devices with their start and end apart: 13 -> 13, of which waited for: 2 -> 2; matrix products, arithmetic and copies ran while one was open for 32% -> 33% of each run, Pallas kernels for 10% -> 10%
where the time goes in v15:
time: 110 us; the launch traced here: 109 us
  local copies, waits for them, and re-layouts  37.1 us (34%)
  starting transfers between devices  34.1 us (31%)
  Pallas kernels  22.5 us (20%)
  waiting for transfers between devices  7.76 us (7%)
  other arithmetic  6.33 us (6%)
  between operations  1.2 us (1%)
    ppermute x10, starting transfers between devices, fetch(): return lax.ppermute(block, axes[0], pairs)  23.1 us
    pallas_call x2, Pallas kernels, run_tick(): pl.pallas_call(functools.partial(tick_kernel, row=row, depth=depth, width...  22.5 us
    ppermute x3, starting transfers between devices, fetch(): return lax.ppermute(block, tuple(axes), pairs)  11 us
    ppermute x3, waiting for transfers between devices, fetch(): return lax.ppermute(block, tuple(axes), pairs)  5.44 us
    ppermute x4, local copies, waits for them, and re-layouts, fetch(): return lax.ppermute(block, axes[0], pairs)  4.5 us
    slice x2, local copies, waits for them, and re-layouts, per_device(): high_later = [fetch(r[:, :width, :], ('tx',), (1,)) for r in later]  3.58 us
    concatenate x1, local copies, waits for them, and re-layouts, per_device(): packed = jnp.concatenate(segments, axis=-1)  3.31 us
    slice x2, local copies, waits for them, and re-layouts, per_device(): corner_low = fetch(rims[..., ny - width:], ('ty',), (-1,))  3.27 us
  transfers between devices with their start and end apart: 13, of which 2 were waited for; matrix products, arithmetic and copies ran while one was open for 33% of the time, Pallas kernels for 10%

profile of v15, /device:TPU:12, one launch (start us, length us, event | category | flops | bytes accessed | tf_op | source)
XLA Modules:
  0.0 109.0 jit_solution(6782425147511784921)
XLA Ops:
  0.7 1.3 %fusion.4 = (f32[1,2,2,64,4,128]{5,4,3,2,1,0:T(4,128)S(1)}, f32[1,2,2,64,4,128]{5,4,3,2,1,0:T(4,128)S(1)}) fusion(f32[2,2,2,64,4,128]{5,4,3,2,1,0:T(4,128)} %param.6), kind=kLoop, calls=%fused_computation.57 | loop fusion | bytes 2097152 | tf_op jit(solution)/shard_map/slice | solution.py:209
  2.2 1.0 fusion.6
  3.2 3.4 %collective-permute-start = (f32[325,3,128]{2,0,1:T(8,128)}, f32[325,3,128]{2,0,1:T(8,128)S(1)}, u32[]{:S(2)}, u32[]{:S(2)}) collective-permute-start(f32[325,3,128]{2,0,1:T(8,128)} %get-tuple-element.49), channel_id=1, source_target_pairs={{0,2},{2,4},{4,6},{1,3},{3,5},{5,7},{8,10},{10,12},{12,14},{9,11},... | collective-permute-start | bytes 1497608 | tf_op jit(solution)/shard_map/ppermute | solution.py:39
  6.6 3.3 %collective-permute-start.1 = (f32[325,3,128]{2,0,1:T(8,128)}, f32[325,3,128]{2,0,1:T(8,128)S(1)}, u32[]{:S(2)}, u32[]{:S(2)}) collective-permute-start(f32[325,3,128]{2,0,1:T(8,128)} %get-tuple-element.48), channel_id=1, source_target_pairs={{2,0},{4,2},{6,4},{3,1},{5,3},{7,5},{10,8},{12,10},{14,12},{11,9},... | collective-permute-start | bytes 1497608 | tf_op jit(solution)/shard_map/ppermute | solution.py:39
  10.0 0.5 concatenate.42
  10.5 1.4 %fusion.3 = (f32[581,4,3]{2,0,1:T(8,128)}, f32[581,4,3]{2,0,1:T(8,128)S(1)}) fusion(f32[581,4,128]{2,0,1:T(8,128)S(1)} %concatenate.42), kind=kLoop, calls=%fused_computation.56 | loop fusion | bytes 111552 | tf_op jit(solution)/shard_map/slice | solution.py:45
  12.0 1.7 %copy.29 = f32[581,4,3]{0,1,2:T(4,128)S(1)} copy(f32[581,4,3]{2,0,1:T(8,128)} %get-tuple-element.36) | data formatting | bytes 55776 | tf_op jit(solution)/shard_map/slice | solution.py:45
  13.6 1.4 %collective-permute-start.4 = (f32[581,4,3]{0,1,2:T(4,128)S(1)}, f32[581,4,3]{0,1,2:T(4,128)S(1)}, u32[]{:S(2)}, u32[]{:S(2)}) collective-permute-start(f32[581,4,3]{0,1,2:T(4,128)S(1)} %copy.29), channel_id=1, source_target_pairs={{0,1},{2,3},{4,5},{6,7},{8,9},{10,11},{12,13},{14,15},{16,17},{18,... | collective-permute-start | bytes 83672 | tf_op jit(solution)/shard_map/ppermute | solution.py:39
  15.1 0.4 copy.30
  15.5 1.3 %collective-permute-start.5 = (f32[581,4,3]{0,1,2:T(4,128)S(1)}, f32[581,4,3]{0,1,2:T(4,128)S(1)}, u32[]{:S(2)}, u32[]{:S(2)}) collective-permute-start(f32[581,4,3]{0,1,2:T(4,128)S(1)} %copy.30), channel_id=1, source_target_pairs={{1,0},{3,2},{5,4},{7,6},{9,8},{11,10},{13,12},{15,14},{17,16},{19,... | collective-permute-start | bytes 83672 | tf_op jit(solution)/shard_map/ppermute | solution.py:39
  16.8 1.0 copy.47
  17.8 0.1 maximum_maximum_fusion
  18.0 0.1 broadcast_and_fusion
  18.1 0.1 convert_element_type.24
  18.2 0.6 pad_convert_fusion.ins_ref
  18.8 0.6 slice_bitcast_fusion.36
  19.4 0.7 fusion
  20.1 0.0 collective-permute-done.4
  20.1 0.4 copy.31
  20.5 0.0 collective-permute-done.5
  20.5 1.5 %copy.32 = f32[581,4,3]{2,0,1:T(8,128)} copy(f32[581,4,3]{0,1,2:T(4,128)S(1)} %collective-permute-done.5) | data formatting | bytes 55776 | tf_op jit(solution)/shard_map/ppermute | solution.py:39
  22.0 2.3 %pad_maximum_fusion = f32[581,4,134]{2,0,1:T(8,128)S(1)} fusion(f32[581,4,3]{2,0,1:T(8,128)} %copy.32, f32[581,4,128]{2,0,1:T(8,128)S(1)} %concatenate.42, f32[581,4,3]{2,0,1:T(8,128)S(1)} %copy.31), kind=kLoop, calls=%fused_computation | loop fusion | flops 622832 | bytes 2491328 | tf_op jit(solution)/shard_map/concatenate | solution.py:47
  24.2 1.4 %fusion.2 = (f32[256,3,134]{2,0,1:T(8,128)}, f32[256,3,134]{2,0,1:T(8,128)}) fusion(f32[581,4,134]{2,0,1:T(8,128)S(1)} %pad_maximum_fusion), kind=kLoop, calls=%fused_computation.55 | loop fusion | bytes 1646592 | tf_op jit(solution)/shard_map/slice | solution.py:251
  25.7 0.4 copy-done
  26.1 2.3 %collective-permute-done.1 = f32[325,3,128]{2,0,1:T(8,128)S(1)} collective-permute-done((f32[325,3,128]{2,0,1:T(8,128)}, f32[325,3,128]{2,0,1:T(8,128)S(1)}, u32[]{:S(2)}, u32[]{:S(2)}) %collective-permute-start.1) | collective-permute-done | bytes 499232 | tf_op jit(solution)/shard_map/ppermute | solution.py:39
  28.5 1.6 %fusion.5 = (f32[325,6,3]{2,0,1:T(8,128)}, f32[325,6,3]{2,0,1:T(8,128)}) fusion(f32[325,6,128]{2,0,1:T(8,128)S(1)} %constant_dynamic-update-slice_fusion), kind=kLoop, calls=%fused_computation.58 | loop fusion | bytes 93600 | tf_op jit(solution)/shard_map/slice | solution.py:222
  30.1 1.7 %copy.23 = f32[325,6,3]{0,1,2:T(8,128)S(1)} copy(f32[325,6,3]{2,0,1:T(8,128)} %get-tuple-element.40) | data formatting | bytes 46800 | tf_op jit(solution)/shard_map/slice | solution.py:222
  31.8 1.3 %collective-permute-start.2 = (f32[325,6,3]{0,1,2:T(8,128)S(1)}, f32[325,6,3]{0,1,2:T(8,128)S(1)}, u32[]{:S(2)}, u32[]{:S(2)}) collective-permute-start(f32[325,6,3]{0,1,2:T(8,128)S(1)} %copy.23), channel_id=1, source_target_pairs={{0,1},{2,3},{4,5},{6,7},{8,9},{10,11},{12,13},{14,15},{16,17},{18,... | collective-permute-start | bytes 70208 | tf_op jit(solution)/shard_map/ppermute | solution.py:39
  33.1 1.7 %copy.24 = f32[325,6,3]{0,1,2:T(8,128)S(1)} copy(f32[325,6,3]{2,0,1:T(8,128)} %get-tuple-element.41) | data formatting | bytes 46800 | tf_op jit(solution)/shard_map/slice | solution.py:223
  34.7 1.3 %collective-permute-start.3 = (f32[325,6,3]{0,1,2:T(8,128)S(1)}, f32[325,6,3]{0,1,2:T(8,128)S(1)}, u32[]{:S(2)}, u32[]{:S(2)}) collective-permute-start(f32[325,6,3]{0,1,2:T(8,128)S(1)} %copy.24), channel_id=1, source_target_pairs={{1,0},{3,2},{5,4},{7,6},{9,8},{11,10},{13,12},{15,14},{17,16},{19,... | collective-permute-start | bytes 70208 | tf_op jit(solution)/shard_map/ppermute | solution.py:39
  36.1 1.0 slice_bitcast_fusion.13
  37.1 2.1 %copy.34 = f32[256,3,134]{0,2,1:T(8,128)} copy(f32[256,3,134]{2,0,1:T(8,128)} %get-tuple-element.25) | data formatting | bytes 823296 | tf_op jit(solution)/shard_map/slice | solution.py:250
  39.2 2.0 %collective-permute-start.6 = (f32[256,3,134]{0,2,1:T(8,128)}, f32[256,3,134]{0,2,1:T(8,128)}, u32[]{:S(2)}, u32[]{:S(2)}) collective-permute-start(f32[256,3,134]{0,2,1:T(8,128)} %copy.34), channel_id=1, source_target_pairs={{0,2},{2,4},{4,6},{1,3},{3,5},{5,7},{8,10},{10,12},{12,14},{9,11},... | collective-permute-start | bytes 1234952 | tf_op jit(solution)/shard_map/ppermute | solution.py:39
  41.2 2.1 %copy.35 = f32[256,3,134]{0,2,1:T(8,128)} copy(f32[256,3,134]{2,0,1:T(8,128)} %get-tuple-element.24) | data formatting | bytes 823296 | tf_op jit(solution)/shard_map/slice | solution.py:251
  43.4 5.1 %collective-permute-start.7 = (f32[256,3,134]{0,2,1:T(8,128)}, f32[256,3,134]{0,2,1:T(8,128)}, u32[]{:S(2)}, u32[]{:S(2)}) collective-permute-start(f32[256,3,134]{0,2,1:T(8,128)} %copy.35), channel_id=1, source_target_pairs={{2,0},{4,2},{6,4},{3,1},{5,3},{7,5},{10,8},{12,10},{14,12},{11,9},... | collective-permute-start | bytes 1234952 | tf_op jit(solution)/shard_map/ppermute | solution.py:39
  48.5 1.3 %copy.25 = f32[325,6,3]{2,0,1:T(8,128)} copy(f32[325,6,3]{0,1,2:T(8,128)S(1)} %collective-permute-done.2) | data formatting | bytes 46800 | tf_op jit(solution)/shard_map/ppermute | solution.py:39
  49.8 0.0 collective-permute-done.3
  49.8 1.3 %copy.26 = f32[325,6,3]{2,0,1:T(8,128)} copy(f32[325,6,3]{0,1,2:T(8,128)S(1)} %collective-permute-done.3) | data formatting | bytes 46800 | tf_op jit(solution)/shard_map/ppermute | solution.py:39
  51.1 2.4 %pad_maximum_fusion.1 = f32[325,6,134]{2,0,1:T(8,128)S(1)} fusion(f32[325,6,3]{2,0,1:T(8,128)} %copy.26, f32[325,6,128]{2,0,1:T(8,128)S(1)} %constant_dynamic-update-slice_fusion, f32[325,6,3]{2,0,1:T(8,128)} %copy.25), kind=kLoop, calls=%fused_computation.1 | loop fusion | flops 522600 | bytes 2090400 | tf_op jit(solution)/shard_map/concatenate | solution.py:224
  53.5 1.6 %slice_bitcast_fusion = (f32[325,134]{1,0:T(8,128)S(1)}, f32[325,134]{1,0:T(8,128)S(1)}, f32[325,134]{1,0:T(8,128)}, f32[325,134]{1,0:T(8,128)}, f32[325,134]{1,...) fusion(f32[325,6,134]{2,0,1:T(8,128)S(1)} %pad_maximum_fusion.1, ...), kind=kLoop, calls=%fused_computation.5 | loop fusion | bytes 3484000 | tf_op jit(solution)/shard_map/squeeze | solution.py:232
  55.1 3.3 %concatenate.44.frc_ref.pk_ref = f32[325,1408]{1,0:T(8,128)S(1)} concatenate(f32[325,134]{1,0:T(8,128)} %get-tuple-element.35, f32[325,134]{1,0:T(8,128)} %get-tuple-element.34, f32[325,134]{1,0:T(8,128)} %get-tuple-element.33, f32[325,134]{1,0:T(8,128)} %get-tuple-element.74, f32[325,134]{1,0:T(8,128)} %get-tuple-element.75, f32[325,134]{1,0:T(8,128)} %get-tuple-element.76, ...), dimensions={1} | concatenate | bytes 3660800 | tf_op jit(solution)/shard_map/concatenate | solution.py:234
  58.4 0.7 reshape.62.inc_ref
  59.1 0.5 copy-done.2
  59.6 11.1 %shard_map.77 = (f32[1,2,2,64,4,128]{5,4,3,2,1,0:T(4,128)}, f32[2,2,4,128]{3,2,1,0:T(4,128)}) custom-call(s32[2]{0:T(128)} %get-tuple-element.72.order_ref, f32[325,1408]{1,0:T(8,128)} %copy-done.2, f32[325,1408]{1,0:T(8,128)} %copy-done.2, f32[2,2,1408]{2,1,0:T(2,128)} %reshape.62.inc_ref, f32[1,1408]{1,0:T(1,128)} %pad_convert_fusion.ins_ref, ...), custom_call_target="tpu_custom_call" | custom-call | flops 4429185024 | bytes 2812288 | tf_op jit(solution)/shard_map/pallas_call | solution.py:165
  70.7 0.7 copy.42
  71.4 0.1 fusion.8
  71.5 2.7 %collective-permute-start.8 = (f32[2,2,4,3]{3,1,0,2:T(2,128)S(1)}, f32[2,2,4,3]{3,1,0,2:T(2,128)S(1)}, u32[]{:S(2)}, u32[]{:S(2)}) collective-permute-start(f32[2,2,4,3]{3,1,0,2:T(2,128)S(1)} %get-tuple-element.70), channel_id=1, source_target_pairs={{0,1},{2,3},{4,5},{6,7},{8,9},{10,11},{12,13},{14,15},{16,17},{18,... | collective-permute-start | bytes 584 | tf_op jit(solution)/shard_map/ppermute | solution.py:39
  74.3 1.3 %collective-permute-start.9 = (f32[2,2,4,3]{3,1,0,2:T(2,128)S(1)}, f32[2,2,4,3]{3,1,0,2:T(2,128)S(1)}, u32[]{:S(2)}, u32[]{:S(2)}) collective-permute-start(f32[2,2,4,3]{3,1,0,2:T(2,128)S(1)} %get-tuple-element.71), channel_id=1, source_target_pairs={{1,0},{3,2},{5,4},{7,6},{9,8},{11,10},{13,12},{15,14},{17,16},{19,... | collective-permute-start | bytes 584 | tf_op jit(solution)/shard_map/ppermute | solution.py:39
  75.6 0.0 collective-permute-done.7
  75.6 1.3 %copy.39 = f32[256,3,134]{2,0,1:T(8,128)S(1)} copy(f32[256,3,134]{0,2,1:T(8,128)} %collective-permute-done.7) | data formatting | bytes 823296 | tf_op jit(solution)/shard_map/optimization_barrier | solution.py:262
  76.9 0.1 slice_bitcast_fusion.10
  77.0 1.3 %copy.36 = f32[256,3,134]{2,0,1:T(8,128)S(1)} copy(f32[256,3,134]{0,2,1:T(8,128)} %collective-permute-done.6) | data formatting | bytes 823296 | tf_op jit(solution)/shard_map/optimization_barrier | solution.py:262
  78.3 0.0 collective-permute-done.9
  78.3 0.1 pad_maximum_fusion.4
  78.4 5.6 %collective-permute-start.12 = (f32[2,2,3,134]{3,1,0,2:T(2,128)S(1)}, f32[2,2,3,134]{3,1,0,2:T(2,128)S(1)}, u32[]{:S(2)}, u32[]{:S(2)}) collective-permute-start(f32[2,2,3,134]{3,1,0,2:T(2,128)S(1)} %get-tuple-element.58), channel_id=1, source_target_pairs={{2,8},{4,10},{6,12},{10,16},{12,18},{14,20},{18,24},{20,26},{22,28... | collective-permute-start | bytes 19304 | tf_op jit(solution)/shard_map/ppermute | solution.py:40
  84.0 0.1 slice_bitcast_fusion.17
  84.1 1.8 %concatenate.49.frc_ref = f32[256,1408]{1,0:T(8,128)} concatenate(f32[256,134]{1,0:T(8,128)S(1)} %get-tuple-element.47, f32[256,134]{1,0:T(8,128)S(1)} %get-tuple-element.46, f32[256,134]{1,0:T(8,128)S(1)} %get-tuple-element.45, f32[256,134]{1,0:T(8,128)S(1)} %copy-done.6, f32[256,134]{1,0:T(8,128)S(1)} %copy-done.5, f32[256,134]{1,0:T(8,128)S(1)} %copy-done.4, ...), dimensions={1} | concatenate | bytes 2883584 | tf_op jit(solution)/shard_map/concatenate | solution.py:267
  86.0 3.5 %collective-permute-start.11 = (f32[2,2,4,134]{3,1,0,2:T(2,128)S(1)}, f32[2,2,4,134]{3,1,0,2:T(2,128)S(1)}, u32[]{:S(2)}, u32[]{:S(2)}) collective-permute-start(f32[2,2,4,134]{3,1,0,2:T(2,128)S(1)} %pad_maximum_fusion.4), channel_id=1, source_target_pairs={{0,8},{2,10},{4,12},{6,14},{8,16},{10,18},{12,20},{14,22},{16,24},... | collective-permute-start | bytes 25736 | tf_op jit(solution)/shard_map/ppermute | solution.py:40
  89.5 1.9 %collective-permute-start.10 = (f32[2,2,3,134]{3,1,0,2:T(2,128)S(1)}, f32[2,2,3,134]{3,1,0,2:T(2,128)S(1)}, u32[]{:S(2)}, u32[]{:S(2)}) collective-permute-start(f32[2,2,3,134]{3,1,0,2:T(2,128)S(1)} %get-tuple-element.59), channel_id=1, source_target_pairs={{0,10},{2,12},{4,14},{8,18},{10,20},{12,22},{16,26},{18,28},{20,30... | collective-permute-start | bytes 19304 | tf_op jit(solution)/shard_map/ppermute | solution.py:40
  91.4 0.0 collective-permute-done.12
  91.4 5.4 %collective-permute-done.10 = f32[2,2,3,134]{3,1,0,2:T(2,128)S(1)} collective-permute-done((f32[2,2,3,134]{3,1,0,2:T(2,128)S(1)}, f32[2,2,3,134]{3,1,0,2:T(2,128)S(1)}, u32[]{:S(2)}, u32[]{:S(2)}) %collective-permute-start.10) | collective-permute-done | bytes 6464 | tf_op jit(solution)/shard_map/ppermute | solution.py:40
  96.9 0.0 collective-permute-done.11
  96.9 0.8 concatenate.51.inc_ref
  97.6 11.4 %shard_map.78 = (f32[2,2,2,64,4,128]{5,4,3,2,1,0:T(4,128)}, f32[2,2,4,128]{3,2,1,0:T(4,128)}) custom-call(s32[2]{0:T(128)} %get-tuple-element.73.order_ref, f32[256,1408]{1,0:T(8,128)} %concatenate.49.frc_ref, f32[325,1408]{1,0:T(8,128)} %copy-done.2, f32[2,2,1408]{2,1,0:T(2,128)} %concatenate.51.inc_ref, f32[1,1408]{1,0:T(1,128)} %pad_convert_fusion.ins_ref, ...), custom_call_target="tpu_custom_call" | custom-call | flops 4429185024 | bytes 2423680 | tf_op jit(solution)/shard_map/pallas_call | solution.py:165
  (45 shorter events, 0.4 us)
Async XLA Ops:
  0.6 1.4 %copy-start.7 = (f32[64,4,128]{2,1,0:T(4,128)S(1)}, f32[64,4,128]{2,1,0:T(4,128)}, u32[]{:S(2)}) copy-start(f32[64,4,128]{2,1,0:T(4,128)} %param.7) | copy-start | bytes 393220
  0.6 1.4 %copy-start.8 = (f32[2,2,1,4,128]{4,3,2,1,0:T(4,128)S(1)}, f32[2,2,1,4,128]{4,3,2,1,0:T(4,128)}, u32[]{:S(2)}) copy-start(f32[2,2,1,4,128]{4,3,2,1,0:T(4,128)} %param.11) | copy-start | bytes 24580
  0.7 1.5 %copy-start.9 = (s32[1,4,128]{2,1,0:T(4,128)S(1)}, s32[1,4,128]{2,1,0:T(4,128)}, u32[]{:S(2)}) copy-start(s32[1,4,128]{2,1,0:T(4,128)} %param.9) | copy-start | bytes 6148
  3.2 22.5 %collective-permute-start = (f32[325,3,128]{2,0,1:T(8,128)}, f32[325,3,128]{2,0,1:T(8,128)S(1)}, u32[]{:S(2)}, u32[]{:S(2)}) collective-permute-start(f32[325,3,128]{2,0,1:T(8,128)} %get-tuple-element.49), channel_id=1, source_target_pairs={{0,2},{2,4},{4,6},{1,3},{3,5},{5,7},{8,10},{10,12},{12,14},{9,11},... | collective-permute-start | bytes 1497608 | tf_op jit(solution)/shard_map/ppermute | solution.py:39
  6.6 21.8 %collective-permute-start.1 = (f32[325,3,128]{2,0,1:T(8,128)}, f32[325,3,128]{2,0,1:T(8,128)S(1)}, u32[]{:S(2)}, u32[]{:S(2)}) collective-permute-start(f32[325,3,128]{2,0,1:T(8,128)} %get-tuple-element.48), channel_id=1, source_target_pairs={{2,0},{4,2},{6,4},{3,1},{5,3},{7,5},{10,8},{12,10},{14,12},{11,9},... | collective-permute-start | bytes 1497608 | tf_op jit(solution)/shard_map/ppermute | solution.py:39
  13.6 5.2 %copy-start.10 = (s32[2,1,2]{2,1,0:T(1,128)S(1)}, s32[2,1,2]{2,1,0:T(1,128)}, u32[]{:S(2)}) copy-start(s32[2,1,2]{2,1,0:T(1,128)} %param.10) | copy-start | bytes 52
  13.6 6.5 %collective-permute-start.4 = (f32[581,4,3]{0,1,2:T(4,128)S(1)}, f32[581,4,3]{0,1,2:T(4,128)S(1)}, u32[]{:S(2)}, u32[]{:S(2)}) collective-permute-start(f32[581,4,3]{0,1,2:T(4,128)S(1)} %copy.29), channel_id=1, source_target_pairs={{0,1},{2,3},{4,5},{6,7},{8,9},{10,11},{12,13},{14,15},{16,17},{18,... | collective-permute-start | bytes 83672 | tf_op jit(solution)/shard_map/ppermute | solution.py:39
  15.5 5.0 %collective-permute-start.5 = (f32[581,4,3]{0,1,2:T(4,128)S(1)}, f32[581,4,3]{0,1,2:T(4,128)S(1)}, u32[]{:S(2)}, u32[]{:S(2)}) collective-permute-start(f32[581,4,3]{0,1,2:T(4,128)S(1)} %copy.30), channel_id=1, source_target_pairs={{1,0},{3,2},{5,4},{7,6},{9,8},{11,10},{13,12},{15,14},{17,16},{19,... | collective-permute-start | bytes 83672 | tf_op jit(solution)/shard_map/ppermute | solution.py:39
  24.2 1.9 %copy-start = (f32[581,4,134]{2,0,1:T(8,128)}, f32[581,4,134]{2,0,1:T(8,128)S(1)}, u32[]{:S(2)}) copy-start(f32[581,4,134]{2,0,1:T(8,128)S(1)} %pad_maximum_fusion) | copy-start | bytes 3736996
  28.5 7.6 %copy-start.1 = (f32[581,4,134]{2,0,1:T(8,128)S(1)}, f32[581,4,134]{2,0,1:T(8,128)}, u32[]{:S(2)}) copy-start(f32[581,4,134]{2,0,1:T(8,128)} %copy-done) | copy-start | bytes 3736996
  31.8 16.7 %collective-permute-start.2 = (f32[325,6,3]{0,1,2:T(8,128)S(1)}, f32[325,6,3]{0,1,2:T(8,128)S(1)}, u32[]{:S(2)}, u32[]{:S(2)}) collective-permute-start(f32[325,6,3]{0,1,2:T(8,128)S(1)} %copy.23), channel_id=1, source_target_pairs={{0,1},{2,3},{4,5},{6,7},{8,9},{10,11},{12,13},{14,15},{16,17},{18,... | collective-permute-start | bytes 70208 | tf_op jit(solution)/shard_map/ppermute | solution.py:39
  34.7 15.1 %collective-permute-start.3 = (f32[325,6,3]{0,1,2:T(8,128)S(1)}, f32[325,6,3]{0,1,2:T(8,128)S(1)}, u32[]{:S(2)}, u32[]{:S(2)}) collective-permute-start(f32[325,6,3]{0,1,2:T(8,128)S(1)} %copy.24), channel_id=1, source_target_pairs={{1,0},{3,2},{5,4},{7,6},{9,8},{11,10},{13,12},{15,14},{17,16},{19,... | collective-permute-start | bytes 70208 | tf_op jit(solution)/shard_map/ppermute | solution.py:39
  39.2 36.3 %collective-permute-start.6 = (f32[256,3,134]{0,2,1:T(8,128)}, f32[256,3,134]{0,2,1:T(8,128)}, u32[]{:S(2)}, u32[]{:S(2)}) collective-permute-start(f32[256,3,134]{0,2,1:T(8,128)} %copy.34), channel_id=1, source_target_pairs={{0,2},{2,4},{4,6},{1,3},{3,5},{5,7},{8,10},{10,12},{12,14},{9,11},... | collective-permute-start | bytes 1234952 | tf_op jit(solution)/shard_map/ppermute | solution.py:39
  43.4 32.2 %collective-permute-start.7 = (f32[256,3,134]{0,2,1:T(8,128)}, f32[256,3,134]{0,2,1:T(8,128)}, u32[]{:S(2)}, u32[]{:S(2)}) collective-permute-start(f32[256,3,134]{0,2,1:T(8,128)} %copy.35), channel_id=1, source_target_pairs={{2,0},{4,2},{6,4},{3,1},{5,3},{7,5},{10,8},{12,10},{14,12},{11,9},... | collective-permute-start | bytes 1234952 | tf_op jit(solution)/shard_map/ppermute | solution.py:39
  58.4 1.3 %copy-start.2 = (f32[325,1408]{1,0:T(8,128)}, f32[325,1408]{1,0:T(8,128)S(1)}, u32[]{:S(2)}) copy-start(f32[325,1408]{1,0:T(8,128)S(1)} %concatenate.44.frc_ref.pk_ref) | copy-start | bytes 5491204
  71.5 6.8 %collective-permute-start.8 = (f32[2,2,4,3]{3,1,0,2:T(2,128)S(1)}, f32[2,2,4,3]{3,1,0,2:T(2,128)S(1)}, u32[]{:S(2)}, u32[]{:S(2)}) collective-permute-start(f32[2,2,4,3]{3,1,0,2:T(2,128)S(1)} %get-tuple-element.70), channel_id=1, source_target_pairs={{0,1},{2,3},{4,5},{6,7},{8,9},{10,11},{12,13},{14,15},{16,17},{18,... | collective-permute-start | bytes 584 | tf_op jit(solution)/shard_map/ppermute | solution.py:39
  74.3 4.1 %collective-permute-start.9 = (f32[2,2,4,3]{3,1,0,2:T(2,128)S(1)}, f32[2,2,4,3]{3,1,0,2:T(2,128)S(1)}, u32[]{:S(2)}, u32[]{:S(2)}) collective-permute-start(f32[2,2,4,3]{3,1,0,2:T(2,128)S(1)} %get-tuple-element.71), channel_id=1, source_target_pairs={{1,0},{3,2},{5,4},{7,6},{9,8},{11,10},{13,12},{15,14},{17,16},{19,... | collective-permute-start | bytes 584 | tf_op jit(solution)/shard_map/ppermute | solution.py:39
  76.9 7.3 %copy-start.3 = (f32[256,134]{1,0:T(8,128)S(1)}, f32[256,134]{1,0:T(8,128)}, u32[]{:S(2)}) copy-start(f32[256,134]{1,0:T(8,128)} %get-tuple-element.20) | copy-start | bytes 411652
  76.9 7.3 %copy-start.4 = (f32[256,134]{1,0:T(8,128)S(1)}, f32[256,134]{1,0:T(8,128)}, u32[]{:S(2)}) copy-start(f32[256,134]{1,0:T(8,128)} %get-tuple-element.21) | copy-start | bytes 411652
  76.9 7.3 %copy-start.5 = (f32[256,134]{1,0:T(8,128)S(1)}, f32[256,134]{1,0:T(8,128)}, u32[]{:S(2)}) copy-start(f32[256,134]{1,0:T(8,128)} %get-tuple-element.22) | copy-start | bytes 411652
  76.9 7.3 %copy-start.6 = (f32[256,134]{1,0:T(8,128)S(1)}, f32[256,134]{1,0:T(8,128)}, u32[]{:S(2)}) copy-start(f32[256,134]{1,0:T(8,128)} %get-tuple-element.23) | copy-start | bytes 411652
  78.4 13.0 %collective-permute-start.12 = (f32[2,2,3,134]{3,1,0,2:T(2,128)S(1)}, f32[2,2,3,134]{3,1,0,2:T(2,128)S(1)}, u32[]{:S(2)}, u32[]{:S(2)}) collective-permute-start(f32[2,2,3,134]{3,1,0,2:T(2,128)S(1)} %get-tuple-element.58), channel_id=1, source_target_pairs={{2,8},{4,10},{6,12},{10,16},{12,18},{14,20},{18,24},{20,26},{22,28... | collective-permute-start | bytes 19304 | tf_op jit(solution)/shard_map/ppermute | solution.py:40
  86.0 10.9 %collective-permute-start.11 = (f32[2,2,4,134]{3,1,0,2:T(2,128)S(1)}, f32[2,2,4,134]{3,1,0,2:T(2,128)S(1)}, u32[]{:S(2)}, u32[]{:S(2)}) collective-permute-start(f32[2,2,4,134]{3,1,0,2:T(2,128)S(1)} %pad_maximum_fusion.4), channel_id=1, source_target_pairs={{0,8},{2,10},{4,12},{6,14},{8,16},{10,18},{12,20},{14,22},{16,24},... | collective-permute-start | bytes 25736 | tf_op jit(solution)/shard_map/ppermute | solution.py:40
  89.5 7.4 %collective-permute-start.10 = (f32[2,2,3,134]{3,1,0,2:T(2,128)S(1)}, f32[2,2,3,134]{3,1,0,2:T(2,128)S(1)}, u32[]{:S(2)}, u32[]{:S(2)}) collective-permute-start(f32[2,2,3,134]{3,1,0,2:T(2,128)S(1)} %get-tuple-element.59), channel_id=1, source_target_pairs={{0,10},{2,12},{4,14},{8,18},{10,20},{12,22},{16,26},{18,28},{20,30... | collective-permute-start | bytes 19304 | tf_op jit(solution)/shard_map/ppermute | solution.py:40

commit v16 on v15

--- a/solution.py
+++ b/solution.py
@@ -211,8 +211,14 @@
     )
     rows_now = per_tick.shape[1] + depth + nsrc * two + 1
     now = packed[:rows_now]
-    low_x = fetch(now[:, nx - width :, :], ("tx",), (-1,))
-    high_x = fetch(now[:, :width, :], ("tx",), (1,))
+    sources = [
+        per_tick[0],
+        wavenumber_sq,
+        pending_trace.reshape(-1, nx, ny),
+        column_class[0][None].astype(jnp.float32),
+    ]
+    low_x = fetch(jnp.concatenate([p[:, nx - width :, :] for p in sources], axis=0), ("tx",), (-1,))
+    high_x = fetch(jnp.concatenate([p[:, :width, :] for p in sources], axis=0), ("tx",), (1,))
     widened = extend_y(packed, width)
     later = [
         widened[rows_now + (t - 1) * per_tick.shape[1] : rows_now + t * per_tick.shape[1]]

time: 110 us -> 110 us (level)
  no operation moved by 1% of the time
where the time goes in v16:
time: 110 us; the launch traced here: 109 us
  local copies, waits for them, and re-layouts  37.7 us (34%)
  starting transfers between devices  34.2 us (31%)
  Pallas kernels  22.5 us (20%)
  other arithmetic  7.15 us (6%)
  waiting for transfers between devices  6.7 us (6%)
  between operations  1.2 us (1%)
    ppermute x10, starting transfers between devices, fetch(): return lax.ppermute(block, axes[0], pairs)  23.3 us
    pallas_call x2, Pallas kernels, run_tick(): pl.pallas_call(functools.partial(tick_kernel, row=row, depth=depth, width...  22.5 us
    ppermute x3, starting transfers between devices, fetch(): return lax.ppermute(block, tuple(axes), pairs)  11 us
    ppermute x3, waiting for transfers between devices, fetch(): return lax.ppermute(block, tuple(axes), pairs)  5.44 us
    ppermute x4, local copies, waits for them, and re-layouts, fetch(): return lax.ppermute(block, axes[0], pairs)  4.51 us
    slice x2, local copies, waits for them, and re-layouts, per_device(): high_later = [fetch(r[:, :width, :], ('tx',), (1,)) for r in later]  3.56 us
    concatenate x1, local copies, waits for them, and re-layouts, per_device(): packed = jnp.concatenate(segments, axis=-1)  3.31 us
    slice x2, local copies, waits for them, and re-layouts, per_device(): corner_low = fetch(rims[..., ny - width:], ('ty',), (-1,))  3.27 us
  transfers between devices with their start and end apart: 13, of which 2 were waited for; matrix products, arithmetic and copies ran while one was open for 33% of the time, Pallas kernels for 10%

profile of v16, /device:TPU:12, one launch (start us, length us, event | category | flops | bytes accessed | tf_op | source)
XLA Modules:
  0.0 109.5 jit_solution(16433951776452598866)
XLA Ops:
  0.6 1.3 %fusion.4 = (f32[1,2,2,64,4,128]{5,4,3,2,1,0:T(4,128)S(1)}, f32[1,2,2,64,4,128]{5,4,3,2,1,0:T(4,128)S(1)}) fusion(f32[2,2,2,64,4,128]{5,4,3,2,1,0:T(4,128)} %param.6), kind=kLoop, calls=%fused_computation.58 | loop fusion | bytes 2097152 | tf_op jit(solution)/shard_map/slice | solution.py:209
  2.0 0.0 copy-start.8
  2.0 0.0 copy-start.9
  2.0 0.1 fusion.6
  2.1 0.5 copy-done.8
  2.7 3.4 %collective-permute-start = (f32[325,3,128]{2,0,1:T(8,128)S(1)}, f32[325,3,128]{2,0,1:T(8,128)S(1)}, u32[]{:S(2)}, u32[]{:S(2)}) collective-permute-start(f32[325,3,128]{2,0,1:T(8,128)S(1)} %pad_maximum_fusion.2), channel_id=1, source_target_pairs={{0,2},{2,4},{4,6},{1,3},{3,5},{5,7},{8,10},{10,12},{12,14},{9,11},... | collective-permute-start | bytes 1497608 | tf_op jit(solution)/shard_map/ppermute | solution.py:39
  6.2 0.8 pad_maximum_fusion.3
  7.0 3.3 %collective-permute-start.1 = (f32[325,3,128]{2,0,1:T(8,128)}, f32[325,3,128]{2,0,1:T(8,128)}, u32[]{:S(2)}, u32[]{:S(2)}) collective-permute-start(f32[325,3,128]{2,0,1:T(8,128)} %pad_maximum_fusion.3), channel_id=1, source_target_pairs={{2,0},{4,2},{6,4},{3,1},{5,3},{7,5},{10,8},{12,10},{14,12},{11,9},... | collective-permute-start | bytes 1497608 | tf_op jit(solution)/shard_map/ppermute | solution.py:39
  10.4 0.5 concatenate.46
  10.9 1.4 %fusion.3 = (f32[581,4,3]{2,0,1:T(8,128)}, f32[581,4,3]{2,0,1:T(8,128)S(1)}) fusion(f32[581,4,128]{2,0,1:T(8,128)S(1)} %concatenate.46), kind=kLoop, calls=%fused_computation.57 | loop fusion | bytes 111552 | tf_op jit(solution)/shard_map/slice | solution.py:45
  12.3 1.7 %copy.31 = f32[581,4,3]{0,1,2:T(4,128)S(1)} copy(f32[581,4,3]{2,0,1:T(8,128)} %get-tuple-element.36) | data formatting | bytes 55776 | tf_op jit(solution)/shard_map/slice | solution.py:45
  14.0 1.4 %collective-permute-start.4 = (f32[581,4,3]{0,1,2:T(4,128)S(1)}, f32[581,4,3]{0,1,2:T(4,128)S(1)}, u32[]{:S(2)}, u32[]{:S(2)}) collective-permute-start(f32[581,4,3]{0,1,2:T(4,128)S(1)} %copy.31), channel_id=1, source_target_pairs={{0,1},{2,3},{4,5},{6,7},{8,9},{10,11},{12,13},{14,15},{16,17},{18,... | collective-permute-start | bytes 83672 | tf_op jit(solution)/shard_map/ppermute | solution.py:39
  15.4 0.4 copy.32
  15.8 1.3 %collective-permute-start.5 = (f32[581,4,3]{0,1,2:T(4,128)S(1)}, f32[581,4,3]{0,1,2:T(4,128)S(1)}, u32[]{:S(2)}, u32[]{:S(2)}) collective-permute-start(f32[581,4,3]{0,1,2:T(4,128)S(1)} %copy.32), channel_id=1, source_target_pairs={{1,0},{3,2},{5,4},{7,6},{9,8},{11,10},{13,12},{15,14},{17,16},{19,... | collective-permute-start | bytes 83672 | tf_op jit(solution)/shard_map/ppermute | solution.py:39
  17.1 1.0 copy.49
  18.1 0.1 maximum_maximum_fusion
  18.3 0.1 broadcast_and_fusion
  18.4 0.1 convert_element_type.25
  18.5 0.6 pad_convert_fusion.ins_ref
  19.1 0.5 slice_bitcast_fusion.36
  19.7 0.7 fusion
  20.4 0.0 collective-permute-done.4
  20.4 0.4 copy.33
  20.8 0.0 collective-permute-done.5
  20.9 1.5 %copy.34 = f32[581,4,3]{2,0,1:T(8,128)} copy(f32[581,4,3]{0,1,2:T(4,128)S(1)} %collective-permute-done.5) | data formatting | bytes 55776 | tf_op jit(solution)/shard_map/ppermute | solution.py:39
  22.3 2.3 %pad_maximum_fusion = f32[581,4,134]{2,0,1:T(8,128)S(1)} fusion(f32[581,4,3]{2,0,1:T(8,128)} %copy.34, f32[581,4,128]{2,0,1:T(8,128)S(1)} %concatenate.46, f32[581,4,3]{2,0,1:T(8,128)S(1)} %copy.33), kind=kLoop, calls=%fused_computation | loop fusion | flops 622832 | bytes 2491328 | tf_op jit(solution)/shard_map/concatenate | solution.py:47
  24.6 1.4 %fusion.2 = (f32[256,3,134]{2,0,1:T(8,128)}, f32[256,3,134]{2,0,1:T(8,128)}) fusion(f32[581,4,134]{2,0,1:T(8,128)S(1)} %pad_maximum_fusion), kind=kLoop, calls=%fused_computation.56 | loop fusion | bytes 1646592 | tf_op jit(solution)/shard_map/slice | solution.py:257
  26.0 0.5 copy-done
  26.5 1.2 %collective-permute-done.1 = f32[325,3,128]{2,0,1:T(8,128)} collective-permute-done((f32[325,3,128]{2,0,1:T(8,128)}, f32[325,3,128]{2,0,1:T(8,128)}, u32[]{:S(2)}, u32[]{:S(2)}) %collective-permute-start.1) | collective-permute-done | bytes 499232 | tf_op jit(solution)/shard_map/ppermute | solution.py:39
  27.8 1.1 constant_dynamic-update-slice_fusion
  28.9 1.6 %fusion.5 = (f32[325,6,3]{2,0,1:T(8,128)}, f32[325,6,3]{2,0,1:T(8,128)}) fusion(f32[325,6,128]{2,0,1:T(8,128)S(1)} %constant_dynamic-update-slice_fusion), kind=kLoop, calls=%fused_computation.59 | loop fusion | bytes 93600 | tf_op jit(solution)/shard_map/slice | solution.py:228
  30.4 1.7 %copy.25 = f32[325,6,3]{0,1,2:T(8,128)S(1)} copy(f32[325,6,3]{2,0,1:T(8,128)} %get-tuple-element.40) | data formatting | bytes 46800 | tf_op jit(solution)/shard_map/slice | solution.py:228
  32.1 1.8 %collective-permute-start.2 = (f32[325,6,3]{0,1,2:T(8,128)S(1)}, f32[325,6,3]{0,1,2:T(8,128)S(1)}, u32[]{:S(2)}, u32[]{:S(2)}) collective-permute-start(f32[325,6,3]{0,1,2:T(8,128)S(1)} %copy.25), channel_id=1, source_target_pairs={{0,1},{2,3},{4,5},{6,7},{8,9},{10,11},{12,13},{14,15},{16,17},{18,... | collective-permute-start | bytes 70208 | tf_op jit(solution)/shard_map/ppermute | solution.py:39
  33.9 1.7 %copy.26 = f32[325,6,3]{0,1,2:T(8,128)S(1)} copy(f32[325,6,3]{2,0,1:T(8,128)} %get-tuple-element.41) | data formatting | bytes 46800 | tf_op jit(solution)/shard_map/slice | solution.py:229
  35.6 1.3 %collective-permute-start.3 = (f32[325,6,3]{0,1,2:T(8,128)S(1)}, f32[325,6,3]{0,1,2:T(8,128)S(1)}, u32[]{:S(2)}, u32[]{:S(2)}) collective-permute-start(f32[325,6,3]{0,1,2:T(8,128)S(1)} %copy.26), channel_id=1, source_target_pairs={{1,0},{3,2},{5,4},{7,6},{9,8},{11,10},{13,12},{15,14},{17,16},{19,... | collective-permute-start | bytes 70208 | tf_op jit(solution)/shard_map/ppermute | solution.py:39
  36.9 1.0 slice_bitcast_fusion.13
  37.9 2.1 %copy.36 = f32[256,3,134]{0,2,1:T(8,128)} copy(f32[256,3,134]{2,0,1:T(8,128)} %get-tuple-element.25) | data formatting | bytes 823296 | tf_op jit(solution)/shard_map/slice | solution.py:256
  40.1 3.3 %collective-permute-start.6 = (f32[256,3,134]{0,2,1:T(8,128)}, f32[256,3,134]{0,2,1:T(8,128)}, u32[]{:S(2)}, u32[]{:S(2)}) collective-permute-start(f32[256,3,134]{0,2,1:T(8,128)} %copy.36), channel_id=1, source_target_pairs={{0,2},{2,4},{4,6},{1,3},{3,5},{5,7},{8,10},{10,12},{12,14},{9,11},... | collective-permute-start | bytes 1234952 | tf_op jit(solution)/shard_map/ppermute | solution.py:39
  43.4 2.1 %copy.37 = f32[256,3,134]{0,2,1:T(8,128)} copy(f32[256,3,134]{2,0,1:T(8,128)} %get-tuple-element.24) | data formatting | bytes 823296 | tf_op jit(solution)/shard_map/slice | solution.py:257
  45.5 3.5 %collective-permute-start.7 = (f32[256,3,134]{0,2,1:T(8,128)}, f32[256,3,134]{0,2,1:T(8,128)}, u32[]{:S(2)}, u32[]{:S(2)}) collective-permute-start(f32[256,3,134]{0,2,1:T(8,128)} %copy.37), channel_id=1, source_target_pairs={{2,0},{4,2},{6,4},{3,1},{5,3},{7,5},{10,8},{12,10},{14,12},{11,9},... | collective-permute-start | bytes 1234952 | tf_op jit(solution)/shard_map/ppermute | solution.py:39
  49.0 1.3 %copy.27 = f32[325,6,3]{2,0,1:T(8,128)} copy(f32[325,6,3]{0,1,2:T(8,128)S(1)} %collective-permute-done.2) | data formatting | bytes 46800 | tf_op jit(solution)/shard_map/ppermute | solution.py:39
  50.3 1.3 %copy.28 = f32[325,6,3]{2,0,1:T(8,128)} copy(f32[325,6,3]{0,1,2:T(8,128)S(1)} %collective-permute-done.3) | data formatting | bytes 46800 | tf_op jit(solution)/shard_map/ppermute | solution.py:39
  51.6 2.4 %pad_maximum_fusion.1 = f32[325,6,134]{2,0,1:T(8,128)S(1)} fusion(f32[325,6,3]{2,0,1:T(8,128)} %copy.28, f32[325,6,128]{2,0,1:T(8,128)S(1)} %constant_dynamic-update-slice_fusion, f32[325,6,3]{2,0,1:T(8,128)} %copy.27), kind=kLoop, calls=%fused_computation.1 | loop fusion | flops 522600 | bytes 2090400 | tf_op jit(solution)/shard_map/concatenate | solution.py:230
  54.0 1.5 %slice_bitcast_fusion = (f32[325,134]{1,0:T(8,128)S(1)}, f32[325,134]{1,0:T(8,128)S(1)}, f32[325,134]{1,0:T(8,128)}, f32[325,134]{1,0:T(8,128)}, f32[325,134]{1,...) fusion(f32[325,6,134]{2,0,1:T(8,128)S(1)} %pad_maximum_fusion.1, ...), kind=kLoop, calls=%fused_computation.6 | loop fusion | bytes 3484000 | tf_op jit(solution)/shard_map/squeeze | solution.py:238
  55.5 3.3 %concatenate.48.frc_ref.pk_ref = f32[325,1408]{1,0:T(8,128)S(1)} concatenate(f32[325,134]{1,0:T(8,128)} %get-tuple-element.35, f32[325,134]{1,0:T(8,128)} %get-tuple-element.34, f32[325,134]{1,0:T(8,128)} %get-tuple-element.33, f32[325,134]{1,0:T(8,128)} %get-tuple-element.80, f32[325,134]{1,0:T(8,128)} %get-tuple-element.81, f32[325,134]{1,0:T(8,128)} %get-tuple-element.82, ...), dimensions={1} | concatenate | bytes 3660800 | tf_op jit(solution)/shard_map/concatenate | solution.py:240
  58.9 0.7 reshape.63.inc_ref
  59.6 0.5 copy-done.2
  60.1 11.1 %shard_map.77 = (f32[1,2,2,64,4,128]{5,4,3,2,1,0:T(4,128)}, f32[2,2,4,128]{3,2,1,0:T(4,128)}) custom-call(s32[2]{0:T(128)} %get-tuple-element.78.order_ref, f32[325,1408]{1,0:T(8,128)} %copy-done.2, f32[325,1408]{1,0:T(8,128)} %copy-done.2, f32[2,2,1408]{2,1,0:T(2,128)} %reshape.63.inc_ref, f32[1,1408]{1,0:T(1,128)} %pad_convert_fusion.ins_ref, ...), custom_call_target="tpu_custom_call" | custom-call | flops 4429185024 | bytes 2812288 | tf_op jit(solution)/shard_map/pallas_call | solution.py:165
  71.3 0.7 copy.44
  72.0 0.1 fusion.9
  72.0 2.7 %collective-permute-start.8 = (f32[2,2,4,3]{3,1,0,2:T(2,128)S(1)}, f32[2,2,4,3]{3,1,0,2:T(2,128)S(1)}, u32[]{:S(2)}, u32[]{:S(2)}) collective-permute-start(f32[2,2,4,3]{3,1,0,2:T(2,128)S(1)} %get-tuple-element.72), channel_id=1, source_target_pairs={{0,1},{2,3},{4,5},{6,7},{8,9},{10,11},{12,13},{14,15},{16,17},{18,... | collective-permute-start | bytes 584 | tf_op jit(solution)/shard_map/ppermute | solution.py:39
  74.7 1.3 %collective-permute-start.9 = (f32[2,2,4,3]{3,1,0,2:T(2,128)S(1)}, f32[2,2,4,3]{3,1,0,2:T(2,128)S(1)}, u32[]{:S(2)}, u32[]{:S(2)}) collective-permute-start(f32[2,2,4,3]{3,1,0,2:T(2,128)S(1)} %get-tuple-element.73), channel_id=1, source_target_pairs={{1,0},{3,2},{5,4},{7,6},{9,8},{11,10},{13,12},{15,14},{17,16},{19,... | collective-permute-start | bytes 584 | tf_op jit(solution)/shard_map/ppermute | solution.py:39
  76.1 1.3 %copy.41 = f32[256,3,134]{2,0,1:T(8,128)S(1)} copy(f32[256,3,134]{0,2,1:T(8,128)} %collective-permute-done.7) | data formatting | bytes 823296 | tf_op jit(solution)/shard_map/optimization_barrier | solution.py:268
  77.4 0.1 slice_bitcast_fusion.10
  77.4 1.3 %copy.38 = f32[256,3,134]{2,0,1:T(8,128)S(1)} copy(f32[256,3,134]{0,2,1:T(8,128)} %collective-permute-done.6) | data formatting | bytes 823296 | tf_op jit(solution)/shard_map/optimization_barrier | solution.py:268
  78.8 0.1 pad_maximum_fusion.5
  78.9 5.6 %collective-permute-start.12 = (f32[2,2,3,134]{3,1,0,2:T(2,128)S(1)}, f32[2,2,3,134]{3,1,0,2:T(2,128)S(1)}, u32[]{:S(2)}, u32[]{:S(2)}) collective-permute-start(f32[2,2,3,134]{3,1,0,2:T(2,128)S(1)} %get-tuple-element.60), channel_id=1, source_target_pairs={{2,8},{4,10},{6,12},{10,16},{12,18},{14,20},{18,24},{20,26},{22,28... | collective-permute-start | bytes 19304 | tf_op jit(solution)/shard_map/ppermute | solution.py:40
  84.5 0.1 slice_bitcast_fusion.17
  84.6 1.8 %concatenate.53.frc_ref = f32[256,1408]{1,0:T(8,128)} concatenate(f32[256,134]{1,0:T(8,128)S(1)} %get-tuple-element.47, f32[256,134]{1,0:T(8,128)S(1)} %get-tuple-element.46, f32[256,134]{1,0:T(8,128)S(1)} %get-tuple-element.45, f32[256,134]{1,0:T(8,128)S(1)} %copy-done.6, f32[256,134]{1,0:T(8,128)S(1)} %copy-done.5, f32[256,134]{1,0:T(8,128)S(1)} %copy-done.4, ...), dimensions={1} | concatenate | bytes 2883584 | tf_op jit(solution)/shard_map/concatenate | solution.py:273
  86.5 3.5 %collective-permute-start.11 = (f32[2,2,4,134]{3,1,0,2:T(2,128)S(1)}, f32[2,2,4,134]{3,1,0,2:T(2,128)S(1)}, u32[]{:S(2)}, u32[]{:S(2)}) collective-permute-start(f32[2,2,4,134]{3,1,0,2:T(2,128)S(1)} %pad_maximum_fusion.5), channel_id=1, source_target_pairs={{0,8},{2,10},{4,12},{6,14},{8,16},{10,18},{12,20},{14,22},{16,24},... | collective-permute-start | bytes 25736 | tf_op jit(solution)/shard_map/ppermute | solution.py:40
  90.0 1.9 %collective-permute-start.10 = (f32[2,2,3,134]{3,1,0,2:T(2,128)S(1)}, f32[2,2,3,134]{3,1,0,2:T(2,128)S(1)}, u32[]{:S(2)}, u32[]{:S(2)}) collective-permute-start(f32[2,2,3,134]{3,1,0,2:T(2,128)S(1)} %get-tuple-element.61), channel_id=1, source_target_pairs={{0,10},{2,12},{4,14},{8,18},{10,20},{12,22},{16,26},{18,28},{20,30... | collective-permute-start | bytes 19304 | tf_op jit(solution)/shard_map/ppermute | solution.py:40
  91.9 5.4 %collective-permute-done.10 = f32[2,2,3,134]{3,1,0,2:T(2,128)S(1)} collective-permute-done((f32[2,2,3,134]{3,1,0,2:T(2,128)S(1)}, f32[2,2,3,134]{3,1,0,2:T(2,128)S(1)}, u32[]{:S(2)}, u32[]{:S(2)}) %collective-permute-start.10) | collective-permute-done | bytes 6464 | tf_op jit(solution)/shard_map/ppermute | solution.py:40
  97.4 0.7 concatenate.55.inc_ref
  98.1 11.4 %shard_map.78 = (f32[2,2,2,64,4,128]{5,4,3,2,1,0:T(4,128)}, f32[2,2,4,128]{3,2,1,0:T(4,128)}) custom-call(s32[2]{0:T(128)} %get-tuple-element.79.order_ref, f32[256,1408]{1,0:T(8,128)} %concatenate.53.frc_ref, f32[325,1408]{1,0:T(8,128)} %copy-done.2, f32[2,2,1408]{2,1,0:T(2,128)} %concatenate.55.inc_ref, f32[1,1408]{1,0:T(1,128)} %pad_convert_fusion.ins_ref, ...), custom_call_target="tpu_custom_call" | custom-call | flops 4429185024 | bytes 2423680 | tf_op jit(solution)/shard_map/pallas_call | solution.py:165
  (49 shorter events, 0.4 us)
Async XLA Ops:
  0.6 1.5 %copy-start.7 = (f32[64,4,128]{2,1,0:T(4,128)S(1)}, f32[64,4,128]{2,1,0:T(4,128)}, u32[]{:S(2)}) copy-start(f32[64,4,128]{2,1,0:T(4,128)} %param.7) | copy-start | bytes 393220
  2.0 0.7 copy-start.8
  2.0 0.7 copy-start.9
  2.7 23.3 %collective-permute-start = (f32[325,3,128]{2,0,1:T(8,128)S(1)}, f32[325,3,128]{2,0,1:T(8,128)S(1)}, u32[]{:S(2)}, u32[]{:S(2)}) collective-permute-start(f32[325,3,128]{2,0,1:T(8,128)S(1)} %pad_maximum_fusion.2), channel_id=1, source_target_pairs={{0,2},{2,4},{4,6},{1,3},{3,5},{5,7},{8,10},{10,12},{12,14},{9,11},... | collective-permute-start | bytes 1497608 | tf_op jit(solution)/shard_map/ppermute | solution.py:39
  7.0 20.8 %collective-permute-start.1 = (f32[325,3,128]{2,0,1:T(8,128)}, f32[325,3,128]{2,0,1:T(8,128)}, u32[]{:S(2)}, u32[]{:S(2)}) collective-permute-start(f32[325,3,128]{2,0,1:T(8,128)} %pad_maximum_fusion.3), channel_id=1, source_target_pairs={{2,0},{4,2},{6,4},{3,1},{5,3},{7,5},{10,8},{12,10},{14,12},{11,9},... | collective-permute-start | bytes 1497608 | tf_op jit(solution)/shard_map/ppermute | solution.py:39
  14.0 5.2 %copy-start.10 = (s32[2,1,2]{2,1,0:T(1,128)S(1)}, s32[2,1,2]{2,1,0:T(1,128)}, u32[]{:S(2)}) copy-start(s32[2,1,2]{2,1,0:T(1,128)} %param.10) | copy-start | bytes 52
  14.0 6.4 %collective-permute-start.4 = (f32[581,4,3]{0,1,2:T(4,128)S(1)}, f32[581,4,3]{0,1,2:T(4,128)S(1)}, u32[]{:S(2)}, u32[]{:S(2)}) collective-permute-start(f32[581,4,3]{0,1,2:T(4,128)S(1)} %copy.31), channel_id=1, source_target_pairs={{0,1},{2,3},{4,5},{6,7},{8,9},{10,11},{12,13},{14,15},{16,17},{18,... | collective-permute-start | bytes 83672 | tf_op jit(solution)/shard_map/ppermute | solution.py:39
  15.8 5.0 %collective-permute-start.5 = (f32[581,4,3]{0,1,2:T(4,128)S(1)}, f32[581,4,3]{0,1,2:T(4,128)S(1)}, u32[]{:S(2)}, u32[]{:S(2)}) collective-permute-start(f32[581,4,3]{0,1,2:T(4,128)S(1)} %copy.32), channel_id=1, source_target_pairs={{1,0},{3,2},{5,4},{7,6},{9,8},{11,10},{13,12},{15,14},{17,16},{19,... | collective-permute-start | bytes 83672 | tf_op jit(solution)/shard_map/ppermute | solution.py:39
  24.6 2.0 %copy-start = (f32[581,4,134]{2,0,1:T(8,128)}, f32[581,4,134]{2,0,1:T(8,128)S(1)}, u32[]{:S(2)}) copy-start(f32[581,4,134]{2,0,1:T(8,128)S(1)} %pad_maximum_fusion) | copy-start | bytes 3736996
  28.8 8.1 %copy-start.1 = (f32[581,4,134]{2,0,1:T(8,128)S(1)}, f32[581,4,134]{2,0,1:T(8,128)}, u32[]{:S(2)}) copy-start(f32[581,4,134]{2,0,1:T(8,128)} %copy-done) | copy-start | bytes 3736996
  32.1 16.8 %collective-permute-start.2 = (f32[325,6,3]{0,1,2:T(8,128)S(1)}, f32[325,6,3]{0,1,2:T(8,128)S(1)}, u32[]{:S(2)}, u32[]{:S(2)}) collective-permute-start(f32[325,6,3]{0,1,2:T(8,128)S(1)} %copy.25), channel_id=1, source_target_pairs={{0,1},{2,3},{4,5},{6,7},{8,9},{10,11},{12,13},{14,15},{16,17},{18,... | collective-permute-start | bytes 70208 | tf_op jit(solution)/shard_map/ppermute | solution.py:39
  35.6 14.7 %collective-permute-start.3 = (f32[325,6,3]{0,1,2:T(8,128)S(1)}, f32[325,6,3]{0,1,2:T(8,128)S(1)}, u32[]{:S(2)}, u32[]{:S(2)}) collective-permute-start(f32[325,6,3]{0,1,2:T(8,128)S(1)} %copy.26), channel_id=1, source_target_pairs={{1,0},{3,2},{5,4},{7,6},{9,8},{11,10},{13,12},{15,14},{17,16},{19,... | collective-permute-start | bytes 70208 | tf_op jit(solution)/shard_map/ppermute | solution.py:39
  40.1 36.0 %collective-permute-start.6 = (f32[256,3,134]{0,2,1:T(8,128)}, f32[256,3,134]{0,2,1:T(8,128)}, u32[]{:S(2)}, u32[]{:S(2)}) collective-permute-start(f32[256,3,134]{0,2,1:T(8,128)} %copy.36), channel_id=1, source_target_pairs={{0,2},{2,4},{4,6},{1,3},{3,5},{5,7},{8,10},{10,12},{12,14},{9,11},... | collective-permute-start | bytes 1234952 | tf_op jit(solution)/shard_map/ppermute | solution.py:39
  45.5 30.6 %collective-permute-start.7 = (f32[256,3,134]{0,2,1:T(8,128)}, f32[256,3,134]{0,2,1:T(8,128)}, u32[]{:S(2)}, u32[]{:S(2)}) collective-permute-start(f32[256,3,134]{0,2,1:T(8,128)} %copy.37), channel_id=1, source_target_pairs={{2,0},{4,2},{6,4},{3,1},{5,3},{7,5},{10,8},{12,10},{14,12},{11,9},... | collective-permute-start | bytes 1234952 | tf_op jit(solution)/shard_map/ppermute | solution.py:39
  58.9 1.3 %copy-start.2 = (f32[325,1408]{1,0:T(8,128)}, f32[325,1408]{1,0:T(8,128)S(1)}, u32[]{:S(2)}) copy-start(f32[325,1408]{1,0:T(8,128)S(1)} %concatenate.48.frc_ref.pk_ref) | copy-start | bytes 5491204
  72.0 6.8 %collective-permute-start.8 = (f32[2,2,4,3]{3,1,0,2:T(2,128)S(1)}, f32[2,2,4,3]{3,1,0,2:T(2,128)S(1)}, u32[]{:S(2)}, u32[]{:S(2)}) collective-permute-start(f32[2,2,4,3]{3,1,0,2:T(2,128)S(1)} %get-tuple-element.72), channel_id=1, source_target_pairs={{0,1},{2,3},{4,5},{6,7},{8,9},{10,11},{12,13},{14,15},{16,17},{18,... | collective-permute-start | bytes 584 | tf_op jit(solution)/shard_map/ppermute | solution.py:39
  74.7 4.1 %collective-permute-start.9 = (f32[2,2,4,3]{3,1,0,2:T(2,128)S(1)}, f32[2,2,4,3]{3,1,0,2:T(2,128)S(1)}, u32[]{:S(2)}, u32[]{:S(2)}) collective-permute-start(f32[2,2,4,3]{3,1,0,2:T(2,128)S(1)} %get-tuple-element.73), channel_id=1, source_target_pairs={{1,0},{3,2},{5,4},{7,6},{9,8},{11,10},{13,12},{15,14},{17,16},{19,... | collective-permute-start | bytes 584 | tf_op jit(solution)/shard_map/ppermute | solution.py:39
  77.3 7.3 %copy-start.3 = (f32[256,134]{1,0:T(8,128)S(1)}, f32[256,134]{1,0:T(8,128)}, u32[]{:S(2)}) copy-start(f32[256,134]{1,0:T(8,128)} %get-tuple-element.20) | copy-start | bytes 411652
  77.4 7.3 %copy-start.4 = (f32[256,134]{1,0:T(8,128)S(1)}, f32[256,134]{1,0:T(8,128)}, u32[]{:S(2)}) copy-start(f32[256,134]{1,0:T(8,128)} %get-tuple-element.21) | copy-start | bytes 411652
  77.4 7.3 %copy-start.5 = (f32[256,134]{1,0:T(8,128)S(1)}, f32[256,134]{1,0:T(8,128)}, u32[]{:S(2)}) copy-start(f32[256,134]{1,0:T(8,128)} %get-tuple-element.22) | copy-start | bytes 411652
  77.4 7.3 %copy-start.6 = (f32[256,134]{1,0:T(8,128)S(1)}, f32[256,134]{1,0:T(8,128)}, u32[]{:S(2)}) copy-start(f32[256,134]{1,0:T(8,128)} %get-tuple-element.23) | copy-start | bytes 411652
  78.9 13.0 %collective-permute-start.12 = (f32[2,2,3,134]{3,1,0,2:T(2,128)S(1)}, f32[2,2,3,134]{3,1,0,2:T(2,128)S(1)}, u32[]{:S(2)}, u32[]{:S(2)}) collective-permute-start(f32[2,2,3,134]{3,1,0,2:T(2,128)S(1)} %get-tuple-element.60), channel_id=1, source_target_pairs={{2,8},{4,10},{6,12},{10,16},{12,18},{14,20},{18,24},{20,26},{22,28... | collective-permute-start | bytes 19304 | tf_op jit(solution)/shard_map/ppermute | solution.py:40
  86.5 10.9 %collective-permute-start.11 = (f32[2,2,4,134]{3,1,0,2:T(2,128)S(1)}, f32[2,2,4,134]{3,1,0,2:T(2,128)S(1)}, u32[]{:S(2)}, u32[]{:S(2)}) collective-permute-start(f32[2,2,4,134]{3,1,0,2:T(2,128)S(1)} %pad_maximum_fusion.5), channel_id=1, source_target_pairs={{0,8},{2,10},{4,12},{6,14},{8,16},{10,18},{12,20},{14,22},{16,24},... | collective-permute-start | bytes 25736 | tf_op jit(solution)/shard_map/ppermute | solution.py:40
  90.0 7.4 %collective-permute-start.10 = (f32[2,2,3,134]{3,1,0,2:T(2,128)S(1)}, f32[2,2,3,134]{3,1,0,2:T(2,128)S(1)}, u32[]{:S(2)}, u32[]{:S(2)}) collective-permute-start(f32[2,2,3,134]{3,1,0,2:T(2,128)S(1)} %get-tuple-element.61), channel_id=1, source_target_pairs={{0,10},{2,12},{4,14},{8,18},{10,20},{12,22},{16,26},{18,28},{20,30... | collective-permute-start | bytes 19304 | tf_op jit(solution)/shard_map/ppermute | solution.py:40

commit v17 on v15

--- a/solution.py
+++ b/solution.py
@@ -133,16 +133,16 @@
         )
         top, _ = edges(0, cols)
         rhs = jnp.where(top, forcing + layer, forcing)
-        field_ref[...] = precond(rhs, 0, cols)
+        field_ref[s] = precond(rhs, 0, cols)
         for step in range(1, CORR + 1):
             a = (step * row) // lanes * lanes
             b = min(-(-((extent - step) * row) // lanes) * lanes, cols)
             lo = max(a - 2 * lanes, 0)
             hi = min(b + 2 * lanes, cols)
-            stencil = apply_a(field_ref[:, lo:hi], lo, hi)[:, a - lo : b - lo]
+            stencil = apply_a(field_ref[s, :, lo:hi], lo, hi)[:, a - lo : b - lo]
             residual = ins_ref[:, a:b] * (rhs[:, a:b] - stencil)
-            field_ref[:, a:b] = field_ref[:, a:b] + precond(residual, a, b)
-        u = field_ref[...]
+            field_ref[s, :, a:b] = field_ref[s, :, a:b] + precond(residual, a, b)
+        u = field_ref[s]
         for x in range(owned // lanes):
             begin = (x + width) * row + width
             chunk = pltpu.roll(u, cols - begin, 1)[:, :lanes]
@@ -153,7 +153,8 @@
                 trace_ref[s, part, pl.ds(x, 1), :] = chunk[bottom : bottom + 1, :]
         return carry
 
-    lax.fori_loop(0, nsrc, one_source, 0)
+    for s in range(nsrc):
+        one_source(s, 0)
 
 
 def run_tick(order, forcing, packed, incoming, ins, bhi, blo, row, depth, width, owned, tick, done):
@@ -170,7 +171,7 @@
         ),
         in_specs=[pl.BlockSpec(memory_space=pltpu.SMEM)] + [vmem] * (6 + (tick > 0)),
         out_specs=(vmem, vmem),
-        scratch_shapes=[pltpu.VMEM((rows, cols), jnp.float32)],
+        scratch_shapes=[pltpu.VMEM((nsrc, rows, cols), jnp.float32)],
         cost_estimate=pl.CostEstimate(
             flops=flops,
             transcendentals=0,

time: 110 us -> 109 us (level)
  no operation moved by 1% of the time
where the time goes in v17:
time: 109 us
  local copies, waits for them, and re-layouts  37.1 us (34%)
  starting transfers between devices  34.4 us (32%)
  Pallas kernels  22 us (20%)
  waiting for transfers between devices  7.54 us (7%)
  other arithmetic  6.33 us (6%)
  between operations  1.2 us (1%)
    ppermute x10, starting transfers between devices, fetch(): return lax.ppermute(block, axes[0], pairs)  23.4 us
    pallas_call x2, Pallas kernels, run_tick(): pl.pallas_call(functools.partial(tick_kernel, row=row, depth=depth, width...  22 us
    ppermute x3, starting transfers between devices, fetch(): return lax.ppermute(block, tuple(axes), pairs)  11 us
    ppermute x3, waiting for transfers between devices, fetch(): return lax.ppermute(block, tuple(axes), pairs)  5.22 us
    ppermute x4, local copies, waits for them, and re-layouts, fetch(): return lax.ppermute(block, axes[0], pairs)  4.5 us
    slice x2, local copies, waits for them, and re-layouts, per_device(): high_later = [fetch(r[:, :width, :], ('tx',), (1,)) for r in later]  3.58 us
    concatenate x1, local copies, waits for them, and re-layouts, per_device(): packed = jnp.concatenate(segments, axis=-1)  3.31 us
    slice x2, local copies, waits for them, and re-layouts, per_device(): corner_low = fetch(rims[..., ny - width:], ('ty',), (-1,))  3.27 us
  transfers between devices with their start and end apart: 13, of which 2 were waited for; matrix products, arithmetic and copies ran while one was open for 33% of the time, Pallas kernels for 10%

profile of v17, /device:TPU:12, one launch (start us, length us, event | category | flops | bytes accessed | tf_op | source)
XLA Modules:
  0.0 108.6 jit_solution(15664751925632934611)
XLA Ops:
  0.7 1.3 %fusion.4 = (f32[1,2,2,64,4,128]{5,4,3,2,1,0:T(4,128)S(1)}, f32[1,2,2,64,4,128]{5,4,3,2,1,0:T(4,128)S(1)}) fusion(f32[2,2,2,64,4,128]{5,4,3,2,1,0:T(4,128)} %param.6), kind=kLoop, calls=%fused_computation.57 | loop fusion | bytes 2097152 | tf_op jit(solution)/shard_map/slice | solution.py:210
  2.2 1.0 fusion.6
  3.2 3.4 %collective-permute-start = (f32[325,3,128]{2,0,1:T(8,128)}, f32[325,3,128]{2,0,1:T(8,128)S(1)}, u32[]{:S(2)}, u32[]{:S(2)}) collective-permute-start(f32[325,3,128]{2,0,1:T(8,128)} %get-tuple-element.49), channel_id=1, source_target_pairs={{0,2},{2,4},{4,6},{1,3},{3,5},{5,7},{8,10},{10,12},{12,14},{9,11},... | collective-permute-start | bytes 1497608 | tf_op jit(solution)/shard_map/ppermute | solution.py:39
  6.6 3.3 %collective-permute-start.1 = (f32[325,3,128]{2,0,1:T(8,128)}, f32[325,3,128]{2,0,1:T(8,128)S(1)}, u32[]{:S(2)}, u32[]{:S(2)}) collective-permute-start(f32[325,3,128]{2,0,1:T(8,128)} %get-tuple-element.48), channel_id=1, source_target_pairs={{2,0},{4,2},{6,4},{3,1},{5,3},{7,5},{10,8},{12,10},{14,12},{11,9},... | collective-permute-start | bytes 1497608 | tf_op jit(solution)/shard_map/ppermute | solution.py:39
  10.0 0.5 concatenate.42
  10.5 1.4 %fusion.3 = (f32[581,4,3]{2,0,1:T(8,128)}, f32[581,4,3]{2,0,1:T(8,128)S(1)}) fusion(f32[581,4,128]{2,0,1:T(8,128)S(1)} %concatenate.42), kind=kLoop, calls=%fused_computation.56 | loop fusion | bytes 111552 | tf_op jit(solution)/shard_map/slice | solution.py:45
  12.0 1.7 %copy.29 = f32[581,4,3]{0,1,2:T(4,128)S(1)} copy(f32[581,4,3]{2,0,1:T(8,128)} %get-tuple-element.36) | data formatting | bytes 55776 | tf_op jit(solution)/shard_map/slice | solution.py:45
  13.6 1.4 %collective-permute-start.4 = (f32[581,4,3]{0,1,2:T(4,128)S(1)}, f32[581,4,3]{0,1,2:T(4,128)S(1)}, u32[]{:S(2)}, u32[]{:S(2)}) collective-permute-start(f32[581,4,3]{0,1,2:T(4,128)S(1)} %copy.29), channel_id=1, source_target_pairs={{0,1},{2,3},{4,5},{6,7},{8,9},{10,11},{12,13},{14,15},{16,17},{18,... | collective-permute-start | bytes 83672 | tf_op jit(solution)/shard_map/ppermute | solution.py:39
  15.1 0.4 copy.30
  15.5 1.3 %collective-permute-start.5 = (f32[581,4,3]{0,1,2:T(4,128)S(1)}, f32[581,4,3]{0,1,2:T(4,128)S(1)}, u32[]{:S(2)}, u32[]{:S(2)}) collective-permute-start(f32[581,4,3]{0,1,2:T(4,128)S(1)} %copy.30), channel_id=1, source_target_pairs={{1,0},{3,2},{5,4},{7,6},{9,8},{11,10},{13,12},{15,14},{17,16},{19,... | collective-permute-start | bytes 83672 | tf_op jit(solution)/shard_map/ppermute | solution.py:39
  16.8 1.0 copy.47
  17.8 0.1 maximum_maximum_fusion
  18.0 0.1 broadcast_and_fusion
  18.1 0.1 convert_element_type.24
  18.2 0.6 pad_convert_fusion.ins_ref
  18.8 0.6 slice_bitcast_fusion.36
  19.4 0.7 fusion
  20.1 0.0 collective-permute-done.4
  20.1 0.4 copy.31
  20.5 0.0 collective-permute-done.5
  20.5 1.5 %copy.32 = f32[581,4,3]{2,0,1:T(8,128)} copy(f32[581,4,3]{0,1,2:T(4,128)S(1)} %collective-permute-done.5) | data formatting | bytes 55776 | tf_op jit(solution)/shard_map/ppermute | solution.py:39
  22.0 2.3 %pad_maximum_fusion = f32[581,4,134]{2,0,1:T(8,128)S(1)} fusion(f32[581,4,3]{2,0,1:T(8,128)} %copy.32, f32[581,4,128]{2,0,1:T(8,128)S(1)} %concatenate.42, f32[581,4,3]{2,0,1:T(8,128)S(1)} %copy.31), kind=kLoop, calls=%fused_computation | loop fusion | flops 622832 | bytes 2491328 | tf_op jit(solution)/shard_map/concatenate | solution.py:47
  24.2 1.4 %fusion.2 = (f32[256,3,134]{2,0,1:T(8,128)}, f32[256,3,134]{2,0,1:T(8,128)}) fusion(f32[581,4,134]{2,0,1:T(8,128)S(1)} %pad_maximum_fusion), kind=kLoop, calls=%fused_computation.55 | loop fusion | bytes 1646592 | tf_op jit(solution)/shard_map/slice | solution.py:252
  25.7 0.0 collective-permute-done
  25.7 0.4 copy-done
  26.1 2.3 %collective-permute-done.1 = f32[325,3,128]{2,0,1:T(8,128)S(1)} collective-permute-done((f32[325,3,128]{2,0,1:T(8,128)}, f32[325,3,128]{2,0,1:T(8,128)S(1)}, u32[]{:S(2)}, u32[]{:S(2)}) %collective-permute-start.1) | collective-permute-done | bytes 499232 | tf_op jit(solution)/shard_map/ppermute | solution.py:39
  28.5 1.6 %fusion.5 = (f32[325,6,3]{2,0,1:T(8,128)}, f32[325,6,3]{2,0,1:T(8,128)}) fusion(f32[325,6,128]{2,0,1:T(8,128)S(1)} %constant_dynamic-update-slice_fusion), kind=kLoop, calls=%fused_computation.58 | loop fusion | bytes 93600 | tf_op jit(solution)/shard_map/slice | solution.py:223
  30.1 1.7 %copy.23 = f32[325,6,3]{0,1,2:T(8,128)S(1)} copy(f32[325,6,3]{2,0,1:T(8,128)} %get-tuple-element.40) | data formatting | bytes 46800 | tf_op jit(solution)/shard_map/slice | solution.py:223
  31.8 1.3 %collective-permute-start.2 = (f32[325,6,3]{0,1,2:T(8,128)S(1)}, f32[325,6,3]{0,1,2:T(8,128)S(1)}, u32[]{:S(2)}, u32[]{:S(2)}) collective-permute-start(f32[325,6,3]{0,1,2:T(8,128)S(1)} %copy.23), channel_id=1, source_target_pairs={{0,1},{2,3},{4,5},{6,7},{8,9},{10,11},{12,13},{14,15},{16,17},{18,... | collective-permute-start | bytes 70208 | tf_op jit(solution)/shard_map/ppermute | solution.py:39
  33.1 1.7 %copy.24 = f32[325,6,3]{0,1,2:T(8,128)S(1)} copy(f32[325,6,3]{2,0,1:T(8,128)} %get-tuple-element.41) | data formatting | bytes 46800 | tf_op jit(solution)/shard_map/slice | solution.py:224
  34.7 1.3 %collective-permute-start.3 = (f32[325,6,3]{0,1,2:T(8,128)S(1)}, f32[325,6,3]{0,1,2:T(8,128)S(1)}, u32[]{:S(2)}, u32[]{:S(2)}) collective-permute-start(f32[325,6,3]{0,1,2:T(8,128)S(1)} %copy.24), channel_id=1, source_target_pairs={{1,0},{3,2},{5,4},{7,6},{9,8},{11,10},{13,12},{15,14},{17,16},{19,... | collective-permute-start | bytes 70208 | tf_op jit(solution)/shard_map/ppermute | solution.py:39
  36.1 1.0 slice_bitcast_fusion.13
  37.1 2.1 %copy.34 = f32[256,3,134]{0,2,1:T(8,128)} copy(f32[256,3,134]{2,0,1:T(8,128)} %get-tuple-element.25) | data formatting | bytes 823296 | tf_op jit(solution)/shard_map/slice | solution.py:251
  39.2 2.0 %collective-permute-start.6 = (f32[256,3,134]{0,2,1:T(8,128)}, f32[256,3,134]{0,2,1:T(8,128)}, u32[]{:S(2)}, u32[]{:S(2)}) collective-permute-start(f32[256,3,134]{0,2,1:T(8,128)} %copy.34), channel_id=1, source_target_pairs={{0,2},{2,4},{4,6},{1,3},{3,5},{5,7},{8,10},{10,12},{12,14},{9,11},... | collective-permute-start | bytes 1234952 | tf_op jit(solution)/shard_map/ppermute | solution.py:39
  41.2 2.1 %copy.35 = f32[256,3,134]{0,2,1:T(8,128)} copy(f32[256,3,134]{2,0,1:T(8,128)} %get-tuple-element.24) | data formatting | bytes 823296 | tf_op jit(solution)/shard_map/slice | solution.py:252
  43.4 5.3 %collective-permute-start.7 = (f32[256,3,134]{0,2,1:T(8,128)}, f32[256,3,134]{0,2,1:T(8,128)}, u32[]{:S(2)}, u32[]{:S(2)}) collective-permute-start(f32[256,3,134]{0,2,1:T(8,128)} %copy.35), channel_id=1, source_target_pairs={{2,0},{4,2},{6,4},{3,1},{5,3},{7,5},{10,8},{12,10},{14,12},{11,9},... | collective-permute-start | bytes 1234952 | tf_op jit(solution)/shard_map/ppermute | solution.py:39
  48.7 0.0 collective-permute-done.2
  48.7 1.3 %copy.25 = f32[325,6,3]{2,0,1:T(8,128)} copy(f32[325,6,3]{0,1,2:T(8,128)S(1)} %collective-permute-done.2) | data formatting | bytes 46800 | tf_op jit(solution)/shard_map/ppermute | solution.py:39
  50.0 0.0 collective-permute-done.3
  50.0 1.3 %copy.26 = f32[325,6,3]{2,0,1:T(8,128)} copy(f32[325,6,3]{0,1,2:T(8,128)S(1)} %collective-permute-done.3) | data formatting | bytes 46800 | tf_op jit(solution)/shard_map/ppermute | solution.py:39
  51.3 2.4 %pad_maximum_fusion.1 = f32[325,6,134]{2,0,1:T(8,128)S(1)} fusion(f32[325,6,3]{2,0,1:T(8,128)} %copy.26, f32[325,6,128]{2,0,1:T(8,128)S(1)} %constant_dynamic-update-slice_fusion, f32[325,6,3]{2,0,1:T(8,128)} %copy.25), kind=kLoop, calls=%fused_computation.1 | loop fusion | flops 522600 | bytes 2090400 | tf_op jit(solution)/shard_map/concatenate | solution.py:225
  53.7 1.6 %slice_bitcast_fusion = (f32[325,134]{1,0:T(8,128)S(1)}, f32[325,134]{1,0:T(8,128)S(1)}, f32[325,134]{1,0:T(8,128)}, f32[325,134]{1,0:T(8,128)}, f32[325,134]{1,...) fusion(f32[325,6,134]{2,0,1:T(8,128)S(1)} %pad_maximum_fusion.1, ...), kind=kLoop, calls=%fused_computation.5 | loop fusion | bytes 3484000 | tf_op jit(solution)/shard_map/squeeze | solution.py:233
  55.2 3.3 %concatenate.44.frc_ref.pk_ref = f32[325,1408]{1,0:T(8,128)S(1)} concatenate(f32[325,134]{1,0:T(8,128)} %get-tuple-element.35, f32[325,134]{1,0:T(8,128)} %get-tuple-element.34, f32[325,134]{1,0:T(8,128)} %get-tuple-element.33, f32[325,134]{1,0:T(8,128)} %get-tuple-element.74, f32[325,134]{1,0:T(8,128)} %get-tuple-element.75, f32[325,134]{1,0:T(8,128)} %get-tuple-element.76, ...), dimensions={1} | concatenate | bytes 3660800 | tf_op jit(solution)/shard_map/concatenate | solution.py:235
  58.6 0.7 reshape.62.inc_ref
  59.3 0.5 copy-done.2
  59.8 10.9 %shard_map.77 = (f32[1,2,2,64,4,128]{5,4,3,2,1,0:T(4,128)}, f32[2,2,4,128]{3,2,1,0:T(4,128)}) custom-call(s32[2]{0:T(128)} %get-tuple-element.72.order_ref, f32[325,1408]{1,0:T(8,128)} %copy-done.2, f32[325,1408]{1,0:T(8,128)} %copy-done.2, f32[2,2,1408]{2,1,0:T(2,128)} %reshape.62.inc_ref, f32[1,1408]{1,0:T(1,128)} %pad_convert_fusion.ins_ref, ...), custom_call_target="tpu_custom_call" | custom-call | flops 4429185024 | bytes 2812288 | tf_op jit(solution)/shard_map/pallas_call | solution.py:166
  70.7 0.7 copy.42
  71.4 0.1 fusion.8
  71.5 2.8 %collective-permute-start.8 = (f32[2,2,4,3]{3,1,0,2:T(2,128)S(1)}, f32[2,2,4,3]{3,1,0,2:T(2,128)S(1)}, u32[]{:S(2)}, u32[]{:S(2)}) collective-permute-start(f32[2,2,4,3]{3,1,0,2:T(2,128)S(1)} %get-tuple-element.70), channel_id=1, source_target_pairs={{0,1},{2,3},{4,5},{6,7},{8,9},{10,11},{12,13},{14,15},{16,17},{18,... | collective-permute-start | bytes 584 | tf_op jit(solution)/shard_map/ppermute | solution.py:39
  74.3 1.3 %collective-permute-start.9 = (f32[2,2,4,3]{3,1,0,2:T(2,128)S(1)}, f32[2,2,4,3]{3,1,0,2:T(2,128)S(1)}, u32[]{:S(2)}, u32[]{:S(2)}) collective-permute-start(f32[2,2,4,3]{3,1,0,2:T(2,128)S(1)} %get-tuple-element.71), channel_id=1, source_target_pairs={{1,0},{3,2},{5,4},{7,6},{9,8},{11,10},{13,12},{15,14},{17,16},{19,... | collective-permute-start | bytes 584 | tf_op jit(solution)/shard_map/ppermute | solution.py:39
  75.6 1.3 %copy.39 = f32[256,3,134]{2,0,1:T(8,128)S(1)} copy(f32[256,3,134]{0,2,1:T(8,128)} %collective-permute-done.7) | data formatting | bytes 823296 | tf_op jit(solution)/shard_map/optimization_barrier | solution.py:263
  76.9 0.1 slice_bitcast_fusion.10
  77.0 1.3 %copy.36 = f32[256,3,134]{2,0,1:T(8,128)S(1)} copy(f32[256,3,134]{0,2,1:T(8,128)} %collective-permute-done.6) | data formatting | bytes 823296 | tf_op jit(solution)/shard_map/optimization_barrier | solution.py:263
  78.3 0.0 collective-permute-done.9
  78.3 0.1 pad_maximum_fusion.4
  78.4 5.4 %collective-permute-start.12 = (f32[2,2,3,134]{3,1,0,2:T(2,128)S(1)}, f32[2,2,3,134]{3,1,0,2:T(2,128)S(1)}, u32[]{:S(2)}, u32[]{:S(2)}) collective-permute-start(f32[2,2,3,134]{3,1,0,2:T(2,128)S(1)} %get-tuple-element.58), channel_id=1, source_target_pairs={{2,8},{4,10},{6,12},{10,16},{12,18},{14,20},{18,24},{20,26},{22,28... | collective-permute-start | bytes 19304 | tf_op jit(solution)/shard_map/ppermute | solution.py:40
  83.9 0.1 slice_bitcast_fusion.17
  84.0 1.8 %concatenate.49.frc_ref = f32[256,1408]{1,0:T(8,128)} concatenate(f32[256,134]{1,0:T(8,128)S(1)} %get-tuple-element.47, f32[256,134]{1,0:T(8,128)S(1)} %get-tuple-element.46, f32[256,134]{1,0:T(8,128)S(1)} %get-tuple-element.45, f32[256,134]{1,0:T(8,128)S(1)} %copy-done.6, f32[256,134]{1,0:T(8,128)S(1)} %copy-done.5, f32[256,134]{1,0:T(8,128)S(1)} %copy-done.4, ...), dimensions={1} | concatenate | bytes 2883584 | tf_op jit(solution)/shard_map/concatenate | solution.py:268
  85.8 3.5 %collective-permute-start.11 = (f32[2,2,4,134]{3,1,0,2:T(2,128)S(1)}, f32[2,2,4,134]{3,1,0,2:T(2,128)S(1)}, u32[]{:S(2)}, u32[]{:S(2)}) collective-permute-start(f32[2,2,4,134]{3,1,0,2:T(2,128)S(1)} %pad_maximum_fusion.4), channel_id=1, source_target_pairs={{0,8},{2,10},{4,12},{6,14},{8,16},{10,18},{12,20},{14,22},{16,24},... | collective-permute-start | bytes 25736 | tf_op jit(solution)/shard_map/ppermute | solution.py:40
  89.3 2.1 %collective-permute-start.10 = (f32[2,2,3,134]{3,1,0,2:T(2,128)S(1)}, f32[2,2,3,134]{3,1,0,2:T(2,128)S(1)}, u32[]{:S(2)}, u32[]{:S(2)}) collective-permute-start(f32[2,2,3,134]{3,1,0,2:T(2,128)S(1)} %get-tuple-element.59), channel_id=1, source_target_pairs={{0,10},{2,12},{4,14},{8,18},{10,20},{12,22},{16,26},{18,28},{20,30... | collective-permute-start | bytes 19304 | tf_op jit(solution)/shard_map/ppermute | solution.py:40
  91.4 0.0 collective-permute-done.12
  91.5 5.2 %collective-permute-done.10 = f32[2,2,3,134]{3,1,0,2:T(2,128)S(1)} collective-permute-done((f32[2,2,3,134]{3,1,0,2:T(2,128)S(1)}, f32[2,2,3,134]{3,1,0,2:T(2,128)S(1)}, u32[]{:S(2)}, u32[]{:S(2)}) %collective-permute-start.10) | collective-permute-done | bytes 6464 | tf_op jit(solution)/shard_map/ppermute | solution.py:40
  96.7 0.8 concatenate.51.inc_ref
  97.4 11.2 %shard_map.78 = (f32[2,2,2,64,4,128]{5,4,3,2,1,0:T(4,128)}, f32[2,2,4,128]{3,2,1,0:T(4,128)}) custom-call(s32[2]{0:T(128)} %get-tuple-element.73.order_ref, f32[256,1408]{1,0:T(8,128)} %concatenate.49.frc_ref, f32[325,1408]{1,0:T(8,128)} %copy-done.2, f32[2,2,1408]{2,1,0:T(2,128)} %concatenate.51.inc_ref, f32[1,1408]{1,0:T(1,128)} %pad_convert_fusion.ins_ref, ...), custom_call_target="tpu_custom_call" | custom-call | flops 4429185024 | bytes 2423680 | tf_op jit(solution)/shard_map/pallas_call | solution.py:166
  (45 shorter events, 0.4 us)
Async XLA Ops:
  0.6 1.4 %copy-start.7 = (f32[64,4,128]{2,1,0:T(4,128)S(1)}, f32[64,4,128]{2,1,0:T(4,128)}, u32[]{:S(2)}) copy-start(f32[64,4,128]{2,1,0:T(4,128)} %param.7) | copy-start | bytes 393220
  0.6 1.4 %copy-start.8 = (f32[2,2,1,4,128]{4,3,2,1,0:T(4,128)S(1)}, f32[2,2,1,4,128]{4,3,2,1,0:T(4,128)}, u32[]{:S(2)}) copy-start(f32[2,2,1,4,128]{4,3,2,1,0:T(4,128)} %param.11) | copy-start | bytes 24580
  0.7 1.5 %copy-start.9 = (s32[1,4,128]{2,1,0:T(4,128)S(1)}, s32[1,4,128]{2,1,0:T(4,128)}, u32[]{:S(2)}) copy-start(s32[1,4,128]{2,1,0:T(4,128)} %param.9) | copy-start | bytes 6148
  3.2 22.5 %collective-permute-start = (f32[325,3,128]{2,0,1:T(8,128)}, f32[325,3,128]{2,0,1:T(8,128)S(1)}, u32[]{:S(2)}, u32[]{:S(2)}) collective-permute-start(f32[325,3,128]{2,0,1:T(8,128)} %get-tuple-element.49), channel_id=1, source_target_pairs={{0,2},{2,4},{4,6},{1,3},{3,5},{5,7},{8,10},{10,12},{12,14},{9,11},... | collective-permute-start | bytes 1497608 | tf_op jit(solution)/shard_map/ppermute | solution.py:39
  6.6 21.8 %collective-permute-start.1 = (f32[325,3,128]{2,0,1:T(8,128)}, f32[325,3,128]{2,0,1:T(8,128)S(1)}, u32[]{:S(2)}, u32[]{:S(2)}) collective-permute-start(f32[325,3,128]{2,0,1:T(8,128)} %get-tuple-element.48), channel_id=1, source_target_pairs={{2,0},{4,2},{6,4},{3,1},{5,3},{7,5},{10,8},{12,10},{14,12},{11,9},... | collective-permute-start | bytes 1497608 | tf_op jit(solution)/shard_map/ppermute | solution.py:39
  13.6 5.2 %copy-start.10 = (s32[2,1,2]{2,1,0:T(1,128)S(1)}, s32[2,1,2]{2,1,0:T(1,128)}, u32[]{:S(2)}) copy-start(s32[2,1,2]{2,1,0:T(1,128)} %param.10) | copy-start | bytes 52
  13.6 6.5 %collective-permute-start.4 = (f32[581,4,3]{0,1,2:T(4,128)S(1)}, f32[581,4,3]{0,1,2:T(4,128)S(1)}, u32[]{:S(2)}, u32[]{:S(2)}) collective-permute-start(f32[581,4,3]{0,1,2:T(4,128)S(1)} %copy.29), channel_id=1, source_target_pairs={{0,1},{2,3},{4,5},{6,7},{8,9},{10,11},{12,13},{14,15},{16,17},{18,... | collective-permute-start | bytes 83672 | tf_op jit(solution)/shard_map/ppermute | solution.py:39
  15.5 5.0 %collective-permute-start.5 = (f32[581,4,3]{0,1,2:T(4,128)S(1)}, f32[581,4,3]{0,1,2:T(4,128)S(1)}, u32[]{:S(2)}, u32[]{:S(2)}) collective-permute-start(f32[581,4,3]{0,1,2:T(4,128)S(1)} %copy.30), channel_id=1, source_target_pairs={{1,0},{3,2},{5,4},{7,6},{9,8},{11,10},{13,12},{15,14},{17,16},{19,... | collective-permute-start | bytes 83672 | tf_op jit(solution)/shard_map/ppermute | solution.py:39
  24.2 1.9 %copy-start = (f32[581,4,134]{2,0,1:T(8,128)}, f32[581,4,134]{2,0,1:T(8,128)S(1)}, u32[]{:S(2)}) copy-start(f32[581,4,134]{2,0,1:T(8,128)S(1)} %pad_maximum_fusion) | copy-start | bytes 3736996
  28.5 7.6 %copy-start.1 = (f32[581,4,134]{2,0,1:T(8,128)S(1)}, f32[581,4,134]{2,0,1:T(8,128)}, u32[]{:S(2)}) copy-start(f32[581,4,134]{2,0,1:T(8,128)} %copy-done) | copy-start | bytes 3736996
  31.8 16.9 %collective-permute-start.2 = (f32[325,6,3]{0,1,2:T(8,128)S(1)}, f32[325,6,3]{0,1,2:T(8,128)S(1)}, u32[]{:S(2)}, u32[]{:S(2)}) collective-permute-start(f32[325,6,3]{0,1,2:T(8,128)S(1)} %copy.23), channel_id=1, source_target_pairs={{0,1},{2,3},{4,5},{6,7},{8,9},{10,11},{12,13},{14,15},{16,17},{18,... | collective-permute-start | bytes 70208 | tf_op jit(solution)/shard_map/ppermute | solution.py:39
  34.7 15.2 %collective-permute-start.3 = (f32[325,6,3]{0,1,2:T(8,128)S(1)}, f32[325,6,3]{0,1,2:T(8,128)S(1)}, u32[]{:S(2)}, u32[]{:S(2)}) collective-permute-start(f32[325,6,3]{0,1,2:T(8,128)S(1)} %copy.24), channel_id=1, source_target_pairs={{1,0},{3,2},{5,4},{7,6},{9,8},{11,10},{13,12},{15,14},{17,16},{19,... | collective-permute-start | bytes 70208 | tf_op jit(solution)/shard_map/ppermute | solution.py:39
  39.2 36.3 %collective-permute-start.6 = (f32[256,3,134]{0,2,1:T(8,128)}, f32[256,3,134]{0,2,1:T(8,128)}, u32[]{:S(2)}, u32[]{:S(2)}) collective-permute-start(f32[256,3,134]{0,2,1:T(8,128)} %copy.34), channel_id=1, source_target_pairs={{0,2},{2,4},{4,6},{1,3},{3,5},{5,7},{8,10},{10,12},{12,14},{9,11},... | collective-permute-start | bytes 1234952 | tf_op jit(solution)/shard_map/ppermute | solution.py:39
  43.4 32.2 %collective-permute-start.7 = (f32[256,3,134]{0,2,1:T(8,128)}, f32[256,3,134]{0,2,1:T(8,128)}, u32[]{:S(2)}, u32[]{:S(2)}) collective-permute-start(f32[256,3,134]{0,2,1:T(8,128)} %copy.35), channel_id=1, source_target_pairs={{2,0},{4,2},{6,4},{3,1},{5,3},{7,5},{10,8},{12,10},{14,12},{11,9},... | collective-permute-start | bytes 1234952 | tf_op jit(solution)/shard_map/ppermute | solution.py:39
  58.6 1.3 %copy-start.2 = (f32[325,1408]{1,0:T(8,128)}, f32[325,1408]{1,0:T(8,128)S(1)}, u32[]{:S(2)}) copy-start(f32[325,1408]{1,0:T(8,128)S(1)} %concatenate.44.frc_ref.pk_ref) | copy-start | bytes 5491204
  71.5 6.8 %collective-permute-start.8 = (f32[2,2,4,3]{3,1,0,2:T(2,128)S(1)}, f32[2,2,4,3]{3,1,0,2:T(2,128)S(1)}, u32[]{:S(2)}, u32[]{:S(2)}) collective-permute-start(f32[2,2,4,3]{3,1,0,2:T(2,128)S(1)} %get-tuple-element.70), channel_id=1, source_target_pairs={{0,1},{2,3},{4,5},{6,7},{8,9},{10,11},{12,13},{14,15},{16,17},{18,... | collective-permute-start | bytes 584 | tf_op jit(solution)/shard_map/ppermute | solution.py:39
  74.3 4.1 %collective-permute-start.9 = (f32[2,2,4,3]{3,1,0,2:T(2,128)S(1)}, f32[2,2,4,3]{3,1,0,2:T(2,128)S(1)}, u32[]{:S(2)}, u32[]{:S(2)}) collective-permute-start(f32[2,2,4,3]{3,1,0,2:T(2,128)S(1)} %get-tuple-element.71), channel_id=1, source_target_pairs={{1,0},{3,2},{5,4},{7,6},{9,8},{11,10},{13,12},{15,14},{17,16},{19,... | collective-permute-start | bytes 584 | tf_op jit(solution)/shard_map/ppermute | solution.py:39
  76.9 7.1 %copy-start.3 = (f32[256,134]{1,0:T(8,128)S(1)}, f32[256,134]{1,0:T(8,128)}, u32[]{:S(2)}) copy-start(f32[256,134]{1,0:T(8,128)} %get-tuple-element.20) | copy-start | bytes 411652
  76.9 7.1 %copy-start.4 = (f32[256,134]{1,0:T(8,128)S(1)}, f32[256,134]{1,0:T(8,128)}, u32[]{:S(2)}) copy-start(f32[256,134]{1,0:T(8,128)} %get-tuple-element.21) | copy-start | bytes 411652
  76.9 7.1 %copy-start.5 = (f32[256,134]{1,0:T(8,128)S(1)}, f32[256,134]{1,0:T(8,128)}, u32[]{:S(2)}) copy-start(f32[256,134]{1,0:T(8,128)} %get-tuple-element.22) | copy-start | bytes 411652
  76.9 7.1 %copy-start.6 = (f32[256,134]{1,0:T(8,128)S(1)}, f32[256,134]{1,0:T(8,128)}, u32[]{:S(2)}) copy-start(f32[256,134]{1,0:T(8,128)} %get-tuple-element.23) | copy-start | bytes 411652
  78.4 13.0 %collective-permute-start.12 = (f32[2,2,3,134]{3,1,0,2:T(2,128)S(1)}, f32[2,2,3,134]{3,1,0,2:T(2,128)S(1)}, u32[]{:S(2)}, u32[]{:S(2)}) collective-permute-start(f32[2,2,3,134]{3,1,0,2:T(2,128)S(1)} %get-tuple-element.58), channel_id=1, source_target_pairs={{2,8},{4,10},{6,12},{10,16},{12,18},{14,20},{18,24},{20,26},{22,28... | collective-permute-start | bytes 19304 | tf_op jit(solution)/shard_map/ppermute | solution.py:40
  85.8 10.9 %collective-permute-start.11 = (f32[2,2,4,134]{3,1,0,2:T(2,128)S(1)}, f32[2,2,4,134]{3,1,0,2:T(2,128)S(1)}, u32[]{:S(2)}, u32[]{:S(2)}) collective-permute-start(f32[2,2,4,134]{3,1,0,2:T(2,128)S(1)} %pad_maximum_fusion.4), channel_id=1, source_target_pairs={{0,8},{2,10},{4,12},{6,14},{8,16},{10,18},{12,20},{14,22},{16,24},... | collective-permute-start | bytes 25736 | tf_op jit(solution)/shard_map/ppermute | solution.py:40
  89.3 7.4 %collective-permute-start.10 = (f32[2,2,3,134]{3,1,0,2:T(2,128)S(1)}, f32[2,2,3,134]{3,1,0,2:T(2,128)S(1)}, u32[]{:S(2)}, u32[]{:S(2)}) collective-permute-start(f32[2,2,3,134]{3,1,0,2:T(2,128)S(1)} %get-tuple-element.59), channel_id=1, source_target_pairs={{0,10},{2,12},{4,14},{8,18},{10,20},{12,22},{16,26},{18,28},{20,30... | collective-permute-start | bytes 19304 | tf_op jit(solution)/shard_map/ppermute | solution.py:40
